TPU v7x, 256 devices: a whole 4x4x8 slice. The times are simulated.
256 devices in a mesh: curve: 16 (over y, x), line: 16 (over z, core).
Axes of the slice: x: 4, y: 4, z: 8, core: 2. Of those that a mesh axis runs over, the one named last changes fastest.
Arguments:
- scaled_distributions: float32 [16, 16, 6, 27, 512], P('curve', 'line'), may hold values from 0.1 to 2.5, as said below
- remaining_brick_places: int32 [16, 16, 6], P('curve', 'line'), may hold values from -1 to 7, as said below
- retained_wavenumbers: int32 [8], replicated, may hold values from 1 to 16, as said below
- regional_amplitudes: float32 [3, 2, 512, 16], P(None, None, 'curve'), may hold values from -0.12 to 0.12
- relaxation_frequencies: float32 [27], replicated, may hold values from 0.6 to 1.8
Outputs:
- new_populations: float32 [16, 16, 6, 27, 512], P('curve', 'line')
Inputs may be any that keep to these rules, and one draw needn't show every extreme that they name: `scaled_distributions`: positive values. `remaining_brick_places`: distinct tile positions (row of the block times 4 plus its column) of one device's surviving blocks, -1 in empty slots, which may stand anywhere; at least half of each device's slots are used, and on some device all 6 are. `retained_wavenumbers`: distinct mode numbers; 16 is always among them.
All inputs are finite; a program needn't handle non-finite values.
Results may differ from a plain program's by a relative error of at most 0.0003.
Values sent between devices are 32-bit elements; how exact they have to be, the bound alone decides.
No kernel may reach another device: no remote copies, remote signals or barrier semaphores. Data moves between devices by JAX's collectives and lax.ppermute only.
A program may use at most 64 MiB of HBM per device.

v0:
```python
import jax
import jax.numpy as jnp
import numpy as np
from jax import lax
from jax.sharding import PartitionSpec as P

BE = 16
TX = 4
TY = 2


NUDGE_GAIN = 0.5
TWO_PI = 6.283185307179586
HIGHEST = lax.Precision.HIGHEST


def with_halo(block, sides, width):
    for axis, dim in sides:
        count = lax.axis_size(axis)
        forward = [(i, i + 1) for i in range(count - 1)]
        forward.append((count - 1, 0))
        backward = [(target, source) for source, target in forward]
        low = lax.ppermute(
            lax.slice_in_dim(block, block.shape[dim] - width, None, axis=dim), axis, forward
        )
        high = lax.ppermute(lax.slice_in_dim(block, 0, width, axis=dim), axis, backward)
        block = jnp.concatenate([low, block, high], axis=dim)
    return block


def lattice_tables():
    one_weights = np.array([1.0 / 6.0, 2.0 / 3.0, 1.0 / 6.0])
    speeds = np.array(
        [
            [along_x - 1, along_y - 1, along_z - 1]
            for along_x in range(3)
            for along_y in range(3)
            for along_z in range(3)
        ]
    )
    weights = np.array(
        [
            one_weights[along_x] * one_weights[along_y] * one_weights[along_z]
            for along_x in range(3)
            for along_y in range(3)
            for along_z in range(3)
        ]
    )
    vander = np.array([[1.0, 1.0, 1.0], [-1.0, 0.0, 1.0], [1.0, 0.0, 1.0]])
    undo_vander = np.array([[0.0, -0.5, 0.5], [1.0, 0.0, -1.0], [0.0, 0.5, 0.5]])
    moment_matrix = np.kron(vander, np.kron(vander, vander))
    inverse = np.kron(undo_vander, np.kron(undo_vander, undo_vander))
    forward = jnp.asarray(moment_matrix * weights[None, :], dtype=jnp.float32)
    backward = jnp.asarray(inverse / weights[:, None], dtype=jnp.float32)
    return (forward, backward, speeds)


def mode_basis_at(mode_ids, positions, length):
    phase_ids = positions[:, None] * mode_ids[None, :] % length
    angles = phase_ids.astype(jnp.float32) * (TWO_PI / length)
    return jnp.concatenate([jnp.cos(angles), jnp.sin(angles)], axis=1)


def tile_velocity(moments, safe_density):
    return jnp.stack([moments[9], moments[3], moments[1]], axis=0) / safe_density[None]


def collide_tile(moments, velocity, nudge_tile, backward, relaxation_frequencies):
    density = moments[0]
    shifted = velocity + nudge_tile
    powers = jnp.stack([jnp.ones_like(shifted), shifted, shifted * shifted + 1.0 / 3.0], axis=0)
    equilibrium = (
        density[None, None, None]
        * powers[:, None, None, 0]
        * powers[None, :, None, 1]
        * powers[None, None, :, 2]
    )
    equilibrium = equilibrium.reshape(moments.shape)
    relaxed = moments - relaxation_frequencies[:, None, None, None] * (moments - equilibrium)
    return jnp.einsum("ij,jlrc->ilrc", backward, relaxed, precision=HIGHEST)


def slot_lookup(living_brick_keys, tile_blocks):
    positions = jnp.arange(tile_blocks, dtype=jnp.int32)
    matches = living_brick_keys[None, :] == positions[:, None]
    slot_numbers = jnp.arange(living_brick_keys.shape[0], dtype=jnp.int32)
    slot_of = jnp.sum(jnp.where(matches, slot_numbers[None, :], 0), axis=1)
    present = jnp.any(matches, axis=1)
    return (slot_of, present)


def compact_to_tile(packed_arrangement, slot_of, present, rows_blocks, cols_blocks, block_edge):
    channels = packed_arrangement.shape[1]
    levels = packed_arrangement.shape[2] // (block_edge * block_edge)
    picked = jnp.take(packed_arrangement, slot_of, axis=0) * present[:, None, None].astype(
        packed_arrangement.dtype
    )
    shaped = picked.reshape(rows_blocks, cols_blocks, channels, levels, block_edge, block_edge)
    return shaped.transpose(2, 3, 0, 4, 1, 5).reshape(
        channels, levels, rows_blocks * block_edge, cols_blocks * block_edge
    )


def tile_to_compact(tile_data, living_brick_keys, rows_blocks, cols_blocks, block_edge):
    channels = tile_data.shape[0]
    levels = tile_data.shape[1]
    shaped = tile_data.reshape(
        channels, levels, rows_blocks, block_edge, cols_blocks, block_edge
    ).transpose(2, 4, 0, 1, 3, 5)
    blocks = shaped.reshape(rows_blocks * cols_blocks, channels, levels * block_edge * block_edge)
    occupied_seats = living_brick_keys >= 0
    picked = jnp.take(blocks, jnp.maximum(living_brick_keys, 0), axis=0)
    return picked * occupied_seats[:, None, None].astype(tile_data.dtype)


def on_device(
    scaled_distributions,
    remaining_brick_places,
    retained_wavenumbers,
    regional_amplitudes,
    relaxation_frequencies,
):
    forward, backward, speeds = lattice_tables()
    slot_state = scaled_distributions[0, 0]
    living_brick_keys = remaining_brick_places[0, 0]
    rows_tile = TY * BE
    cols_tile = TX * BE
    slot_of, present = slot_lookup(living_brick_keys, TX * TY)
    fluid_map = present.reshape(TY, TX).astype(jnp.float32)
    fluid_map = jnp.repeat(jnp.repeat(fluid_map, BE, axis=0), BE, axis=1)
    solid_tile = 1.0 - fluid_map
    pops_tile = compact_to_tile(slot_state, slot_of, present, TY, TX, BE)
    moments = jnp.einsum("ij,jlrc->ilrc", forward, pops_tile, precision=HIGHEST)
    safe_density = jnp.where(fluid_map[None] > 0.5, moments[0], 1.0)
    wind_tile = tile_velocity(moments, safe_density)
    line_length = lax.axis_size("line") * cols_tile
    whole_lines = lax.all_to_all(wind_tile, "line", split_axis=2, concat_axis=3, tiled=True)
    rows_each = whole_lines.shape[2]
    mode_basis = mode_basis_at(
        retained_wavenumbers, jnp.arange(line_length, dtype=jnp.int32), line_length
    )
    coefficients = jnp.einsum("klrx,xm->klrm", whole_lines, mode_basis, precision=HIGHEST)
    target = lax.dynamic_slice_in_dim(
        regional_amplitudes, lax.axis_index("line") * rows_each, rows_each, 2
    )
    misfit = target - 2.0 / line_length * coefficients
    forcing_adjustment = NUDGE_GAIN * jnp.einsum(
        "klrm,xm->klrx", misfit, mode_basis, precision=HIGHEST
    )
    nudge_tile = lax.all_to_all(forcing_adjustment, "line", split_axis=3, concat_axis=2, tiled=True)
    post_tile = collide_tile(moments, wind_tile, nudge_tile, backward, relaxation_frequencies)
    levels = post_tile.shape[1]
    solid_plane = jnp.broadcast_to(solid_tile[None, None], (1, levels, rows_tile, cols_tile))
    extended = jnp.concatenate([post_tile, solid_plane], axis=0)
    padded = with_halo(extended, (("curve", 2), ("line", 3)), 1)
    pops_pad = padded[:27]
    solid_pad = padded[27, 0]
    read = []
    for discrete_heading in range(27):
        carry_eastward = int(speeds[discrete_heading, 0])
        carry_northward = int(speeds[discrete_heading, 1])
        step_z = int(speeds[discrete_heading, 2])
        rows_slice = slice(1 - carry_northward, 1 - carry_northward + rows_tile)
        cols_slice = slice(1 - carry_eastward, 1 - carry_eastward + cols_tile)
        carried_sheet = pops_pad[discrete_heading, :, rows_slice, cols_slice]
        blocked = solid_pad[rows_slice, cols_slice] > 0.5
        bounced_distributions = post_tile[26 - discrete_heading]
        if step_z == 0:
            source = carried_sheet
            block_both = jnp.stack([blocked, blocked])
        elif step_z == 1:
            source = jnp.stack([carried_sheet[0], carried_sheet[0]])
            block_both = jnp.stack([jnp.ones_like(blocked), blocked])
        else:
            mirror_sheet = pops_pad[discrete_heading + 2, 1, rows_slice, cols_slice]
            source = jnp.stack([carried_sheet[1], mirror_sheet])
            block_both = jnp.stack([blocked, blocked])
        read.append(jnp.where(block_both, bounced_distributions, source))
    read_tile = jnp.stack(read, axis=0)
    new_state = tile_to_compact(read_tile, living_brick_keys, TY, TX, BE)
    return new_state[None, None]


def solution(mesh):
    return jax.shard_map(
        on_device,
        mesh=mesh,
        in_specs=(
            P("curve", "line", None, None, None),
            P("curve", "line", None),
            P(),
            P(None, None, "curve", None),
            P(),
        ),
        out_specs=P("curve", "line", None, None, None),
        check_vma=False,
    )
```

profile of v0, /device:TPU:30, one launch (start us, length us, event | category | flops | bytes accessed | tf_op | source)
XLA Modules:
  0.0 132.9 jit_solution(11512532406489722994)
XLA Ops:
  2.3 1.0 copy.401
  4.8 2.9 %gather.13 = f32[2,4,27,2,16,16]{5,4,3,1,0,2:T(8,128)} reshape(f32[8,27,512]{2,0,1:T(8,128)S(1)} %copy.274) | data formatting | bytes 884736 | tf_op jit(solution)/shard_map/jit(_take)/gather | solution.py:95
  7.8 4.6 %multiply_bitcast_fusion = f32[27,2,2,16,4,16]{5,3,1,4,2,0:T(8,128)} fusion(f32[2,4,27,2,16,16]{5,4,3,1,0,2:T(8,128)} %gather.13, f32[2,4]{1,0:T(2,128)S(1)} %reshape.361, pred[2,4]{1,0:T(4,128)(4,1)S(1)} %compare_and_fusion), kind=kLoop, calls=%fused_computation.2 | loop fusion | flops 221184 | bytes 884776 | tf_op jit(solution)/shard_map/transpose | solution.py:99
  12.4 3.6 %copy.275 = f32[27,2,2,16,4,16]{0,5,4,3,2,1:T(8,128)S(1)} copy(f32[27,2,2,16,4,16]{5,3,1,4,2,0:T(8,128)} %multiply_bitcast_fusion) | data formatting | bytes 884736 | tf_op jit(solution)/shard_map/transpose | solution.py:99
  16.4 5.8 %fusion.58 = f32[27,2,32,64]{3,0,2,1:T(8,128)S(1)} fusion(f32[27,27,1,1]{1,0,3,2:T(8,128)S(1)} %copy-done.22, f32[27,2,32,64]{0,3,2,1:T(8,128)S(1)} %bitcast.189), kind=kOutput, calls=%fused_computation.237 | convolution fusion | flops 35831808 | bytes 887652 | tf_op jit(solution)/shard_map/ij,jlrc->ilrc/dot_general | solution.py:133
  23.3 8.6 %all-to-all-start = ((f32[16,1,768]{2,1,0:T(1,128)}), f32[16,1,768]{2,1,0:T(1,128)S(1)}, u32[]{:S(2)}, u32[]{:S(2)}) async-start(f32[16,1,768]{2,1,0:T(1,128)} %reshape.390), calls=%async_computation | async-start | bytes 98304 | tf_op jit(solution)/shard_map/all_to_all | solution.py:137
  32.3 7.3 %all-to-all-done = f32[16,1,768]{2,1,0:T(1,128)S(1)} async-done(((f32[16,1,768]{2,1,0:T(1,128)}), f32[16,1,768]{2,1,0:T(1,128)S(1)}, u32[]{:S(2)}, u32[]{:S(2)}) %all-to-all-start) | async-done | bytes 49184 | tf_op jit(solution)/shard_map/all_to_all | solution.py:137
  41.7 1.4 %copy.285 = f32[3,2,2,1024]{0,2,1,3:T(2,128)S(1)} copy(f32[3,2,2,1024]{3,0,2,1:T(4,128)S(1)} %convolution_multiply_fusion) | data formatting | bytes 98304 | tf_op jit(solution)/shard_map/mul | solution.py:147
  43.1 3.6 %reshape.392 = f32[16,1,768]{2,1,0:T(1,128)} reshape(f32[1024,2,2,3]{3,2,1,0:T(2,128)S(1)} %bitcast.187) | data formatting | bytes 98304
  46.7 3.7 %all-to-all-start.1 = ((f32[16,1,768]{2,1,0:T(1,128)}), f32[16,1,768]{2,1,0:T(1,128)S(1)}, u32[]{:S(2)}, u32[]{:S(2)}) async-start(f32[16,1,768]{2,1,0:T(1,128)} %reshape.392), calls=%async_computation.1 | async-start | bytes 98304 | tf_op jit(solution)/shard_map/all_to_all | solution.py:150
  50.7 7.1 %all-to-all-done.1 = f32[16,1,768]{2,1,0:T(1,128)S(1)} async-done(((f32[16,1,768]{2,1,0:T(1,128)}), f32[16,1,768]{2,1,0:T(1,128)S(1)}, u32[]{:S(2)}, u32[]{:S(2)}) %all-to-all-start.1) | async-done | bytes 49184 | tf_op jit(solution)/shard_map/all_to_all | solution.py:150
  58.6 3.1 %reshape.393 = f32[1024,2,2,3]{3,2,1,0:T(2,128)S(1)} reshape(f32[16,768]{1,0:T(8,128)S(1)} %reduce.5) | data formatting | bytes 98304
  61.7 1.6 %copy.359 = f32[3,2,2,16,64]{4,3,2,1,0:T(8,128)S(1)} copy(f32[3,2,2,16,64]{0,2,1,4,3:T(2,128)S(1)} %bitcast.188) | data formatting | bytes 98304 | tf_op jit(solution)/shard_map/all_to_all | solution.py:150
  63.7 1.5 %fusion.3 = f32[27,2,32,64]{3,0,2,1:T(8,128)S(1)} fusion(f32[27,27,1,1]{1,0,3,2:T(8,128)S(1)} %copy-done.21, f32[27,2,32,64]{3,0,2,1:T(8,128)S(1)} %fusion.58, f32[27,2,32,64]{3,2,1,0:T(8,128)S(1)} %bitcast.190, f32[27]{0:T(128)S(1)} %copy-done.26), kind=kOutput, calls=%fused_computation.10 | convolution fusion | flops 36163584 | bytes 1330128 | tf_op jit(solution)/shard_map/ij,jlrc->ilrc/dot_general | solution.py:80
  66.1 1.9 %collective-permute-start.1 = (f32[28,2,1,64]{3,2,1,0:T(1,128)S(1)}, f32[28,2,1,64]{3,2,1,0:T(1,128)S(1)}, u32[]{:S(2)}, u32[]{:S(2)}) collective-permute-start(f32[28,2,1,64]{3,2,1,0:T(1,128)S(1)} %get-tuple-element.35), channel_id=1, source_target_pairs={{16,0},{32,16},{48,32},{64,48},{80,64},{96,80},{112,96},{128,112},... | collective-permute-start | bytes 43016 | tf_op jit(solution)/shard_map/ppermute | solution.py:26
  68.6 1.3 collective-permute-done
  69.8 3.6 %collective-permute-done.1 = f32[28,2,1,64]{3,2,1,0:T(1,128)S(1)} collective-permute-done((f32[28,2,1,64]{3,2,1,0:T(1,128)S(1)}, f32[28,2,1,64]{3,2,1,0:T(1,128)S(1)}, u32[]{:S(2)}, u32[]{:S(2)}) %collective-permute-start.1) | collective-permute-done | bytes 14368 | tf_op jit(solution)/shard_map/ppermute | solution.py:26
  75.0 3.0 %collective-permute-start.3 = (f32[28,2,34,1]{2,1,3,0:T(2,128)S(1)}, f32[28,2,34,1]{2,1,3,0:T(2,128)S(1)}, u32[]{:S(2)}, u32[]{:S(2)}) collective-permute-start(f32[28,2,34,1]{2,1,3,0:T(2,128)S(1)} %copy.293), channel_id=1, source_target_pairs={{1,0},{2,1},{3,2},{4,3},{5,4},{6,5},{7,6},{8,7},{9,8},{10,9},{11,1... | collective-permute-start | bytes 22856 | tf_op jit(solution)/shard_map/ppermute | solution.py:26
  78.0 1.1 fusion.56
  85.8 1.4 %fusion.14 = (f32[2,32,64]{2,1,0:T(8,128)}, f32[2,32,64]{2,1,0:T(8,128)}, f32[2,32,64]{2,1,0:T(8,128)}, f32[2,32,64]{2,1,0:T(8,128)S(1)}) fusion(f32[27,2,32,64]{3,2,1,0:T(8,128)S(1)} %copy.291, f32[1,32,64]{2,1,0:T(8,128)} %get-tuple-element.9, pred[1,32,64]{2,1,0:T(8,128)(4,1)S(1)} %bitcast.216, f32[1,32,64]{2,1,0:T(8,128)S(1)} %copy-done.18, ...), kind=kLoop, calls=%fused_computation.74 | loop fusion | flops 32768 | bytes 172032 | tf_op jit(solution)/shard_map/jit(_where)/select_n | solution.py:178
  90.3 1.4 %maximum_select_fusion.4 = (f32[1,2,32,64]{3,2,1,0:T(8,128)}, f32[1,2,32,64]{3,2,1,0:T(8,128)S(1)}) fusion(f32[28,2,1,64]{3,2,1,0:T(1,128)S(1)} %collective-permute-done.1, f32[1,2,32,64]{3,2,1,0:T(8,128)S(1)} %broadcast_in_dim.80, f32[27,2,32,64]{3,2,1,0:T(8,128)S(1)} %copy.291, pred[1,1,32,64]{3,2,1,0:T(8,128)(4,1)} %bitcast.226), kind=kLoop, calls=%fused_computation.114 | loop fusion | flops 57344 | bytes 1046528 | tf_op jit(solution)/shard_map/jit(_where)/select_n | solution.py:178
  93.3 1.5 %maximum_select_fusion.1 = (f32[1,2,32,64]{3,2,1,0:T(8,128)S(1)}, f32[1,2,32,64]{3,2,1,0:T(8,128)}) fusion(f32[28,2,34,1]{3,2,1,0:T(8,128)S(1)} %copy.294, f32[28,2,1,64]{3,2,1,0:T(1,128)S(1)} %collective-permute-done.1, f32[28,2,1,64]{3,2,1,0:T(1,128)S(1)} %collective-permute-done, f32[1,2,32,64]{3,2,1,0:T(8,128)S(1)} %broadcast_in_dim.80, ...), kind=kLoop, calls=%fused_computation.75 | loop fusion | flops 49152 | bytes 3371008 | tf_op jit(solution)/shard_map/jit(_where)/select_n | solution.py:178
  94.8 0.9 stack.317
  95.7 0.8 fusion.32
  96.7 0.9 fusion.24
  105.0 1.6 %copy_dynamic-update-slice_fusion.25 = f32[27,2,2,16,4,16]{5,3,1,4,2,0:T(8,128)} fusion(f32[27,2,2,16,4,16]{5,3,1,4,2,0:T(8,128)} %copy_dynamic-update-slice_fusion.26, f32[1,2,2,16,4,16]{5,4,3,2,1,0:T(4,128)} %stack.308), kind=kLoop, calls=%fused_computation.44 | loop fusion | bytes 262144
  106.6 1.6 %copy_dynamic-update-slice_fusion.24 = f32[27,2,2,16,4,16]{5,3,1,4,2,0:T(8,128)} fusion(f32[27,2,2,16,4,16]{5,3,1,4,2,0:T(8,128)} %copy_dynamic-update-slice_fusion.25, f32[1,2,2,16,4,16]{5,4,3,2,1,0:T(4,128)} %stack.312), kind=kLoop, calls=%fused_computation.43 | loop fusion | bytes 262144
  109.5 1.6 %copy_dynamic-update-slice_fusion.21 = f32[27,2,2,16,4,16]{5,3,1,4,2,0:T(8,128)} fusion(f32[27,2,2,16,4,16]{5,3,1,4,2,0:T(8,128)} %copy_dynamic-update-slice_fusion.22, f32[1,2,2,16,4,16]{5,4,3,2,1,0:T(4,128)} %stack.321), kind=kLoop, calls=%fused_computation.40 | loop fusion | bytes 262144
  111.7 1.6 %copy_dynamic-update-slice_fusion.19 = f32[27,2,2,16,4,16]{5,3,1,4,2,0:T(8,128)} fusion(f32[27,2,2,16,4,16]{5,3,1,4,2,0:T(8,128)} %copy_dynamic-update-slice_fusion.20, f32[1,2,2,16,4,16]{5,4,3,2,1,0:T(4,128)} %stack.326), kind=kLoop, calls=%fused_computation.38 | loop fusion | bytes 262144
  113.3 1.6 %copy_dynamic-update-slice_fusion.18 = f32[27,2,2,16,4,16]{5,3,1,4,2,0:T(8,128)} fusion(f32[27,2,2,16,4,16]{5,3,1,4,2,0:T(8,128)} %copy_dynamic-update-slice_fusion.19, f32[1,2,2,16,4,16]{5,4,3,2,1,0:T(4,128)} %stack.330), kind=kLoop, calls=%fused_computation.37 | loop fusion | bytes 262144
  126.8 4.0 %reshape.360 = f32[8,27,512]{2,0,1:T(8,128)S(1)} reshape(f32[2,4,27,2,16,16]{5,4,3,1,0,2:T(8,128)} %bitcast.191) | data formatting | bytes 884736 | tf_op jit(solution)/shard_map/reshape | solution.py:110
  131.9 1.1 copy.354
  (181 shorter events, 45.8 us)
Async XLA Ops:
  0.0 32.1 %copy-start = (f32[3,2,32,16]{2,3,1,0:T(8,128)S(1)}, f32[3,2,32,16]{2,3,1,0:T(8,128)}, u32[]{:S(2)}) copy-start(f32[3,2,32,16]{2,3,1,0:T(8,128)} %param.10) | copy-start | bytes 36868
  12.4 4.0 %copy-start.22 = (f32[27,27,1,1]{1,0,3,2:T(8,128)S(1)}, f32[27,27,1,1]{1,0,3,2:T(8,128)}, u32[]{:S(2)}) copy-start(f32[27,27,1,1]{1,0,3,2:T(8,128)} %constant.100) | copy-start | bytes 8752
  12.4 19.5 %copy-start.23 = (s32[8]{0:T(128)S(1)}, s32[8]{0:T(128)}, u32[]{:S(2)}) copy-start(s32[8]{0:T(128)} %param.9) | copy-start | bytes 100
  23.3 16.3 %all-to-all-start = ((f32[16,1,768]{2,1,0:T(1,128)}), f32[16,1,768]{2,1,0:T(1,128)S(1)}, u32[]{:S(2)}, u32[]{:S(2)}) async-start(f32[16,1,768]{2,1,0:T(1,128)} %reshape.390), calls=%async_computation | async-start | bytes 98304 | tf_op jit(solution)/shard_map/all_to_all | solution.py:137
  46.7 11.1 %all-to-all-start.1 = ((f32[16,1,768]{2,1,0:T(1,128)}), f32[16,1,768]{2,1,0:T(1,128)S(1)}, u32[]{:S(2)}, u32[]{:S(2)}) async-start(f32[16,1,768]{2,1,0:T(1,128)} %reshape.392), calls=%async_computation.1 | async-start | bytes 98304 | tf_op jit(solution)/shard_map/all_to_all | solution.py:150
  58.6 5.2 %copy-start.21 = (f32[27,27,1,1]{1,0,3,2:T(8,128)S(1)}, f32[27,27,1,1]{1,0,3,2:T(8,128)}, u32[]{:S(2)}) copy-start(f32[27,27,1,1]{1,0,3,2:T(8,128)} %constant.99) | copy-start | bytes 8752
  58.6 5.2 %copy-start.26 = (f32[27]{0:T(128)S(1)}, f32[27]{0:T(128)}, u32[]{:S(2)}) copy-start(f32[27]{0:T(128)} %param.11) | copy-start | bytes 328
  63.6 4.4 %copy-start.27 = (s32[1,1,6]{2,1,0:T(1,128)S(1)}, s32[1,1,6]{2,1,0:T(1,128)}, u32[]{:S(2)}) copy-start(s32[1,1,6]{2,1,0:T(1,128)} %param.8) | copy-start | bytes 76
  65.3 8.2 %copy-start.1 = (f32[27,2,32,64]{3,0,2,1:T(8,128)}, f32[27,2,32,64]{3,0,2,1:T(8,128)S(1)}, u32[]{:S(2)}) copy-start(f32[27,2,32,64]{3,0,2,1:T(8,128)S(1)} %fusion.3) | copy-start | bytes 1327108
  65.9 3.9 %collective-permute-start = (f32[28,2,1,64]{3,2,1,0:T(1,128)S(1)}, f32[28,2,1,64]{3,2,1,0:T(1,128)S(1)}, u32[]{:S(2)}, u32[]{:S(2)}) collective-permute-start(f32[28,2,1,64]{3,2,1,0:T(1,128)S(1)} %get-tuple-element.34), channel_id=1, source_target_pairs={{0,16},{16,32},{32,48},{48,64},{64,80},{80,96},{96,112},{112,128},... | collective-permute-start | bytes 43016 | tf_op jit(solution)/shard_map/ppermute | solution.py:23
  66.1 7.4 %collective-permute-start.1 = (f32[28,2,1,64]{3,2,1,0:T(1,128)S(1)}, f32[28,2,1,64]{3,2,1,0:T(1,128)S(1)}, u32[]{:S(2)}, u32[]{:S(2)}) collective-permute-start(f32[28,2,1,64]{3,2,1,0:T(1,128)S(1)} %get-tuple-element.35), channel_id=1, source_target_pairs={{16,0},{32,16},{48,32},{64,48},{80,64},{96,80},{112,96},{128,112},... | collective-permute-start | bytes 43016 | tf_op jit(solution)/shard_map/ppermute | solution.py:26
  74.5 6.0 %collective-permute-start.2 = (f32[28,2,34,1]{2,1,3,0:T(2,128)S(1)}, f32[28,2,34,1]{2,1,3,0:T(2,128)S(1)}, u32[]{:S(2)}, u32[]{:S(2)}) collective-permute-start(f32[28,2,34,1]{2,1,3,0:T(2,128)S(1)} %copy.292), channel_id=1, source_target_pairs={{0,1},{1,2},{2,3},{3,4},{4,5},{5,6},{6,7},{7,8},{8,9},{9,10},{10,1... | collective-permute-start | bytes 22856 | tf_op jit(solution)/shard_map/ppermute | solution.py:23
  75.0 6.0 %collective-permute-start.3 = (f32[28,2,34,1]{2,1,3,0:T(2,128)S(1)}, f32[28,2,34,1]{2,1,3,0:T(2,128)S(1)}, u32[]{:S(2)}, u32[]{:S(2)}) collective-permute-start(f32[28,2,34,1]{2,1,3,0:T(2,128)S(1)} %copy.293), channel_id=1, source_target_pairs={{1,0},{2,1},{3,2},{4,3},{5,4},{6,5},{7,6},{8,7},{9,8},{10,9},{11,1... | collective-permute-start | bytes 22856 | tf_op jit(solution)/shard_map/ppermute | solution.py:26
  82.3 3.4 %copy-start.16 = (pred[32,64]{1,0:T(8,128)(4,1)}, pred[32,64]{1,0:T(8,128)(4,1)S(1)}, u32[]{:S(2)}) copy-start(pred[32,64]{1,0:T(8,128)(4,1)S(1)} %get-tuple-element.51) | copy-start | bytes 6148
  82.3 3.4 %copy-start.19 = (pred[32,64]{1,0:T(8,128)(4,1)}, pred[32,64]{1,0:T(8,128)(4,1)S(1)}, u32[]{:S(2)}) copy-start(pred[32,64]{1,0:T(8,128)(4,1)S(1)} %get-tuple-element.53) | copy-start | bytes 6148
  96.5 5.9 %copy-start.12 = (f32[1,2,32,64]{3,2,1,0:T(8,128)S(1)}, f32[1,2,32,64]{3,2,1,0:T(8,128)}, u32[]{:S(2)}) copy-start(f32[1,2,32,64]{3,2,1,0:T(8,128)} %get-tuple-element.30) | copy-start | bytes 49156
  96.5 7.5 %copy-start.20 = (pred[32,64]{1,0:T(8,128)(4,1)S(1)}, pred[32,64]{1,0:T(8,128)(4,1)}, u32[]{:S(2)}) copy-start(pred[32,64]{1,0:T(8,128)(4,1)} %copy-done.19) | copy-start | bytes 6148
  98.3 6.0 %copy-start.15 = (f32[2,32,64]{2,1,0:T(8,128)S(1)}, f32[2,32,64]{2,1,0:T(8,128)}, u32[]{:S(2)}) copy-start(f32[2,32,64]{2,1,0:T(8,128)} %get-tuple-element.41) | copy-start | bytes 49156
  98.3 6.1 %copy-start.14 = (f32[2,32,64]{2,1,0:T(8,128)S(1)}, f32[2,32,64]{2,1,0:T(8,128)}, u32[]{:S(2)}) copy-start(f32[2,32,64]{2,1,0:T(8,128)} %get-tuple-element.40) | copy-start | bytes 49156
  98.3 6.4 %copy-start.13 = (f32[2,32,64]{2,1,0:T(8,128)S(1)}, f32[2,32,64]{2,1,0:T(8,128)}, u32[]{:S(2)}) copy-start(f32[2,32,64]{2,1,0:T(8,128)} %get-tuple-element.39) | copy-start | bytes 49156
  99.2 11.9 %copy-start.9 = (f32[1,2,2,16,4,16]{5,4,3,2,1,0:T(4,128)S(1)}, f32[1,2,2,16,4,16]{5,4,3,2,1,0:T(4,128)}, u32[]{:S(2)}) copy-start(f32[1,2,2,16,4,16]{5,4,3,2,1,0:T(4,128)} %stack.325) | copy-start | bytes 49156
  99.2 15.7 %copy-start.8 = (f32[1,2,2,16,4,16]{5,4,3,2,1,0:T(4,128)S(1)}, f32[1,2,2,16,4,16]{5,4,3,2,1,0:T(4,128)}, u32[]{:S(2)}) copy-start(f32[1,2,2,16,4,16]{5,4,3,2,1,0:T(4,128)} %stack.334) | copy-start | bytes 49156
  99.3 17.6 %copy-start.7 = (f32[1,2,2,16,4,16]{5,4,3,2,1,0:T(4,128)S(1)}, f32[1,2,2,16,4,16]{5,4,3,2,1,0:T(4,128)}, u32[]{:S(2)}) copy-start(f32[1,2,2,16,4,16]{5,4,3,2,1,0:T(4,128)} %stack.343) | copy-start | bytes 49156
  99.3 18.2 %copy-start.2 = (f32[1,2,2,16,4,16]{5,4,3,2,1,0:T(4,128)S(1)}, f32[1,2,2,16,4,16]{5,4,3,2,1,0:T(4,128)}, u32[]{:S(2)}) copy-start(f32[1,2,2,16,4,16]{5,4,3,2,1,0:T(4,128)} %stack.344) | copy-start | bytes 49156
  99.3 18.9 %copy-start.6 = (f32[1,2,2,16,4,16]{5,4,3,2,1,0:T(4,128)S(1)}, f32[1,2,2,16,4,16]{5,4,3,2,1,0:T(4,128)}, u32[]{:S(2)}) copy-start(f32[1,2,2,16,4,16]{5,4,3,2,1,0:T(4,128)} %stack.348) | copy-start | bytes 49156
  103.2 17.6 %copy-start.5 = (f32[1,2,2,16,4,16]{5,4,3,2,1,0:T(4,128)S(1)}, f32[1,2,2,16,4,16]{5,4,3,2,1,0:T(4,128)}, u32[]{:S(2)}) copy-start(f32[1,2,2,16,4,16]{5,4,3,2,1,0:T(4,128)} %stack.361) | copy-start | bytes 49156
  104.0 17.5 %copy-start.4 = (f32[1,2,2,16,4,16]{5,4,3,2,1,0:T(4,128)S(1)}, f32[1,2,2,16,4,16]{5,4,3,2,1,0:T(4,128)}, u32[]{:S(2)}) copy-start(f32[1,2,2,16,4,16]{5,4,3,2,1,0:T(4,128)} %stack.362) | copy-start | bytes 49156
  104.0 11.5 %copy-start.10 = (f32[1,2,2,16,4,16]{5,4,3,2,1,0:T(4,128)S(1)}, f32[1,2,2,16,4,16]{5,4,3,2,1,0:T(4,128)}, u32[]{:S(2)}) copy-start(f32[1,2,2,16,4,16]{5,4,3,2,1,0:T(4,128)} %stack.335) | copy-start | bytes 49156
  104.0 12.2 %copy-start.11 = (f32[1,2,2,16,4,16]{5,4,3,2,1,0:T(4,128)S(1)}, f32[1,2,2,16,4,16]{5,4,3,2,1,0:T(4,128)}, u32[]{:S(2)}) copy-start(f32[1,2,2,16,4,16]{5,4,3,2,1,0:T(4,128)} %stack.339) | copy-start | bytes 49156
  104.0 18.8 %copy-start.3 = (f32[1,2,2,16,4,16]{5,4,3,2,1,0:T(4,128)S(1)}, f32[1,2,2,16,4,16]{5,4,3,2,1,0:T(4,128)}, u32[]{:S(2)}) copy-start(f32[1,2,2,16,4,16]{5,4,3,2,1,0:T(4,128)} %stack.370) | copy-start | bytes 49156
  123.5 8.2 %copy-start.24 = (pred[6]{0:T(512)(128)(4,1)S(1)}, pred[6]{0:T(512)(128)(4,1)}, u32[]{:S(2)}) copy-start(pred[6]{0:T(512)(128)(4,1)} %get-tuple-element.59) | copy-start | bytes 22
  123.5 8.2 %copy-start.25 = (f32[6]{0:T(128)S(1)}, f32[6]{0:T(128)}, u32[]{:S(2)}) copy-start(f32[6]{0:T(128)} %get-tuple-element.60) | copy-start | bytes 76
  (2 other events, 4.4 us)
where the time goes:
time: 134 us; the launch traced here: 133 us
  local copies, waits for them, and re-layouts  67.7 us (51%)
  other arithmetic  20.1 us (15%)
  waiting for transfers between devices  19.3 us (14%)
  starting transfers between devices  17.3 us (13%)
  matrix products  7.84 us (6%)
    unnamed x88, local copies, waits for them, and re-layouts  30.5 us
    another operation x28, local copies, waits for them, and re-layouts, on_device(): read_tile = jnp.stack(read, axis=0)  14.4 us
    all_to_all x1, starting transfers between devices, on_device(): lax.all_to_all(wind_tile, 'line', split_axis=2, concat_axis=3, tiled=True)  8.57 us
    select_n x14, other arithmetic, on_device(): read.append(jnp.where(block_both, bounced_distributions, source))  7.39 us
    all_to_all x1, waiting for transfers between devices, on_device(): lax.all_to_all(wind_tile, 'line', split_axis=2, concat_axis=3, tiled=True)  7.31 us
    all_to_all x1, waiting for transfers between devices, on_device(): lax.all_to_all(forcing_adjustment, 'line', split_axis=3, concat_axis=2, t...  7.12 us
    dot_general x1, matrix products, on_device(): moments = jnp.einsum('ij,jlrc->ilrc', forward, pops_tile, precision=HIGHEST)  5.79 us
    ppermute x2, starting transfers between devices, with_halo(): lax.ppermute(lax.slice_in_dim(block, 0, width, axis=dim), axis, backward)  4.84 us
  transfers between devices with their start and end apart: 6, of which 4 were waited for; matrix products, arithmetic and copies ran while one was open for 4% of the time, Pallas kernels for 0%

commit v1 on v0

--- a/solution.py
+++ b/solution.py
@@ -134,20 +134,14 @@
     safe_density = jnp.where(fluid_map[None] > 0.5, moments[0], 1.0)
     wind_tile = tile_velocity(moments, safe_density)
     line_length = lax.axis_size("line") * cols_tile
-    whole_lines = lax.all_to_all(wind_tile, "line", split_axis=2, concat_axis=3, tiled=True)
-    rows_each = whole_lines.shape[2]
-    mode_basis = mode_basis_at(
-        retained_wavenumbers, jnp.arange(line_length, dtype=jnp.int32), line_length
-    )
-    coefficients = jnp.einsum("klrx,xm->klrm", whole_lines, mode_basis, precision=HIGHEST)
-    target = lax.dynamic_slice_in_dim(
-        regional_amplitudes, lax.axis_index("line") * rows_each, rows_each, 2
-    )
-    misfit = target - 2.0 / line_length * coefficients
-    forcing_adjustment = NUDGE_GAIN * jnp.einsum(
+    own_columns = lax.axis_index("line") * cols_tile + jnp.arange(cols_tile, dtype=jnp.int32)
+    mode_basis = mode_basis_at(retained_wavenumbers, own_columns, line_length)
+    partial = jnp.einsum("klrx,xm->klrm", wind_tile, mode_basis, precision=HIGHEST)
+    coefficients = lax.psum(partial, "line")
+    misfit = regional_amplitudes - 2.0 / line_length * coefficients
+    nudge_tile = NUDGE_GAIN * jnp.einsum(
         "klrm,xm->klrx", misfit, mode_basis, precision=HIGHEST
     )
-    nudge_tile = lax.all_to_all(forcing_adjustment, "line", split_axis=3, concat_axis=2, tiled=True)
     post_tile = collide_tile(moments, wind_tile, nudge_tile, backward, relaxation_frequencies)
     levels = post_tile.shape[1]
     solid_plane = jnp.broadcast_to(solid_tile[None, None], (1, levels, rows_tile, cols_tile))

time: 134 us -> 146 us (1.090)
  blocking collectives: 0 us -> 51 us
  starting transfers between devices: 17.3 us -> 2.62 us
  waiting for transfers between devices: 19.3 us -> 7.98 us
  local copies, waits for them, and re-layouts: 67.7 us -> 61 us
  other arithmetic: 20.1 us -> 14.3 us
    psum x0 -> x1, blocking collectives: none -> 51 us  [on_device(): coefficients = lax.psum(partial, 'line')]
    all_to_all x2 -> x0, waiting for transfers between devices: 14.4 us -> none  [the longest x1 7.31 us: on_device(): lax.all_to_all(wind_tile, 'line', split_axis=2, concat_axis=3, tiled=True)]
    all_to_all x2 -> x0, starting transfers between devices: 12.3 us -> none  [the longest x1 8.57 us: on_device(): lax.all_to_all(wind_tile, 'line', split_axis=2, concat_axis=3, tiled=True)]
    unnamed x88 -> x75, local copies, waits for them, and re-layouts: 30.5 us -> 20.5 us
    another operation x28, local copies, waits for them, and re-layouts: 14.4 us -> 21.8 us  [on_device(): read_tile = jnp.stack(read, axis=0)]
    select_n x14, other arithmetic: 7.39 us -> 4.2 us  [on_device(): read.append(jnp.where(block_both, bounced_distributions, source))]
    ppermute x2, waiting for transfers between devices: 1.26 us -> 4.39 us  [with_halo(): lax.ppermute(lax.slice_in_dim(block, block.shape[dim] - width, None, axis...]
    ppermute x2, starting transfers between devices: 4.84 us -> 1.9 us  [with_halo(): lax.ppermute(lax.slice_in_dim(block, 0, width, axis=dim), axis, backward)]
  transfers between devices with their start and end apart: 6 -> 4, of which waited for: 4 -> 3; matrix products, arithmetic and copies ran while one was open for 4% -> 1% of each run, Pallas kernels for 0% -> 0%
where the time goes in v1:
time: 146 us
  local copies, waits for them, and re-layouts  61 us (42%)
  blocking collectives  51 us (35%)
  other arithmetic  14.3 us (10%)
  matrix products  8.14 us (6%)
  waiting for transfers between devices  7.98 us (5%)
  starting transfers between devices  2.62 us (2%)
    psum x1, blocking collectives, on_device(): coefficients = lax.psum(partial, 'line')  51 us
    another operation x28, local copies, waits for them, and re-layouts, on_device(): read_tile = jnp.stack(read, axis=0)  21.8 us
    unnamed x75, local copies, waits for them, and re-layouts  20.5 us
    dot_general x1, matrix products, on_device(): moments = jnp.einsum('ij,jlrc->ilrc', forward, pops_tile, precision=HIGHEST)  5.79 us
    reshape x2, local copies, waits for them, and re-layouts, tile_to_compact(): shaped.reshape(rows_blocks * cols_blocks, channels, levels * block_edge *...  4.88 us
    ppermute x2, waiting for transfers between devices, with_halo(): lax.ppermute(lax.slice_in_dim(block, block.shape[dim] - width, None, axis...  4.39 us
    select_n x14, other arithmetic, on_device(): read.append(jnp.where(block_both, bounced_distributions, source))  4.2 us
    gather x3, local copies, waits for them, and re-layouts, compact_to_tile(): jnp.take(packed_arrangement, slot_of, axis=0)  3.8 us
  transfers between devices with their start and end apart: 4, of which 3 were waited for; matrix products, arithmetic and copies ran while one was open for 1% of the time, Pallas kernels for 0%

profile of v1, /device:TPU:30, one launch (start us, length us, event | category | flops | bytes accessed | tf_op | source)
XLA Modules:
  0.0 145.7 jit_solution(17351706727084608125)
XLA Ops:
  4.7 1.0 copy.376
  6.9 1.0 copy.254
  8.0 2.2 %gather.13 = f32[2,4,27,2,16,16]{5,4,3,1,0,2:T(8,128)S(1)} reshape(f32[8,27,512]{2,0,1:T(8,128)} %copy.254) | data formatting | bytes 884736 | tf_op jit(solution)/shard_map/jit(_take)/gather | solution.py:95
  10.2 3.0 %multiply_bitcast_fusion = f32[27,2,2,16,4,16]{5,3,1,4,2,0:T(8,128)} fusion(f32[2,4,27,2,16,16]{5,4,3,1,0,2:T(8,128)S(1)} %gather.13, f32[2,4]{1,0:T(2,128)} %copy-done.17, pred[2,4]{1,0:T(4,128)(4,1)} %compare_and_fusion), kind=kLoop, calls=%fused_computation.2 | loop fusion | flops 221184 | bytes 884776 | tf_op jit(solution)/shard_map/transpose | solution.py:99
  13.1 3.6 %copy.255 = f32[27,2,2,16,4,16]{0,5,4,3,2,1:T(8,128)S(1)} copy(f32[27,2,2,16,4,16]{5,3,1,4,2,0:T(8,128)} %multiply_bitcast_fusion) | data formatting | bytes 884736 | tf_op jit(solution)/shard_map/transpose | solution.py:99
  17.0 5.8 %fusion.60 = f32[27,2,32,64]{3,0,2,1:T(8,128)S(1)} fusion(f32[27,27,1,1]{1,0,3,2:T(8,128)S(1)} %copy-done.15, f32[27,2,32,64]{0,3,2,1:T(8,128)S(1)} %bitcast.163), kind=kOutput, calls=%fused_computation.236 | convolution fusion | flops 35831808 | bytes 887652 | tf_op jit(solution)/shard_map/ij,jlrc->ilrc/dot_general | solution.py:133
  23.5 51.0 %psum.7 = f32[3,2,32,16]{2,3,1,0:T(8,128)S(1)} all-reduce(f32[3,2,32,16]{2,3,1,0:T(8,128)S(1)} %fusion.7), channel_id=1, replica_groups=mesh['curve'=16,'line'=16] {'line'}, use_global_device_ids=true, to_apply=%region_2.3 | all-reduce | flops 3072 | bytes 24576 | tf_op jit(solution)/shard_map/psum | solution.py:140
  75.6 1.5 %fusion.2 = f32[27,2,32,64]{3,0,2,1:T(8,128)S(1)} fusion(f32[27,27,1,1]{1,0,3,2:T(8,128)S(1)} %copy-done.14, f32[27,2,32,64]{3,0,2,1:T(8,128)S(1)} %fusion.60, f32[27,2,32,64]{3,2,1,0:T(8,128)S(1)} %bitcast.164, f32[27]{0:T(128)S(1)} %copy-done.22), kind=kOutput, calls=%fused_computation.7 | convolution fusion | flops 36163584 | bytes 1330128 | tf_op jit(solution)/shard_map/ij,jlrc->ilrc/dot_general | solution.py:80
  78.0 1.9 %collective-permute-start.1 = (f32[28,2,1,64]{3,2,1,0:T(1,128)S(1)}, f32[28,2,1,64]{3,2,1,0:T(1,128)S(1)}, u32[]{:S(2)}, u32[]{:S(2)}) collective-permute-start(f32[28,2,1,64]{3,2,1,0:T(1,128)S(1)} %get-tuple-element.33), channel_id=1, source_target_pairs={{16,0},{32,16},{48,32},{64,48},{80,64},{96,80},{112,96},{128,112},... | collective-permute-start | bytes 43016 | tf_op jit(solution)/shard_map/ppermute | solution.py:26
  80.0 1.7 %collective-permute-done = f32[28,2,1,64]{3,2,1,0:T(1,128)S(1)} collective-permute-done((f32[28,2,1,64]{3,2,1,0:T(1,128)S(1)}, f32[28,2,1,64]{3,2,1,0:T(1,128)S(1)}, u32[]{:S(2)}, u32[]{:S(2)}) %collective-permute-start) | collective-permute-done | bytes 14368 | tf_op jit(solution)/shard_map/ppermute | solution.py:23
  81.7 3.6 %collective-permute-done.1 = f32[28,2,1,64]{3,2,1,0:T(1,128)S(1)} collective-permute-done((f32[28,2,1,64]{3,2,1,0:T(1,128)S(1)}, f32[28,2,1,64]{3,2,1,0:T(1,128)S(1)}, u32[]{:S(2)}, u32[]{:S(2)}) %collective-permute-start.1) | collective-permute-done | bytes 14368 | tf_op jit(solution)/shard_map/ppermute | solution.py:26
  88.7 2.7 %collective-permute-done.2 = f32[28,2,34,1]{2,1,3,0:T(2,128)S(1)} collective-permute-done((f32[28,2,34,1]{2,1,3,0:T(2,128)S(1)}, f32[28,2,34,1]{2,1,3,0:T(2,128)S(1)}, u32[]{:S(2)}, u32[]{:S(2)}) %collective-permute-start.2) | collective-permute-done | bytes 7648 | tf_op jit(solution)/shard_map/ppermute | solution.py:23
  101.8 1.3 fusion.15
  118.5 1.0 copy_dynamic-update-slice_fusion.26
  119.4 0.9 copy_dynamic-update-slice_fusion.25
  120.4 0.9 copy_dynamic-update-slice_fusion.24
  121.3 0.9 copy_dynamic-update-slice_fusion.23
  122.2 0.9 copy_dynamic-update-slice_fusion.22
  123.1 0.9 copy_dynamic-update-slice_fusion.21
  124.0 0.9 copy_dynamic-update-slice_fusion.20
  124.9 0.9 copy_dynamic-update-slice_fusion.19
  125.9 0.9 copy_dynamic-update-slice_fusion.18
  126.8 0.9 copy_dynamic-update-slice_fusion.17
  127.7 0.9 copy_dynamic-update-slice_fusion.16
  128.6 0.9 copy_dynamic-update-slice_fusion.15
  129.5 0.9 copy_dynamic-update-slice_fusion.14
  130.5 0.9 copy_dynamic-update-slice_fusion.13
  131.4 0.9 copy_dynamic-update-slice_fusion.10
  132.4 0.9 copy_dynamic-update-slice_fusion.8
  138.9 3.6 %reshape.290 = f32[8,27,512]{2,0,1:T(8,128)} reshape(f32[2,4,27,2,16,16]{5,4,3,1,0,2:T(8,128)S(1)} %bitcast.165) | data formatting | bytes 884736 | tf_op jit(solution)/shard_map/reshape | solution.py:110
  142.5 1.3 copy.326
  144.6 1.1 copy.327
  (156 shorter events, 44.1 us)
Async XLA Ops:
  2.4 1.1 copy-start.17
  13.1 3.7 %copy-start.20 = (s32[8]{0:T(128)S(1)}, s32[8]{0:T(128)}, u32[]{:S(2)}) copy-start(s32[8]{0:T(128)} %param.9) | copy-start | bytes 100
  13.1 3.7 %copy-start.21 = (s32[64]{0:T(128)S(1)}, s32[64]{0:T(128)}, u32[]{:S(2)}) copy-start(s32[64]{0:T(128)} %iota_add_fusion) | copy-start | bytes 772
  13.1 3.8 %copy-start.15 = (f32[27,27,1,1]{1,0,3,2:T(8,128)S(1)}, f32[27,27,1,1]{1,0,3,2:T(8,128)}, u32[]{:S(2)}) copy-start(f32[27,27,1,1]{1,0,3,2:T(8,128)} %constant.98) | copy-start | bytes 8752
  13.1 9.6 %copy-start.16 = (pred[32,64]{1,0:T(8,128)(4,1)S(1)}, pred[32,64]{1,0:T(8,128)(4,1)}, u32[]{:S(2)}) copy-start(pred[32,64]{1,0:T(8,128)(4,1)} %copy.258) | copy-start | bytes 6148
  13.1 61.4 %copy-start.12 = (f32[3,2,32,16]{2,3,1,0:T(8,128)S(1)}, f32[3,2,32,16]{2,3,1,0:T(8,128)}, u32[]{:S(2)}) copy-start(f32[3,2,32,16]{2,3,1,0:T(8,128)} %param.10) | copy-start | bytes 36868
  16.9 58.7 %copy-start.14 = (f32[27,27,1,1]{1,0,3,2:T(8,128)S(1)}, f32[27,27,1,1]{1,0,3,2:T(8,128)}, u32[]{:S(2)}) copy-start(f32[27,27,1,1]{1,0,3,2:T(8,128)} %constant.97) | copy-start | bytes 8752
  16.9 58.7 %copy-start.22 = (f32[27]{0:T(128)S(1)}, f32[27]{0:T(128)}, u32[]{:S(2)}) copy-start(f32[27]{0:T(128)} %param.11) | copy-start | bytes 328
  77.8 3.9 %collective-permute-start = (f32[28,2,1,64]{3,2,1,0:T(1,128)S(1)}, f32[28,2,1,64]{3,2,1,0:T(1,128)S(1)}, u32[]{:S(2)}, u32[]{:S(2)}) collective-permute-start(f32[28,2,1,64]{3,2,1,0:T(1,128)S(1)} %get-tuple-element.32), channel_id=1, source_target_pairs={{0,16},{16,32},{32,48},{48,64},{64,80},{80,96},{96,112},{112,128},... | collective-permute-start | bytes 43016 | tf_op jit(solution)/shard_map/ppermute | solution.py:23
  78.0 7.3 %collective-permute-start.1 = (f32[28,2,1,64]{3,2,1,0:T(1,128)S(1)}, f32[28,2,1,64]{3,2,1,0:T(1,128)S(1)}, u32[]{:S(2)}, u32[]{:S(2)}) collective-permute-start(f32[28,2,1,64]{3,2,1,0:T(1,128)S(1)} %get-tuple-element.33), channel_id=1, source_target_pairs={{16,0},{32,16},{48,32},{64,48},{80,64},{96,80},{112,96},{128,112},... | collective-permute-start | bytes 43016 | tf_op jit(solution)/shard_map/ppermute | solution.py:26
  85.5 1.9 %copy-start.23 = (s32[1,1,6]{2,1,0:T(1,128)S(1)}, s32[1,1,6]{2,1,0:T(1,128)}, u32[]{:S(2)}) copy-start(s32[1,1,6]{2,1,0:T(1,128)} %param.8) | copy-start | bytes 76
  86.8 5.1 %collective-permute-start.3 = (f32[28,2,34,1]{2,1,3,0:T(2,128)S(1)}, f32[28,2,34,1]{2,1,3,0:T(2,128)S(1)}, u32[]{:S(2)}, u32[]{:S(2)}) collective-permute-start(f32[28,2,34,1]{2,1,3,0:T(2,128)S(1)} %copy.266), channel_id=1, source_target_pairs={{1,0},{2,1},{3,2},{4,3},{5,4},{6,5},{7,6},{8,7},{9,8},{10,9},{11,1... | collective-permute-start | bytes 22856 | tf_op jit(solution)/shard_map/ppermute | solution.py:26
  86.9 4.5 %collective-permute-start.2 = (f32[28,2,34,1]{2,1,3,0:T(2,128)S(1)}, f32[28,2,34,1]{2,1,3,0:T(2,128)S(1)}, u32[]{:S(2)}, u32[]{:S(2)}) collective-permute-start(f32[28,2,34,1]{2,1,3,0:T(2,128)S(1)} %copy.265), channel_id=1, source_target_pairs={{0,1},{1,2},{2,3},{3,4},{4,5},{5,6},{6,7},{7,8},{8,9},{9,10},{10,1... | collective-permute-start | bytes 22856 | tf_op jit(solution)/shard_map/ppermute | solution.py:23
  93.2 2.5 %copy-start.13 = (pred[32,64]{1,0:T(8,128)(4,1)}, pred[32,64]{1,0:T(8,128)(4,1)S(1)}, u32[]{:S(2)}) copy-start(pred[32,64]{1,0:T(8,128)(4,1)S(1)} %get-tuple-element.55) | copy-start | bytes 6148
  105.8 2.6 %copy-start.11 = (f32[1,32,64]{2,1,0:T(8,128)S(1)}, f32[1,32,64]{2,1,0:T(8,128)}, u32[]{:S(2)}) copy-start(f32[1,32,64]{2,1,0:T(8,128)} %get-tuple-element.5) | copy-start | bytes 24580
  105.8 4.1 %copy-start.6 = (f32[2,32,64]{2,1,0:T(8,128)S(1)}, f32[2,32,64]{2,1,0:T(8,128)}, u32[]{:S(2)}) copy-start(f32[2,32,64]{2,1,0:T(8,128)} %get-tuple-element.43) | copy-start | bytes 49156
  105.8 4.9 %copy-start.5 = (f32[2,32,64]{2,1,0:T(8,128)S(1)}, f32[2,32,64]{2,1,0:T(8,128)}, u32[]{:S(2)}) copy-start(f32[2,32,64]{2,1,0:T(8,128)} %get-tuple-element.44) | copy-start | bytes 49156
  105.8 8.7 %copy-start.10 = (f32[1,2,32,64]{3,2,1,0:T(8,128)S(1)}, f32[1,2,32,64]{3,2,1,0:T(8,128)}, u32[]{:S(2)}) copy-start(f32[1,2,32,64]{3,2,1,0:T(8,128)} %get-tuple-element.25) | copy-start | bytes 49156
  105.8 10.3 %copy-start.9 = (f32[2,32,64]{2,1,0:T(8,128)S(1)}, f32[2,32,64]{2,1,0:T(8,128)}, u32[]{:S(2)}) copy-start(f32[2,32,64]{2,1,0:T(8,128)} %get-tuple-element.38) | copy-start | bytes 49156
  105.8 11.0 %copy-start.8 = (f32[2,32,64]{2,1,0:T(8,128)S(1)}, f32[2,32,64]{2,1,0:T(8,128)}, u32[]{:S(2)}) copy-start(f32[2,32,64]{2,1,0:T(8,128)} %get-tuple-element.39) | copy-start | bytes 49156
  105.8 11.8 %copy-start.7 = (f32[2,32,64]{2,1,0:T(8,128)S(1)}, f32[2,32,64]{2,1,0:T(8,128)}, u32[]{:S(2)}) copy-start(f32[2,32,64]{2,1,0:T(8,128)} %get-tuple-element.40) | copy-start | bytes 49156
  118.4 12.9 %copy-start.4 = (f32[1,2,2,16,4,16]{5,4,3,2,1,0:T(4,128)S(1)}, f32[1,2,2,16,4,16]{5,4,3,2,1,0:T(4,128)}, u32[]{:S(2)}) copy-start(f32[1,2,2,16,4,16]{5,4,3,2,1,0:T(4,128)} %stack.342) | copy-start | bytes 49156
  118.4 13.0 %copy-start.3 = (f32[1,2,2,16,4,16]{5,4,3,2,1,0:T(4,128)S(1)}, f32[1,2,2,16,4,16]{5,4,3,2,1,0:T(4,128)}, u32[]{:S(2)}) copy-start(f32[1,2,2,16,4,16]{5,4,3,2,1,0:T(4,128)} %stack.346) | copy-start | bytes 49156
  118.4 13.9 %copy-start.2 = (f32[1,2,2,16,4,16]{5,4,3,2,1,0:T(4,128)S(1)}, f32[1,2,2,16,4,16]{5,4,3,2,1,0:T(4,128)}, u32[]{:S(2)}) copy-start(f32[1,2,2,16,4,16]{5,4,3,2,1,0:T(4,128)} %stack.351) | copy-start | bytes 49156
  118.4 14.9 %copy-start = (f32[1,2,2,16,4,16]{5,4,3,2,1,0:T(4,128)S(1)}, f32[1,2,2,16,4,16]{5,4,3,2,1,0:T(4,128)}, u32[]{:S(2)}) copy-start(f32[1,2,2,16,4,16]{5,4,3,2,1,0:T(4,128)} %stack.356) | copy-start | bytes 49156
  118.4 14.9 %copy-start.1 = (f32[1,2,2,16,4,16]{5,4,3,2,1,0:T(4,128)S(1)}, f32[1,2,2,16,4,16]{5,4,3,2,1,0:T(4,128)}, u32[]{:S(2)}) copy-start(f32[1,2,2,16,4,16]{5,4,3,2,1,0:T(4,128)} %stack.360) | copy-start | bytes 49156
  134.3 10.2 %copy-start.18 = (pred[6]{0:T(512)(128)(4,1)S(1)}, pred[6]{0:T(512)(128)(4,1)}, u32[]{:S(2)}) copy-start(pred[6]{0:T(512)(128)(4,1)} %get-tuple-element.62) | copy-start | bytes 22
  134.3 10.2 %copy-start.19 = (f32[6]{0:T(128)S(1)}, f32[6]{0:T(128)}, u32[]{:S(2)}) copy-start(f32[6]{0:T(128)} %get-tuple-element.63) | copy-start | bytes 76

commit v2 on v1

--- a/solution.py
+++ b/solution.py
@@ -26,6 +26,15 @@
         high = lax.ppermute(lax.slice_in_dim(block, 0, width, axis=dim), axis, backward)
         block = jnp.concatenate([low, block, high], axis=dim)
     return block
+
+
+def butterfly_sum(value, axis):
+    count = lax.axis_size(axis)
+    stride = 1
+    while stride < count:
+        value = value + lax.ppermute(value, axis, [(i, i ^ stride) for i in range(count)])
+        stride *= 2
+    return value
 
 
 def lattice_tables():
@@ -137,7 +146,7 @@
     own_columns = lax.axis_index("line") * cols_tile + jnp.arange(cols_tile, dtype=jnp.int32)
     mode_basis = mode_basis_at(retained_wavenumbers, own_columns, line_length)
     partial = jnp.einsum("klrx,xm->klrm", wind_tile, mode_basis, precision=HIGHEST)
-    coefficients = lax.psum(partial, "line")
+    coefficients = butterfly_sum(partial, "line")
     misfit = regional_amplitudes - 2.0 / line_length * coefficients
     nudge_tile = NUDGE_GAIN * jnp.einsum(
         "klrm,xm->klrx", misfit, mode_basis, precision=HIGHEST

time: 146 us -> 115 us (0.79)
  blocking collectives: 51 us -> 0 us
  starting transfers between devices: 2.62 us -> 15 us
  waiting for transfers between devices: 7.98 us -> 15.9 us
  other arithmetic: 14.3 us -> 12.7 us
    psum x1 -> x0, blocking collectives: 51 us -> none  [on_device(): coefficients = lax.psum(partial, 'line')]
    ppermute x0 -> x4, starting transfers between devices: none -> 12.2 us  [butterfly_sum(): lax.ppermute(value, axis, [(i, i ^ stride) for i in range(count)])]
    ppermute x0 -> x4, waiting for transfers between devices: none -> 7.49 us  [butterfly_sum(): lax.ppermute(value, axis, [(i, i ^ stride) for i in range(count)])]
    unnamed x75 -> x71, local copies, waits for them, and re-layouts: 20.5 us -> 20.5 us
  transfers between devices with their start and end apart: 4 -> 8, of which waited for: 3 -> 7; matrix products, arithmetic and copies ran while one was open for 1% -> 3% of each run, Pallas kernels for 0% -> 0%
where the time goes in v2:
time: 115 us; the launch traced here: 114 us
  local copies, waits for them, and re-layouts  61.4 us (53%)
  waiting for transfers between devices  15.9 us (14%)
  starting transfers between devices  15 us (13%)
  other arithmetic  12.7 us (11%)
  matrix products  8.15 us (7%)
    another operation x28, local copies, waits for them, and re-layouts, on_device(): read_tile = jnp.stack(read, axis=0)  21.7 us
    unnamed x71, local copies, waits for them, and re-layouts  20.5 us
    ppermute x4, starting transfers between devices, butterfly_sum(): lax.ppermute(value, axis, [(i, i ^ stride) for i in range(count)])  12.2 us
    ppermute x4, waiting for transfers between devices, butterfly_sum(): lax.ppermute(value, axis, [(i, i ^ stride) for i in range(count)])  7.49 us
    dot_general x1, matrix products, on_device(): moments = jnp.einsum('ij,jlrc->ilrc', forward, pops_tile, precision=HIGHEST)  5.79 us
    reshape x2, local copies, waits for them, and re-layouts, tile_to_compact(): shaped.reshape(rows_blocks * cols_blocks, channels, levels * block_edge *...  4.87 us
    ppermute x2, waiting for transfers between devices, with_halo(): lax.ppermute(lax.slice_in_dim(block, 0, width, axis=dim), axis, backward)  4.32 us
    select_n x14, other arithmetic, on_device(): read.append(jnp.where(block_both, bounced_distributions, source))  4.19 us
  transfers between devices with their start and end apart: 8, of which 7 were waited for; matrix products, arithmetic and copies ran while one was open for 3% of the time, Pallas kernels for 0%

profile of v2, /device:TPU:30, one launch (start us, length us, event | category | flops | bytes accessed | tf_op | source)
XLA Modules:
  0.0 113.8 jit_solution(4308471101854842006)
XLA Ops:
  2.8 1.0 copy.378
  5.0 1.0 copy.256
  6.0 2.2 %gather.13 = f32[2,4,27,2,16,16]{5,4,3,1,0,2:T(8,128)S(1)} reshape(f32[8,27,512]{2,0,1:T(8,128)} %copy.256) | data formatting | bytes 884736 | tf_op jit(solution)/shard_map/jit(_take)/gather | solution.py:104
  8.2 2.3 %multiply_bitcast_fusion = f32[27,2,2,16,4,16]{5,3,1,4,2,0:T(8,128)} fusion(f32[2,4,27,2,16,16]{5,4,3,1,0,2:T(8,128)S(1)} %gather.13, f32[2,4]{1,0:T(2,128)S(1)} %reshape.291, pred[2,4]{1,0:T(4,128)(4,1)S(1)} %compare_and_fusion), kind=kLoop, calls=%fused_computation.2 | loop fusion | flops 221184 | bytes 884776 | tf_op jit(solution)/shard_map/transpose | solution.py:108
  10.5 3.6 %copy.257 = f32[27,2,2,16,4,16]{0,5,4,3,2,1:T(8,128)S(1)} copy(f32[27,2,2,16,4,16]{5,3,1,4,2,0:T(8,128)} %multiply_bitcast_fusion) | data formatting | bytes 884736 | tf_op jit(solution)/shard_map/transpose | solution.py:108
  14.3 5.8 %fusion.61 = f32[27,2,32,64]{3,0,2,1:T(8,128)S(1)} fusion(f32[27,27,1,1]{1,0,3,2:T(8,128)S(1)} %copy-done.16, f32[27,2,32,64]{0,3,2,1:T(8,128)S(1)} %bitcast.163), kind=kOutput, calls=%fused_computation.237 | convolution fusion | flops 35831808 | bytes 887652 | tf_op jit(solution)/shard_map/ij,jlrc->ilrc/dot_general | solution.py:142
  21.0 1.2 %collective-permute-done = f32[3,2,32,16]{2,3,1,0:T(8,128)S(1)} collective-permute-done((f32[3,2,32,16]{2,3,1,0:T(8,128)S(1)}, f32[3,2,32,16]{2,3,1,0:T(8,128)S(1)}, u32[]{:S(2)}, u32[]{:S(2)}) %collective-permute-start) | collective-permute-done | bytes 12320 | tf_op jit(solution)/shard_map/ppermute | solution.py:35
  22.2 2.0 %collective-permute-start.1 = (f32[3,2,32,16]{2,3,1,0:T(8,128)S(1)}, f32[3,2,32,16]{2,3,1,0:T(8,128)S(1)}, u32[]{:S(2)}, u32[]{:S(2)}) collective-permute-start(f32[3,2,32,16]{2,3,1,0:T(8,128)S(1)} %add.60), channel_id=1, source_target_pairs={{0,2},{1,3},{2,0},{3,1},{4,6},{5,7},{6,4},{7,5},{8,10},{9,11},{10,... | collective-permute-start | bytes 36872 | tf_op jit(solution)/shard_map/ppermute | solution.py:35
  24.2 2.2 %collective-permute-done.1 = f32[3,2,32,16]{2,3,1,0:T(8,128)S(1)} collective-permute-done((f32[3,2,32,16]{2,3,1,0:T(8,128)S(1)}, f32[3,2,32,16]{2,3,1,0:T(8,128)S(1)}, u32[]{:S(2)}, u32[]{:S(2)}) %collective-permute-start.1) | collective-permute-done | bytes 12320 | tf_op jit(solution)/shard_map/ppermute | solution.py:35
  26.4 3.4 %collective-permute-start.2 = (f32[3,2,32,16]{2,3,1,0:T(8,128)S(1)}, f32[3,2,32,16]{2,3,1,0:T(8,128)S(1)}, u32[]{:S(2)}, u32[]{:S(2)}) collective-permute-start(f32[3,2,32,16]{2,3,1,0:T(8,128)S(1)} %add.61), channel_id=1, source_target_pairs={{0,4},{1,5},{2,6},{3,7},{4,0},{5,1},{6,2},{7,3},{8,12},{9,13},{10,... | collective-permute-start | bytes 36872 | tf_op jit(solution)/shard_map/ppermute | solution.py:35
  29.8 2.3 %collective-permute-done.2 = f32[3,2,32,16]{2,3,1,0:T(8,128)S(1)} collective-permute-done((f32[3,2,32,16]{2,3,1,0:T(8,128)S(1)}, f32[3,2,32,16]{2,3,1,0:T(8,128)S(1)}, u32[]{:S(2)}, u32[]{:S(2)}) %collective-permute-start.2) | collective-permute-done | bytes 12320 | tf_op jit(solution)/shard_map/ppermute | solution.py:35
  32.0 6.7 %collective-permute-start.3 = (f32[3,2,32,16]{2,3,1,0:T(8,128)S(1)}, f32[3,2,32,16]{2,3,1,0:T(8,128)S(1)}, u32[]{:S(2)}, u32[]{:S(2)}) collective-permute-start(f32[3,2,32,16]{2,3,1,0:T(8,128)S(1)} %add.62), channel_id=1, source_target_pairs={{0,8},{1,9},{2,10},{3,11},{4,12},{5,13},{6,14},{7,15},{8,0},{9,1},... | collective-permute-start | bytes 36872 | tf_op jit(solution)/shard_map/ppermute | solution.py:35
  39.1 1.8 %collective-permute-done.3 = f32[3,2,32,16]{2,3,1,0:T(8,128)S(1)} collective-permute-done((f32[3,2,32,16]{2,3,1,0:T(8,128)S(1)}, f32[3,2,32,16]{2,3,1,0:T(8,128)S(1)}, u32[]{:S(2)}, u32[]{:S(2)}) %collective-permute-start.3) | collective-permute-done | bytes 12320 | tf_op jit(solution)/shard_map/ppermute | solution.py:35
  42.1 1.5 %fusion.2 = f32[27,2,32,64]{3,0,2,1:T(8,128)S(1)} fusion(f32[27,27,1,1]{1,0,3,2:T(8,128)S(1)} %copy-done.15, f32[27,2,32,64]{3,0,2,1:T(8,128)S(1)} %fusion.61, f32[27,2,32,64]{3,2,1,0:T(8,128)S(1)} %bitcast.164, f32[27]{0:T(128)S(1)} %copy-done.20), kind=kOutput, calls=%fused_computation.7 | convolution fusion | flops 36163584 | bytes 1330128 | tf_op jit(solution)/shard_map/ij,jlrc->ilrc/dot_general | solution.py:89
  44.2 1.3 %collective-permute-start.4 = (f32[28,2,1,64]{3,2,1,0:T(1,128)S(1)}, f32[28,2,1,64]{3,2,1,0:T(1,128)S(1)}, u32[]{:S(2)}, u32[]{:S(2)}) collective-permute-start(f32[28,2,1,64]{3,2,1,0:T(1,128)S(1)} %get-tuple-element.32), channel_id=1, source_target_pairs={{0,16},{16,32},{32,48},{48,64},{64,80},{80,96},{96,112},{112,128},... | collective-permute-start | bytes 43016 | tf_op jit(solution)/shard_map/ppermute | solution.py:23
  45.5 1.0 collective-permute-start.5
  47.1 1.3 %collective-permute-done.4 = f32[28,2,1,64]{3,2,1,0:T(1,128)S(1)} collective-permute-done((f32[28,2,1,64]{3,2,1,0:T(1,128)S(1)}, f32[28,2,1,64]{3,2,1,0:T(1,128)S(1)}, u32[]{:S(2)}, u32[]{:S(2)}) %collective-permute-start.4) | collective-permute-done | bytes 14368 | tf_op jit(solution)/shard_map/ppermute | solution.py:23
  48.4 4.3 %collective-permute-done.5 = f32[28,2,1,64]{3,2,1,0:T(1,128)S(1)} collective-permute-done((f32[28,2,1,64]{3,2,1,0:T(1,128)S(1)}, f32[28,2,1,64]{3,2,1,0:T(1,128)S(1)}, u32[]{:S(2)}, u32[]{:S(2)}) %collective-permute-start.5) | collective-permute-done | bytes 14368 | tf_op jit(solution)/shard_map/ppermute | solution.py:26
  54.7 1.1 %fusion.58 = (f32[1,2,32,64]{3,0,2,1:T(1,128)S(1)}, f32[2,32,64]{2,1,0:T(8,128)S(1)}) fusion(f32[27,2,32,64]{3,0,2,1:T(8,128)} %copy-done), kind=kLoop, calls=%fused_computation.234 | loop fusion | bytes 65536 | tf_op jit(solution)/shard_map/slice | solution.py:170
  56.7 2.9 %collective-permute-done.6 = f32[28,2,34,1]{2,1,3,0:T(2,128)S(1)} collective-permute-done((f32[28,2,34,1]{2,1,3,0:T(2,128)S(1)}, f32[28,2,34,1]{2,1,3,0:T(2,128)S(1)}, u32[]{:S(2)}, u32[]{:S(2)}) %collective-permute-start.6) | collective-permute-done | bytes 7648 | tf_op jit(solution)/shard_map/ppermute | solution.py:23
  70.0 1.3 %fusion.16 = (f32[2,32,64]{2,1,0:T(8,128)S(1)}, f32[2,32,64]{2,1,0:T(8,128)}, f32[2,32,64]{2,1,0:T(8,128)}, f32[2,32,64]{2,1,0:T(8,128)}) fusion(f32[27,2,32,64]{3,2,1,0:T(8,128)S(1)} %copy.266, f32[1,32,64]{2,1,0:T(8,128)S(1)} %get-tuple-element.7, pred[1,32,64]{2,1,0:T(8,128)(4,1)S(1)} %bitcast.176, f32[1,32,64]{2,1,0:T(8,128)S(1)} %get-tuple-element.6, ...), kind=kLoop, calls=%fused_computation.67 | loop fusion | flops 32768 | bytes 172032 | tf_op jit(solution)/shard_map/jit(_where)/select_n | solution.py:181
  86.5 1.0 copy_dynamic-update-slice_fusion.26
  87.5 0.9 copy_dynamic-update-slice_fusion.25
  92.1 0.9 copy_dynamic-update-slice_fusion.20
  93.0 0.9 copy_dynamic-update-slice_fusion.19
  94.0 0.9 copy_dynamic-update-slice_fusion.18
  102.4 0.9 copy_dynamic-update-slice_fusion.4
  103.3 0.9 copy_dynamic-update-slice_fusion.3
  104.2 0.9 copy_dynamic-update-slice_fusion.2
  107.0 3.6 %reshape.290 = f32[8,27,512]{2,0,1:T(8,128)} reshape(f32[2,4,27,2,16,16]{5,4,3,1,0,2:T(8,128)S(1)} %bitcast.165) | data formatting | bytes 884736 | tf_op jit(solution)/shard_map/reshape | solution.py:119
  110.6 1.3 %copy.328 = f32[8,27,512]{2,1,0:T(8,128)S(1)} copy(f32[8,27,512]{2,0,1:T(8,128)} %reshape.290) | data formatting | bytes 884736 | tf_op jit(solution)/shard_map/reshape | solution.py:119
  112.7 1.1 copy.329
  (162 shorter events, 49.5 us)
Async XLA Ops:
  10.5 3.6 %copy-start.19 = (s32[8]{0:T(128)S(1)}, s32[8]{0:T(128)}, u32[]{:S(2)}) copy-start(s32[8]{0:T(128)} %param.9) | copy-start | bytes 100
  10.5 3.8 %copy-start.16 = (f32[27,27,1,1]{1,0,3,2:T(8,128)S(1)}, f32[27,27,1,1]{1,0,3,2:T(8,128)}, u32[]{:S(2)}) copy-start(f32[27,27,1,1]{1,0,3,2:T(8,128)} %constant.98) | copy-start | bytes 8752
  14.2 26.8 %copy-start.13 = (f32[3,2,32,16]{2,3,1,0:T(8,128)S(1)}, f32[3,2,32,16]{2,3,1,0:T(8,128)}, u32[]{:S(2)}) copy-start(f32[3,2,32,16]{2,3,1,0:T(8,128)} %param.10) | copy-start | bytes 36868
  14.3 27.8 %copy-start.15 = (f32[27,27,1,1]{1,0,3,2:T(8,128)S(1)}, f32[27,27,1,1]{1,0,3,2:T(8,128)}, u32[]{:S(2)}) copy-start(f32[27,27,1,1]{1,0,3,2:T(8,128)} %constant.97) | copy-start | bytes 8752
  14.3 27.8 %copy-start.20 = (f32[27]{0:T(128)S(1)}, f32[27]{0:T(128)}, u32[]{:S(2)}) copy-start(f32[27]{0:T(128)} %param.11) | copy-start | bytes 328
  20.9 1.3 %collective-permute-start = (f32[3,2,32,16]{2,3,1,0:T(8,128)S(1)}, f32[3,2,32,16]{2,3,1,0:T(8,128)S(1)}, u32[]{:S(2)}, u32[]{:S(2)}) collective-permute-start(f32[3,2,32,16]{2,3,1,0:T(8,128)S(1)} %fusion.7), channel_id=1, source_target_pairs={{0,1},{1,0},{2,3},{3,2},{4,5},{5,4},{6,7},{7,6},{8,9},{9,8},{10,11... | collective-permute-start | bytes 36872 | tf_op jit(solution)/shard_map/ppermute | solution.py:35
  22.2 4.2 %collective-permute-start.1 = (f32[3,2,32,16]{2,3,1,0:T(8,128)S(1)}, f32[3,2,32,16]{2,3,1,0:T(8,128)S(1)}, u32[]{:S(2)}, u32[]{:S(2)}) collective-permute-start(f32[3,2,32,16]{2,3,1,0:T(8,128)S(1)} %add.60), channel_id=1, source_target_pairs={{0,2},{1,3},{2,0},{3,1},{4,6},{5,7},{6,4},{7,5},{8,10},{9,11},{10,... | collective-permute-start | bytes 36872 | tf_op jit(solution)/shard_map/ppermute | solution.py:35
  26.4 5.6 %collective-permute-start.2 = (f32[3,2,32,16]{2,3,1,0:T(8,128)S(1)}, f32[3,2,32,16]{2,3,1,0:T(8,128)S(1)}, u32[]{:S(2)}, u32[]{:S(2)}) collective-permute-start(f32[3,2,32,16]{2,3,1,0:T(8,128)S(1)} %add.61), channel_id=1, source_target_pairs={{0,4},{1,5},{2,6},{3,7},{4,0},{5,1},{6,2},{7,3},{8,12},{9,13},{10,... | collective-permute-start | bytes 36872 | tf_op jit(solution)/shard_map/ppermute | solution.py:35
  32.0 8.9 %collective-permute-start.3 = (f32[3,2,32,16]{2,3,1,0:T(8,128)S(1)}, f32[3,2,32,16]{2,3,1,0:T(8,128)S(1)}, u32[]{:S(2)}, u32[]{:S(2)}) collective-permute-start(f32[3,2,32,16]{2,3,1,0:T(8,128)S(1)} %add.62), channel_id=1, source_target_pairs={{0,8},{1,9},{2,10},{3,11},{4,12},{5,13},{6,14},{7,15},{8,0},{9,1},... | collective-permute-start | bytes 36872 | tf_op jit(solution)/shard_map/ppermute | solution.py:35
  42.0 4.6 %copy-start.21 = (s32[1,1,6]{2,1,0:T(1,128)S(1)}, s32[1,1,6]{2,1,0:T(1,128)}, u32[]{:S(2)}) copy-start(s32[1,1,6]{2,1,0:T(1,128)} %param.8) | copy-start | bytes 76
  43.6 9.1 %copy-start = (f32[27,2,32,64]{3,0,2,1:T(8,128)}, f32[27,2,32,64]{3,0,2,1:T(8,128)S(1)}, u32[]{:S(2)}) copy-start(f32[27,2,32,64]{3,0,2,1:T(8,128)S(1)} %fusion.2) | copy-start | bytes 1327108
  44.2 4.1 %collective-permute-start.4 = (f32[28,2,1,64]{3,2,1,0:T(1,128)S(1)}, f32[28,2,1,64]{3,2,1,0:T(1,128)S(1)}, u32[]{:S(2)}, u32[]{:S(2)}) collective-permute-start(f32[28,2,1,64]{3,2,1,0:T(1,128)S(1)} %get-tuple-element.32), channel_id=1, source_target_pairs={{0,16},{16,32},{32,48},{48,64},{64,80},{80,96},{96,112},{112,128},... | collective-permute-start | bytes 43016 | tf_op jit(solution)/shard_map/ppermute | solution.py:23
  45.5 7.2 %collective-permute-start.5 = (f32[28,2,1,64]{3,2,1,0:T(1,128)S(1)}, f32[28,2,1,64]{3,2,1,0:T(1,128)S(1)}, u32[]{:S(2)}, u32[]{:S(2)}) collective-permute-start(f32[28,2,1,64]{3,2,1,0:T(1,128)S(1)} %get-tuple-element.33), channel_id=1, source_target_pairs={{16,0},{32,16},{48,32},{64,48},{80,64},{96,80},{112,96},{128,112},... | collective-permute-start | bytes 43016 | tf_op jit(solution)/shard_map/ppermute | solution.py:26
  54.2 5.8 %collective-permute-start.7 = (f32[28,2,34,1]{2,1,3,0:T(2,128)S(1)}, f32[28,2,34,1]{2,1,3,0:T(2,128)S(1)}, u32[]{:S(2)}, u32[]{:S(2)}) collective-permute-start(f32[28,2,34,1]{2,1,3,0:T(2,128)S(1)} %copy.268), channel_id=1, source_target_pairs={{1,0},{2,1},{3,2},{4,3},{5,4},{6,5},{7,6},{8,7},{9,8},{10,9},{11,1... | collective-permute-start | bytes 22856 | tf_op jit(solution)/shard_map/ppermute | solution.py:26
  54.2 5.3 %collective-permute-start.6 = (f32[28,2,34,1]{2,1,3,0:T(2,128)S(1)}, f32[28,2,34,1]{2,1,3,0:T(2,128)S(1)}, u32[]{:S(2)}, u32[]{:S(2)}) collective-permute-start(f32[28,2,34,1]{2,1,3,0:T(2,128)S(1)} %copy.267), channel_id=1, source_target_pairs={{0,1},{1,2},{2,3},{3,4},{4,5},{5,6},{6,7},{7,8},{8,9},{9,10},{10,1... | collective-permute-start | bytes 22856 | tf_op jit(solution)/shard_map/ppermute | solution.py:23
  61.3 2.5 %copy-start.14 = (pred[32,64]{1,0:T(8,128)(4,1)}, pred[32,64]{1,0:T(8,128)(4,1)S(1)}, u32[]{:S(2)}) copy-start(pred[32,64]{1,0:T(8,128)(4,1)S(1)} %get-tuple-element.55) | copy-start | bytes 6148
  73.9 2.6 %copy-start.12 = (f32[1,32,64]{2,1,0:T(8,128)S(1)}, f32[1,32,64]{2,1,0:T(8,128)}, u32[]{:S(2)}) copy-start(f32[1,32,64]{2,1,0:T(8,128)} %get-tuple-element.5) | copy-start | bytes 24580
  73.9 4.1 %copy-start.7 = (f32[2,32,64]{2,1,0:T(8,128)S(1)}, f32[2,32,64]{2,1,0:T(8,128)}, u32[]{:S(2)}) copy-start(f32[2,32,64]{2,1,0:T(8,128)} %get-tuple-element.43) | copy-start | bytes 49156
  73.9 4.9 %copy-start.6 = (f32[2,32,64]{2,1,0:T(8,128)S(1)}, f32[2,32,64]{2,1,0:T(8,128)}, u32[]{:S(2)}) copy-start(f32[2,32,64]{2,1,0:T(8,128)} %get-tuple-element.44) | copy-start | bytes 49156
  74.0 8.7 %copy-start.11 = (f32[1,2,32,64]{3,2,1,0:T(8,128)S(1)}, f32[1,2,32,64]{3,2,1,0:T(8,128)}, u32[]{:S(2)}) copy-start(f32[1,2,32,64]{3,2,1,0:T(8,128)} %get-tuple-element.25) | copy-start | bytes 49156
  74.0 10.2 %copy-start.10 = (f32[2,32,64]{2,1,0:T(8,128)S(1)}, f32[2,32,64]{2,1,0:T(8,128)}, u32[]{:S(2)}) copy-start(f32[2,32,64]{2,1,0:T(8,128)} %get-tuple-element.38) | copy-start | bytes 49156
  74.0 11.0 %copy-start.9 = (f32[2,32,64]{2,1,0:T(8,128)S(1)}, f32[2,32,64]{2,1,0:T(8,128)}, u32[]{:S(2)}) copy-start(f32[2,32,64]{2,1,0:T(8,128)} %get-tuple-element.39) | copy-start | bytes 49156
  74.0 11.8 %copy-start.8 = (f32[2,32,64]{2,1,0:T(8,128)S(1)}, f32[2,32,64]{2,1,0:T(8,128)}, u32[]{:S(2)}) copy-start(f32[2,32,64]{2,1,0:T(8,128)} %get-tuple-element.40) | copy-start | bytes 49156
  86.5 12.9 %copy-start.5 = (f32[1,2,2,16,4,16]{5,4,3,2,1,0:T(4,128)S(1)}, f32[1,2,2,16,4,16]{5,4,3,2,1,0:T(4,128)}, u32[]{:S(2)}) copy-start(f32[1,2,2,16,4,16]{5,4,3,2,1,0:T(4,128)} %stack.342) | copy-start | bytes 49156
  86.5 13.0 %copy-start.4 = (f32[1,2,2,16,4,16]{5,4,3,2,1,0:T(4,128)S(1)}, f32[1,2,2,16,4,16]{5,4,3,2,1,0:T(4,128)}, u32[]{:S(2)}) copy-start(f32[1,2,2,16,4,16]{5,4,3,2,1,0:T(4,128)} %stack.346) | copy-start | bytes 49156
  86.5 13.9 %copy-start.3 = (f32[1,2,2,16,4,16]{5,4,3,2,1,0:T(4,128)S(1)}, f32[1,2,2,16,4,16]{5,4,3,2,1,0:T(4,128)}, u32[]{:S(2)}) copy-start(f32[1,2,2,16,4,16]{5,4,3,2,1,0:T(4,128)} %stack.351) | copy-start | bytes 49156
  86.5 14.9 %copy-start.1 = (f32[1,2,2,16,4,16]{5,4,3,2,1,0:T(4,128)S(1)}, f32[1,2,2,16,4,16]{5,4,3,2,1,0:T(4,128)}, u32[]{:S(2)}) copy-start(f32[1,2,2,16,4,16]{5,4,3,2,1,0:T(4,128)} %stack.356) | copy-start | bytes 49156
  86.5 14.9 %copy-start.2 = (f32[1,2,2,16,4,16]{5,4,3,2,1,0:T(4,128)S(1)}, f32[1,2,2,16,4,16]{5,4,3,2,1,0:T(4,128)}, u32[]{:S(2)}) copy-start(f32[1,2,2,16,4,16]{5,4,3,2,1,0:T(4,128)} %stack.360) | copy-start | bytes 49156
  102.4 10.2 %copy-start.17 = (pred[6]{0:T(512)(128)(4,1)S(1)}, pred[6]{0:T(512)(128)(4,1)}, u32[]{:S(2)}) copy-start(pred[6]{0:T(512)(128)(4,1)} %get-tuple-element.62) | copy-start | bytes 22
  102.4 10.2 %copy-start.18 = (f32[6]{0:T(128)S(1)}, f32[6]{0:T(128)}, u32[]{:S(2)}) copy-start(f32[6]{0:T(128)} %get-tuple-element.63) | copy-start | bytes 76

commit v3 on v2

v3 whole, which is shorter than its diff:
```python
import jax
import jax.numpy as jnp
import numpy as np
from jax import lax
from jax.experimental import pallas as pl
from jax.experimental.pallas import tpu as pltpu
from jax.sharding import PartitionSpec as P

BE = 16
TX = 4
TY = 2


NUDGE_GAIN = 0.5
TWO_PI = 6.283185307179586
HIGHEST = lax.Precision.HIGHEST


def butterfly_sum(value, axis):
    count = lax.axis_size(axis)
    stride = 1
    while stride < count:
        value = value + lax.ppermute(value, axis, [(i, i ^ stride) for i in range(count)])
        stride *= 2
    return value


def ring_pairs(axis):
    count = lax.axis_size(axis)
    forward = [(i, (i + 1) % count) for i in range(count)]
    backward = [(target, source) for source, target in forward]
    return forward, backward


def lattice_tables():
    one_weights = np.array([1.0 / 6.0, 2.0 / 3.0, 1.0 / 6.0])
    speeds = np.array(
        [
            [along_x - 1, along_y - 1, along_z - 1]
            for along_x in range(3)
            for along_y in range(3)
            for along_z in range(3)
        ]
    )
    weights = np.array(
        [
            one_weights[along_x] * one_weights[along_y] * one_weights[along_z]
            for along_x in range(3)
            for along_y in range(3)
            for along_z in range(3)
        ]
    )
    vander = np.array([[1.0, 1.0, 1.0], [-1.0, 0.0, 1.0], [1.0, 0.0, 1.0]])
    undo_vander = np.array([[0.0, -0.5, 0.5], [1.0, 0.0, -1.0], [0.0, 0.5, 0.5]])
    moment_matrix = np.kron(vander, np.kron(vander, vander))
    inverse = np.kron(undo_vander, np.kron(undo_vander, undo_vander))
    forward = jnp.asarray(moment_matrix * weights[None, :], dtype=jnp.float32)
    backward = jnp.asarray(inverse / weights[:, None], dtype=jnp.float32)
    return (forward, backward, speeds)


def mode_basis_at(mode_ids, positions, length):
    phase_ids = positions[:, None] * mode_ids[None, :] % length
    angles = phase_ids.astype(jnp.float32) * (TWO_PI / length)
    return jnp.concatenate([jnp.cos(angles), jnp.sin(angles)], axis=1)


def collide_tile(moments, velocity, nudge_tile, backward, relaxation_frequencies):
    density = moments[0]
    shifted = velocity + nudge_tile
    powers = jnp.stack([jnp.ones_like(shifted), shifted, shifted * shifted + 1.0 / 3.0], axis=0)
    equilibrium = (
        density[None, None, None]
        * powers[:, None, None, 0]
        * powers[None, :, None, 1]
        * powers[None, None, :, 2]
    )
    equilibrium = equilibrium.reshape(moments.shape)
    relaxed = moments - relaxation_frequencies[:, None, None] * (moments - equilibrium)
    return jnp.einsum("ij,jrl->irl", backward, relaxed, precision=HIGHEST)


def stream_kernel(pad_ref, side_ref, out_ref):
    rows = out_ref.shape[1]
    lanes = out_ref.shape[2]
    half = lanes // 2
    _, _, speeds = lattice_tables()
    lane = lax.broadcasted_iota(jnp.int32, (rows, lanes), 1)
    upper = lane >= half
    column = lane % half
    solid_channel = pad_ref.shape[0] - 1

    def joined(channel, cx, cy):
        window = slice(1 - cy, 1 - cy + rows)
        plane = pad_ref[channel, window, :]
        if cx == 1:
            low = side_ref[channel, window, 0:1]
            high = side_ref[channel, window, 1:2]
            plane = jnp.where(lane == lanes - 1, low, jnp.where(lane == half - 1, high, plane))
        elif cx == -1:
            low = side_ref[channel, window, 2:3]
            high = side_ref[channel, window, 3:4]
            plane = jnp.where(lane == half, low, jnp.where(lane == 0, high, plane))
        return plane

    def moved(plane, shift):
        shift = shift % lanes
        if shift == 0:
            return plane
        return pltpu.roll(plane, shift, 1)

    blocked_of = {}
    for cx in (-1, 0, 1):
        for cy in (-1, 0, 1):
            blocked_of[(cx, cy)] = moved(joined(solid_channel, cx, cy), cx) > 0.5
    for heading in range(27):
        cx, cy, cz = (int(v) for v in speeds[heading])
        blocked = blocked_of[(cx, cy)]
        bounced = pad_ref[26 - heading, 1:1 + rows, :]
        if cz == 0:
            source = moved(joined(heading, cx, cy), cx)
        elif cz == 1:
            source = moved(joined(heading, cx, cy), half + cx)
            blocked = jnp.logical_or(blocked, jnp.logical_not(upper))
        else:
            source = jnp.where(
                upper,
                moved(joined(heading + 2, cx, cy), cx),
                moved(joined(heading, cx, cy), half + cx),
            )
        out_ref[heading] = jnp.where(blocked, bounced, source)


def stream(padded, sides):
    channels = padded.shape[0] - 1
    rows = padded.shape[1] - 2
    lanes = padded.shape[2]
    return pl.pallas_call(
        stream_kernel,
        out_shape=jax.ShapeDtypeStruct((channels, rows, lanes), jnp.float32),
        in_specs=[
            pl.BlockSpec(memory_space=pltpu.VMEM),
            pl.BlockSpec(memory_space=pltpu.VMEM),
        ],
        out_specs=pl.BlockSpec(memory_space=pltpu.VMEM),
    )(padded, sides)


def on_device(
    scaled_distributions,
    remaining_brick_places,
    retained_wavenumbers,
    regional_amplitudes,
    relaxation_frequencies,
):
    forward, backward, speeds = lattice_tables()
    slot_state = scaled_distributions[0, 0]
    living_brick_keys = remaining_brick_places[0, 0]
    seats = living_brick_keys.shape[0]
    channels = slot_state.shape[1]
    levels = slot_state.shape[2] // (BE * BE)
    rows_tile = TY * BE
    cols_tile = TX * BE
    lanes = levels * cols_tile
    positions = jnp.arange(TX * TY, dtype=jnp.int32)
    matches = living_brick_keys[None, :] == positions[:, None]
    slot_of = jnp.sum(jnp.where(matches, jnp.arange(seats, dtype=jnp.int32)[None, :], 0), axis=1)
    present = jnp.any(matches, axis=1)
    picked = jnp.take(slot_state, slot_of, axis=0) * present[:, None, None].astype(jnp.float32)
    pops_tile = (
        picked.reshape(TY, TX, channels, levels, BE, BE)
        .transpose(2, 0, 4, 3, 1, 5)
        .reshape(channels, rows_tile, lanes)
    )
    fluid_blocks = present.reshape(TY, TX).astype(jnp.float32)
    fluid_map = jnp.broadcast_to(
        fluid_blocks[:, None, None, :, None], (TY, BE, levels, TX, BE)
    ).reshape(rows_tile, lanes)
    moments = jnp.einsum("ij,jrl->irl", forward, pops_tile, precision=HIGHEST)
    safe_density = jnp.where(fluid_map > 0.5, moments[0], 1.0)
    wind_tile = jnp.stack([moments[9], moments[3], moments[1]], axis=0) / safe_density[None]
    line_length = lax.axis_size("line") * cols_tile
    own_columns = lax.axis_index("line") * cols_tile + jnp.arange(cols_tile, dtype=jnp.int32)
    mode_basis = mode_basis_at(retained_wavenumbers, own_columns, line_length)
    partial = jnp.einsum(
        "krzx,xm->kzrm", wind_tile.reshape(3, rows_tile, levels, cols_tile), mode_basis,
        precision=HIGHEST,
    )
    coefficients = butterfly_sum(partial, "line")
    misfit = regional_amplitudes - 2.0 / line_length * coefficients
    nudge_tile = NUDGE_GAIN * jnp.einsum(
        "kzrm,xm->krzx", misfit, mode_basis, precision=HIGHEST
    ).reshape(3, rows_tile, lanes)
    post_tile = collide_tile(moments, wind_tile, nudge_tile, backward, relaxation_frequencies)
    extended = jnp.concatenate([post_tile, (1.0 - fluid_map)[None]], axis=0)
    ahead, behind = ring_pairs("curve")
    below = lax.ppermute(extended[:, rows_tile - 1:], "curve", ahead)
    above = lax.ppermute(extended[:, :1], "curve", behind)
    padded = jnp.concatenate([below, extended, above], axis=1)
    ahead, behind = ring_pairs("line")
    half = cols_tile
    to_right = jnp.stack([padded[:, :, half - 1], padded[:, :, lanes - 1]], axis=2)
    to_left = jnp.stack([padded[:, :, 0], padded[:, :, half]], axis=2)
    from_left = lax.ppermute(to_right, "line", ahead)
    from_right = lax.ppermute(to_left, "line", behind)
    sides = jnp.concatenate([from_left, from_right], axis=2)
    read_tile = stream(padded, sides)
    blocks = (
        read_tile.reshape(channels, TY, BE, levels, TX, BE)
        .transpose(1, 4, 0, 3, 2, 5)
        .reshape(TY * TX, channels, levels * BE * BE)
    )
    occupied = living_brick_keys >= 0
    new_state = jnp.take(blocks, jnp.maximum(living_brick_keys, 0), axis=0)
    new_state = new_state * occupied[:, None, None].astype(jnp.float32)
    return new_state[None, None]


def solution(mesh):
    return jax.shard_map(
        on_device,
        mesh=mesh,
        in_specs=(
            P("curve", "line", None, None, None),
            P("curve", "line", None),
            P(),
            P(None, None, "curve", None),
            P(),
        ),
        out_specs=P("curve", "line", None, None, None),
        check_vma=False,
    )
```

time: 115 us -> 76 us (0.66)
  the two profiles are of different devices: /device:TPU:30 before, /device:TPU:111 now
where the time goes in v3:
time: 76 us; the launch traced here: 75.7 us
  local copies, waits for them, and re-layouts  27.7 us (36%)
  waiting for transfers between devices  19.4 us (26%)
  starting transfers between devices  14.4 us (19%)
  other arithmetic  5.96 us (8%)
  Pallas kernels  3.98 us (5%)
  matrix products  3.89 us (5%)
    ppermute x4, waiting for transfers between devices, butterfly_sum(): lax.ppermute(value, axis, [(i, i ^ stride) for i in range(count)])  10.5 us
    reshape x2, local copies, waits for them, and re-layouts, on_device(): blocks = read_tile.reshape(channels, TY, BE, levels, TX, BE).transpose(1,...  7.95 us
    ppermute x1, starting transfers between devices, on_device(): from_left = lax.ppermute(to_right, 'line', ahead)  7.81 us
    ppermute x4, starting transfers between devices, butterfly_sum(): lax.ppermute(value, axis, [(i, i ^ stride) for i in range(count)])  5 us
    transpose x1, local copies, waits for them, and re-layouts, on_device(): pops_tile = picked.reshape(TY, TX, channels, levels, BE, BE).transpose(2,...  4.53 us
    ppermute x1, waiting for transfers between devices, on_device(): from_right = lax.ppermute(to_left, 'line', behind)  4.15 us
    pallas_call x1, Pallas kernels, stream(): pl.pallas_call(stream_kernel, out_shape=jax.ShapeDtypeStruct((channels, r...  3.98 us
    gather x3, local copies, waits for them, and re-layouts, on_device(): jnp.take(slot_state, slot_of, axis=0)  3.79 us
  transfers between devices with their start and end apart: 8, of which 8 were waited for; matrix products, arithmetic and copies ran while one was open for 1% of the time, Pallas kernels for 0%

profile of v3, /device:TPU:111, one launch (start us, length us, event | category | flops | bytes accessed | tf_op | source)
XLA Modules:
  0.0 75.7 jit_solution(8075334643518401068)
XLA Ops:
  0.0 0.7 maximum_bitcast_fusion.3
  0.7 0.8 %select_reduce_fusion = s32[8]{0:T(128)S(1)} fusion(s32[6]{0:T(128)} %bitcast.72), kind=kLoop, calls=%fused_computation.52 | loop fusion | flops 136 | bytes 56 | tf_op jit(solution)/shard_map/reduce_sum | solution.py:167
  1.4 0.8 %fusion.21 = pred[8]{0:T(512)(128)(4,1)S(1)} fusion(s32[6]{0:T(128)} %bitcast.73), kind=kLoop, calls=%fused_computation.54 | loop fusion | flops 88 | bytes 32 | tf_op jit(solution)/shard_map/reduce_or | solution.py:168
  2.3 1.0 %copy.112 = f32[1,1,6,27,512]{4,3,1,2,0:T(8,128)S(1)} copy(f32[1,1,6,27,512]{4,1,3,2,0:T(1,128)} %param.7) | data formatting | bytes 663552
  3.3 0.6 gather_fusion
  3.9 1.0 %copy.75 = f32[8,27,512]{2,0,1:T(8,128)} copy(f32[8,27,512]{2,1,0:T(8,128)S(1)} %gather_fusion) | data formatting | bytes 884736 | tf_op jit(solution)/shard_map/jit(_take)/gather | solution.py:169
  4.9 2.2 %gather.13 = f32[2,4,27,2,16,16]{5,4,3,1,0,2:T(8,128)S(1)} reshape(f32[8,27,512]{2,0,1:T(8,128)} %copy.75) | data formatting | bytes 884736 | tf_op jit(solution)/shard_map/jit(_take)/gather | solution.py:169
  7.2 2.3 %multiply_bitcast_fusion = f32[27,2,16,2,4,16]{5,2,3,4,1,0:T(8,128)} fusion(f32[2,4,27,2,16,16]{5,4,3,1,0,2:T(8,128)S(1)} %gather.13, f32[2,4]{1,0:T(2,128)S(1)} %reshape.224, pred[2,4]{1,0:T(4,128)(4,1)S(1)} %compare_and_fusion), kind=kLoop, calls=%fused_computation.2 | loop fusion | flops 221184 | bytes 884776 | tf_op jit(solution)/shard_map/transpose | solution.py:172
  9.6 4.5 %copy.76 = f32[27,2,16,2,4,16]{0,5,4,3,2,1:T(8,128)S(1)} copy(f32[27,2,16,2,4,16]{5,2,3,4,1,0:T(8,128)} %multiply_bitcast_fusion) | data formatting | bytes 884736 | tf_op jit(solution)/shard_map/transpose | solution.py:172
  14.4 2.2 %fusion.32 = f32[27,32,128]{2,0,1:T(8,128)S(1)} fusion(f32[27,27,1]{1,0,2:T(8,128)S(1)} %copy-done.3, f32[27,32,128]{0,2,1:T(8,128)S(1)} %bitcast.61), kind=kOutput, calls=%fused_computation.74 | convolution fusion | flops 35831808 | bytes 887652 | tf_op jit(solution)/shard_map/ij,jrl->irl/dot_general | solution.py:179
  16.5 0.5 broadcast.212
  17.1 0.8 %fusion.29 = (f32[32,128]{1,0:T(8,128)S(1)}, f32[1,32,128]{2,0,1:T(1,128)S(1)}, f32[1,32,128]{2,0,1:T(1,128)S(1)}, f32[1,32,128]{2,0,1:T(1,128)S(1)}, f32[32,128...) fusion(f32[]{:T(128)} %broadcast.212, pred[1,32,128]{2,0,1:T(4,128)(4,1)S(1)} %gt.20, ...), kind=kLoop, calls=%fused_computation.71 | loop fusion | flops 4096 | bytes 184324 | tf_op jit(solution)/shard_map/jit(_where)/select_n | solution.py:180
  18.9 0.8 %collective-permute-start = (f32[3,2,32,16]{2,3,1,0:T(8,128)S(1)}, f32[3,2,32,16]{2,3,1,0:T(8,128)S(1)}, u32[]{:S(2)}, u32[]{:S(2)}) collective-permute-start(f32[3,2,32,16]{2,3,1,0:T(8,128)S(1)} %convolution_bitcast_fusion), channel_id=1, source_target_pairs={{0,1},{1,0},{2,3},{3,2},{4,5},{5,4},{6,7},{7,6},{8,9},{9,8},{10,11... | collective-permute-start | bytes 36872 | tf_op jit(solution)/shard_map/ppermute | solution.py:23
  19.6 0.9 %collective-permute-done = f32[3,2,32,16]{2,3,1,0:T(8,128)S(1)} collective-permute-done((f32[3,2,32,16]{2,3,1,0:T(8,128)S(1)}, f32[3,2,32,16]{2,3,1,0:T(8,128)S(1)}, u32[]{:S(2)}, u32[]{:S(2)}) %collective-permute-start) | collective-permute-done | bytes 12320 | tf_op jit(solution)/shard_map/ppermute | solution.py:23
  20.6 2.9 %collective-permute-done.1 = f32[3,2,32,16]{2,3,1,0:T(8,128)S(1)} collective-permute-done((f32[3,2,32,16]{2,3,1,0:T(8,128)S(1)}, f32[3,2,32,16]{2,3,1,0:T(8,128)S(1)}, u32[]{:S(2)}, u32[]{:S(2)}) %collective-permute-start.1) | collective-permute-done | bytes 12320 | tf_op jit(solution)/shard_map/ppermute | solution.py:23
  23.7 4.1 %collective-permute-done.2 = f32[3,2,32,16]{2,3,1,0:T(8,128)S(1)} collective-permute-done((f32[3,2,32,16]{2,3,1,0:T(8,128)S(1)}, f32[3,2,32,16]{2,3,1,0:T(8,128)S(1)}, u32[]{:S(2)}, u32[]{:S(2)}) %collective-permute-start.2) | collective-permute-done | bytes 12320 | tf_op jit(solution)/shard_map/ppermute | solution.py:23
  27.8 4.1 %collective-permute-start.3 = (f32[3,2,32,16]{2,3,1,0:T(8,128)S(1)}, f32[3,2,32,16]{2,3,1,0:T(8,128)S(1)}, u32[]{:S(2)}, u32[]{:S(2)}) collective-permute-start(f32[3,2,32,16]{2,3,1,0:T(8,128)S(1)} %add.80), channel_id=1, source_target_pairs={{0,8},{1,9},{2,10},{3,11},{4,12},{5,13},{6,14},{7,15},{8,0},{9,1},... | collective-permute-start | bytes 36872 | tf_op jit(solution)/shard_map/ppermute | solution.py:23
  32.0 2.6 %collective-permute-done.3 = f32[3,2,32,16]{2,3,1,0:T(8,128)S(1)} collective-permute-done((f32[3,2,32,16]{2,3,1,0:T(8,128)S(1)}, f32[3,2,32,16]{2,3,1,0:T(8,128)S(1)}, u32[]{:S(2)}, u32[]{:S(2)}) %collective-permute-start.3) | collective-permute-done | bytes 12320 | tf_op jit(solution)/shard_map/ppermute | solution.py:23
  35.5 0.9 %fusion.3 = f32[27,32,128]{2,0,1:T(8,128)S(1)} fusion(f32[27,27,1]{1,0,2:T(8,128)S(1)} %copy-done.2, f32[27,32,128]{2,0,1:T(8,128)S(1)} %fusion.32, f32[27,32,128]{2,1,0:T(8,128)S(1)} %bitcast.64, f32[27]{0:T(128)S(1)} %copy-done.4), kind=kOutput, calls=%fused_computation.10 | convolution fusion | flops 36163584 | bytes 1330128 | tf_op jit(solution)/shard_map/ij,jrl->irl/dot_general | solution.py:80
  36.7 1.3 %collective-permute-start.4 = (f32[28,1,128]{2,1,0:T(1,128)S(1)}, f32[28,1,128]{2,1,0:T(1,128)S(1)}, u32[]{:S(2)}, u32[]{:S(2)}) collective-permute-start(f32[28,1,128]{2,1,0:T(1,128)S(1)} %get-tuple-element.18), channel_id=1, source_target_pairs={{0,16},{16,32},{32,48},{48,64},{64,80},{80,96},{96,112},{112,128},... | collective-permute-start | bytes 43016 | tf_op jit(solution)/shard_map/ppermute | solution.py:197
  38.2 1.1 %collective-permute-done.4 = f32[28,1,128]{2,1,0:T(1,128)S(1)} collective-permute-done((f32[28,1,128]{2,1,0:T(1,128)S(1)}, f32[28,1,128]{2,1,0:T(1,128)S(1)}, u32[]{:S(2)}, u32[]{:S(2)}) %collective-permute-start.4) | collective-permute-done | bytes 14368 | tf_op jit(solution)/shard_map/ppermute | solution.py:197
  39.3 3.3 %collective-permute-done.5 = f32[28,1,128]{2,1,0:T(1,128)S(1)} collective-permute-done((f32[28,1,128]{2,1,0:T(1,128)S(1)}, f32[28,1,128]{2,1,0:T(1,128)S(1)}, u32[]{:S(2)}, u32[]{:S(2)}) %collective-permute-start.5) | collective-permute-done | bytes 14368 | tf_op jit(solution)/shard_map/ppermute | solution.py:198
  42.7 0.5 fusion.30
  43.9 7.8 %collective-permute-start.6 = (f32[28,34,2]{1,2,0:T(2,128)S(1)}, f32[28,34,2]{1,2,0:T(2,128)S(1)}, u32[]{:S(2)}, u32[]{:S(2)}) collective-permute-start(f32[28,34,2]{1,2,0:T(2,128)S(1)} %pad_maximum_fusion.3), channel_id=1, source_target_pairs={{0,1},{1,2},{2,3},{3,4},{4,5},{5,6},{6,7},{7,8},{8,9},{9,10},{10,1... | collective-permute-start | bytes 22856 | tf_op jit(solution)/shard_map/ppermute | solution.py:204
  52.7 4.1 %collective-permute-done.7 = f32[28,34,2]{1,2,0:T(2,128)S(1)} collective-permute-done((f32[28,34,2]{1,2,0:T(2,128)S(1)}, f32[28,34,2]{1,2,0:T(2,128)S(1)}, u32[]{:S(2)}, u32[]{:S(2)}) %collective-permute-start.7) | collective-permute-done | bytes 7648 | tf_op jit(solution)/shard_map/ppermute | solution.py:205
  56.9 1.1 %copy.92.side_ref = f32[28,34,4]{2,1,0:T(8,128)} copy(f32[28,34,4]{1,2,0:T(4,128)S(1)} %pad_maximum_fusion.2) | data formatting | bytes 30464 | tf_op jit(solution)/shard_map/concatenate | solution.py:206
  58.0 4.0 %shard_map.73 = f32[27,32,128]{2,1,0:T(8,128)} custom-call(f32[28,34,128]{2,1,0:T(8,128)} %copy-done, f32[28,34,4]{2,1,0:T(8,128)} %copy.92.side_ref), custom_call_target="tpu_custom_call" | custom-call | tf_op jit(solution)/shard_map/pallas_call | solution.py:138
  62.0 3.0 %copy.93 = f32[27,32,128]{0,2,1:T(8,128)} copy(f32[27,32,128]{2,1,0:T(8,128)} %shard_map.73) | data formatting | bytes 884736 | tf_op jit(solution)/shard_map/pallas_call | solution.py:138
  65.0 4.4 %copy.99 = f32[2,4,27,2,16,16]{5,4,3,2,1,0:T(8,128)S(1)} copy(f32[2,4,27,2,16,16]{2,5,1,3,4,0:T(8,128)} %bitcast.62) | data formatting | bytes 884736 | tf_op jit(solution)/shard_map/reshape | solution.py:211
  69.4 3.6 %reshape.245 = f32[8,27,512]{2,1,0:T(8,128)} reshape(f32[2,4,27,2,16,16]{5,4,3,2,1,0:T(8,128)S(1)} %copy.99) | data formatting | bytes 884736 | tf_op jit(solution)/shard_map/reshape | solution.py:211
  72.9 1.6 %gather_fusion.1 = f32[6,27,512]{2,1,0:T(8,128)S(1)} fusion(f32[8,27,512]{2,1,0:T(8,128)} %reshape.245, s32[1024]{0:T(1024)S(1)} %get-tuple-element.26), kind=kCustom, calls=%fused_computation.1 | custom fusion | bytes 663576 | tf_op jit(solution)/shard_map/jit(_take)/gather | solution.py:214
  74.7 1.1 %copy.96 = f32[1,1,6,27,512]{4,1,3,2,0:T(1,128)} copy(f32[1,1,6,27,512]{4,3,2,1,0:T(8,128)S(1)} %fusion.5) | data formatting | bytes 663552 | tf_op jit(solution)/shard_map/mul | solution.py:215
  (68 shorter events, 4.9 us)
Async XLA Ops:
  9.6 4.8 %copy-start.3 = (f32[27,27,1]{1,0,2:T(8,128)S(1)}, f32[27,27,1]{1,0,2:T(8,128)}, u32[]{:S(2)}) copy-start(f32[27,27,1]{1,0,2:T(8,128)} %constant.77) | copy-start | bytes 8752
  9.6 8.7 %copy-start.5 = (s32[8]{0:T(128)S(1)}, s32[8]{0:T(128)}, u32[]{:S(2)}) copy-start(s32[8]{0:T(128)} %param.9) | copy-start | bytes 100
  14.1 20.6 %copy-start.1 = (f32[3,2,32,16]{2,3,1,0:T(8,128)S(1)}, f32[3,2,32,16]{2,3,1,0:T(8,128)}, u32[]{:S(2)}) copy-start(f32[3,2,32,16]{2,3,1,0:T(8,128)} %param.10) | copy-start | bytes 36868
  14.1 21.4 %copy-start.2 = (f32[27,27,1]{1,0,2:T(8,128)S(1)}, f32[27,27,1]{1,0,2:T(8,128)}, u32[]{:S(2)}) copy-start(f32[27,27,1]{1,0,2:T(8,128)} %constant.76) | copy-start | bytes 8752
  14.1 21.4 %copy-start.4 = (f32[27]{0:T(128)S(1)}, f32[27]{0:T(128)}, u32[]{:S(2)}) copy-start(f32[27]{0:T(128)} %param.11) | copy-start | bytes 328
  18.9 1.6 %collective-permute-start = (f32[3,2,32,16]{2,3,1,0:T(8,128)S(1)}, f32[3,2,32,16]{2,3,1,0:T(8,128)S(1)}, u32[]{:S(2)}, u32[]{:S(2)}) collective-permute-start(f32[3,2,32,16]{2,3,1,0:T(8,128)S(1)} %convolution_bitcast_fusion), channel_id=1, source_target_pairs={{0,1},{1,0},{2,3},{3,2},{4,5},{5,4},{6,7},{7,6},{8,9},{9,8},{10,11... | collective-permute-start | bytes 36872 | tf_op jit(solution)/shard_map/ppermute | solution.py:23
  20.5 3.0 %collective-permute-start.1 = (f32[3,2,32,16]{2,3,1,0:T(8,128)S(1)}, f32[3,2,32,16]{2,3,1,0:T(8,128)S(1)}, u32[]{:S(2)}, u32[]{:S(2)}) collective-permute-start(f32[3,2,32,16]{2,3,1,0:T(8,128)S(1)} %add.78), channel_id=1, source_target_pairs={{0,2},{1,3},{2,0},{3,1},{4,6},{5,7},{6,4},{7,5},{8,10},{9,11},{10,... | collective-permute-start | bytes 36872 | tf_op jit(solution)/shard_map/ppermute | solution.py:23
  23.6 4.2 %collective-permute-start.2 = (f32[3,2,32,16]{2,3,1,0:T(8,128)S(1)}, f32[3,2,32,16]{2,3,1,0:T(8,128)S(1)}, u32[]{:S(2)}, u32[]{:S(2)}) collective-permute-start(f32[3,2,32,16]{2,3,1,0:T(8,128)S(1)} %add.79), channel_id=1, source_target_pairs={{0,4},{1,5},{2,6},{3,7},{4,0},{5,1},{6,2},{7,3},{8,12},{9,13},{10,... | collective-permute-start | bytes 36872 | tf_op jit(solution)/shard_map/ppermute | solution.py:23
  27.8 6.9 %collective-permute-start.3 = (f32[3,2,32,16]{2,3,1,0:T(8,128)S(1)}, f32[3,2,32,16]{2,3,1,0:T(8,128)S(1)}, u32[]{:S(2)}, u32[]{:S(2)}) collective-permute-start(f32[3,2,32,16]{2,3,1,0:T(8,128)S(1)} %add.80), channel_id=1, source_target_pairs={{0,8},{1,9},{2,10},{3,11},{4,12},{5,13},{6,14},{7,15},{8,0},{9,1},... | collective-permute-start | bytes 36872 | tf_op jit(solution)/shard_map/ppermute | solution.py:23
  36.7 2.6 %collective-permute-start.4 = (f32[28,1,128]{2,1,0:T(1,128)S(1)}, f32[28,1,128]{2,1,0:T(1,128)S(1)}, u32[]{:S(2)}, u32[]{:S(2)}) collective-permute-start(f32[28,1,128]{2,1,0:T(1,128)S(1)} %get-tuple-element.18), channel_id=1, source_target_pairs={{0,16},{16,32},{32,48},{48,64},{64,80},{80,96},{96,112},{112,128},... | collective-permute-start | bytes 43016 | tf_op jit(solution)/shard_map/ppermute | solution.py:197
  38.0 4.7 %collective-permute-start.5 = (f32[28,1,128]{2,1,0:T(1,128)S(1)}, f32[28,1,128]{2,1,0:T(1,128)S(1)}, u32[]{:S(2)}, u32[]{:S(2)}) collective-permute-start(f32[28,1,128]{2,1,0:T(1,128)S(1)} %get-tuple-element.19), channel_id=1, source_target_pairs={{16,0},{32,16},{48,32},{64,48},{80,64},{96,80},{112,96},{128,112},... | collective-permute-start | bytes 43016 | tf_op jit(solution)/shard_map/ppermute | solution.py:198
  42.7 14.1 %copy-start = (f32[28,34,128]{2,1,0:T(8,128)}, f32[28,34,128]{2,1,0:T(8,128)S(1)}, u32[]{:S(2)}) copy-start(f32[28,34,128]{2,1,0:T(8,128)S(1)} %pad_maximum_fusion.pad_ref) | copy-start | bytes 1462276
  42.7 9.6 %copy-start.6 = (s32[1,1,6]{2,1,0:T(1,128)S(1)}, s32[1,1,6]{2,1,0:T(1,128)}, u32[]{:S(2)}) copy-start(s32[1,1,6]{2,1,0:T(1,128)} %param.8) | copy-start | bytes 76
  43.9 8.8 %collective-permute-start.6 = (f32[28,34,2]{1,2,0:T(2,128)S(1)}, f32[28,34,2]{1,2,0:T(2,128)S(1)}, u32[]{:S(2)}, u32[]{:S(2)}) collective-permute-start(f32[28,34,2]{1,2,0:T(2,128)S(1)} %pad_maximum_fusion.3), channel_id=1, source_target_pairs={{0,1},{1,2},{2,3},{3,4},{4,5},{5,6},{6,7},{7,8},{8,9},{9,10},{10,1... | collective-permute-start | bytes 22856 | tf_op jit(solution)/shard_map/ppermute | solution.py:204
  52.3 4.5 %collective-permute-start.7 = (f32[28,34,2]{1,2,0:T(2,128)S(1)}, f32[28,34,2]{1,2,0:T(2,128)S(1)}, u32[]{:S(2)}, u32[]{:S(2)}) collective-permute-start(f32[28,34,2]{1,2,0:T(2,128)S(1)} %pad_maximum_fusion.4), channel_id=1, source_target_pairs={{1,0},{2,1},{3,2},{4,3},{5,4},{6,5},{7,6},{8,7},{9,8},{10,9},{11,1... | collective-permute-start | bytes 22856 | tf_op jit(solution)/shard_map/ppermute | solution.py:205

commit v4 on v3

v4 whole, which is shorter than its diff:
```python
import jax
import jax.numpy as jnp
import numpy as np
from jax import lax
from jax.experimental import pallas as pl
from jax.experimental.pallas import tpu as pltpu
from jax.sharding import PartitionSpec as P

BE = 16
TX = 4
TY = 2


NUDGE_GAIN = 0.5
TWO_PI = 6.283185307179586
HIGHEST = lax.Precision.HIGHEST


def butterfly_sum(value, axis):
    count = lax.axis_size(axis)
    stride = 1
    while stride < count:
        value = value + lax.ppermute(value, axis, [(i, i ^ stride) for i in range(count)])
        stride *= 2
    return value


def ring_pairs(axis):
    count = lax.axis_size(axis)
    forward = [(i, (i + 1) % count) for i in range(count)]
    backward = [(target, source) for source, target in forward]
    return forward, backward


def lattice_tables():
    one_weights = np.array([1.0 / 6.0, 2.0 / 3.0, 1.0 / 6.0])
    speeds = np.array(
        [
            [along_x - 1, along_y - 1, along_z - 1]
            for along_x in range(3)
            for along_y in range(3)
            for along_z in range(3)
        ]
    )
    weights = np.array(
        [
            one_weights[along_x] * one_weights[along_y] * one_weights[along_z]
            for along_x in range(3)
            for along_y in range(3)
            for along_z in range(3)
        ]
    )
    vander = np.array([[1.0, 1.0, 1.0], [-1.0, 0.0, 1.0], [1.0, 0.0, 1.0]])
    undo_vander = np.array([[0.0, -0.5, 0.5], [1.0, 0.0, -1.0], [0.0, 0.5, 0.5]])
    moment_matrix = np.kron(vander, np.kron(vander, vander))
    inverse = np.kron(undo_vander, np.kron(undo_vander, undo_vander))
    forward = jnp.asarray(moment_matrix * weights[None, :], dtype=jnp.float32)
    backward = jnp.asarray(inverse / weights[:, None], dtype=jnp.float32)
    return (forward, backward, speeds)


def mode_basis_at(mode_ids, positions, length):
    phase_ids = positions[:, None] * mode_ids[None, :] % length
    angles = phase_ids.astype(jnp.float32) * (TWO_PI / length)
    return jnp.concatenate([jnp.cos(angles), jnp.sin(angles)], axis=1)


def collide_blocks(moments, velocity, nudge, backward, relaxation_frequencies):
    density = moments[0]
    shifted = velocity + nudge
    powers = jnp.stack([jnp.ones_like(shifted), shifted, shifted * shifted + 1.0 / 3.0], axis=0)
    equilibrium = (
        density[None, None, None]
        * powers[:, None, None, 0]
        * powers[None, :, None, 1]
        * powers[None, None, :, 2]
    )
    equilibrium = equilibrium.reshape(moments.shape)
    relaxed = moments - relaxation_frequencies[:, None, None, None] * (moments - equilibrium)
    return jnp.einsum("ij,jzpl->izpl", backward, relaxed, precision=HIGHEST)


def stream_kernel(pad_ref, side_ref, out_ref):
    blocks = out_ref.shape[2]
    cells = out_ref.shape[3]
    _, _, speeds = lattice_tables()
    lane = lax.broadcasted_iota(jnp.int32, (blocks, cells), 1)
    seat = lax.broadcasted_iota(jnp.int32, (blocks, cells), 0)
    q = lane % BE
    r = lane // BE
    px = seat % TX
    py = seat // TX
    solid_channel = pad_ref.shape[0] - 1
    base = 2 * blocks // 2

    def moved(plane, shift):
        shift = shift % cells
        if shift == 0:
            return plane
        return pltpu.roll(plane, shift, 1)

    def gathered(channel, level, cx, cy):
        shift = cy * BE + cx

        def window(dy, dx):
            start = base - TX * dy - dx
            plane = pad_ref[channel, level, start:start + blocks, :]
            if dx != 0:
                edge = TX - 1 if dx == -1 else 0
                first = (1 - dy) if dx == 1 else (TY + 3 - dy)
                plane = jnp.where(
                    seat == edge,
                    side_ref[channel, level, first:first + 1, :],
                    jnp.where(
                        seat == edge + TX,
                        side_ref[channel, level, first + 1:first + 2, :],
                        plane,
                    ),
                )
            return plane

        value = moved(window(0, 0), shift)
        if cy != 0:
            ycross = r == (0 if cy == 1 else BE - 1)
            value = jnp.where(ycross, moved(window(cy, 0), shift), value)
        if cx != 0:
            xcross = q == (0 if cx == 1 else BE - 1)
            xvalue = moved(window(0, cx), shift - BE * cx)
            if cy != 0:
                xvalue = jnp.where(ycross, moved(window(cy, cx), shift - BE * cx), xvalue)
            value = jnp.where(xcross, xvalue, value)
        return value

    blocked_of = {}
    for cx in (-1, 0, 1):
        for cy in (-1, 0, 1):
            blocked_of[(cx, cy)] = gathered(solid_channel, 0, cx, cy) > 0.5
    for heading in range(27):
        cx, cy, cz = (int(v) for v in speeds[heading])
        blocked = blocked_of[(cx, cy)]
        for level in range(2):
            bounced = pad_ref[26 - heading, level, base:base + blocks, :]
            if cz == 1 and level == 0:
                out_ref[heading, level] = bounced
                continue
            if cz == 0:
                source = gathered(heading, level, cx, cy)
            elif cz == 1:
                source = gathered(heading, 0, cx, cy)
            elif level == 0:
                source = gathered(heading, 1, cx, cy)
            else:
                source = gathered(heading + 2, 1, cx, cy)
            out_ref[heading, level] = jnp.where(blocked, bounced, source)


def stream(padded, sides):
    channels = padded.shape[0] - 1
    levels = padded.shape[1]
    cells = padded.shape[3]
    return pl.pallas_call(
        stream_kernel,
        out_shape=jax.ShapeDtypeStruct((channels, levels, TX * TY, cells), jnp.float32),
        in_specs=[
            pl.BlockSpec(memory_space=pltpu.VMEM),
            pl.BlockSpec(memory_space=pltpu.VMEM),
        ],
        out_specs=pl.BlockSpec(memory_space=pltpu.VMEM),
    )(padded, sides)


def on_device(
    scaled_distributions,
    remaining_brick_places,
    retained_wavenumbers,
    regional_amplitudes,
    relaxation_frequencies,
):
    forward, backward, speeds = lattice_tables()
    slot_state = scaled_distributions[0, 0]
    living_brick_keys = remaining_brick_places[0, 0]
    seats = living_brick_keys.shape[0]
    channels = slot_state.shape[1]
    cells = BE * BE
    levels = slot_state.shape[2] // cells
    blocks = TX * TY
    rows_tile = TY * BE
    cols_tile = TX * BE
    positions = jnp.arange(blocks, dtype=jnp.int32)
    matches = living_brick_keys[None, :] == positions[:, None]
    slot_of = jnp.sum(jnp.where(matches, jnp.arange(seats, dtype=jnp.int32)[None, :], 0), axis=1)
    present = jnp.any(matches, axis=1)
    fluid = present.astype(jnp.float32)
    picked = jnp.take(slot_state.reshape(seats, channels, levels, cells), slot_of, axis=0)
    pops = picked.transpose(1, 2, 0, 3) * fluid[None, None, :, None]
    moments = jnp.einsum("ij,jzpl->izpl", forward, pops, precision=HIGHEST)
    safe_density = jnp.where(present[None, :, None], moments[0], 1.0)
    wind = jnp.stack([moments[9], moments[3], moments[1]], axis=0) / safe_density[None]
    line_length = lax.axis_size("line") * cols_tile
    own_columns = lax.axis_index("line") * cols_tile + jnp.arange(cols_tile, dtype=jnp.int32)
    mode_basis = mode_basis_at(retained_wavenumbers, own_columns, line_length).reshape(TX, BE, -1)
    partial = jnp.einsum(
        "kzyxrq,xqm->kzyrm", wind.reshape(3, levels, TY, TX, BE, BE), mode_basis,
        precision=HIGHEST,
    ).reshape(3, levels, rows_tile, -1)
    coefficients = butterfly_sum(partial, "line")
    misfit = regional_amplitudes - 2.0 / line_length * coefficients
    nudge = NUDGE_GAIN * jnp.einsum(
        "kzyrm,xqm->kzyxrq", misfit.reshape(3, levels, TY, BE, -1), mode_basis,
        precision=HIGHEST,
    ).reshape(3, levels, blocks, cells)
    post = collide_blocks(moments, wind, nudge, backward, relaxation_frequencies)
    solid = jnp.broadcast_to((1.0 - fluid)[None, None, :, None], (1, levels, blocks, cells))
    extended = jnp.concatenate([post, solid], axis=0)
    ahead, behind = ring_pairs("curve")
    top_row = extended[:, :, blocks - TX:, cells - BE:]
    bottom_row = extended[:, :, :TX, :BE]
    below = lax.ppermute(top_row, "curve", ahead)
    above = lax.ppermute(bottom_row, "curve", behind)
    width = channels + 1
    spread_below = jnp.pad(below, ((0, 0), (0, 0), (0, 0), (cells - BE, 0)))
    spread_above = jnp.pad(above, ((0, 0), (0, 0), (0, 0), (0, cells - BE)))
    filler = jnp.zeros((width, levels, TX, cells), jnp.float32)
    padded = jnp.concatenate([filler, spread_below, extended, spread_above, filler], axis=2)
    ahead, behind = ring_pairs("line")
    by_rows = extended.reshape(width, levels, TY, TX, BE, BE)
    right_cols = by_rows[:, :, :, TX - 1, :, BE - 1]
    left_cols = by_rows[:, :, :, 0, :, 0]
    to_right = jnp.concatenate(
        [
            jnp.broadcast_to(below[:, :, TX - 1:, BE - 1:], (width, levels, 1, BE)),
            right_cols,
            jnp.broadcast_to(above[:, :, TX - 1:, BE - 1:], (width, levels, 1, BE)),
        ],
        axis=2,
    )
    to_left = jnp.concatenate(
        [
            jnp.broadcast_to(below[:, :, :1, :1], (width, levels, 1, BE)),
            left_cols,
            jnp.broadcast_to(above[:, :, :1, :1], (width, levels, 1, BE)),
        ],
        axis=2,
    )
    from_left = lax.ppermute(to_right, "line", ahead)
    from_right = lax.ppermute(to_left, "line", behind)
    sides = jnp.concatenate(
        [
            jnp.pad(from_left[..., None], ((0, 0), (0, 0), (0, 0), (0, 0), (BE - 1, 0))),
            jnp.pad(from_right[..., None], ((0, 0), (0, 0), (0, 0), (0, 0), (0, BE - 1))),
        ],
        axis=2,
    ).reshape(width, levels, 2 * (TY + 2), cells)
    result = stream(padded, sides)
    by_block = result.transpose(2, 0, 1, 3).reshape(blocks, channels, levels * cells)
    occupied = living_brick_keys >= 0
    new_state = jnp.take(by_block, jnp.maximum(living_brick_keys, 0), axis=0)
    new_state = new_state * occupied[:, None, None].astype(jnp.float32)
    return new_state[None, None]


def solution(mesh):
    return jax.shard_map(
        on_device,
        mesh=mesh,
        in_specs=(
            P("curve", "line", None, None, None),
            P("curve", "line", None),
            P(),
            P(None, None, "curve", None),
            P(),
        ),
        out_specs=P("curve", "line", None, None, None),
        check_vma=False,
    )
```

time: 76 us -> 55.6 us (0.73)
  the two profiles are of different devices: /device:TPU:111 before, /device:TPU:30 now
where the time goes in v4:
time: 55.6 us; the launch traced here: 55 us
  starting transfers between devices  17.5 us (31%)
  waiting for transfers between devices  14.6 us (26%)
  local copies, waits for them, and re-layouts  12.3 us (22%)
  other arithmetic  4.86 us (9%)
  matrix products  2.72 us (5%)
  Pallas kernels  2.58 us (5%)
    ppermute x4, starting transfers between devices, butterfly_sum(): lax.ppermute(value, axis, [(i, i ^ stride) for i in range(count)])  12.2 us
    ppermute x4, waiting for transfers between devices, butterfly_sum(): lax.ppermute(value, axis, [(i, i ^ stride) for i in range(count)])  7.77 us
    ppermute x1, waiting for transfers between devices, on_device(): above = lax.ppermute(bottom_row, 'curve', behind)  4.41 us
    ppermute x1, starting transfers between devices, on_device(): from_right = lax.ppermute(to_left, 'line', behind)  2.95 us
    concatenate x1, local copies, waits for them, and re-layouts, on_device(): jnp.concatenate([filler, spread_below, extended, spread_above, filler], a...  2.76 us
    pallas_call x1, Pallas kernels, stream(): pl.pallas_call(stream_kernel, out_shape=jax.ShapeDtypeStruct((channels, l...  2.58 us
    ppermute x1, waiting for transfers between devices, on_device(): below = lax.ppermute(top_row, 'curve', ahead)  2.46 us
    unnamed x1, other arithmetic  1.77 us
  transfers between devices with their start and end apart: 8, of which 6 were waited for; matrix products, arithmetic and copies ran while one was open for 6% of the time, Pallas kernels for 0%

profile of v4, /device:TPU:30, one launch (start us, length us, event | category | flops | bytes accessed | tf_op | source)
XLA Modules:
  0.0 55.0 jit_solution(903067789560738552)
XLA Ops:
  0.0 0.8 %fusion.20 = pred[8]{0:T(512)(128)(4,1)S(1)} fusion(s32[6]{0:T(128)} %bitcast.95), kind=kLoop, calls=%fused_computation.65 | loop fusion | flops 88 | bytes 32 | tf_op jit(solution)/shard_map/reduce_or | solution.py:192
  0.8 0.8 %select_reduce_fusion = s32[8]{0:T(128)S(1)} fusion(s32[6]{0:T(128)} %bitcast.96), kind=kLoop, calls=%fused_computation.63 | loop fusion | flops 136 | bytes 56 | tf_op jit(solution)/shard_map/reduce_sum | solution.py:191
  1.6 1.8 %reduce = f32[6,27,512]{2,1,0:T(8,128)S(1)} reduce(f32[1,1,6,27,512]{4,1,3,2,0:T(1,128)} %param.7, f32[]{:T(128)} %constant.90), dimensions={0,1}, to_apply=%param.7.reduce_sub_computation | reduce | bytes 663556 | tf_op args[0]
  3.4 0.2 reshape_squeeze.3
  3.6 1.0 %gather_fusion = f32[8,27,2,256]{3,2,1,0:T(2,128)S(1)} fusion(f32[6,27,2,256]{3,2,1,0:T(2,128)S(1)} %reshape_squeeze.3, s32[1024]{0:T(1024)S(1)} %pad_clamp_fusion.1), kind=kCustom, calls=%fused_computation | custom fusion | bytes 884768 | tf_op jit(solution)/shard_map/jit(_take)/gather | solution.py:194
  4.6 0.3 multiply_bitcast_fusion
  4.9 0.6 %fusion.5 = f32[27,2,8,256]{3,0,2,1:T(8,128)S(1)} fusion(f32[27,27,1,1]{1,0,3,2:T(8,128)S(1)} %copy-done.2, f32[27,2,8,256]{3,1,0,2:T(2,128)S(1)} %multiply_bitcast_fusion), kind=kOutput, calls=%fused_computation.15 | convolution fusion | flops 35831808 | bytes 887652 | tf_op jit(solution)/shard_map/ij,jzpl->izpl/dot_general | solution.py:196
  6.4 0.2 dot_general.23
  6.8 0.3 convolution_bitcast_fusion
  7.2 1.2 %collective-permute-done = f32[3,2,32,16]{2,3,1,0:T(8,128)S(1)} collective-permute-done((f32[3,2,32,16]{2,3,1,0:T(8,128)S(1)}, f32[3,2,32,16]{2,3,1,0:T(8,128)S(1)}, u32[]{:S(2)}, u32[]{:S(2)}) %collective-permute-start) | collective-permute-done | bytes 12320 | tf_op jit(solution)/shard_map/ppermute | solution.py:23
  8.4 2.0 %collective-permute-start.1 = (f32[3,2,32,16]{2,3,1,0:T(8,128)S(1)}, f32[3,2,32,16]{2,3,1,0:T(8,128)S(1)}, u32[]{:S(2)}, u32[]{:S(2)}) collective-permute-start(f32[3,2,32,16]{2,3,1,0:T(8,128)S(1)} %add.88), channel_id=1, source_target_pairs={{0,2},{1,3},{2,0},{3,1},{4,6},{5,7},{6,4},{7,5},{8,10},{9,11},{10,... | collective-permute-start | bytes 36872 | tf_op jit(solution)/shard_map/ppermute | solution.py:23
  10.4 2.2 %collective-permute-done.1 = f32[3,2,32,16]{2,3,1,0:T(8,128)S(1)} collective-permute-done((f32[3,2,32,16]{2,3,1,0:T(8,128)S(1)}, f32[3,2,32,16]{2,3,1,0:T(8,128)S(1)}, u32[]{:S(2)}, u32[]{:S(2)}) %collective-permute-start.1) | collective-permute-done | bytes 12320 | tf_op jit(solution)/shard_map/ppermute | solution.py:23
  12.6 3.4 %collective-permute-start.2 = (f32[3,2,32,16]{2,3,1,0:T(8,128)S(1)}, f32[3,2,32,16]{2,3,1,0:T(8,128)S(1)}, u32[]{:S(2)}, u32[]{:S(2)}) collective-permute-start(f32[3,2,32,16]{2,3,1,0:T(8,128)S(1)} %add.89), channel_id=1, source_target_pairs={{0,4},{1,5},{2,6},{3,7},{4,0},{5,1},{6,2},{7,3},{8,12},{9,13},{10,... | collective-permute-start | bytes 36872 | tf_op jit(solution)/shard_map/ppermute | solution.py:23
  15.9 2.3 %collective-permute-done.2 = f32[3,2,32,16]{2,3,1,0:T(8,128)S(1)} collective-permute-done((f32[3,2,32,16]{2,3,1,0:T(8,128)S(1)}, f32[3,2,32,16]{2,3,1,0:T(8,128)S(1)}, u32[]{:S(2)}, u32[]{:S(2)}) %collective-permute-start.2) | collective-permute-done | bytes 12320 | tf_op jit(solution)/shard_map/ppermute | solution.py:23
  18.2 6.7 %collective-permute-start.3 = (f32[3,2,32,16]{2,3,1,0:T(8,128)S(1)}, f32[3,2,32,16]{2,3,1,0:T(8,128)S(1)}, u32[]{:S(2)}, u32[]{:S(2)}) collective-permute-start(f32[3,2,32,16]{2,3,1,0:T(8,128)S(1)} %add.90), channel_id=1, source_target_pairs={{0,8},{1,9},{2,10},{3,11},{4,12},{5,13},{6,14},{7,15},{8,0},{9,1},... | collective-permute-start | bytes 36872 | tf_op jit(solution)/shard_map/ppermute | solution.py:23
  25.0 2.1 %collective-permute-done.3 = f32[3,2,32,16]{2,3,1,0:T(8,128)S(1)} collective-permute-done((f32[3,2,32,16]{2,3,1,0:T(8,128)S(1)}, f32[3,2,32,16]{2,3,1,0:T(8,128)S(1)}, u32[]{:S(2)}, u32[]{:S(2)}) %collective-permute-start.3) | collective-permute-done | bytes 12320 | tf_op jit(solution)/shard_map/ppermute | solution.py:23
  27.2 1.0 %fusion = f32[3,2,2,4,16,16]{4,5,2,1,0,3:T(8,128)S(1)} fusion(f32[3,2,2,16,16,1]{4,3,2,1,0,5:T(8,128)S(1)} %bitcast.86, f32[4,16,8]{1,2,0:T(8,128)S(1)} %get-tuple-element.30, f32[4,16,8]{1,2,0:T(8,128)S(1)} %get-tuple-element.29), kind=kOutput, calls=%fused_computation.6 | convolution fusion | flops 2372608 | bytes 65536 | tf_op jit(solution)/shard_map/kzyrm,xqm->kzyxrq/dot_general | solution.py:208
  29.1 0.9 %fusion.3 = f32[27,2,8,256]{3,0,2,1:T(8,128)S(1)} fusion(f32[27,27,1,1]{1,0,3,2:T(8,128)S(1)} %copy-done.1, f32[27,2,8,256]{3,0,2,1:T(8,128)S(1)} %fusion.5, f32[27,2,8,256]{3,2,1,0:T(8,128)S(1)} %bitcast.84, f32[27]{0:T(128)S(1)} %copy-done.4), kind=kOutput, calls=%fused_computation.14 | convolution fusion | flops 36163584 | bytes 1330128 | tf_op jit(solution)/shard_map/ij,jzpl->izpl/dot_general | solution.py:80
  30.0 0.3 copy.69
  30.5 0.7 %copy.71 = f32[28,2,8,256]{0,3,2,1:T(8,128)S(1)} copy(f32[28,2,8,256]{3,2,1,0:T(8,128)S(1)} %pad_maximum_fusion) | data formatting | bytes 917504 | tf_op jit(solution)/shard_map/concatenate | solution.py:214
  31.2 1.1 %collective-permute-start.4 = (f32[28,2,4,16]{3,2,1,0:T(4,128)S(1)}, f32[28,2,4,16]{3,2,1,0:T(4,128)S(1)}, u32[]{:S(2)}, u32[]{:S(2)}) collective-permute-start(f32[28,2,4,16]{3,2,1,0:T(4,128)S(1)} %get-tuple-element.22), channel_id=1, source_target_pairs={{0,16},{16,32},{32,48},{48,64},{64,80},{80,96},{96,112},{112,128},... | collective-permute-start | bytes 43016 | tf_op jit(solution)/shard_map/ppermute | solution.py:218
  32.3 1.3 %collective-permute-start.5 = (f32[28,2,4,16]{3,2,1,0:T(4,128)S(1)}, f32[28,2,4,16]{3,2,1,0:T(4,128)S(1)}, u32[]{:S(2)}, u32[]{:S(2)}) collective-permute-start(f32[28,2,4,16]{3,2,1,0:T(4,128)S(1)} %get-tuple-element.21), channel_id=1, source_target_pairs={{16,0},{32,16},{48,32},{64,48},{80,64},{96,80},{112,96},{128,112},... | collective-permute-start | bytes 43016 | tf_op jit(solution)/shard_map/ppermute | solution.py:219
  33.6 2.5 %collective-permute-done.4 = f32[28,2,4,16]{3,2,1,0:T(4,128)S(1)} collective-permute-done((f32[28,2,4,16]{3,2,1,0:T(4,128)S(1)}, f32[28,2,4,16]{3,2,1,0:T(4,128)S(1)}, u32[]{:S(2)}, u32[]{:S(2)}) %collective-permute-start.4) | collective-permute-done | bytes 14368 | tf_op jit(solution)/shard_map/ppermute | solution.py:218
  36.2 4.4 %collective-permute-done.5 = f32[28,2,4,16]{3,2,1,0:T(4,128)S(1)} collective-permute-done((f32[28,2,4,16]{3,2,1,0:T(4,128)S(1)}, f32[28,2,4,16]{3,2,1,0:T(4,128)S(1)}, u32[]{:S(2)}, u32[]{:S(2)}) %collective-permute-start.5) | collective-permute-done | bytes 14368 | tf_op jit(solution)/shard_map/ppermute | solution.py:219
  41.1 3.0 %collective-permute-start.7 = (f32[28,2,4,16]{0,3,2,1:T(8,128)S(1)}, f32[28,2,4,16]{0,3,2,1:T(8,128)S(1)}, u32[]{:S(2)}, u32[]{:S(2)}) collective-permute-start(f32[28,2,4,16]{0,3,2,1:T(8,128)S(1)} %pad_maximum_fusion.3), channel_id=1, source_target_pairs={{1,0},{2,1},{3,2},{4,3},{5,4},{6,5},{7,6},{8,7},{9,8},{10,9},{11,1... | collective-permute-start | bytes 43016 | tf_op jit(solution)/shard_map/ppermute | solution.py:246
  44.3 2.8 %concatenate.33.pad_ref = f32[28,2,24,256]{3,2,1,0:T(8,128)} concatenate(f32[28,2,4,256]{3,2,1,0:T(4,128)S(1)} %broadcast_in_dim.98, f32[28,2,4,256]{3,2,1,0:T(4,128)S(1)} %pad.16, f32[28,2,8,256]{3,2,1,0:T(8,128)S(1)} %pad_maximum_fusion, f32[28,2,4,256]{3,2,1,0:T(4,128)S(1)} %pad.17, f32[28,2,4,256]{3,2,1,0:T(4,128)S(1)} %broadcast_in_dim.98), dimensions={2} | concatenate | bytes 2752512 | tf_op jit(solution)/shard_map/concatenate | solution.py:224
  47.3 0.7 %copy.75 = f32[28,2,8,16,16]{0,4,3,2,1:T(8,128)S(1)} copy(f32[28,2,8,16,16]{0,3,4,2,1:T(8,128)S(1)} %select_maximum_fusion) | data formatting | bytes 917504 | tf_op jit(solution)/shard_map/concatenate | solution.py:247
  47.9 1.5 %copy.76.side_ref = f32[28,2,8,256]{3,2,1,0:T(8,128)} copy(f32[28,2,8,256]{0,3,2,1:T(8,128)S(1)} %bitcast.82) | data formatting | bytes 917504 | tf_op jit(solution)/shard_map/reshape | solution.py:253
  49.4 2.6 %shard_map.73 = f32[27,2,8,256]{3,2,1,0:T(8,128)} custom-call(f32[28,2,24,256]{3,2,1,0:T(8,128)} %concatenate.33.pad_ref, f32[28,2,8,256]{3,2,1,0:T(8,128)} %copy.76.side_ref), custom_call_target="tpu_custom_call" | custom-call | tf_op jit(solution)/shard_map/pallas_call | solution.py:161
  52.0 1.3 %copy.77 = f32[8,27,512]{2,1,0:T(8,128)S(1)} copy(f32[8,27,512]{2,0,1:T(8,128)} %bitcast.85) | data formatting | bytes 884736 | tf_op jit(solution)/shard_map/reshape | solution.py:255
  53.3 0.6 %gather_fusion.1 = f32[6,27,512]{2,1,0:T(8,128)S(1)} fusion(f32[8,27,512]{2,1,0:T(8,128)S(1)} %copy.77, s32[1024]{0:T(1024)S(1)} %pad_clamp_fusion), kind=kCustom, calls=%fused_computation.1 | custom fusion | bytes 663576 | tf_op jit(solution)/shard_map/jit(_take)/gather | solution.py:257
  54.0 1.1 %copy.78 = f32[1,1,6,27,512]{4,1,3,2,0:T(1,128)} copy(f32[1,1,6,27,512]{4,3,2,1,0:T(8,128)S(1)} %fusion.8) | data formatting | bytes 663552 | tf_op jit(solution)/shard_map/mul | solution.py:258
  (72 shorter events, 3.4 us)
Async XLA Ops:
  0.0 4.9 %copy-start.2 = (f32[27,27,1,1]{1,0,3,2:T(8,128)S(1)}, f32[27,27,1,1]{1,0,3,2:T(8,128)}, u32[]{:S(2)}) copy-start(f32[27,27,1,1]{1,0,3,2:T(8,128)} %constant.89) | copy-start | bytes 8752
  4.9 1.7 %copy-start.3 = (s32[8]{0:T(128)S(1)}, s32[8]{0:T(128)}, u32[]{:S(2)}) copy-start(s32[8]{0:T(128)} %param.9) | copy-start | bytes 100
  4.9 5.5 %copy-start.5 = (s32[1,1,6]{2,1,0:T(1,128)S(1)}, s32[1,1,6]{2,1,0:T(1,128)}, u32[]{:S(2)}) copy-start(s32[1,1,6]{2,1,0:T(1,128)} %param.8) | copy-start | bytes 76
  5.5 21.6 %copy-start = (f32[3,2,32,16]{2,3,1,0:T(8,128)S(1)}, f32[3,2,32,16]{2,3,1,0:T(8,128)}, u32[]{:S(2)}) copy-start(f32[3,2,32,16]{2,3,1,0:T(8,128)} %param.10) | copy-start | bytes 36868
  7.1 1.3 %collective-permute-start = (f32[3,2,32,16]{2,3,1,0:T(8,128)S(1)}, f32[3,2,32,16]{2,3,1,0:T(8,128)S(1)}, u32[]{:S(2)}, u32[]{:S(2)}) collective-permute-start(f32[3,2,32,16]{2,3,1,0:T(8,128)S(1)} %convolution_bitcast_fusion), channel_id=1, source_target_pairs={{0,1},{1,0},{2,3},{3,2},{4,5},{5,4},{6,7},{7,6},{8,9},{9,8},{10,11... | collective-permute-start | bytes 36872 | tf_op jit(solution)/shard_map/ppermute | solution.py:23
  8.4 4.2 %collective-permute-start.1 = (f32[3,2,32,16]{2,3,1,0:T(8,128)S(1)}, f32[3,2,32,16]{2,3,1,0:T(8,128)S(1)}, u32[]{:S(2)}, u32[]{:S(2)}) collective-permute-start(f32[3,2,32,16]{2,3,1,0:T(8,128)S(1)} %add.88), channel_id=1, source_target_pairs={{0,2},{1,3},{2,0},{3,1},{4,6},{5,7},{6,4},{7,5},{8,10},{9,11},{10,... | collective-permute-start | bytes 36872 | tf_op jit(solution)/shard_map/ppermute | solution.py:23
  12.6 5.6 %collective-permute-start.2 = (f32[3,2,32,16]{2,3,1,0:T(8,128)S(1)}, f32[3,2,32,16]{2,3,1,0:T(8,128)S(1)}, u32[]{:S(2)}, u32[]{:S(2)}) collective-permute-start(f32[3,2,32,16]{2,3,1,0:T(8,128)S(1)} %add.89), channel_id=1, source_target_pairs={{0,4},{1,5},{2,6},{3,7},{4,0},{5,1},{6,2},{7,3},{8,12},{9,13},{10,... | collective-permute-start | bytes 36872 | tf_op jit(solution)/shard_map/ppermute | solution.py:23
  18.2 8.9 %collective-permute-start.3 = (f32[3,2,32,16]{2,3,1,0:T(8,128)S(1)}, f32[3,2,32,16]{2,3,1,0:T(8,128)S(1)}, u32[]{:S(2)}, u32[]{:S(2)}) collective-permute-start(f32[3,2,32,16]{2,3,1,0:T(8,128)S(1)} %add.90), channel_id=1, source_target_pairs={{0,8},{1,9},{2,10},{3,11},{4,12},{5,13},{6,14},{7,15},{8,0},{9,1},... | collective-permute-start | bytes 36872 | tf_op jit(solution)/shard_map/ppermute | solution.py:23
  25.0 4.1 %copy-start.1 = (f32[27,27,1,1]{1,0,3,2:T(8,128)S(1)}, f32[27,27,1,1]{1,0,3,2:T(8,128)}, u32[]{:S(2)}) copy-start(f32[27,27,1,1]{1,0,3,2:T(8,128)} %constant.88) | copy-start | bytes 8752
  25.0 4.1 %copy-start.4 = (f32[27]{0:T(128)S(1)}, f32[27]{0:T(128)}, u32[]{:S(2)}) copy-start(f32[27]{0:T(128)} %param.11) | copy-start | bytes 328
  31.2 4.9 %collective-permute-start.4 = (f32[28,2,4,16]{3,2,1,0:T(4,128)S(1)}, f32[28,2,4,16]{3,2,1,0:T(4,128)S(1)}, u32[]{:S(2)}, u32[]{:S(2)}) collective-permute-start(f32[28,2,4,16]{3,2,1,0:T(4,128)S(1)} %get-tuple-element.22), channel_id=1, source_target_pairs={{0,16},{16,32},{32,48},{48,64},{64,80},{80,96},{96,112},{112,128},... | collective-permute-start | bytes 43016 | tf_op jit(solution)/shard_map/ppermute | solution.py:218
  32.3 8.4 %collective-permute-start.5 = (f32[28,2,4,16]{3,2,1,0:T(4,128)S(1)}, f32[28,2,4,16]{3,2,1,0:T(4,128)S(1)}, u32[]{:S(2)}, u32[]{:S(2)}) collective-permute-start(f32[28,2,4,16]{3,2,1,0:T(4,128)S(1)} %get-tuple-element.21), channel_id=1, source_target_pairs={{16,0},{32,16},{48,32},{64,48},{80,64},{96,80},{112,96},{128,112},... | collective-permute-start | bytes 43016 | tf_op jit(solution)/shard_map/ppermute | solution.py:219
  40.9 6.2 %collective-permute-start.6 = (f32[28,2,4,16]{0,3,2,1:T(8,128)S(1)}, f32[28,2,4,16]{0,3,2,1:T(8,128)S(1)}, u32[]{:S(2)}, u32[]{:S(2)}) collective-permute-start(f32[28,2,4,16]{0,3,2,1:T(8,128)S(1)} %pad_maximum_fusion.2), channel_id=1, source_target_pairs={{0,1},{1,2},{2,3},{3,4},{4,5},{5,6},{6,7},{7,8},{8,9},{9,10},{10,1... | collective-permute-start | bytes 43016 | tf_op jit(solution)/shard_map/ppermute | solution.py:245
  41.1 5.9 %collective-permute-start.7 = (f32[28,2,4,16]{0,3,2,1:T(8,128)S(1)}, f32[28,2,4,16]{0,3,2,1:T(8,128)S(1)}, u32[]{:S(2)}, u32[]{:S(2)}) collective-permute-start(f32[28,2,4,16]{0,3,2,1:T(8,128)S(1)} %pad_maximum_fusion.3), channel_id=1, source_target_pairs={{1,0},{2,1},{3,2},{4,3},{5,4},{6,5},{7,6},{8,7},{9,8},{10,9},{11,1... | collective-permute-start | bytes 43016 | tf_op jit(solution)/shard_map/ppermute | solution.py:246

commit v5 on v4

--- a/solution.py
+++ b/solution.py
@@ -65,7 +65,12 @@
     return jnp.concatenate([jnp.cos(angles), jnp.sin(angles)], axis=1)
 
 
-def collide_blocks(moments, velocity, nudge, backward, relaxation_frequencies):
+def velocity_of(moments, solid):
+    safe_density = jnp.where(solid > 0.5, 1.0, moments[0])
+    return jnp.stack([moments[9], moments[3], moments[1]], axis=0) / safe_density[None]
+
+
+def collide_cells(moments, velocity, nudge, backward, relaxation_frequencies):
     density = moments[0]
     shifted = velocity + nudge
     powers = jnp.stack([jnp.ones_like(shifted), shifted, shifted * shifted + 1.0 / 3.0], axis=0)
@@ -76,8 +81,9 @@
         * powers[None, None, :, 2]
     )
     equilibrium = equilibrium.reshape(moments.shape)
-    relaxed = moments - relaxation_frequencies[:, None, None, None] * (moments - equilibrium)
-    return jnp.einsum("ij,jzpl->izpl", backward, relaxed, precision=HIGHEST)
+    rates = relaxation_frequencies.reshape((-1,) + (1,) * (moments.ndim - 1))
+    relaxed = moments - rates * (moments - equilibrium)
+    return jnp.einsum("ij,j...->i...", backward, relaxed, precision=HIGHEST)
 
 
 def stream_kernel(pad_ref, side_ref, out_ref):
@@ -193,57 +199,109 @@
     fluid = present.astype(jnp.float32)
     picked = jnp.take(slot_state.reshape(seats, channels, levels, cells), slot_of, axis=0)
     pops = picked.transpose(1, 2, 0, 3) * fluid[None, None, :, None]
+    solid = jnp.broadcast_to((1.0 - fluid)[None, None, :, None], (1, levels, blocks, cells))
+    extended = jnp.concatenate([pops, solid], axis=0)
+    width = channels + 1
+    modes = regional_amplitudes.shape[3]
+
+    ahead, behind = ring_pairs("curve")
+    top_row = extended[:, :, blocks - TX:, cells - BE:]
+    bottom_row = extended[:, :, :TX, :BE]
+    row_size = top_row.size
+
+    def packed(row, amplitude_row):
+        return jnp.concatenate([row.reshape(-1), amplitude_row.reshape(-1)])
+
+    below_message = lax.ppermute(packed(top_row, regional_amplitudes[:, :, rows_tile - 1:]), "curve", ahead)
+    above_message = lax.ppermute(packed(bottom_row, regional_amplitudes[:, :, :1]), "curve", behind)
+    below_pre = below_message[:row_size].reshape(top_row.shape)
+    above_pre = above_message[:row_size].reshape(top_row.shape)
+    amplitude_below = below_message[row_size:].reshape(3, levels, 1, modes)
+    amplitude_above = above_message[row_size:].reshape(3, levels, 1, modes)
+
+    ahead, behind = ring_pairs("line")
+    by_rows = extended.reshape(width, levels, TY, TX, BE, BE)
+    to_right = jnp.concatenate(
+        [
+            jnp.broadcast_to(below_pre[:, :, TX - 1:, BE - 1:], (width, levels, 1, BE)),
+            by_rows[:, :, :, TX - 1, :, BE - 1],
+            jnp.broadcast_to(above_pre[:, :, TX - 1:, BE - 1:], (width, levels, 1, BE)),
+        ],
+        axis=2,
+    )
+    to_left = jnp.concatenate(
+        [
+            jnp.broadcast_to(below_pre[:, :, :1, :1], (width, levels, 1, BE)),
+            by_rows[:, :, :, 0, :, 0],
+            jnp.broadcast_to(above_pre[:, :, :1, :1], (width, levels, 1, BE)),
+        ],
+        axis=2,
+    )
+    left_pre = lax.ppermute(to_right, "line", ahead)
+    right_pre = lax.ppermute(to_left, "line", behind)
+
+    line_length = lax.axis_size("line") * cols_tile
+    first_column = lax.axis_index("line") * cols_tile
+    own_columns = first_column + jnp.arange(cols_tile, dtype=jnp.int32)
+    mode_basis = mode_basis_at(retained_wavenumbers, own_columns, line_length).reshape(TX, BE, -1)
+    edge_columns = jnp.stack([first_column - 1, first_column + cols_tile]) % line_length
+    edge_basis = mode_basis_at(retained_wavenumbers, edge_columns, line_length)
+
     moments = jnp.einsum("ij,jzpl->izpl", forward, pops, precision=HIGHEST)
-    safe_density = jnp.where(present[None, :, None], moments[0], 1.0)
-    wind = jnp.stack([moments[9], moments[3], moments[1]], axis=0) / safe_density[None]
-    line_length = lax.axis_size("line") * cols_tile
-    own_columns = lax.axis_index("line") * cols_tile + jnp.arange(cols_tile, dtype=jnp.int32)
-    mode_basis = mode_basis_at(retained_wavenumbers, own_columns, line_length).reshape(TX, BE, -1)
+    wind = velocity_of(moments, solid[0])
     partial = jnp.einsum(
         "kzyxrq,xqm->kzyrm", wind.reshape(3, levels, TY, TX, BE, BE), mode_basis,
         precision=HIGHEST,
     ).reshape(3, levels, rows_tile, -1)
-    coefficients = butterfly_sum(partial, "line")
-    misfit = regional_amplitudes - 2.0 / line_length * coefficients
+    halo_rows = jnp.stack([below_pre, above_pre], axis=2)
+    halo_row_moments = jnp.einsum("ij,jzhxq->izhxq", forward, halo_rows[:channels], precision=HIGHEST)
+    halo_row_wind = velocity_of(halo_row_moments, halo_rows[channels])
+    halo_partial = jnp.einsum("kzhxq,xqm->kzhm", halo_row_wind, mode_basis, precision=HIGHEST)
+    partial_rows = jnp.concatenate([halo_partial[:, :, :1], partial, halo_partial[:, :, 1:]], axis=2)
+    coefficients = butterfly_sum(partial_rows, "line")
+    amplitudes = jnp.concatenate([amplitude_below, regional_amplitudes, amplitude_above], axis=2)
+    misfit = amplitudes - 2.0 / line_length * coefficients
+
     nudge = NUDGE_GAIN * jnp.einsum(
-        "kzyrm,xqm->kzyxrq", misfit.reshape(3, levels, TY, BE, -1), mode_basis,
+        "kzyrm,xqm->kzyxrq", misfit[:, :, 1:rows_tile + 1].reshape(3, levels, TY, BE, -1), mode_basis,
         precision=HIGHEST,
     ).reshape(3, levels, blocks, cells)
-    post = collide_blocks(moments, wind, nudge, backward, relaxation_frequencies)
-    solid = jnp.broadcast_to((1.0 - fluid)[None, None, :, None], (1, levels, blocks, cells))
+    post = collide_cells(moments, wind, nudge, backward, relaxation_frequencies)
     extended = jnp.concatenate([post, solid], axis=0)
-    ahead, behind = ring_pairs("curve")
-    top_row = extended[:, :, blocks - TX:, cells - BE:]
-    bottom_row = extended[:, :, :TX, :BE]
-    below = lax.ppermute(top_row, "curve", ahead)
-    above = lax.ppermute(bottom_row, "curve", behind)
-    width = channels + 1
+
+    halo_row_misfit = jnp.stack([misfit[:, :, 0], misfit[:, :, rows_tile + 1]], axis=2)
+    halo_row_nudge = NUDGE_GAIN * jnp.einsum(
+        "kzhm,xqm->kzhxq", halo_row_misfit, mode_basis, precision=HIGHEST
+    )
+    halo_row_post = collide_cells(
+        halo_row_moments, halo_row_wind, halo_row_nudge, backward, relaxation_frequencies
+    )
+    below = jnp.concatenate([halo_row_post[:, :, 0], below_pre[channels:]], axis=0)
+    above = jnp.concatenate([halo_row_post[:, :, 1], above_pre[channels:]], axis=0)
+
+    column_misfit = jnp.concatenate(
+        [
+            jnp.broadcast_to(misfit[:, :, :1, None], (3, levels, 1, BE, modes)),
+            misfit[:, :, 1:rows_tile + 1].reshape(3, levels, TY, BE, modes),
+            jnp.broadcast_to(misfit[:, :, rows_tile + 1:, None], (3, levels, 1, BE, modes)),
+        ],
+        axis=2,
+    )
+    columns_pre = jnp.stack([left_pre, right_pre], axis=2)
+    column_moments = jnp.einsum("ij,jzsyr->izsyr", forward, columns_pre[:channels], precision=HIGHEST)
+    column_wind = velocity_of(column_moments, columns_pre[channels])
+    column_nudge = NUDGE_GAIN * jnp.einsum(
+        "kzyrm,sm->kzsyr", column_misfit, edge_basis, precision=HIGHEST
+    )
+    column_post = collide_cells(
+        column_moments, column_wind, column_nudge, backward, relaxation_frequencies
+    )
+    from_left = jnp.concatenate([column_post[:, :, 0], left_pre[channels:]], axis=0)
+    from_right = jnp.concatenate([column_post[:, :, 1], right_pre[channels:]], axis=0)
     spread_below = jnp.pad(below, ((0, 0), (0, 0), (0, 0), (cells - BE, 0)))
     spread_above = jnp.pad(above, ((0, 0), (0, 0), (0, 0), (0, cells - BE)))
     filler = jnp.zeros((width, levels, TX, cells), jnp.float32)
     padded = jnp.concatenate([filler, spread_below, extended, spread_above, filler], axis=2)
-    ahead, behind = ring_pairs("line")
-    by_rows = extended.reshape(width, levels, TY, TX, BE, BE)
-    right_cols = by_rows[:, :, :, TX - 1, :, BE - 1]
-    left_cols = by_rows[:, :, :, 0, :, 0]
-    to_right = jnp.concatenate(
-        [
-            jnp.broadcast_to(below[:, :, TX - 1:, BE - 1:], (width, levels, 1, BE)),
-            right_cols,
-            jnp.broadcast_to(above[:, :, TX - 1:, BE - 1:], (width, levels, 1, BE)),
-        ],
-        axis=2,
-    )
-    to_left = jnp.concatenate(
-        [
-            jnp.broadcast_to(below[:, :, :1, :1], (width, levels, 1, BE)),
-            left_cols,
-            jnp.broadcast_to(above[:, :, :1, :1], (width, levels, 1, BE)),
-        ],
-        axis=2,
-    )
-    from_left = lax.ppermute(to_right, "line", ahead)
-    from_right = lax.ppermute(to_left, "line", behind)
     sides = jnp.concatenate(
         [
             jnp.pad(from_left[..., None], ((0, 0), (0, 0), (0, 0), (0, 0), (BE - 1, 0))),

time: 55.6 us -> 60.5 us (1.088)
  starting transfers between devices: 17.5 us -> 12.1 us
  local copies, waits for them, and re-layouts: 12.3 us -> 17.4 us
  matrix products: 2.72 us -> 6 us
  other arithmetic: 4.86 us -> 6.99 us
  waiting for transfers between devices: 14.6 us -> 13.5 us
    ppermute x4, starting transfers between devices: 12.2 us -> 5.96 us  [butterfly_sum(): lax.ppermute(value, axis, [(i, i ^ stride) for i in range(count)])]
    ppermute x4, waiting for transfers between devices: 6.87 us -> 4.1 us  [the longest x1 2.96 us: on_device(): lax.ppermute(packed(bottom_row, regional_amplitudes[:, :, :1]), 'curve',...]
    dot_general x2 -> x5, matrix products: 1.9 us -> 4.17 us  [the longest x1 1.5 us: on_device(): jnp.einsum('kzyrm,sm->kzsyr', column_misfit, edge_basis, precision=HIGHEST)]
    ppermute x4, waiting for transfers between devices: 7.77 us -> 9.42 us  [butterfly_sum(): lax.ppermute(value, axis, [(i, i ^ stride) for i in range(count)])]
    unnamed x13 -> x26, local copies, waits for them, and re-layouts: 0.04 us -> 1.32 us
    slice x7 -> x24, local copies, waits for them, and re-layouts: 0.66 us -> 1.75 us  [the longest x2 0.22 us: on_device(): above_pre[:, :, TX - 1:, BE - 1:]]
    unnamed x0 -> x4, matrix products: none -> 1.01 us
    reshape x1 -> x9, local copies, waits for them, and re-layouts: 0.08 us -> 1.08 us  [the longest x4 0.41 us: packed(): return jnp.concatenate([row.reshape(-1), amplitude_row.reshape(-1)])]
  transfers between devices with their start and end apart: 8 -> 8, of which waited for: 6 -> 5; matrix products, arithmetic and copies ran while one was open for 6% -> 14% of each run, Pallas kernels for 0% -> 0%
where the time goes in v5:
time: 60.5 us; the launch traced here: 59.5 us
  local copies, waits for them, and re-layouts  17.4 us (29%)
  waiting for transfers between devices  13.5 us (22%)
  starting transfers between devices  12.1 us (20%)
  other arithmetic  6.99 us (12%)
  matrix products  6 us (10%)
  Pallas kernels  2.59 us (4%)
  between operations  0.87 us (1%)
    ppermute x4, waiting for transfers between devices, butterfly_sum(): lax.ppermute(value, axis, [(i, i ^ stride) for i in range(count)])  9.42 us
    ppermute x4, starting transfers between devices, butterfly_sum(): lax.ppermute(value, axis, [(i, i ^ stride) for i in range(count)])  5.96 us
    ppermute x1, starting transfers between devices, on_device(): right_pre = lax.ppermute(to_left, 'line', behind)  3.96 us
    ppermute x1, waiting for transfers between devices, on_device(): lax.ppermute(packed(bottom_row, regional_amplitudes[:, :, :1]), 'curve',...  2.96 us
    concatenate x1, local copies, waits for them, and re-layouts, on_device(): jnp.concatenate([filler, spread_below, extended, spread_above, filler], a...  2.75 us
    pallas_call x1, Pallas kernels, stream(): pl.pallas_call(stream_kernel, out_shape=jax.ShapeDtypeStruct((channels, l...  2.59 us
    ppermute x1, starting transfers between devices, on_device(): lax.ppermute(packed(top_row, regional_amplitudes[:, :, rows_tile - 1:]),...  1.92 us
    unnamed x1, other arithmetic  1.77 us
  transfers between devices with their start and end apart: 8, of which 5 were waited for; matrix products, arithmetic and copies ran while one was open for 14% of the time, Pallas kernels for 0%

profile of v5, /device:TPU:30, one launch (start us, length us, event | category | flops | bytes accessed | tf_op | source)
XLA Modules:
  0.0 59.5 jit_solution(9909249317717709103)
XLA Ops:
  0.0 0.8 %fusion.39 = pred[8]{0:T(512)(128)(4,1)S(1)} fusion(s32[6]{0:T(128)} %bitcast.229), kind=kLoop, calls=%fused_computation.126 | loop fusion | flops 88 | bytes 32 | tf_op jit(solution)/shard_map/reduce_or | solution.py:198
  0.8 0.8 %select_reduce_fusion = s32[8]{0:T(128)S(1)} fusion(s32[6]{0:T(128)} %bitcast.230), kind=kLoop, calls=%fused_computation.124 | loop fusion | flops 136 | bytes 56 | tf_op jit(solution)/shard_map/reduce_sum | solution.py:197
  1.6 1.8 %reduce = f32[6,27,512]{2,1,0:T(8,128)S(1)} reduce(f32[1,1,6,27,512]{4,1,3,2,0:T(1,128)} %param.7, f32[]{:T(128)} %constant.115), dimensions={0,1}, to_apply=%param.7.reduce_sub_computation | reduce | bytes 663556 | tf_op args[0]
  3.6 1.0 %gather_fusion = f32[8,27,2,256]{3,2,1,0:T(2,128)S(1)} fusion(f32[6,27,2,256]{3,2,1,0:T(2,128)S(1)} %reshape_squeeze.3, s32[1024]{0:T(1024)S(1)} %pad_clamp_fusion.1), kind=kCustom, calls=%fused_computation | custom fusion | bytes 884768 | tf_op jit(solution)/shard_map/jit(_take)/gather | solution.py:200
  5.6 1.9 %collective-permute-start = (f32[3680]{0:T(1024)S(1)}, f32[3680]{0:T(1024)S(1)}, u32[]{:S(2)}, u32[]{:S(2)}) collective-permute-start(f32[3680]{0:T(1024)S(1)} %pad_maximum_fusion.11), channel_id=1, source_target_pairs={{0,16},{16,32},{32,48},{48,64},{64,80},{80,96},{96,112},{112,128},... | collective-permute-start | bytes 44168 | tf_op jit(solution)/shard_map/ppermute | solution.py:215
  8.3 0.8 %copy.241 = f32[28,2,8,256]{0,3,2,1:T(8,128)S(1)} copy(f32[28,2,8,256]{3,1,0,2:T(2,128)S(1)} %pad_maximum_fusion) | data formatting | bytes 917504 | tf_op jit(solution)/shard_map/concatenate | solution.py:203
  9.2 0.6 fusion.5
  11.4 0.3 convolution_bitcast_fusion
  12.0 3.0 %collective-permute-done.1 = f32[3680]{0:T(1024)S(1)} collective-permute-done((f32[3680]{0:T(1024)S(1)}, f32[3680]{0:T(1024)S(1)}, u32[]{:S(2)}, u32[]{:S(2)}) %collective-permute-start.1) | collective-permute-done | bytes 14752 | tf_op jit(solution)/shard_map/ppermute | solution.py:216
  16.4 0.3 slice_reduce_fusion.1
  17.4 0.3 convolution_bitcast_fusion.1
  18.0 0.4 collective-permute-start.2
  18.4 4.0 %collective-permute-start.7 = (f32[28,2,4,16]{0,3,2,1:T(8,128)S(1)}, f32[28,2,4,16]{0,3,2,1:T(8,128)S(1)}, u32[]{:S(2)}, u32[]{:S(2)}) collective-permute-start(f32[28,2,4,16]{0,3,2,1:T(8,128)S(1)} %pad_maximum_fusion.8), channel_id=1, source_target_pairs={{1,0},{2,1},{3,2},{4,3},{5,4},{6,5},{7,6},{8,7},{9,8},{10,9},{11,1... | collective-permute-start | bytes 43016 | tf_op jit(solution)/shard_map/ppermute | solution.py:241
  23.2 1.1 %collective-permute-done.7 = f32[28,2,4,16]{0,3,2,1:T(8,128)S(1)} collective-permute-done((f32[28,2,4,16]{0,3,2,1:T(8,128)S(1)}, f32[28,2,4,16]{0,3,2,1:T(8,128)S(1)}, u32[]{:S(2)}, u32[]{:S(2)}) %collective-permute-start.7) | collective-permute-done | bytes 14368 | tf_op jit(solution)/shard_map/ppermute | solution.py:241
  24.3 2.9 %collective-permute-done.3 = f32[3,2,34,16]{2,3,1,0:T(8,128)S(1)} collective-permute-done((f32[3,2,34,16]{2,3,1,0:T(8,128)S(1)}, f32[3,2,34,16]{2,3,1,0:T(8,128)S(1)}, u32[]{:S(2)}, u32[]{:S(2)}) %collective-permute-start.3) | collective-permute-done | bytes 13088 | tf_op jit(solution)/shard_map/ppermute | solution.py:23
  27.2 1.0 %collective-permute-start.4 = (f32[3,2,34,16]{2,3,1,0:T(8,128)S(1)}, f32[3,2,34,16]{2,3,1,0:T(8,128)S(1)}, u32[]{:S(2)}, u32[]{:S(2)}) collective-permute-start(f32[3,2,34,16]{2,3,1,0:T(8,128)S(1)} %add.121), channel_id=1, source_target_pairs={{0,4},{1,5},{2,6},{3,7},{4,0},{5,1},{6,2},{7,3},{8,12},{9,13},{10,... | collective-permute-start | bytes 39176 | tf_op jit(solution)/shard_map/ppermute | solution.py:23
  28.5 3.8 %collective-permute-done.4 = f32[3,2,34,16]{2,3,1,0:T(8,128)S(1)} collective-permute-done((f32[3,2,34,16]{2,3,1,0:T(8,128)S(1)}, f32[3,2,34,16]{2,3,1,0:T(8,128)S(1)}, u32[]{:S(2)}, u32[]{:S(2)}) %collective-permute-start.4) | collective-permute-done | bytes 13088 | tf_op jit(solution)/shard_map/ppermute | solution.py:23
  32.3 4.5 %collective-permute-start.5 = (f32[3,2,34,16]{2,3,1,0:T(8,128)S(1)}, f32[3,2,34,16]{2,3,1,0:T(8,128)S(1)}, u32[]{:S(2)}, u32[]{:S(2)}) collective-permute-start(f32[3,2,34,16]{2,3,1,0:T(8,128)S(1)} %add.122), channel_id=1, source_target_pairs={{0,8},{1,9},{2,10},{3,11},{4,12},{5,13},{6,14},{7,15},{8,0},{9,1},... | collective-permute-start | bytes 39176 | tf_op jit(solution)/shard_map/ppermute | solution.py:23
  36.8 0.3 slice_reduce_fusion
  37.9 2.7 %collective-permute-done.5 = f32[3,2,34,16]{2,3,1,0:T(8,128)S(1)} collective-permute-done((f32[3,2,34,16]{2,3,1,0:T(8,128)S(1)}, f32[3,2,34,16]{2,3,1,0:T(8,128)S(1)}, u32[]{:S(2)}, u32[]{:S(2)}) %collective-permute-start.5) | collective-permute-done | bytes 13088 | tf_op jit(solution)/shard_map/ppermute | solution.py:23
  41.1 0.6 fusion.23
  41.7 1.5 %fusion.10 = f32[2,3,2,4,16]{4,0,3,2,1:T(2,128)S(1)} fusion(f32[3,2,1,16,16]{4,3,2,1,0:T(8,128)S(1)} %broadcast_in_dim.132, f32[3,2,2,16,16]{4,3,2,1,0:T(8,128)S(1)} %bitcast.206, f32[3,2,1,16,16]{4,3,2,1,0:T(8,128)S(1)} %broadcast_in_dim.130, f32[2,8]{1,0:T(2,128)S(1)} %get-tuple-element.64, f32[2,8]{1,0:T(2,128)S(1)} %get-tuple-element.63), kind=kOutput, calls=%fused_computation.33 | convolution fusion | flops 159776 | bytes 27776 | tf_op jit(solution)/shard_map/kzyrm,sm->kzsyr/dot_general | solution.py:293
  44.6 1.2 %copy.257 = f32[28,2,8,16,16]{0,4,3,2,1:T(8,128)S(1)} copy(f32[28,2,8,16,16]{0,3,2,1,4:T(8,128)S(1)} %select_maximum_fusion) | data formatting | bytes 917504 | tf_op jit(solution)/shard_map/concatenate | solution.py:305
  45.8 1.5 %copy.258.side_ref = f32[28,2,8,256]{3,2,1,0:T(8,128)} copy(f32[28,2,8,256]{0,3,2,1:T(8,128)S(1)} %bitcast.186) | data formatting | bytes 917504 | tf_op jit(solution)/shard_map/reshape | solution.py:311
  47.3 1.0 %fusion = f32[3,2,2,4,16,16]{4,5,2,1,0,3:T(8,128)S(1)} fusion(f32[3,2,2,16,16,1]{4,3,2,1,0,5:T(8,128)S(1)} %bitcast.207, f32[4,16,16]{2,1,0:T(8,128)S(1)} %pad_maximum_fusion.10), kind=kOutput, calls=%fused_computation.6 | convolution fusion | flops 2371584 | bytes 65536 | tf_op jit(solution)/shard_map/kzyrm,xqm->kzyxrq/dot_general | solution.py:265
  49.1 0.9 %fusion.3 = f32[27,2,8,256]{3,0,2,1:T(8,128)S(1)} fusion(f32[27,27,1,1]{1,0,3,2:T(8,128)S(1)} %copy-done.3, f32[27,2,8,256]{3,0,2,1:T(8,128)S(1)} %fusion.5, f32[27,2,8,256]{3,2,1,0:T(8,128)S(1)} %bitcast.190, f32[27]{0:T(128)S(1)} %copy-done.6), kind=kOutput, calls=%fused_computation.15 | convolution fusion | flops 36163584 | bytes 1330128 | tf_op jit(solution)/shard_map/ij,j...->i.../dot_general | solution.py:86
  49.9 0.3 copy.238
  51.1 2.8 %concatenate.83.pad_ref = f32[28,2,24,256]{3,2,1,0:T(8,128)} concatenate(f32[28,2,4,256]{3,2,1,0:T(4,128)S(1)} %broadcast_in_dim.113, f32[28,2,4,256]{3,2,1,0:T(4,128)S(1)} %select_maximum_fusion.2, f32[28,2,8,256]{3,2,1,0:T(8,128)S(1)} %pad_maximum_fusion.1, f32[28,2,4,256]{3,2,1,0:T(4,128)S(1)} %select_maximum_fusion.1, f32[28,2,4,256]{3,2,1,0:T(4,128)S(1)} %broadcast_in_dim.113), dimensions={2} | concatenate | bytes 2752512 | tf_op jit(solution)/shard_map/concatenate | solution.py:304
  53.8 2.6 %shard_map.73 = f32[27,2,8,256]{3,2,1,0:T(8,128)} custom-call(f32[28,2,24,256]{3,2,1,0:T(8,128)} %concatenate.83.pad_ref, f32[28,2,8,256]{3,2,1,0:T(8,128)} %copy.258.side_ref), custom_call_target="tpu_custom_call" | custom-call | tf_op jit(solution)/shard_map/pallas_call | solution.py:167
  56.4 1.3 %copy.259 = f32[8,27,512]{2,1,0:T(8,128)S(1)} copy(f32[8,27,512]{2,0,1:T(8,128)} %bitcast.191) | data formatting | bytes 884736 | tf_op jit(solution)/shard_map/reshape | solution.py:313
  57.7 0.6 gather_fusion.1
  58.4 1.1 %copy.260 = f32[1,1,6,27,512]{4,1,3,2,0:T(1,128)} copy(f32[1,1,6,27,512]{4,3,2,1,0:T(8,128)S(1)} %fusion.8) | data formatting | bytes 663552 | tf_op jit(solution)/shard_map/mul | solution.py:316
  (154 shorter events, 11.5 us)
Async XLA Ops:
  1.6 3.7 %copy-start = (f32[3,2,32,16]{2,3,1,0:T(8,128)S(1)}, f32[3,2,32,16]{2,3,1,0:T(8,128)}, u32[]{:S(2)}) copy-start(f32[3,2,32,16]{2,3,1,0:T(8,128)} %param.10) | copy-start | bytes 36868
  3.6 4.7 %copy-start.7 = (s32[1,1,6]{2,1,0:T(1,128)S(1)}, s32[1,1,6]{2,1,0:T(1,128)}, u32[]{:S(2)}) copy-start(s32[1,1,6]{2,1,0:T(1,128)} %param.8) | copy-start | bytes 76
  5.3 3.8 %copy-start.4 = (f32[27,27,1,1]{1,0,3,2:T(8,128)S(1)}, f32[27,27,1,1]{1,0,3,2:T(8,128)}, u32[]{:S(2)}) copy-start(f32[27,27,1,1]{1,0,3,2:T(8,128)} %constant.113) | copy-start | bytes 8752
  5.6 6.1 %collective-permute-start = (f32[3680]{0:T(1024)S(1)}, f32[3680]{0:T(1024)S(1)}, u32[]{:S(2)}, u32[]{:S(2)}) collective-permute-start(f32[3680]{0:T(1024)S(1)} %pad_maximum_fusion.11), channel_id=1, source_target_pairs={{0,16},{16,32},{32,48},{48,64},{64,80},{80,96},{96,112},{112,128},... | collective-permute-start | bytes 44168 | tf_op jit(solution)/shard_map/ppermute | solution.py:215
  7.8 7.1 %collective-permute-start.1 = (f32[3680]{0:T(1024)S(1)}, f32[3680]{0:T(1024)S(1)}, u32[]{:S(2)}, u32[]{:S(2)}) collective-permute-start(f32[3680]{0:T(1024)S(1)} %pad_maximum_fusion.12), channel_id=1, source_target_pairs={{16,0},{32,16},{48,32},{64,48},{80,64},{96,80},{112,96},{128,112},... | collective-permute-start | bytes 44168 | tf_op jit(solution)/shard_map/ppermute | solution.py:216
  9.2 1.7 %copy-start.5 = (s32[8]{0:T(128)S(1)}, s32[8]{0:T(128)}, u32[]{:S(2)}) copy-start(s32[8]{0:T(128)} %param.9) | copy-start | bytes 100
  10.4 5.8 %copy-start.2 = (f32[27,27]{1,0:T(8,128)S(1)}, f32[27,27]{1,0:T(8,128)}, u32[]{:S(2)}) copy-start(f32[27,27]{1,0:T(8,128)} %constant.101.clone) | copy-start | bytes 8752
  15.7 7.5 %collective-permute-start.6 = (f32[28,2,4,16]{0,3,2,1:T(8,128)S(1)}, f32[28,2,4,16]{0,3,2,1:T(8,128)S(1)}, u32[]{:S(2)}, u32[]{:S(2)}) collective-permute-start(f32[28,2,4,16]{0,3,2,1:T(8,128)S(1)} %pad_maximum_fusion.7), channel_id=1, source_target_pairs={{0,1},{1,2},{2,3},{3,4},{4,5},{5,6},{6,7},{7,8},{8,9},{9,10},{10,1... | collective-permute-start | bytes 43016 | tf_op jit(solution)/shard_map/ppermute | solution.py:240
  18.0 4.9 %collective-permute-start.2 = (f32[3,2,34,16]{2,3,1,0:T(8,128)S(1)}, f32[3,2,34,16]{2,3,1,0:T(8,128)S(1)}, u32[]{:S(2)}, u32[]{:S(2)}) collective-permute-start(f32[3,2,34,16]{2,3,1,0:T(8,128)S(1)} %pad_maximum_fusion.9), channel_id=1, source_target_pairs={{0,1},{1,0},{2,3},{3,2},{4,5},{5,4},{6,7},{7,6},{8,9},{9,8},{10,11... | collective-permute-start | bytes 39176 | tf_op jit(solution)/shard_map/ppermute | solution.py:23
  18.4 5.9 %collective-permute-start.7 = (f32[28,2,4,16]{0,3,2,1:T(8,128)S(1)}, f32[28,2,4,16]{0,3,2,1:T(8,128)S(1)}, u32[]{:S(2)}, u32[]{:S(2)}) collective-permute-start(f32[28,2,4,16]{0,3,2,1:T(8,128)S(1)} %pad_maximum_fusion.8), channel_id=1, source_target_pairs={{1,0},{2,1},{3,2},{4,3},{5,4},{6,5},{7,6},{8,7},{9,8},{10,9},{11,1... | collective-permute-start | bytes 43016 | tf_op jit(solution)/shard_map/ppermute | solution.py:241
  23.1 4.2 %collective-permute-start.3 = (f32[3,2,34,16]{2,3,1,0:T(8,128)S(1)}, f32[3,2,34,16]{2,3,1,0:T(8,128)S(1)}, u32[]{:S(2)}, u32[]{:S(2)}) collective-permute-start(f32[3,2,34,16]{2,3,1,0:T(8,128)S(1)} %fusion.75), channel_id=1, source_target_pairs={{0,2},{1,3},{2,0},{3,1},{4,6},{5,7},{6,4},{7,5},{8,10},{9,11},{10,... | collective-permute-start | bytes 39176 | tf_op jit(solution)/shard_map/ppermute | solution.py:23
  27.2 5.1 %collective-permute-start.4 = (f32[3,2,34,16]{2,3,1,0:T(8,128)S(1)}, f32[3,2,34,16]{2,3,1,0:T(8,128)S(1)}, u32[]{:S(2)}, u32[]{:S(2)}) collective-permute-start(f32[3,2,34,16]{2,3,1,0:T(8,128)S(1)} %add.121), channel_id=1, source_target_pairs={{0,4},{1,5},{2,6},{3,7},{4,0},{5,1},{6,2},{7,3},{8,12},{9,13},{10,... | collective-permute-start | bytes 39176 | tf_op jit(solution)/shard_map/ppermute | solution.py:23
  32.3 8.3 %collective-permute-start.5 = (f32[3,2,34,16]{2,3,1,0:T(8,128)S(1)}, f32[3,2,34,16]{2,3,1,0:T(8,128)S(1)}, u32[]{:S(2)}, u32[]{:S(2)}) collective-permute-start(f32[3,2,34,16]{2,3,1,0:T(8,128)S(1)} %add.122), channel_id=1, source_target_pairs={{0,8},{1,9},{2,10},{3,11},{4,12},{5,13},{6,14},{7,15},{8,0},{9,1},... | collective-permute-start | bytes 39176 | tf_op jit(solution)/shard_map/ppermute | solution.py:23
  37.4 6.4 %copy-start.6 = (f32[27]{0:T(128)S(1)}, f32[27]{0:T(128)}, u32[]{:S(2)}) copy-start(f32[27]{0:T(128)} %param.11) | copy-start | bytes 328
  40.7 3.2 %copy-start.1 = (f32[27,27]{1,0:T(8,128)S(1)}, f32[27,27]{1,0:T(8,128)}, u32[]{:S(2)}) copy-start(f32[27,27]{1,0:T(8,128)} %constant.102.clone) | copy-start | bytes 8752
  47.3 1.8 %copy-start.3 = (f32[27,27,1,1]{1,0,3,2:T(8,128)S(1)}, f32[27,27,1,1]{1,0,3,2:T(8,128)}, u32[]{:S(2)}) copy-start(f32[27,27,1,1]{1,0,3,2:T(8,128)} %constant.114) | copy-start | bytes 8752

commit v6 on v4

--- a/solution.py
+++ b/solution.py
@@ -80,18 +80,34 @@
     return jnp.einsum("ij,jzpl->izpl", backward, relaxed, precision=HIGHEST)
 
 
-def stream_kernel(pad_ref, side_ref, out_ref):
+def stream_kernel(post_ref, solid_ref, below_ref, above_ref, left_ref, right_ref, out_ref, spread_ref):
+    channels = out_ref.shape[0]
     blocks = out_ref.shape[2]
     cells = out_ref.shape[3]
+    levels = out_ref.shape[1]
     _, _, speeds = lattice_tables()
+    front = 8
+    grid_row = lax.broadcasted_iota(jnp.int32, (BE, cells), 0)
+    grid_lane = lax.broadcasted_iota(jnp.int32, (BE, cells), 1)
+    tile_copy = (grid_lane % BE == grid_row).astype(jnp.float32)
+    group_copy = (grid_lane // BE == grid_row).astype(jnp.float32)
+    halo_rows = below_ref.shape[0]
+    for slot, (source, copier) in enumerate(
+        ((below_ref, tile_copy), (above_ref, tile_copy), (left_ref, group_copy), (right_ref, group_copy))
+    ):
+        spread_ref[slot, front:front + halo_rows, :] = jnp.dot(
+            source[...], copier, precision=HIGHEST, preferred_element_type=jnp.float32
+        )
     lane = lax.broadcasted_iota(jnp.int32, (blocks, cells), 1)
     seat = lax.broadcasted_iota(jnp.int32, (blocks, cells), 0)
     q = lane % BE
     r = lane // BE
-    px = seat % TX
     py = seat // TX
-    solid_channel = pad_ref.shape[0] - 1
-    base = 2 * blocks // 2
+
+    def own(channel, level):
+        if channel == channels:
+            return solid_ref[...]
+        return post_ref[channel, level]
 
     def moved(plane, shift):
         shift = shift % cells
@@ -101,45 +117,49 @@
 
     def gathered(channel, level, cx, cy):
         shift = cy * BE + cx
-
-        def window(dy, dx):
-            start = base - TX * dy - dx
-            plane = pad_ref[channel, level, start:start + blocks, :]
-            if dx != 0:
-                edge = TX - 1 if dx == -1 else 0
-                first = (1 - dy) if dx == 1 else (TY + 3 - dy)
-                plane = jnp.where(
-                    seat == edge,
-                    side_ref[channel, level, first:first + 1, :],
-                    jnp.where(
-                        seat == edge + TX,
-                        side_ref[channel, level, first + 1:first + 2, :],
-                        plane,
-                    ),
-                )
-            return plane
-
-        value = moved(window(0, 0), shift)
+        first = front + (channel * levels + level) * (TY + 2)
+        base = own(channel, level)
+        if cy != 0:
+            stepped = pltpu.roll(base, TX, 0)
+            if cy == 1:
+                halo = spread_ref[0, first:first + blocks, :]
+                yplane = jnp.where(py == 0, halo, stepped)
+            else:
+                halo = spread_ref[1, first - TX:first - TX + blocks, :]
+                yplane = jnp.where(py == TY - 1, halo, stepped)
+
+        def sideways(plane, dy, dx):
+            plane = pltpu.roll(plane, dx % blocks, 0)
+            edge = 0 if dx == 1 else TX - 1
+            side = 2 if dx == 1 else 3
+            at = first + 1 - dy
+            return jnp.where(
+                seat == edge,
+                spread_ref[side, at:at + 1, :],
+                jnp.where(seat == edge + TX, spread_ref[side, at + 1:at + 2, :], plane),
+            )
+
+        value = moved(base, shift)
         if cy != 0:
             ycross = r == (0 if cy == 1 else BE - 1)
-            value = jnp.where(ycross, moved(window(cy, 0), shift), value)
+            value = jnp.where(ycross, moved(yplane, shift), value)
         if cx != 0:
             xcross = q == (0 if cx == 1 else BE - 1)
-            xvalue = moved(window(0, cx), shift - BE * cx)
+            xvalue = moved(sideways(base, 0, cx), shift - BE * cx)
             if cy != 0:
-                xvalue = jnp.where(ycross, moved(window(cy, cx), shift - BE * cx), xvalue)
+                xvalue = jnp.where(ycross, moved(sideways(yplane, cy, cx), shift - BE * cx), xvalue)
             value = jnp.where(xcross, xvalue, value)
         return value
 
     blocked_of = {}
     for cx in (-1, 0, 1):
         for cy in (-1, 0, 1):
-            blocked_of[(cx, cy)] = gathered(solid_channel, 0, cx, cy) > 0.5
+            blocked_of[(cx, cy)] = gathered(channels, 0, cx, cy) > 0.5
     for heading in range(27):
         cx, cy, cz = (int(v) for v in speeds[heading])
         blocked = blocked_of[(cx, cy)]
-        for level in range(2):
-            bounced = pad_ref[26 - heading, level, base:base + blocks, :]
+        for level in range(levels):
+            bounced = post_ref[26 - heading, level]
             if cz == 1 and level == 0:
                 out_ref[heading, level] = bounced
                 continue
@@ -154,19 +174,17 @@
             out_ref[heading, level] = jnp.where(blocked, bounced, source)
 
 
-def stream(padded, sides):
-    channels = padded.shape[0] - 1
-    levels = padded.shape[1]
-    cells = padded.shape[3]
+def stream(post, solid_plane, below, above, from_left, from_right):
+    channels, levels, blocks, cells = post.shape
+    halo_rows = below.shape[0]
+    vmem = pl.BlockSpec(memory_space=pltpu.VMEM)
     return pl.pallas_call(
         stream_kernel,
-        out_shape=jax.ShapeDtypeStruct((channels, levels, TX * TY, cells), jnp.float32),
-        in_specs=[
-            pl.BlockSpec(memory_space=pltpu.VMEM),
-            pl.BlockSpec(memory_space=pltpu.VMEM),
-        ],
-        out_specs=pl.BlockSpec(memory_space=pltpu.VMEM),
-    )(padded, sides)
+        out_shape=jax.ShapeDtypeStruct((channels, levels, blocks, cells), jnp.float32),
+        in_specs=[vmem] * 6,
+        out_specs=vmem,
+        scratch_shapes=[pltpu.VMEM((4, halo_rows + 16, cells), jnp.float32)],
+    )(post, solid_plane, below, above, from_left, from_right)
 
 
 def on_device(
@@ -212,16 +230,12 @@
     post = collide_blocks(moments, wind, nudge, backward, relaxation_frequencies)
     solid = jnp.broadcast_to((1.0 - fluid)[None, None, :, None], (1, levels, blocks, cells))
     extended = jnp.concatenate([post, solid], axis=0)
+    width = channels + 1
     ahead, behind = ring_pairs("curve")
     top_row = extended[:, :, blocks - TX:, cells - BE:]
     bottom_row = extended[:, :, :TX, :BE]
     below = lax.ppermute(top_row, "curve", ahead)
     above = lax.ppermute(bottom_row, "curve", behind)
-    width = channels + 1
-    spread_below = jnp.pad(below, ((0, 0), (0, 0), (0, 0), (cells - BE, 0)))
-    spread_above = jnp.pad(above, ((0, 0), (0, 0), (0, 0), (0, cells - BE)))
-    filler = jnp.zeros((width, levels, TX, cells), jnp.float32)
-    padded = jnp.concatenate([filler, spread_below, extended, spread_above, filler], axis=2)
     ahead, behind = ring_pairs("line")
     by_rows = extended.reshape(width, levels, TY, TX, BE, BE)
     right_cols = by_rows[:, :, :, TX - 1, :, BE - 1]
@@ -244,14 +258,9 @@
     )
     from_left = lax.ppermute(to_right, "line", ahead)
     from_right = lax.ppermute(to_left, "line", behind)
-    sides = jnp.concatenate(
-        [
-            jnp.pad(from_left[..., None], ((0, 0), (0, 0), (0, 0), (0, 0), (BE - 1, 0))),
-            jnp.pad(from_right[..., None], ((0, 0), (0, 0), (0, 0), (0, 0), (0, BE - 1))),
-        ],
-        axis=2,
-    ).reshape(width, levels, 2 * (TY + 2), cells)
-    result = stream(padded, sides)
+    flat = lambda halo: halo.reshape(-1, BE)
+    solid_plane = jnp.broadcast_to((1.0 - fluid)[:, None], (blocks, cells))
+    result = stream(post, solid_plane, flat(below), flat(above), flat(from_left), flat(from_right))
     by_block = result.transpose(2, 0, 1, 3).reshape(blocks, channels, levels * cells)
     occupied = living_brick_keys >= 0
     new_state = jnp.take(by_block, jnp.maximum(living_brick_keys, 0), axis=0)

time: 55.6 us -> 54.3 us (0.977)
  starting transfers between devices: 17.5 us -> 15.1 us
  waiting for transfers between devices: 14.6 us -> 16.8 us
  local copies, waits for them, and re-layouts: 12.3 us -> 11.2 us
    concatenate x2 -> x0, local copies, waits for them, and re-layouts: 3.43 us -> none  [the longest x1 2.76 us: on_device(): jnp.concatenate([filler, spread_below, extended, spread_above, filler], a...]
    ppermute x0 -> x4, local copies, waits for them, and re-layouts: none -> 2.96 us  [the longest x1 0.77 us: on_device(): from_right = lax.ppermute(to_left, 'line', behind)]
    ppermute x1, starting transfers between devices: 2.95 us -> 0.02 us  [on_device(): from_right = lax.ppermute(to_left, 'line', behind)]
    ppermute x1, waiting for transfers between devices: 0.01 us -> 1.93 us  [on_device(): from_left = lax.ppermute(to_right, 'line', ahead)]
    reshape x1 -> x0, local copies, waits for them, and re-layouts: 1.48 us -> none  [on_device(): sides = jnp.concatenate([jnp.pad(from_left[..., None], ((0, 0), (0, 0), (...]
    dot_general x1, local copies, waits for them, and re-layouts: 0.26 us -> 1.03 us  [collide_blocks(): return jnp.einsum('ij,jzpl->izpl', backward, relaxed, precision=HIGHEST)]
    broadcast_in_dim x1, local copies, waits for them, and re-layouts: 0.03 us -> 0.66 us  [on_device(): solid_plane = jnp.broadcast_to((1.0 - fluid)[:, None], (blocks, cells))]
  transfers between devices with their start and end apart: 8 -> 8, of which waited for: 6 -> 7; matrix products, arithmetic and copies ran while one was open for 6% -> 6% of each run, Pallas kernels for 0% -> 0%
where the time goes in v6:
time: 54.3 us; the launch traced here: 53.9 us
  waiting for transfers between devices  16.8 us (31%)
  starting transfers between devices  15.1 us (28%)
  local copies, waits for them, and re-layouts  11.2 us (21%)
  other arithmetic  4.68 us (9%)
  Pallas kernels  2.96 us (5%)
  matrix products  2.72 us (5%)
    ppermute x4, starting transfers between devices, butterfly_sum(): lax.ppermute(value, axis, [(i, i ^ stride) for i in range(count)])  12.2 us
    ppermute x4, waiting for transfers between devices, butterfly_sum(): lax.ppermute(value, axis, [(i, i ^ stride) for i in range(count)])  7.77 us
    ppermute x1, waiting for transfers between devices, on_device(): above = lax.ppermute(bottom_row, 'curve', behind)  4.48 us
    pallas_call x1, Pallas kernels, stream(): pl.pallas_call(stream_kernel, out_shape=jax.ShapeDtypeStruct((channels, l...  2.96 us
    ppermute x1, waiting for transfers between devices, on_device(): below = lax.ppermute(top_row, 'curve', ahead)  2.63 us
    ppermute x1, waiting for transfers between devices, on_device(): from_left = lax.ppermute(to_right, 'line', ahead)  1.93 us
    unnamed x1, other arithmetic  1.77 us
    ppermute x1, starting transfers between devices, on_device(): above = lax.ppermute(bottom_row, 'curve', behind)  1.28 us
  transfers between devices with their start and end apart: 8, of which 7 were waited for; matrix products, arithmetic and copies ran while one was open for 6% of the time, Pallas kernels for 0%

profile of v6, /device:TPU:30, one launch (start us, length us, event | category | flops | bytes accessed | tf_op | source)
XLA Modules:
  0.0 53.9 jit_solution(5370383947489480461)
XLA Ops:
  0.0 0.8 %fusion.20 = pred[8]{0:T(512)(128)(4,1)S(1)} fusion(s32[6]{0:T(128)} %bitcast.89), kind=kLoop, calls=%fused_computation.66 | loop fusion | flops 88 | bytes 32 | tf_op jit(solution)/shard_map/reduce_or | solution.py:210
  0.8 0.8 %select_reduce_fusion = s32[8]{0:T(128)S(1)} fusion(s32[6]{0:T(128)} %bitcast.90), kind=kLoop, calls=%fused_computation.64 | loop fusion | flops 136 | bytes 56 | tf_op jit(solution)/shard_map/reduce_sum | solution.py:209
  1.6 1.8 %reduce = f32[6,27,512]{2,1,0:T(8,128)S(1)} reduce(f32[1,1,6,27,512]{4,1,3,2,0:T(1,128)} %param.7, f32[]{:T(128)} %constant.79), dimensions={0,1}, to_apply=%param.7.reduce_sub_computation | reduce | bytes 663556 | tf_op args[0]
  3.6 1.0 %gather_fusion = f32[8,27,2,256]{3,2,1,0:T(2,128)S(1)} fusion(f32[6,27,2,256]{3,2,1,0:T(2,128)S(1)} %reshape_squeeze.3, s32[1024]{0:T(1024)S(1)} %pad_clamp_fusion.1), kind=kCustom, calls=%fused_computation | custom fusion | bytes 884768 | tf_op jit(solution)/shard_map/jit(_take)/gather | solution.py:212
  4.9 0.6 %fusion.5 = f32[27,2,8,256]{3,0,2,1:T(8,128)S(1)} fusion(f32[27,27,1,1]{1,0,3,2:T(8,128)S(1)} %copy-done.2, f32[27,2,8,256]{3,1,0,2:T(2,128)S(1)} %multiply_bitcast_fusion), kind=kOutput, calls=%fused_computation.12 | convolution fusion | flops 35831808 | bytes 887652 | tf_op jit(solution)/shard_map/ij,jzpl->izpl/dot_general | solution.py:214
  6.8 0.3 convolution_bitcast_fusion
  7.2 1.2 %collective-permute-done = f32[3,2,32,16]{2,3,1,0:T(8,128)S(1)} collective-permute-done((f32[3,2,32,16]{2,3,1,0:T(8,128)S(1)}, f32[3,2,32,16]{2,3,1,0:T(8,128)S(1)}, u32[]{:S(2)}, u32[]{:S(2)}) %collective-permute-start) | collective-permute-done | bytes 12320 | tf_op jit(solution)/shard_map/ppermute | solution.py:23
  8.4 2.0 %collective-permute-start.1 = (f32[3,2,32,16]{2,3,1,0:T(8,128)S(1)}, f32[3,2,32,16]{2,3,1,0:T(8,128)S(1)}, u32[]{:S(2)}, u32[]{:S(2)}) collective-permute-start(f32[3,2,32,16]{2,3,1,0:T(8,128)S(1)} %add.80), channel_id=1, source_target_pairs={{0,2},{1,3},{2,0},{3,1},{4,6},{5,7},{6,4},{7,5},{8,10},{9,11},{10,... | collective-permute-start | bytes 36872 | tf_op jit(solution)/shard_map/ppermute | solution.py:23
  10.4 2.2 %collective-permute-done.1 = f32[3,2,32,16]{2,3,1,0:T(8,128)S(1)} collective-permute-done((f32[3,2,32,16]{2,3,1,0:T(8,128)S(1)}, f32[3,2,32,16]{2,3,1,0:T(8,128)S(1)}, u32[]{:S(2)}, u32[]{:S(2)}) %collective-permute-start.1) | collective-permute-done | bytes 12320 | tf_op jit(solution)/shard_map/ppermute | solution.py:23
  12.6 3.4 %collective-permute-start.2 = (f32[3,2,32,16]{2,3,1,0:T(8,128)S(1)}, f32[3,2,32,16]{2,3,1,0:T(8,128)S(1)}, u32[]{:S(2)}, u32[]{:S(2)}) collective-permute-start(f32[3,2,32,16]{2,3,1,0:T(8,128)S(1)} %add.81), channel_id=1, source_target_pairs={{0,4},{1,5},{2,6},{3,7},{4,0},{5,1},{6,2},{7,3},{8,12},{9,13},{10,... | collective-permute-start | bytes 36872 | tf_op jit(solution)/shard_map/ppermute | solution.py:23
  15.9 2.3 %collective-permute-done.2 = f32[3,2,32,16]{2,3,1,0:T(8,128)S(1)} collective-permute-done((f32[3,2,32,16]{2,3,1,0:T(8,128)S(1)}, f32[3,2,32,16]{2,3,1,0:T(8,128)S(1)}, u32[]{:S(2)}, u32[]{:S(2)}) %collective-permute-start.2) | collective-permute-done | bytes 12320 | tf_op jit(solution)/shard_map/ppermute | solution.py:23
  18.2 6.7 %collective-permute-start.3 = (f32[3,2,32,16]{2,3,1,0:T(8,128)S(1)}, f32[3,2,32,16]{2,3,1,0:T(8,128)S(1)}, u32[]{:S(2)}, u32[]{:S(2)}) collective-permute-start(f32[3,2,32,16]{2,3,1,0:T(8,128)S(1)} %add.82), channel_id=1, source_target_pairs={{0,8},{1,9},{2,10},{3,11},{4,12},{5,13},{6,14},{7,15},{8,0},{9,1},... | collective-permute-start | bytes 36872 | tf_op jit(solution)/shard_map/ppermute | solution.py:23
  25.0 2.1 %collective-permute-done.3 = f32[3,2,32,16]{2,3,1,0:T(8,128)S(1)} collective-permute-done((f32[3,2,32,16]{2,3,1,0:T(8,128)S(1)}, f32[3,2,32,16]{2,3,1,0:T(8,128)S(1)}, u32[]{:S(2)}, u32[]{:S(2)}) %collective-permute-start.3) | collective-permute-done | bytes 12320 | tf_op jit(solution)/shard_map/ppermute | solution.py:23
  27.2 1.0 %fusion = f32[3,2,2,4,16,16]{4,5,2,1,0,3:T(8,128)S(1)} fusion(f32[3,2,2,16,16,1]{4,3,2,1,0,5:T(8,128)S(1)} %bitcast.86, f32[4,16,8]{1,2,0:T(8,128)S(1)} %get-tuple-element.30, f32[4,16,8]{1,2,0:T(8,128)S(1)} %get-tuple-element.29), kind=kOutput, calls=%fused_computation.3 | convolution fusion | flops 2372608 | bytes 65536 | tf_op jit(solution)/shard_map/kzyrm,xqm->kzyxrq/dot_general | solution.py:226
  29.1 0.9 %fusion.3 = f32[27,2,8,256]{3,0,2,1:T(8,128)S(1)} fusion(f32[27,27,1,1]{1,0,3,2:T(8,128)S(1)} %copy-done.1, f32[27,2,8,256]{3,0,2,1:T(8,128)S(1)} %fusion.5, f32[27,2,8,256]{3,2,1,0:T(8,128)S(1)} %bitcast.80, f32[27]{0:T(128)S(1)} %copy-done.4), kind=kOutput, calls=%fused_computation.11 | convolution fusion | flops 36163584 | bytes 1330128 | tf_op jit(solution)/shard_map/ij,jzpl->izpl/dot_general | solution.py:80
  30.2 0.7 %copy.65 = f32[28,2,8,256]{0,3,2,1:T(8,128)S(1)} copy(f32[28,2,8,256]{3,0,2,1:T(8,128)S(1)} %pad_maximum_fusion) | data formatting | bytes 917504 | tf_op jit(solution)/shard_map/concatenate | solution.py:232
  30.9 1.1 %collective-permute-start.4 = (f32[28,2,4,16]{3,0,2,1:T(8,128)S(1)}, f32[28,2,4,16]{3,0,2,1:T(8,128)S(1)}, u32[]{:S(2)}, u32[]{:S(2)}) collective-permute-start(f32[28,2,4,16]{3,0,2,1:T(8,128)S(1)} %get-tuple-element.19), channel_id=1, source_target_pairs={{0,16},{16,32},{32,48},{48,64},{64,80},{80,96},{96,112},{112,128},... | collective-permute-start | bytes 43016 | tf_op jit(solution)/shard_map/ppermute | solution.py:237
  32.0 1.3 %collective-permute-start.5 = (f32[28,2,4,16]{3,0,2,1:T(8,128)S(1)}, f32[28,2,4,16]{3,0,2,1:T(8,128)S(1)}, u32[]{:S(2)}, u32[]{:S(2)}) collective-permute-start(f32[28,2,4,16]{3,0,2,1:T(8,128)S(1)} %get-tuple-element.18), channel_id=1, source_target_pairs={{16,0},{32,16},{48,32},{64,48},{80,64},{96,80},{112,96},{128,112},... | collective-permute-start | bytes 43016 | tf_op jit(solution)/shard_map/ppermute | solution.py:238
  33.3 2.6 %collective-permute-done.4 = f32[28,2,4,16]{3,0,2,1:T(8,128)S(1)} collective-permute-done((f32[28,2,4,16]{3,0,2,1:T(8,128)S(1)}, f32[28,2,4,16]{3,0,2,1:T(8,128)S(1)}, u32[]{:S(2)}, u32[]{:S(2)}) %collective-permute-start.4) | collective-permute-done | bytes 14368 | tf_op jit(solution)/shard_map/ppermute | solution.py:237
  36.1 4.5 %collective-permute-done.5 = f32[28,2,4,16]{3,0,2,1:T(8,128)S(1)} collective-permute-done((f32[28,2,4,16]{3,0,2,1:T(8,128)S(1)}, f32[28,2,4,16]{3,0,2,1:T(8,128)S(1)}, u32[]{:S(2)}, u32[]{:S(2)}) %collective-permute-start.5) | collective-permute-done | bytes 14368 | tf_op jit(solution)/shard_map/ppermute | solution.py:238
  40.8 0.5 collective-permute-start.6
  41.3 1.0 %copy.68.post_ref = f32[27,2,8,256]{3,2,1,0:T(8,128)} copy(f32[27,2,8,256]{3,0,2,1:T(8,128)S(1)} %fusion.3) | data formatting | bytes 884736 | tf_op jit(solution)/shard_map/ij,jzpl->izpl/dot_general | solution.py:80
  42.3 0.7 %copy.63 = f32[28,2,4,16]{3,2,1,0:T(4,128)} copy(f32[28,2,4,16]{3,0,2,1:T(8,128)S(1)} %collective-permute-done.4) | data formatting | bytes 28672 | tf_op jit(solution)/shard_map/ppermute | solution.py:237
  43.0 0.7 %copy.64 = f32[28,2,4,16]{3,2,1,0:T(4,128)} copy(f32[28,2,4,16]{3,0,2,1:T(8,128)S(1)} %collective-permute-done.5) | data formatting | bytes 28672 | tf_op jit(solution)/shard_map/ppermute | solution.py:238
  43.8 0.8 %copy.67 = f32[28,2,4,16]{3,2,1,0:T(4,128)} copy(f32[28,2,4,16]{0,3,2,1:T(8,128)S(1)} %collective-permute-done.7) | data formatting | bytes 28672 | tf_op jit(solution)/shard_map/ppermute | solution.py:260
  44.5 1.9 %collective-permute-done.6 = f32[28,2,4,16]{0,3,2,1:T(8,128)S(1)} collective-permute-done((f32[28,2,4,16]{0,3,2,1:T(8,128)S(1)}, f32[28,2,4,16]{0,3,2,1:T(8,128)S(1)}, u32[]{:S(2)}, u32[]{:S(2)}) %collective-permute-start.6) | collective-permute-done | bytes 14368 | tf_op jit(solution)/shard_map/ppermute | solution.py:259
  46.5 0.8 %copy.66 = f32[28,2,4,16]{3,2,1,0:T(4,128)} copy(f32[28,2,4,16]{0,3,2,1:T(8,128)S(1)} %collective-permute-done.6) | data formatting | bytes 28672 | tf_op jit(solution)/shard_map/ppermute | solution.py:259
  47.2 0.7 %broadcast_in_dim.101.solid_ref = f32[8,256]{1,0:T(8,128)} broadcast(f32[8]{0:T(128)S(1)} %broadcast_subtract_fusion), dimensions={0} | broadcast | bytes 8224 | tf_op jit(solution)/shard_map/broadcast_in_dim | solution.py:262
  47.9 3.0 %shard_map.73 = f32[27,2,8,256]{3,2,1,0:T(8,128)} custom-call(f32[27,2,8,256]{3,2,1,0:T(8,128)} %copy.68.post_ref, f32[8,256]{1,0:T(8,128)} %broadcast_in_dim.101.solid_ref, f32[224,16]{1,0:T(8,128)} %bitcast.82, f32[224,16]{1,0:T(8,128)} %bitcast.83, f32[224,16]{1,0:T(8,128)} %bitcast.85, f32[224,16]{1,0:T(8,128)} %bitcast.84), custom_call_target="tpu_custom_call" | custom-call | tf_op jit(solution)/shard_map/pallas_call | solution.py:181
  50.8 1.3 %copy.69 = f32[8,27,512]{2,1,0:T(8,128)S(1)} copy(f32[8,27,512]{2,0,1:T(8,128)} %bitcast.81) | data formatting | bytes 884736 | tf_op jit(solution)/shard_map/reshape | solution.py:264
  52.1 0.6 %gather_fusion.1 = f32[6,27,512]{2,1,0:T(8,128)S(1)} fusion(f32[8,27,512]{2,1,0:T(8,128)S(1)} %copy.69, s32[1024]{0:T(1024)S(1)} %pad_clamp_fusion), kind=kCustom, calls=%fused_computation.1 | custom fusion | bytes 663576 | tf_op jit(solution)/shard_map/jit(_take)/gather | solution.py:266
  52.8 1.1 %copy.70 = f32[1,1,6,27,512]{4,1,3,2,0:T(1,128)} copy(f32[1,1,6,27,512]{4,3,2,1,0:T(8,128)S(1)} %fusion.8) | data formatting | bytes 663552 | tf_op jit(solution)/shard_map/mul | solution.py:267
  (66 shorter events, 3.5 us)
Async XLA Ops:
  0.0 4.9 %copy-start.2 = (f32[27,27,1,1]{1,0,3,2:T(8,128)S(1)}, f32[27,27,1,1]{1,0,3,2:T(8,128)}, u32[]{:S(2)}) copy-start(f32[27,27,1,1]{1,0,3,2:T(8,128)} %constant.78) | copy-start | bytes 8752
  4.9 1.7 %copy-start.3 = (s32[8]{0:T(128)S(1)}, s32[8]{0:T(128)}, u32[]{:S(2)}) copy-start(s32[8]{0:T(128)} %param.9) | copy-start | bytes 100
  4.9 5.5 %copy-start.5 = (s32[1,1,6]{2,1,0:T(1,128)S(1)}, s32[1,1,6]{2,1,0:T(1,128)}, u32[]{:S(2)}) copy-start(s32[1,1,6]{2,1,0:T(1,128)} %param.8) | copy-start | bytes 76
  5.5 21.6 %copy-start = (f32[3,2,32,16]{2,3,1,0:T(8,128)S(1)}, f32[3,2,32,16]{2,3,1,0:T(8,128)}, u32[]{:S(2)}) copy-start(f32[3,2,32,16]{2,3,1,0:T(8,128)} %param.10) | copy-start | bytes 36868
  7.1 1.3 %collective-permute-start = (f32[3,2,32,16]{2,3,1,0:T(8,128)S(1)}, f32[3,2,32,16]{2,3,1,0:T(8,128)S(1)}, u32[]{:S(2)}, u32[]{:S(2)}) collective-permute-start(f32[3,2,32,16]{2,3,1,0:T(8,128)S(1)} %convolution_bitcast_fusion), channel_id=1, source_target_pairs={{0,1},{1,0},{2,3},{3,2},{4,5},{5,4},{6,7},{7,6},{8,9},{9,8},{10,11... | collective-permute-start | bytes 36872 | tf_op jit(solution)/shard_map/ppermute | solution.py:23
  8.4 4.2 %collective-permute-start.1 = (f32[3,2,32,16]{2,3,1,0:T(8,128)S(1)}, f32[3,2,32,16]{2,3,1,0:T(8,128)S(1)}, u32[]{:S(2)}, u32[]{:S(2)}) collective-permute-start(f32[3,2,32,16]{2,3,1,0:T(8,128)S(1)} %add.80), channel_id=1, source_target_pairs={{0,2},{1,3},{2,0},{3,1},{4,6},{5,7},{6,4},{7,5},{8,10},{9,11},{10,... | collective-permute-start | bytes 36872 | tf_op jit(solution)/shard_map/ppermute | solution.py:23
  12.6 5.6 %collective-permute-start.2 = (f32[3,2,32,16]{2,3,1,0:T(8,128)S(1)}, f32[3,2,32,16]{2,3,1,0:T(8,128)S(1)}, u32[]{:S(2)}, u32[]{:S(2)}) collective-permute-start(f32[3,2,32,16]{2,3,1,0:T(8,128)S(1)} %add.81), channel_id=1, source_target_pairs={{0,4},{1,5},{2,6},{3,7},{4,0},{5,1},{6,2},{7,3},{8,12},{9,13},{10,... | collective-permute-start | bytes 36872 | tf_op jit(solution)/shard_map/ppermute | solution.py:23
  18.2 8.9 %collective-permute-start.3 = (f32[3,2,32,16]{2,3,1,0:T(8,128)S(1)}, f32[3,2,32,16]{2,3,1,0:T(8,128)S(1)}, u32[]{:S(2)}, u32[]{:S(2)}) collective-permute-start(f32[3,2,32,16]{2,3,1,0:T(8,128)S(1)} %add.82), channel_id=1, source_target_pairs={{0,8},{1,9},{2,10},{3,11},{4,12},{5,13},{6,14},{7,15},{8,0},{9,1},... | collective-permute-start | bytes 36872 | tf_op jit(solution)/shard_map/ppermute | solution.py:23
  25.0 4.1 %copy-start.1 = (f32[27,27,1,1]{1,0,3,2:T(8,128)S(1)}, f32[27,27,1,1]{1,0,3,2:T(8,128)}, u32[]{:S(2)}) copy-start(f32[27,27,1,1]{1,0,3,2:T(8,128)} %constant.77) | copy-start | bytes 8752
  25.0 4.1 %copy-start.4 = (f32[27]{0:T(128)S(1)}, f32[27]{0:T(128)}, u32[]{:S(2)}) copy-start(f32[27]{0:T(128)} %param.11) | copy-start | bytes 328
  30.9 5.0 %collective-permute-start.4 = (f32[28,2,4,16]{3,0,2,1:T(8,128)S(1)}, f32[28,2,4,16]{3,0,2,1:T(8,128)S(1)}, u32[]{:S(2)}, u32[]{:S(2)}) collective-permute-start(f32[28,2,4,16]{3,0,2,1:T(8,128)S(1)} %get-tuple-element.19), channel_id=1, source_target_pairs={{0,16},{16,32},{32,48},{48,64},{64,80},{80,96},{96,112},{112,128},... | collective-permute-start | bytes 43016 | tf_op jit(solution)/shard_map/ppermute | solution.py:237
  32.0 8.5 %collective-permute-start.5 = (f32[28,2,4,16]{3,0,2,1:T(8,128)S(1)}, f32[28,2,4,16]{3,0,2,1:T(8,128)S(1)}, u32[]{:S(2)}, u32[]{:S(2)}) collective-permute-start(f32[28,2,4,16]{3,0,2,1:T(8,128)S(1)} %get-tuple-element.18), channel_id=1, source_target_pairs={{16,0},{32,16},{48,32},{64,48},{80,64},{96,80},{112,96},{128,112},... | collective-permute-start | bytes 43016 | tf_op jit(solution)/shard_map/ppermute | solution.py:238
  40.7 3.0 %collective-permute-start.7 = (f32[28,2,4,16]{0,3,2,1:T(8,128)S(1)}, f32[28,2,4,16]{0,3,2,1:T(8,128)S(1)}, u32[]{:S(2)}, u32[]{:S(2)}) collective-permute-start(f32[28,2,4,16]{0,3,2,1:T(8,128)S(1)} %pad_maximum_fusion.3), channel_id=1, source_target_pairs={{1,0},{2,1},{3,2},{4,3},{5,4},{6,5},{7,6},{8,7},{9,8},{10,9},{11,1... | collective-permute-start | bytes 43016 | tf_op jit(solution)/shard_map/ppermute | solution.py:260
  40.8 5.7 %collective-permute-start.6 = (f32[28,2,4,16]{0,3,2,1:T(8,128)S(1)}, f32[28,2,4,16]{0,3,2,1:T(8,128)S(1)}, u32[]{:S(2)}, u32[]{:S(2)}) collective-permute-start(f32[28,2,4,16]{0,3,2,1:T(8,128)S(1)} %pad_maximum_fusion.2), channel_id=1, source_target_pairs={{0,1},{1,2},{2,3},{3,4},{4,5},{5,6},{6,7},{7,8},{8,9},{9,10},{10,1... | collective-permute-start | bytes 43016 | tf_op jit(solution)/shard_map/ppermute | solution.py:259

commit v7 on v6

--- a/solution.py
+++ b/solution.py
@@ -80,7 +80,7 @@
     return jnp.einsum("ij,jzpl->izpl", backward, relaxed, precision=HIGHEST)
 
 
-def stream_kernel(post_ref, solid_ref, below_ref, above_ref, left_ref, right_ref, out_ref, spread_ref):
+def stream_kernel(fluid_ref, post_ref, below_ref, above_ref, left_ref, right_ref, out_ref, spread_ref):
     channels = out_ref.shape[0]
     blocks = out_ref.shape[2]
     cells = out_ref.shape[3]
@@ -104,9 +104,13 @@
     r = lane // BE
     py = seat // TX
 
+    solid_plane = jnp.zeros((blocks, cells), jnp.float32)
+    for block in range(blocks):
+        solid_plane = jnp.where(seat == block, 1.0 - fluid_ref[block], solid_plane)
+
     def own(channel, level):
         if channel == channels:
-            return solid_ref[...]
+            return solid_plane
         return post_ref[channel, level]
 
     def moved(plane, shift):
@@ -174,17 +178,18 @@
             out_ref[heading, level] = jnp.where(blocked, bounced, source)
 
 
-def stream(post, solid_plane, below, above, from_left, from_right):
+def stream(fluid, post, below, above, from_left, from_right):
     channels, levels, blocks, cells = post.shape
     halo_rows = below.shape[0]
     vmem = pl.BlockSpec(memory_space=pltpu.VMEM)
+    smem = pl.BlockSpec(memory_space=pltpu.SMEM)
     return pl.pallas_call(
         stream_kernel,
         out_shape=jax.ShapeDtypeStruct((channels, levels, blocks, cells), jnp.float32),
-        in_specs=[vmem] * 6,
+        in_specs=[smem] + [vmem] * 5,
         out_specs=vmem,
         scratch_shapes=[pltpu.VMEM((4, halo_rows + 16, cells), jnp.float32)],
-    )(post, solid_plane, below, above, from_left, from_right)
+    )(fluid, post, below, above, from_left, from_right)
 
 
 def on_device(
@@ -232,10 +237,14 @@
     extended = jnp.concatenate([post, solid], axis=0)
     width = channels + 1
     ahead, behind = ring_pairs("curve")
+    flat = lambda halo: halo.reshape(-1, BE)
+    halo_shape = (width, levels, TX, BE)
     top_row = extended[:, :, blocks - TX:, cells - BE:]
     bottom_row = extended[:, :, :TX, :BE]
-    below = lax.ppermute(top_row, "curve", ahead)
-    above = lax.ppermute(bottom_row, "curve", behind)
+    below_flat = lax.ppermute(flat(top_row), "curve", ahead)
+    above_flat = lax.ppermute(flat(bottom_row), "curve", behind)
+    below = below_flat.reshape(halo_shape)
+    above = above_flat.reshape(halo_shape)
     ahead, behind = ring_pairs("line")
     by_rows = extended.reshape(width, levels, TY, TX, BE, BE)
     right_cols = by_rows[:, :, :, TX - 1, :, BE - 1]
@@ -256,11 +265,9 @@
         ],
         axis=2,
     )
-    from_left = lax.ppermute(to_right, "line", ahead)
-    from_right = lax.ppermute(to_left, "line", behind)
-    flat = lambda halo: halo.reshape(-1, BE)
-    solid_plane = jnp.broadcast_to((1.0 - fluid)[:, None], (blocks, cells))
-    result = stream(post, solid_plane, flat(below), flat(above), flat(from_left), flat(from_right))
+    from_left = lax.ppermute(flat(to_right), "line", ahead)
+    from_right = lax.ppermute(flat(to_left), "line", behind)
+    result = stream(fluid, post, below_flat, above_flat, from_left, from_right)
     by_block = result.transpose(2, 0, 1, 3).reshape(blocks, channels, levels * cells)
     occupied = living_brick_keys >= 0
     new_state = jnp.take(by_block, jnp.maximum(living_brick_keys, 0), axis=0)

time: 54.3 us -> 54.6 us (level)
  waiting for transfers between devices: 16.8 us -> 19.3 us
  local copies, waits for them, and re-layouts: 11.2 us -> 8.96 us
    ppermute x4 -> x0, local copies, waits for them, and re-layouts: 2.96 us -> none  [the longest x1 0.77 us: on_device(): from_right = lax.ppermute(to_left, 'line', behind)]
    ppermute x4, waiting for transfers between devices: 9.04 us -> 11.5 us  [the longest x1 4.48 us: on_device(): above_flat = lax.ppermute(flat(bottom_row), 'curve', behind)]
    unnamed x13 -> x27, local copies, waits for them, and re-layouts: 0.04 us -> 1.07 us
    broadcast_in_dim x1 -> x0, local copies, waits for them, and re-layouts: 0.66 us -> none  [on_device(): solid_plane = jnp.broadcast_to((1.0 - fluid)[:, None], (blocks, cells))]
  transfers between devices with their start and end apart: 8 -> 8, of which waited for: 7 -> 8; matrix products, arithmetic and copies ran while one was open for 6% -> 3% of each run, Pallas kernels for 0% -> 0%
where the time goes in v7:
time: 54.6 us; the launch traced here: 54.2 us
  waiting for transfers between devices  19.3 us (35%)
  starting transfers between devices  15.1 us (28%)
  local copies, waits for them, and re-layouts  8.96 us (16%)
  other arithmetic  4.68 us (9%)
  Pallas kernels  2.99 us (5%)
  matrix products  2.73 us (5%)
    ppermute x4, starting transfers between devices, butterfly_sum(): lax.ppermute(value, axis, [(i, i ^ stride) for i in range(count)])  12.2 us
    ppermute x4, waiting for transfers between devices, butterfly_sum(): lax.ppermute(value, axis, [(i, i ^ stride) for i in range(count)])  7.77 us
    ppermute x1, waiting for transfers between devices, on_device(): above_flat = lax.ppermute(flat(bottom_row), 'curve', behind)  4.48 us
    ppermute x1, waiting for transfers between devices, on_device(): from_left = lax.ppermute(flat(to_right), 'line', ahead)  4.18 us
    pallas_call x1, Pallas kernels, stream(): pl.pallas_call(stream_kernel, out_shape=jax.ShapeDtypeStruct((channels, l...  2.99 us
    ppermute x1, waiting for transfers between devices, on_device(): below_flat = lax.ppermute(flat(top_row), 'curve', ahead)  2.37 us
    unnamed x1, other arithmetic  1.77 us
    ppermute x1, starting transfers between devices, on_device(): above_flat = lax.ppermute(flat(bottom_row), 'curve', behind)  1.29 us
  transfers between devices with their start and end apart: 8, of which 8 were waited for; matrix products, arithmetic and copies ran while one was open for 3% of the time, Pallas kernels for 0%

profile of v7, /device:TPU:30, one launch (start us, length us, event | category | flops | bytes accessed | tf_op | source)
XLA Modules:
  0.0 54.2 jit_solution(2496928863884686446)
XLA Ops:
  0.0 0.8 %fusion.20 = pred[8]{0:T(512)(128)(4,1)S(1)} fusion(s32[6]{0:T(128)} %bitcast.101), kind=kLoop, calls=%fused_computation.62 | loop fusion | flops 88 | bytes 32 | tf_op jit(solution)/shard_map/reduce_or | solution.py:215
  0.8 0.8 %select_reduce_fusion = s32[8]{0:T(128)S(1)} fusion(s32[6]{0:T(128)} %bitcast.102), kind=kLoop, calls=%fused_computation.60 | loop fusion | flops 136 | bytes 56 | tf_op jit(solution)/shard_map/reduce_sum | solution.py:214
  1.6 1.8 %reduce = f32[6,27,512]{2,1,0:T(8,128)S(1)} reduce(f32[1,1,6,27,512]{4,1,3,2,0:T(1,128)} %param.7, f32[]{:T(128)} %constant.79), dimensions={0,1}, to_apply=%param.7.reduce_sub_computation | reduce | bytes 663556 | tf_op args[0]
  3.4 0.2 reshape_squeeze.3
  3.6 1.0 %gather_fusion = f32[8,27,2,256]{3,2,1,0:T(2,128)S(1)} fusion(f32[6,27,2,256]{3,2,1,0:T(2,128)S(1)} %reshape_squeeze.3, s32[1024]{0:T(1024)S(1)} %pad_clamp_fusion.1), kind=kCustom, calls=%fused_computation | custom fusion | bytes 884768 | tf_op jit(solution)/shard_map/jit(_take)/gather | solution.py:217
  4.6 0.3 multiply_bitcast_fusion
  4.9 0.6 %fusion.5 = f32[27,2,8,256]{3,0,2,1:T(8,128)S(1)} fusion(f32[27,27,1,1]{1,0,3,2:T(8,128)S(1)} %copy-done.6, f32[27,2,8,256]{3,1,0,2:T(2,128)S(1)} %multiply_bitcast_fusion), kind=kOutput, calls=%fused_computation.12 | convolution fusion | flops 35831808 | bytes 887652 | tf_op jit(solution)/shard_map/ij,jzpl->izpl/dot_general | solution.py:219
  6.4 0.2 dot_general.23
  6.8 0.3 convolution_bitcast_fusion
  7.2 1.2 %collective-permute-done = f32[3,2,32,16]{2,3,1,0:T(8,128)S(1)} collective-permute-done((f32[3,2,32,16]{2,3,1,0:T(8,128)S(1)}, f32[3,2,32,16]{2,3,1,0:T(8,128)S(1)}, u32[]{:S(2)}, u32[]{:S(2)}) %collective-permute-start) | collective-permute-done | bytes 12320 | tf_op jit(solution)/shard_map/ppermute | solution.py:23
  8.4 2.0 %collective-permute-start.1 = (f32[3,2,32,16]{2,3,1,0:T(8,128)S(1)}, f32[3,2,32,16]{2,3,1,0:T(8,128)S(1)}, u32[]{:S(2)}, u32[]{:S(2)}) collective-permute-start(f32[3,2,32,16]{2,3,1,0:T(8,128)S(1)} %add.80), channel_id=1, source_target_pairs={{0,2},{1,3},{2,0},{3,1},{4,6},{5,7},{6,4},{7,5},{8,10},{9,11},{10,... | collective-permute-start | bytes 36872 | tf_op jit(solution)/shard_map/ppermute | solution.py:23
  10.4 2.2 %collective-permute-done.1 = f32[3,2,32,16]{2,3,1,0:T(8,128)S(1)} collective-permute-done((f32[3,2,32,16]{2,3,1,0:T(8,128)S(1)}, f32[3,2,32,16]{2,3,1,0:T(8,128)S(1)}, u32[]{:S(2)}, u32[]{:S(2)}) %collective-permute-start.1) | collective-permute-done | bytes 12320 | tf_op jit(solution)/shard_map/ppermute | solution.py:23
  12.6 3.4 %collective-permute-start.2 = (f32[3,2,32,16]{2,3,1,0:T(8,128)S(1)}, f32[3,2,32,16]{2,3,1,0:T(8,128)S(1)}, u32[]{:S(2)}, u32[]{:S(2)}) collective-permute-start(f32[3,2,32,16]{2,3,1,0:T(8,128)S(1)} %add.81), channel_id=1, source_target_pairs={{0,4},{1,5},{2,6},{3,7},{4,0},{5,1},{6,2},{7,3},{8,12},{9,13},{10,... | collective-permute-start | bytes 36872 | tf_op jit(solution)/shard_map/ppermute | solution.py:23
  16.0 2.3 %collective-permute-done.2 = f32[3,2,32,16]{2,3,1,0:T(8,128)S(1)} collective-permute-done((f32[3,2,32,16]{2,3,1,0:T(8,128)S(1)}, f32[3,2,32,16]{2,3,1,0:T(8,128)S(1)}, u32[]{:S(2)}, u32[]{:S(2)}) %collective-permute-start.2) | collective-permute-done | bytes 12320 | tf_op jit(solution)/shard_map/ppermute | solution.py:23
  18.2 6.7 %collective-permute-start.3 = (f32[3,2,32,16]{2,3,1,0:T(8,128)S(1)}, f32[3,2,32,16]{2,3,1,0:T(8,128)S(1)}, u32[]{:S(2)}, u32[]{:S(2)}) collective-permute-start(f32[3,2,32,16]{2,3,1,0:T(8,128)S(1)} %add.82), channel_id=1, source_target_pairs={{0,8},{1,9},{2,10},{3,11},{4,12},{5,13},{6,14},{7,15},{8,0},{9,1},... | collective-permute-start | bytes 36872 | tf_op jit(solution)/shard_map/ppermute | solution.py:23
  25.0 2.1 %collective-permute-done.3 = f32[3,2,32,16]{2,3,1,0:T(8,128)S(1)} collective-permute-done((f32[3,2,32,16]{2,3,1,0:T(8,128)S(1)}, f32[3,2,32,16]{2,3,1,0:T(8,128)S(1)}, u32[]{:S(2)}, u32[]{:S(2)}) %collective-permute-start.3) | collective-permute-done | bytes 12320 | tf_op jit(solution)/shard_map/ppermute | solution.py:23
  27.3 1.0 %fusion = f32[3,2,2,4,16,16]{4,5,2,1,0,3:T(8,128)S(1)} fusion(f32[3,2,2,16,16,1]{4,3,2,1,0,5:T(8,128)S(1)} %bitcast.88, f32[4,16,8]{1,2,0:T(8,128)S(1)} %get-tuple-element.30, f32[4,16,8]{1,2,0:T(8,128)S(1)} %get-tuple-element.29), kind=kOutput, calls=%fused_computation.3 | convolution fusion | flops 2372608 | bytes 65536 | tf_op jit(solution)/shard_map/kzyrm,xqm->kzyxrq/dot_general | solution.py:231
  29.1 0.9 %fusion.3 = f32[27,2,8,256]{3,0,2,1:T(8,128)S(1)} fusion(f32[27,27,1,1]{1,0,3,2:T(8,128)S(1)} %copy-done.5, f32[27,2,8,256]{3,0,2,1:T(8,128)S(1)} %fusion.5, f32[27,2,8,256]{3,2,1,0:T(8,128)S(1)} %bitcast.86, f32[27]{0:T(128)S(1)} %copy-done.9), kind=kOutput, calls=%fused_computation.11 | convolution fusion | flops 36163584 | bytes 1330128 | tf_op jit(solution)/shard_map/ij,jzpl->izpl/dot_general | solution.py:80
  30.2 0.7 %copy.78 = f32[28,2,8,256]{0,3,2,1:T(8,128)S(1)} copy(f32[28,2,8,256]{3,0,2,1:T(8,128)S(1)} %pad_maximum_fusion) | data formatting | bytes 917504 | tf_op jit(solution)/shard_map/concatenate | solution.py:237
  31.0 1.1 %collective-permute-start.4 = (f32[224,16]{1,0:T(8,128)S(1)}, f32[224,16]{1,0:T(8,128)S(1)}, u32[]{:S(2)}, u32[]{:S(2)}) collective-permute-start(f32[224,16]{1,0:T(8,128)S(1)} %bitcast.94), channel_id=1, source_target_pairs={{0,16},{16,32},{32,48},{48,64},{64,80},{80,96},{96,112},{112,128},... | collective-permute-start | bytes 43016 | tf_op jit(solution)/shard_map/ppermute | solution.py:244
  32.2 1.3 %collective-permute-start.5 = (f32[224,16]{1,0:T(8,128)S(1)}, f32[224,16]{1,0:T(8,128)S(1)}, u32[]{:S(2)}, u32[]{:S(2)}) collective-permute-start(f32[224,16]{1,0:T(8,128)S(1)} %bitcast.95), channel_id=1, source_target_pairs={{16,0},{32,16},{48,32},{64,48},{80,64},{96,80},{112,96},{128,112},... | collective-permute-start | bytes 43016 | tf_op jit(solution)/shard_map/ppermute | solution.py:245
  33.5 2.4 %collective-permute-done.4.below_ref = f32[224,16]{1,0:T(8,128)S(1)} collective-permute-done((f32[224,16]{1,0:T(8,128)S(1)}, f32[224,16]{1,0:T(8,128)S(1)}, u32[]{:S(2)}, u32[]{:S(2)}) %collective-permute-start.4) | collective-permute-done | bytes 14368 | tf_op jit(solution)/shard_map/ppermute | solution.py:244
  36.1 4.5 %collective-permute-done.5.above_ref = f32[224,16]{1,0:T(8,128)S(1)} collective-permute-done((f32[224,16]{1,0:T(8,128)S(1)}, f32[224,16]{1,0:T(8,128)S(1)}, u32[]{:S(2)}, u32[]{:S(2)}) %collective-permute-start.5) | collective-permute-done | bytes 14368 | tf_op jit(solution)/shard_map/ppermute | solution.py:245
  41.3 0.5 collective-permute-start.6
  41.8 1.0 %copy.84.post_ref = f32[27,2,8,256]{3,2,1,0:T(8,128)} copy(f32[27,2,8,256]{3,0,2,1:T(8,128)S(1)} %fusion.3) | data formatting | bytes 884736 | tf_op jit(solution)/shard_map/ij,jzpl->izpl/dot_general | solution.py:80
  42.8 0.5 collective-permute-done.7.right_ref
  43.3 4.2 %collective-permute-done.6.left_ref = f32[224,16]{1,0:T(8,128)S(1)} collective-permute-done((f32[224,16]{1,0:T(8,128)S(1)}, f32[224,16]{1,0:T(8,128)S(1)}, u32[]{:S(2)}, u32[]{:S(2)}) %collective-permute-start.6) | collective-permute-done | bytes 14368 | tf_op jit(solution)/shard_map/ppermute | solution.py:268
  47.5 0.6 %copy-done.3 = f32[224,16]{1,0:T(8,128)} copy-done((f32[224,16]{1,0:T(8,128)}, f32[224,16]{1,0:T(8,128)S(1)}, u32[]{:S(2)}) %copy-start.3) | copy-done | bytes 14360
  48.2 3.0 %shard_map.73 = f32[27,2,8,256]{3,2,1,0:T(8,128)} custom-call(f32[8]{0:T(128)} %copy-done.7, f32[27,2,8,256]{3,2,1,0:T(8,128)} %copy.84.post_ref, f32[224,16]{1,0:T(8,128)} %copy-done, f32[224,16]{1,0:T(8,128)} %copy-done.1, f32[224,16]{1,0:T(8,128)} %copy-done.3, f32[224,16]{1,0:T(8,128)} %copy-done.2), custom_call_target="tpu_custom_call" | custom-call | tf_op jit(solution)/shard_map/pallas_call | solution.py:186
  51.1 1.3 %copy.85 = f32[8,27,512]{2,1,0:T(8,128)S(1)} copy(f32[8,27,512]{2,0,1:T(8,128)} %bitcast.87) | data formatting | bytes 884736 | tf_op jit(solution)/shard_map/reshape | solution.py:271
  52.4 0.6 %gather_fusion.1 = f32[6,27,512]{2,1,0:T(8,128)S(1)} fusion(f32[8,27,512]{2,1,0:T(8,128)S(1)} %copy.85, s32[1024]{0:T(1024)S(1)} %pad_clamp_fusion), kind=kCustom, calls=%fused_computation.1 | custom fusion | bytes 663576 | tf_op jit(solution)/shard_map/jit(_take)/gather | solution.py:273
  53.1 1.1 %copy.86 = f32[1,1,6,27,512]{4,1,3,2,0:T(1,128)} copy(f32[1,1,6,27,512]{4,3,2,1,0:T(8,128)S(1)} %fusion.8) | data formatting | bytes 663552 | tf_op jit(solution)/shard_map/mul | solution.py:274
  (79 shorter events, 3.5 us)
Async XLA Ops:
  0.0 4.9 %copy-start.6 = (f32[27,27,1,1]{1,0,3,2:T(8,128)S(1)}, f32[27,27,1,1]{1,0,3,2:T(8,128)}, u32[]{:S(2)}) copy-start(f32[27,27,1,1]{1,0,3,2:T(8,128)} %constant.78) | copy-start | bytes 8752
  1.6 3.9 %copy-start.7 = (f32[8]{0:T(128)}, f32[8]{0:T(128)S(1)}, u32[]{:S(2)}) copy-start(f32[8]{0:T(128)S(1)} %convert_element_type.16.fluid_ref) | copy-start | bytes 100
  4.9 1.7 %copy-start.8 = (s32[8]{0:T(128)S(1)}, s32[8]{0:T(128)}, u32[]{:S(2)}) copy-start(s32[8]{0:T(128)} %param.9) | copy-start | bytes 100
  4.9 5.5 %copy-start.10 = (s32[1,1,6]{2,1,0:T(1,128)S(1)}, s32[1,1,6]{2,1,0:T(1,128)}, u32[]{:S(2)}) copy-start(s32[1,1,6]{2,1,0:T(1,128)} %param.8) | copy-start | bytes 76
  5.5 21.6 %copy-start.4 = (f32[3,2,32,16]{2,3,1,0:T(8,128)S(1)}, f32[3,2,32,16]{2,3,1,0:T(8,128)}, u32[]{:S(2)}) copy-start(f32[3,2,32,16]{2,3,1,0:T(8,128)} %param.10) | copy-start | bytes 36868
  7.1 1.3 %collective-permute-start = (f32[3,2,32,16]{2,3,1,0:T(8,128)S(1)}, f32[3,2,32,16]{2,3,1,0:T(8,128)S(1)}, u32[]{:S(2)}, u32[]{:S(2)}) collective-permute-start(f32[3,2,32,16]{2,3,1,0:T(8,128)S(1)} %convolution_bitcast_fusion), channel_id=1, source_target_pairs={{0,1},{1,0},{2,3},{3,2},{4,5},{5,4},{6,7},{7,6},{8,9},{9,8},{10,11... | collective-permute-start | bytes 36872 | tf_op jit(solution)/shard_map/ppermute | solution.py:23
  8.4 4.2 %collective-permute-start.1 = (f32[3,2,32,16]{2,3,1,0:T(8,128)S(1)}, f32[3,2,32,16]{2,3,1,0:T(8,128)S(1)}, u32[]{:S(2)}, u32[]{:S(2)}) collective-permute-start(f32[3,2,32,16]{2,3,1,0:T(8,128)S(1)} %add.80), channel_id=1, source_target_pairs={{0,2},{1,3},{2,0},{3,1},{4,6},{5,7},{6,4},{7,5},{8,10},{9,11},{10,... | collective-permute-start | bytes 36872 | tf_op jit(solution)/shard_map/ppermute | solution.py:23
  12.6 5.6 %collective-permute-start.2 = (f32[3,2,32,16]{2,3,1,0:T(8,128)S(1)}, f32[3,2,32,16]{2,3,1,0:T(8,128)S(1)}, u32[]{:S(2)}, u32[]{:S(2)}) collective-permute-start(f32[3,2,32,16]{2,3,1,0:T(8,128)S(1)} %add.81), channel_id=1, source_target_pairs={{0,4},{1,5},{2,6},{3,7},{4,0},{5,1},{6,2},{7,3},{8,12},{9,13},{10,... | collective-permute-start | bytes 36872 | tf_op jit(solution)/shard_map/ppermute | solution.py:23
  18.2 8.9 %collective-permute-start.3 = (f32[3,2,32,16]{2,3,1,0:T(8,128)S(1)}, f32[3,2,32,16]{2,3,1,0:T(8,128)S(1)}, u32[]{:S(2)}, u32[]{:S(2)}) collective-permute-start(f32[3,2,32,16]{2,3,1,0:T(8,128)S(1)} %add.82), channel_id=1, source_target_pairs={{0,8},{1,9},{2,10},{3,11},{4,12},{5,13},{6,14},{7,15},{8,0},{9,1},... | collective-permute-start | bytes 36872 | tf_op jit(solution)/shard_map/ppermute | solution.py:23
  25.0 4.1 %copy-start.5 = (f32[27,27,1,1]{1,0,3,2:T(8,128)S(1)}, f32[27,27,1,1]{1,0,3,2:T(8,128)}, u32[]{:S(2)}) copy-start(f32[27,27,1,1]{1,0,3,2:T(8,128)} %constant.77) | copy-start | bytes 8752
  25.0 4.1 %copy-start.9 = (f32[27]{0:T(128)S(1)}, f32[27]{0:T(128)}, u32[]{:S(2)}) copy-start(f32[27]{0:T(128)} %param.11) | copy-start | bytes 328
  31.0 4.9 %collective-permute-start.4 = (f32[224,16]{1,0:T(8,128)S(1)}, f32[224,16]{1,0:T(8,128)S(1)}, u32[]{:S(2)}, u32[]{:S(2)}) collective-permute-start(f32[224,16]{1,0:T(8,128)S(1)} %bitcast.94), channel_id=1, source_target_pairs={{0,16},{16,32},{32,48},{48,64},{64,80},{80,96},{96,112},{112,128},... | collective-permute-start | bytes 43016 | tf_op jit(solution)/shard_map/ppermute | solution.py:244
  32.2 8.4 %collective-permute-start.5 = (f32[224,16]{1,0:T(8,128)S(1)}, f32[224,16]{1,0:T(8,128)S(1)}, u32[]{:S(2)}, u32[]{:S(2)}) collective-permute-start(f32[224,16]{1,0:T(8,128)S(1)} %bitcast.95), channel_id=1, source_target_pairs={{16,0},{32,16},{48,32},{64,48},{80,64},{96,80},{112,96},{128,112},... | collective-permute-start | bytes 43016 | tf_op jit(solution)/shard_map/ppermute | solution.py:245
  35.9 11.6 %copy-start = (f32[224,16]{1,0:T(8,128)}, f32[224,16]{1,0:T(8,128)S(1)}, u32[]{:S(2)}) copy-start(f32[224,16]{1,0:T(8,128)S(1)} %collective-permute-done.4.below_ref) | copy-start | bytes 43012
  40.6 6.9 %copy-start.1 = (f32[224,16]{1,0:T(8,128)}, f32[224,16]{1,0:T(8,128)S(1)}, u32[]{:S(2)}) copy-start(f32[224,16]{1,0:T(8,128)S(1)} %collective-permute-done.5.above_ref) | copy-start | bytes 43012
  40.9 2.4 %collective-permute-start.7 = (f32[224,16]{1,0:T(8,128)S(1)}, f32[224,16]{1,0:T(8,128)S(1)}, u32[]{:S(2)}, u32[]{:S(2)}) collective-permute-start(f32[224,16]{1,0:T(8,128)S(1)} %bitcast.93), channel_id=1, source_target_pairs={{1,0},{2,1},{3,2},{4,3},{5,4},{6,5},{7,6},{8,7},{9,8},{10,9},{11,1... | collective-permute-start | bytes 43016 | tf_op jit(solution)/shard_map/ppermute | solution.py:269
  41.3 6.2 %collective-permute-start.6 = (f32[224,16]{1,0:T(8,128)S(1)}, f32[224,16]{1,0:T(8,128)S(1)}, u32[]{:S(2)}, u32[]{:S(2)}) collective-permute-start(f32[224,16]{1,0:T(8,128)S(1)} %bitcast.96), channel_id=1, source_target_pairs={{0,1},{1,2},{2,3},{3,4},{4,5},{5,6},{6,7},{7,8},{8,9},{9,10},{10,1... | collective-permute-start | bytes 43016 | tf_op jit(solution)/shard_map/ppermute | solution.py:268
  43.3 4.2 %copy-start.2 = (f32[224,16]{1,0:T(8,128)}, f32[224,16]{1,0:T(8,128)S(1)}, u32[]{:S(2)}) copy-start(f32[224,16]{1,0:T(8,128)S(1)} %collective-permute-done.7.right_ref) | copy-start | bytes 43012
  47.5 0.6 %copy-start.3 = (f32[224,16]{1,0:T(8,128)}, f32[224,16]{1,0:T(8,128)S(1)}, u32[]{:S(2)}) copy-start(f32[224,16]{1,0:T(8,128)S(1)} %collective-permute-done.6.left_ref) | copy-start | bytes 43012

commit v8 on v7

--- a/solution.py
+++ b/solution.py
@@ -81,10 +81,7 @@
 
 
 def stream_kernel(fluid_ref, post_ref, below_ref, above_ref, left_ref, right_ref, out_ref, spread_ref):
-    channels = out_ref.shape[0]
-    blocks = out_ref.shape[2]
-    cells = out_ref.shape[3]
-    levels = out_ref.shape[1]
+    channels, levels, blocks, cells = post_ref.shape
     _, _, speeds = lattice_tables()
     front = 8
     grid_row = lax.broadcasted_iota(jnp.int32, (BE, cells), 0)
@@ -164,8 +161,9 @@
         blocked = blocked_of[(cx, cy)]
         for level in range(levels):
             bounced = post_ref[26 - heading, level]
+            window = pl.ds(level * cells, cells)
             if cz == 1 and level == 0:
-                out_ref[heading, level] = bounced
+                out_ref[:, heading, window] = bounced
                 continue
             if cz == 0:
                 source = gathered(heading, level, cx, cy)
@@ -175,7 +173,7 @@
                 source = gathered(heading, 1, cx, cy)
             else:
                 source = gathered(heading + 2, 1, cx, cy)
-            out_ref[heading, level] = jnp.where(blocked, bounced, source)
+            out_ref[:, heading, window] = jnp.where(blocked, bounced, source)
 
 
 def stream(fluid, post, below, above, from_left, from_right):
@@ -185,7 +183,7 @@
     smem = pl.BlockSpec(memory_space=pltpu.SMEM)
     return pl.pallas_call(
         stream_kernel,
-        out_shape=jax.ShapeDtypeStruct((channels, levels, blocks, cells), jnp.float32),
+        out_shape=jax.ShapeDtypeStruct((blocks, channels, levels * cells), jnp.float32),
         in_specs=[smem] + [vmem] * 5,
         out_specs=vmem,
         scratch_shapes=[pltpu.VMEM((4, halo_rows + 16, cells), jnp.float32)],
@@ -211,8 +209,9 @@
     cols_tile = TX * BE
     positions = jnp.arange(blocks, dtype=jnp.int32)
     matches = living_brick_keys[None, :] == positions[:, None]
-    slot_of = jnp.sum(jnp.where(matches, jnp.arange(seats, dtype=jnp.int32)[None, :], 0), axis=1)
-    present = jnp.any(matches, axis=1)
+    code = jnp.max(jnp.where(matches, jnp.arange(1, seats + 1, dtype=jnp.int32)[None, :], 0), axis=1)
+    present = code > 0
+    slot_of = jnp.maximum(code - 1, 0)
     fluid = present.astype(jnp.float32)
     picked = jnp.take(slot_state.reshape(seats, channels, levels, cells), slot_of, axis=0)
     pops = picked.transpose(1, 2, 0, 3) * fluid[None, None, :, None]
@@ -268,7 +267,7 @@
     from_left = lax.ppermute(flat(to_right), "line", ahead)
     from_right = lax.ppermute(flat(to_left), "line", behind)
     result = stream(fluid, post, below_flat, above_flat, from_left, from_right)
-    by_block = result.transpose(2, 0, 1, 3).reshape(blocks, channels, levels * cells)
+    by_block = result
     occupied = living_brick_keys >= 0
     new_state = jnp.take(by_block, jnp.maximum(living_brick_keys, 0), axis=0)
     new_state = new_state * occupied[:, None, None].astype(jnp.float32)

time: 54.6 us -> 53.5 us (0.980)
  other arithmetic: 4.68 us -> 3.9 us
    reshape x1 -> x0, local copies, waits for them, and re-layouts: 1.27 us -> none  [on_device(): result.transpose(2, 0, 1, 3).reshape(blocks, channels, levels * cells)]
    gather x1, local copies, waits for them, and re-layouts: 0.57 us -> 1.61 us  [on_device(): new_state = jnp.take(by_block, jnp.maximum(living_brick_keys, 0), axis=0)]
    reduce_or x1 -> x0, other arithmetic: 0.78 us -> none  [on_device(): present = jnp.any(matches, axis=1)]
    reduce_max x0 -> x1, other arithmetic: none -> 0.78 us  [on_device(): jnp.max(jnp.where(matches, jnp.arange(1, seats + 1, dtype=jnp.int32)[None...]
    reduce_sum x1 -> x0, other arithmetic: 0.77 us -> none  [on_device(): jnp.sum(jnp.where(matches, jnp.arange(seats, dtype=jnp.int32)[None, :], 0...]
where the time goes in v8:
time: 53.5 us; the launch traced here: 53.1 us
  waiting for transfers between devices  19.3 us (36%)
  starting transfers between devices  14.9 us (28%)
  local copies, waits for them, and re-layouts  8.73 us (16%)
  other arithmetic  3.9 us (7%)
  Pallas kernels  3.11 us (6%)
  matrix products  2.72 us (5%)
    ppermute x4, starting transfers between devices, butterfly_sum(): lax.ppermute(value, axis, [(i, i ^ stride) for i in range(count)])  12.2 us
    ppermute x4, waiting for transfers between devices, butterfly_sum(): lax.ppermute(value, axis, [(i, i ^ stride) for i in range(count)])  7.77 us
    ppermute x1, waiting for transfers between devices, on_device(): above_flat = lax.ppermute(flat(bottom_row), 'curve', behind)  4.31 us
    ppermute x1, waiting for transfers between devices, on_device(): from_left = lax.ppermute(flat(to_right), 'line', ahead)  4.19 us
    pallas_call x1, Pallas kernels, stream(): pl.pallas_call(stream_kernel, out_shape=jax.ShapeDtypeStruct((blocks, cha...  3.11 us
    ppermute x1, waiting for transfers between devices, on_device(): below_flat = lax.ppermute(flat(top_row), 'curve', ahead)  2.55 us
    unnamed x1, other arithmetic  1.77 us
    gather x1, local copies, waits for them, and re-layouts, on_device(): new_state = jnp.take(by_block, jnp.maximum(living_brick_keys, 0), axis=0)  1.61 us
  transfers between devices with their start and end apart: 8, of which 8 were waited for; matrix products, arithmetic and copies ran while one was open for 3% of the time, Pallas kernels for 0%

profile of v8, /device:TPU:30, one launch (start us, length us, event | category | flops | bytes accessed | tf_op | source)
XLA Modules:
  0.0 53.1 jit_solution(8557492774271563301)
XLA Ops:
  0.0 0.8 %select_reduce_fusion = s32[8]{0:T(128)S(1)} fusion(s32[6]{0:T(128)S(1)} %iota_add_fusion, s32[6]{0:T(128)} %bitcast.93), kind=kLoop, calls=%fused_computation.60 | loop fusion | flops 136 | bytes 80 | tf_op jit(solution)/shard_map/reduce_max | solution.py:212
  0.8 1.8 %reduce = f32[6,27,512]{2,1,0:T(8,128)S(1)} reduce(f32[1,1,6,27,512]{4,1,3,2,0:T(1,128)} %param.7, f32[]{:T(128)} %constant.86), dimensions={0,1}, to_apply=%param.7.reduce_sub_computation | reduce | bytes 663556 | tf_op args[0]
  2.6 0.2 reshape_squeeze.3
  2.8 1.0 %gather_fusion = f32[8,27,2,256]{3,2,1,0:T(2,128)S(1)} fusion(f32[6,27,2,256]{3,2,1,0:T(2,128)S(1)} %reshape_squeeze.3, s32[1024]{0:T(1024)S(1)} %pad_clamp_fusion.1), kind=kCustom, calls=%fused_computation | custom fusion | bytes 884768 | tf_op jit(solution)/shard_map/jit(_take)/gather | solution.py:216
  3.9 0.3 multiply_bitcast_fusion
  4.2 0.6 %fusion.5 = f32[27,2,8,256]{3,0,2,1:T(8,128)S(1)} fusion(f32[27,27,1,1]{1,0,3,2:T(8,128)S(1)} %copy-done.6, f32[27,2,8,256]{3,1,0,2:T(2,128)S(1)} %multiply_bitcast_fusion), kind=kOutput, calls=%fused_computation.12 | convolution fusion | flops 35831808 | bytes 887652 | tf_op jit(solution)/shard_map/ij,jzpl->izpl/dot_general | solution.py:218
  4.7 0.2 fusion.23
  5.4 0.2 copy.47
  5.6 0.2 dot_general.23
  6.0 0.3 convolution_bitcast_fusion
  6.4 1.2 %collective-permute-done = f32[3,2,32,16]{2,3,1,0:T(8,128)S(1)} collective-permute-done((f32[3,2,32,16]{2,3,1,0:T(8,128)S(1)}, f32[3,2,32,16]{2,3,1,0:T(8,128)S(1)}, u32[]{:S(2)}, u32[]{:S(2)}) %collective-permute-start) | collective-permute-done | bytes 12320 | tf_op jit(solution)/shard_map/ppermute | solution.py:23
  7.6 2.0 %collective-permute-start.1 = (f32[3,2,32,16]{2,3,1,0:T(8,128)S(1)}, f32[3,2,32,16]{2,3,1,0:T(8,128)S(1)}, u32[]{:S(2)}, u32[]{:S(2)}) collective-permute-start(f32[3,2,32,16]{2,3,1,0:T(8,128)S(1)} %add.84), channel_id=1, source_target_pairs={{0,2},{1,3},{2,0},{3,1},{4,6},{5,7},{6,4},{7,5},{8,10},{9,11},{10,... | collective-permute-start | bytes 36872 | tf_op jit(solution)/shard_map/ppermute | solution.py:23
  9.6 2.2 %collective-permute-done.1 = f32[3,2,32,16]{2,3,1,0:T(8,128)S(1)} collective-permute-done((f32[3,2,32,16]{2,3,1,0:T(8,128)S(1)}, f32[3,2,32,16]{2,3,1,0:T(8,128)S(1)}, u32[]{:S(2)}, u32[]{:S(2)}) %collective-permute-start.1) | collective-permute-done | bytes 12320 | tf_op jit(solution)/shard_map/ppermute | solution.py:23
  11.8 3.4 %collective-permute-start.2 = (f32[3,2,32,16]{2,3,1,0:T(8,128)S(1)}, f32[3,2,32,16]{2,3,1,0:T(8,128)S(1)}, u32[]{:S(2)}, u32[]{:S(2)}) collective-permute-start(f32[3,2,32,16]{2,3,1,0:T(8,128)S(1)} %add.85), channel_id=1, source_target_pairs={{0,4},{1,5},{2,6},{3,7},{4,0},{5,1},{6,2},{7,3},{8,12},{9,13},{10,... | collective-permute-start | bytes 36872 | tf_op jit(solution)/shard_map/ppermute | solution.py:23
  15.2 2.3 %collective-permute-done.2 = f32[3,2,32,16]{2,3,1,0:T(8,128)S(1)} collective-permute-done((f32[3,2,32,16]{2,3,1,0:T(8,128)S(1)}, f32[3,2,32,16]{2,3,1,0:T(8,128)S(1)}, u32[]{:S(2)}, u32[]{:S(2)}) %collective-permute-start.2) | collective-permute-done | bytes 12320 | tf_op jit(solution)/shard_map/ppermute | solution.py:23
  17.4 6.7 %collective-permute-start.3 = (f32[3,2,32,16]{2,3,1,0:T(8,128)S(1)}, f32[3,2,32,16]{2,3,1,0:T(8,128)S(1)}, u32[]{:S(2)}, u32[]{:S(2)}) collective-permute-start(f32[3,2,32,16]{2,3,1,0:T(8,128)S(1)} %add.86), channel_id=1, source_target_pairs={{0,8},{1,9},{2,10},{3,11},{4,12},{5,13},{6,14},{7,15},{8,0},{9,1},... | collective-permute-start | bytes 36872 | tf_op jit(solution)/shard_map/ppermute | solution.py:23
  24.2 2.1 %collective-permute-done.3 = f32[3,2,32,16]{2,3,1,0:T(8,128)S(1)} collective-permute-done((f32[3,2,32,16]{2,3,1,0:T(8,128)S(1)}, f32[3,2,32,16]{2,3,1,0:T(8,128)S(1)}, u32[]{:S(2)}, u32[]{:S(2)}) %collective-permute-start.3) | collective-permute-done | bytes 12320 | tf_op jit(solution)/shard_map/ppermute | solution.py:23
  26.5 1.0 %fusion = f32[3,2,2,4,16,16]{4,5,2,1,0,3:T(8,128)S(1)} fusion(f32[3,2,2,16,16,1]{4,3,2,1,0,5:T(8,128)S(1)} %bitcast.80, f32[4,16,8]{1,2,0:T(8,128)S(1)} %get-tuple-element.30, f32[4,16,8]{1,2,0:T(8,128)S(1)} %get-tuple-element.29), kind=kOutput, calls=%fused_computation.3 | convolution fusion | flops 2372608 | bytes 65536 | tf_op jit(solution)/shard_map/kzyrm,xqm->kzyxrq/dot_general | solution.py:230
  28.3 0.9 %fusion.3 = f32[27,2,8,256]{3,0,2,1:T(8,128)S(1)} fusion(f32[27,27,1,1]{1,0,3,2:T(8,128)S(1)} %copy-done.5, f32[27,2,8,256]{3,0,2,1:T(8,128)S(1)} %fusion.5, f32[27,2,8,256]{3,2,1,0:T(8,128)S(1)} %bitcast.79, f32[27]{0:T(128)S(1)} %copy-done.9), kind=kOutput, calls=%fused_computation.11 | convolution fusion | flops 36163584 | bytes 1330128 | tf_op jit(solution)/shard_map/ij,jzpl->izpl/dot_general | solution.py:80
  29.5 0.7 %copy.58 = f32[28,2,8,256]{0,3,2,1:T(8,128)S(1)} copy(f32[28,2,8,256]{3,0,2,1:T(8,128)S(1)} %pad_maximum_fusion) | data formatting | bytes 917504 | tf_op jit(solution)/shard_map/concatenate | solution.py:236
  30.2 1.1 %collective-permute-start.4 = (f32[224,16]{1,0:T(8,128)S(1)}, f32[224,16]{1,0:T(8,128)S(1)}, u32[]{:S(2)}, u32[]{:S(2)}) collective-permute-start(f32[224,16]{1,0:T(8,128)S(1)} %bitcast.86), channel_id=1, source_target_pairs={{0,16},{16,32},{32,48},{48,64},{64,80},{80,96},{96,112},{112,128},... | collective-permute-start | bytes 43016 | tf_op jit(solution)/shard_map/ppermute | solution.py:243
  31.4 1.1 %collective-permute-start.5 = (f32[224,16]{1,0:T(8,128)S(1)}, f32[224,16]{1,0:T(8,128)S(1)}, u32[]{:S(2)}, u32[]{:S(2)}) collective-permute-start(f32[224,16]{1,0:T(8,128)S(1)} %bitcast.87), channel_id=1, source_target_pairs={{16,0},{32,16},{48,32},{64,48},{80,64},{96,80},{112,96},{128,112},... | collective-permute-start | bytes 43016 | tf_op jit(solution)/shard_map/ppermute | solution.py:244
  32.5 2.6 %collective-permute-done.4.below_ref = f32[224,16]{1,0:T(8,128)S(1)} collective-permute-done((f32[224,16]{1,0:T(8,128)S(1)}, f32[224,16]{1,0:T(8,128)S(1)}, u32[]{:S(2)}, u32[]{:S(2)}) %collective-permute-start.4) | collective-permute-done | bytes 14368 | tf_op jit(solution)/shard_map/ppermute | solution.py:243
  35.3 4.3 %collective-permute-done.5.above_ref = f32[224,16]{1,0:T(8,128)S(1)} collective-permute-done((f32[224,16]{1,0:T(8,128)S(1)}, f32[224,16]{1,0:T(8,128)S(1)}, u32[]{:S(2)}, u32[]{:S(2)}) %collective-permute-start.5) | collective-permute-done | bytes 14368 | tf_op jit(solution)/shard_map/ppermute | solution.py:244
  40.3 0.5 collective-permute-start.6
  40.9 1.0 %copy.64.post_ref = f32[27,2,8,256]{3,2,1,0:T(8,128)} copy(f32[27,2,8,256]{3,0,2,1:T(8,128)S(1)} %fusion.3) | data formatting | bytes 884736 | tf_op jit(solution)/shard_map/ij,jzpl->izpl/dot_general | solution.py:80
  41.9 0.5 collective-permute-done.7.right_ref
  42.4 4.2 %collective-permute-done.6.left_ref = f32[224,16]{1,0:T(8,128)S(1)} collective-permute-done((f32[224,16]{1,0:T(8,128)S(1)}, f32[224,16]{1,0:T(8,128)S(1)}, u32[]{:S(2)}, u32[]{:S(2)}) %collective-permute-start.6) | collective-permute-done | bytes 14368 | tf_op jit(solution)/shard_map/ppermute | solution.py:267
  46.6 0.6 %copy-done.3 = f32[224,16]{1,0:T(8,128)} copy-done((f32[224,16]{1,0:T(8,128)}, f32[224,16]{1,0:T(8,128)S(1)}, u32[]{:S(2)}) %copy-start.3) | copy-done | bytes 14360
  47.2 3.1 %shard_map.73 = f32[8,27,512]{2,1,0:T(8,128)} custom-call(f32[8]{0:T(128)} %copy-done.7, f32[27,2,8,256]{3,2,1,0:T(8,128)} %copy.64.post_ref, f32[224,16]{1,0:T(8,128)} %copy-done, f32[224,16]{1,0:T(8,128)} %copy-done.1, f32[224,16]{1,0:T(8,128)} %copy-done.3, f32[224,16]{1,0:T(8,128)} %copy-done.2), custom_call_target="tpu_custom_call" | custom-call | tf_op jit(solution)/shard_map/pallas_call | solution.py:184
  50.3 1.6 %gather_fusion.1 = f32[6,27,512]{2,1,0:T(8,128)S(1)} fusion(f32[8,27,512]{2,1,0:T(8,128)} %shard_map.73, s32[1024]{0:T(1024)S(1)} %pad_clamp_fusion), kind=kCustom, calls=%fused_computation.1 | custom fusion | bytes 663576 | tf_op jit(solution)/shard_map/jit(_take)/gather | solution.py:272
  52.1 1.1 %copy.65 = f32[1,1,6,27,512]{4,1,3,2,0:T(1,128)} copy(f32[1,1,6,27,512]{4,3,2,1,0:T(8,128)S(1)} %fusion.8) | data formatting | bytes 663552 | tf_op jit(solution)/shard_map/mul | solution.py:273
  (77 shorter events, 3.1 us)
Async XLA Ops:
  0.0 4.1 %copy-start.6 = (f32[27,27,1,1]{1,0,3,2:T(8,128)S(1)}, f32[27,27,1,1]{1,0,3,2:T(8,128)}, u32[]{:S(2)}) copy-start(f32[27,27,1,1]{1,0,3,2:T(8,128)} %constant.85) | copy-start | bytes 8752
  0.8 3.9 %copy-start.7 = (f32[8]{0:T(128)}, f32[8]{0:T(128)S(1)}, u32[]{:S(2)}) copy-start(f32[8]{0:T(128)S(1)} %get-tuple-element.34.fluid_ref) | copy-start | bytes 100
  4.1 1.7 %copy-start.8 = (s32[8]{0:T(128)S(1)}, s32[8]{0:T(128)}, u32[]{:S(2)}) copy-start(s32[8]{0:T(128)} %param.9) | copy-start | bytes 100
  4.1 5.5 %copy-start.10 = (s32[1,1,6]{2,1,0:T(1,128)S(1)}, s32[1,1,6]{2,1,0:T(1,128)}, u32[]{:S(2)}) copy-start(s32[1,1,6]{2,1,0:T(1,128)} %param.8) | copy-start | bytes 76
  4.7 21.6 %copy-start.4 = (f32[3,2,32,16]{2,3,1,0:T(8,128)S(1)}, f32[3,2,32,16]{2,3,1,0:T(8,128)}, u32[]{:S(2)}) copy-start(f32[3,2,32,16]{2,3,1,0:T(8,128)} %param.10) | copy-start | bytes 36868
  6.3 1.3 %collective-permute-start = (f32[3,2,32,16]{2,3,1,0:T(8,128)S(1)}, f32[3,2,32,16]{2,3,1,0:T(8,128)S(1)}, u32[]{:S(2)}, u32[]{:S(2)}) collective-permute-start(f32[3,2,32,16]{2,3,1,0:T(8,128)S(1)} %convolution_bitcast_fusion), channel_id=1, source_target_pairs={{0,1},{1,0},{2,3},{3,2},{4,5},{5,4},{6,7},{7,6},{8,9},{9,8},{10,11... | collective-permute-start | bytes 36872 | tf_op jit(solution)/shard_map/ppermute | solution.py:23
  7.6 4.2 %collective-permute-start.1 = (f32[3,2,32,16]{2,3,1,0:T(8,128)S(1)}, f32[3,2,32,16]{2,3,1,0:T(8,128)S(1)}, u32[]{:S(2)}, u32[]{:S(2)}) collective-permute-start(f32[3,2,32,16]{2,3,1,0:T(8,128)S(1)} %add.84), channel_id=1, source_target_pairs={{0,2},{1,3},{2,0},{3,1},{4,6},{5,7},{6,4},{7,5},{8,10},{9,11},{10,... | collective-permute-start | bytes 36872 | tf_op jit(solution)/shard_map/ppermute | solution.py:23
  11.8 5.6 %collective-permute-start.2 = (f32[3,2,32,16]{2,3,1,0:T(8,128)S(1)}, f32[3,2,32,16]{2,3,1,0:T(8,128)S(1)}, u32[]{:S(2)}, u32[]{:S(2)}) collective-permute-start(f32[3,2,32,16]{2,3,1,0:T(8,128)S(1)} %add.85), channel_id=1, source_target_pairs={{0,4},{1,5},{2,6},{3,7},{4,0},{5,1},{6,2},{7,3},{8,12},{9,13},{10,... | collective-permute-start | bytes 36872 | tf_op jit(solution)/shard_map/ppermute | solution.py:23
  17.4 8.9 %collective-permute-start.3 = (f32[3,2,32,16]{2,3,1,0:T(8,128)S(1)}, f32[3,2,32,16]{2,3,1,0:T(8,128)S(1)}, u32[]{:S(2)}, u32[]{:S(2)}) collective-permute-start(f32[3,2,32,16]{2,3,1,0:T(8,128)S(1)} %add.86), channel_id=1, source_target_pairs={{0,8},{1,9},{2,10},{3,11},{4,12},{5,13},{6,14},{7,15},{8,0},{9,1},... | collective-permute-start | bytes 36872 | tf_op jit(solution)/shard_map/ppermute | solution.py:23
  24.2 4.1 %copy-start.5 = (f32[27,27,1,1]{1,0,3,2:T(8,128)S(1)}, f32[27,27,1,1]{1,0,3,2:T(8,128)}, u32[]{:S(2)}) copy-start(f32[27,27,1,1]{1,0,3,2:T(8,128)} %constant.84) | copy-start | bytes 8752
  24.2 4.1 %copy-start.9 = (f32[27]{0:T(128)S(1)}, f32[27]{0:T(128)}, u32[]{:S(2)}) copy-start(f32[27]{0:T(128)} %param.11) | copy-start | bytes 328
  30.2 4.9 %collective-permute-start.4 = (f32[224,16]{1,0:T(8,128)S(1)}, f32[224,16]{1,0:T(8,128)S(1)}, u32[]{:S(2)}, u32[]{:S(2)}) collective-permute-start(f32[224,16]{1,0:T(8,128)S(1)} %bitcast.86), channel_id=1, source_target_pairs={{0,16},{16,32},{32,48},{48,64},{64,80},{80,96},{96,112},{112,128},... | collective-permute-start | bytes 43016 | tf_op jit(solution)/shard_map/ppermute | solution.py:243
  31.4 8.2 %collective-permute-start.5 = (f32[224,16]{1,0:T(8,128)S(1)}, f32[224,16]{1,0:T(8,128)S(1)}, u32[]{:S(2)}, u32[]{:S(2)}) collective-permute-start(f32[224,16]{1,0:T(8,128)S(1)} %bitcast.87), channel_id=1, source_target_pairs={{16,0},{32,16},{48,32},{64,48},{80,64},{96,80},{112,96},{128,112},... | collective-permute-start | bytes 43016 | tf_op jit(solution)/shard_map/ppermute | solution.py:244
  35.1 11.5 %copy-start = (f32[224,16]{1,0:T(8,128)}, f32[224,16]{1,0:T(8,128)S(1)}, u32[]{:S(2)}) copy-start(f32[224,16]{1,0:T(8,128)S(1)} %collective-permute-done.4.below_ref) | copy-start | bytes 43012
  39.6 7.0 %copy-start.1 = (f32[224,16]{1,0:T(8,128)}, f32[224,16]{1,0:T(8,128)S(1)}, u32[]{:S(2)}) copy-start(f32[224,16]{1,0:T(8,128)S(1)} %collective-permute-done.5.above_ref) | copy-start | bytes 43012
  40.0 2.4 %collective-permute-start.7 = (f32[224,16]{1,0:T(8,128)S(1)}, f32[224,16]{1,0:T(8,128)S(1)}, u32[]{:S(2)}, u32[]{:S(2)}) collective-permute-start(f32[224,16]{1,0:T(8,128)S(1)} %bitcast.85), channel_id=1, source_target_pairs={{1,0},{2,1},{3,2},{4,3},{5,4},{6,5},{7,6},{8,7},{9,8},{10,9},{11,1... | collective-permute-start | bytes 43016 | tf_op jit(solution)/shard_map/ppermute | solution.py:268
  40.3 6.2 %collective-permute-start.6 = (f32[224,16]{1,0:T(8,128)S(1)}, f32[224,16]{1,0:T(8,128)S(1)}, u32[]{:S(2)}, u32[]{:S(2)}) collective-permute-start(f32[224,16]{1,0:T(8,128)S(1)} %bitcast.88), channel_id=1, source_target_pairs={{0,1},{1,2},{2,3},{3,4},{4,5},{5,6},{6,7},{7,8},{8,9},{9,10},{10,1... | collective-permute-start | bytes 43016 | tf_op jit(solution)/shard_map/ppermute | solution.py:267
  42.4 4.2 %copy-start.2 = (f32[224,16]{1,0:T(8,128)}, f32[224,16]{1,0:T(8,128)S(1)}, u32[]{:S(2)}) copy-start(f32[224,16]{1,0:T(8,128)S(1)} %collective-permute-done.7.right_ref) | copy-start | bytes 43012
  46.6 0.6 %copy-start.3 = (f32[224,16]{1,0:T(8,128)}, f32[224,16]{1,0:T(8,128)S(1)}, u32[]{:S(2)}) copy-start(f32[224,16]{1,0:T(8,128)S(1)} %collective-permute-done.6.left_ref) | copy-start | bytes 43012

commit v9 on v8

--- a/solution.py
+++ b/solution.py
@@ -80,8 +80,10 @@
     return jnp.einsum("ij,jzpl->izpl", backward, relaxed, precision=HIGHEST)
 
 
-def stream_kernel(fluid_ref, post_ref, below_ref, above_ref, left_ref, right_ref, out_ref, spread_ref):
-    channels, levels, blocks, cells = post_ref.shape
+def stream_kernel(
+    fluid_ref, keys_ref, post_ref, below_ref, above_ref, left_ref, right_ref, out_ref, spread_ref, result_ref
+):
+    levels, blocks, channels, cells = post_ref.shape
     _, _, speeds = lattice_tables()
     front = 8
     grid_row = lax.broadcasted_iota(jnp.int32, (BE, cells), 0)
@@ -108,7 +110,7 @@
     def own(channel, level):
         if channel == channels:
             return solid_plane
-        return post_ref[channel, level]
+        return post_ref[level, :, channel, :]
 
     def moved(plane, shift):
         shift = shift % cells
@@ -160,10 +162,10 @@
         cx, cy, cz = (int(v) for v in speeds[heading])
         blocked = blocked_of[(cx, cy)]
         for level in range(levels):
-            bounced = post_ref[26 - heading, level]
+            bounced = post_ref[level, :, 26 - heading, :]
             window = pl.ds(level * cells, cells)
             if cz == 1 and level == 0:
-                out_ref[:, heading, window] = bounced
+                result_ref[:, heading, window] = bounced
                 continue
             if cz == 0:
                 source = gathered(heading, level, cx, cy)
@@ -173,21 +175,29 @@
                 source = gathered(heading, 1, cx, cy)
             else:
                 source = gathered(heading + 2, 1, cx, cy)
-            out_ref[:, heading, window] = jnp.where(blocked, bounced, source)
-
-
-def stream(fluid, post, below, above, from_left, from_right):
+            result_ref[:, heading, window] = jnp.where(blocked, bounced, source)
+    for seat_number in range(out_ref.shape[0]):
+        key = keys_ref[seat_number]
+        picked = result_ref[jnp.maximum(key, 0)]
+        out_ref[seat_number] = jnp.where(key >= 0, picked, 0.0)
+
+
+def stream(fluid, keys, post, below, above, from_left, from_right):
     channels, levels, blocks, cells = post.shape
+    seats = keys.shape[0]
     halo_rows = below.shape[0]
     vmem = pl.BlockSpec(memory_space=pltpu.VMEM)
     smem = pl.BlockSpec(memory_space=pltpu.SMEM)
     return pl.pallas_call(
         stream_kernel,
-        out_shape=jax.ShapeDtypeStruct((blocks, channels, levels * cells), jnp.float32),
-        in_specs=[smem] + [vmem] * 5,
+        out_shape=jax.ShapeDtypeStruct((seats, channels, levels * cells), jnp.float32),
+        in_specs=[smem, smem] + [vmem] * 5,
         out_specs=vmem,
-        scratch_shapes=[pltpu.VMEM((4, halo_rows + 16, cells), jnp.float32)],
-    )(fluid, post, below, above, from_left, from_right)
+        scratch_shapes=[
+            pltpu.VMEM((4, halo_rows + 16, cells), jnp.float32),
+            pltpu.VMEM((blocks, channels, levels * cells), jnp.float32),
+        ],
+    )(fluid, keys, post.transpose(1, 2, 0, 3), below, above, from_left, from_right)
 
 
 def on_device(
@@ -266,11 +276,7 @@
     )
     from_left = lax.ppermute(flat(to_right), "line", ahead)
     from_right = lax.ppermute(flat(to_left), "line", behind)
-    result = stream(fluid, post, below_flat, above_flat, from_left, from_right)
-    by_block = result
-    occupied = living_brick_keys >= 0
-    new_state = jnp.take(by_block, jnp.maximum(living_brick_keys, 0), axis=0)
-    new_state = new_state * occupied[:, None, None].astype(jnp.float32)
+    new_state = stream(fluid, living_brick_keys, post, below_flat, above_flat, from_left, from_right)
     return new_state[None, None]
 
 

time: 53.5 us -> 52.9 us (0.989)
  local copies, waits for them, and re-layouts: 8.73 us -> 7.1 us
  waiting for transfers between devices: 19.3 us -> 20.4 us
    broadcast_in_dim x0 -> x1, local copies, waits for them, and re-layouts: none -> 2.06 us  [on_device(): return new_state[None, None]]
    gather x1 -> x0, local copies, waits for them, and re-layouts: 1.61 us -> none  [on_device(): new_state = jnp.take(by_block, jnp.maximum(living_brick_keys, 0), axis=0)]
    mul x1 -> x0, local copies, waits for them, and re-layouts: 1.07 us -> none  [on_device(): new_state = new_state * occupied[:, None, None].astype(jnp.float32)]
    ppermute x1, waiting for transfers between devices: 0.49 us -> 1.52 us  [on_device(): from_right = lax.ppermute(flat(to_left), 'line', behind)]
    dot_general x1 -> x0, local copies, waits for them, and re-layouts: 1.02 us -> none  [collide_blocks(): return jnp.einsum('ij,jzpl->izpl', backward, relaxed, precision=HIGHEST)]
  transfers between devices with their start and end apart: 8 -> 8, of which waited for: 8 -> 8; matrix products, arithmetic and copies ran while one was open for 3% -> 1% of each run, Pallas kernels for 0% -> 0%
where the time goes in v9:
time: 52.9 us; the launch traced here: 52.5 us
  waiting for transfers between devices  20.4 us (39%)
  starting transfers between devices  14.9 us (28%)
  local copies, waits for them, and re-layouts  7.1 us (13%)
  other arithmetic  3.78 us (7%)
  Pallas kernels  3.18 us (6%)
  matrix products  2.79 us (5%)
    ppermute x4, starting transfers between devices, butterfly_sum(): lax.ppermute(value, axis, [(i, i ^ stride) for i in range(count)])  12.2 us
    ppermute x4, waiting for transfers between devices, butterfly_sum(): lax.ppermute(value, axis, [(i, i ^ stride) for i in range(count)])  7.8 us
    ppermute x1, waiting for transfers between devices, on_device(): above_flat = lax.ppermute(flat(bottom_row), 'curve', behind)  4.3 us
    ppermute x1, waiting for transfers between devices, on_device(): from_left = lax.ppermute(flat(to_right), 'line', ahead)  4.18 us
    pallas_call x1, Pallas kernels, stream(): pl.pallas_call(stream_kernel, out_shape=jax.ShapeDtypeStruct((seats, chan...  3.18 us
    ppermute x1, waiting for transfers between devices, on_device(): below_flat = lax.ppermute(flat(top_row), 'curve', ahead)  2.55 us
    broadcast_in_dim x1, local copies, waits for them, and re-layouts, on_device(): return new_state[None, None]  2.06 us
    unnamed x1, other arithmetic  1.77 us
  transfers between devices with their start and end apart: 8, of which 8 were waited for; matrix products, arithmetic and copies ran while one was open for 1% of the time, Pallas kernels for 0%

profile of v9, /device:TPU:30, one launch (start us, length us, event | category | flops | bytes accessed | tf_op | source)
XLA Modules:
  0.0 52.5 jit_solution(821121483053292318)
XLA Ops:
  0.0 0.8 %select_reduce_fusion = s32[8]{0:T(128)S(1)} fusion(s32[6]{0:T(128)S(1)} %iota_add_fusion, s32[6]{0:T(128)} %bitcast.92), kind=kLoop, calls=%fused_computation.56 | loop fusion | flops 136 | bytes 80 | tf_op jit(solution)/shard_map/reduce_max | solution.py:222
  0.8 1.8 %reduce = f32[6,27,512]{2,1,0:T(8,128)S(1)} reduce(f32[1,1,6,27,512]{4,1,3,2,0:T(1,128)} %param.7, f32[]{:T(128)} %constant.70), dimensions={0,1}, to_apply=%param.7.reduce_sub_computation | reduce | bytes 663556 | tf_op args[0]
  2.6 0.2 reshape_squeeze.3
  2.8 1.0 %gather_fusion = f32[8,27,2,256]{3,2,1,0:T(2,128)S(1)} fusion(f32[6,27,2,256]{3,2,1,0:T(2,128)S(1)} %reshape_squeeze.3, s32[1024]{0:T(1024)S(1)} %pad_clamp_fusion), kind=kCustom, calls=%fused_computation | custom fusion | bytes 884768 | tf_op jit(solution)/shard_map/jit(_take)/gather | solution.py:226
  3.9 0.3 multiply_bitcast_fusion
  4.1 0.6 %fusion.5 = f32[27,2,8,256]{3,0,2,1:T(8,128)S(1)} fusion(f32[27,27,1,1]{1,0,3,2:T(8,128)S(1)} %copy-done.7, f32[27,2,8,256]{3,1,0,2:T(2,128)S(1)} %multiply_bitcast_fusion), kind=kOutput, calls=%fused_computation.11 | convolution fusion | flops 35831808 | bytes 887652 | tf_op jit(solution)/shard_map/ij,jzpl->izpl/dot_general | solution.py:228
  4.7 0.2 fusion.22
  5.4 0.2 copy.45
  5.6 0.2 dot_general.23
  6.0 0.3 convolution_bitcast_fusion
  6.4 1.2 %collective-permute-done = f32[3,2,32,16]{2,3,1,0:T(8,128)S(1)} collective-permute-done((f32[3,2,32,16]{2,3,1,0:T(8,128)S(1)}, f32[3,2,32,16]{2,3,1,0:T(8,128)S(1)}, u32[]{:S(2)}, u32[]{:S(2)}) %collective-permute-start) | collective-permute-done | bytes 12320 | tf_op jit(solution)/shard_map/ppermute | solution.py:23
  7.6 2.0 %collective-permute-start.1 = (f32[3,2,32,16]{2,3,1,0:T(8,128)S(1)}, f32[3,2,32,16]{2,3,1,0:T(8,128)S(1)}, u32[]{:S(2)}, u32[]{:S(2)}) collective-permute-start(f32[3,2,32,16]{2,3,1,0:T(8,128)S(1)} %add.82), channel_id=1, source_target_pairs={{0,2},{1,3},{2,0},{3,1},{4,6},{5,7},{6,4},{7,5},{8,10},{9,11},{10,... | collective-permute-start | bytes 36872 | tf_op jit(solution)/shard_map/ppermute | solution.py:23
  9.6 2.2 %collective-permute-done.1 = f32[3,2,32,16]{2,3,1,0:T(8,128)S(1)} collective-permute-done((f32[3,2,32,16]{2,3,1,0:T(8,128)S(1)}, f32[3,2,32,16]{2,3,1,0:T(8,128)S(1)}, u32[]{:S(2)}, u32[]{:S(2)}) %collective-permute-start.1) | collective-permute-done | bytes 12320 | tf_op jit(solution)/shard_map/ppermute | solution.py:23
  11.8 3.4 %collective-permute-start.2 = (f32[3,2,32,16]{2,3,1,0:T(8,128)S(1)}, f32[3,2,32,16]{2,3,1,0:T(8,128)S(1)}, u32[]{:S(2)}, u32[]{:S(2)}) collective-permute-start(f32[3,2,32,16]{2,3,1,0:T(8,128)S(1)} %add.83), channel_id=1, source_target_pairs={{0,4},{1,5},{2,6},{3,7},{4,0},{5,1},{6,2},{7,3},{8,12},{9,13},{10,... | collective-permute-start | bytes 36872 | tf_op jit(solution)/shard_map/ppermute | solution.py:23
  15.2 2.3 %collective-permute-done.2 = f32[3,2,32,16]{2,3,1,0:T(8,128)S(1)} collective-permute-done((f32[3,2,32,16]{2,3,1,0:T(8,128)S(1)}, f32[3,2,32,16]{2,3,1,0:T(8,128)S(1)}, u32[]{:S(2)}, u32[]{:S(2)}) %collective-permute-start.2) | collective-permute-done | bytes 12320 | tf_op jit(solution)/shard_map/ppermute | solution.py:23
  17.4 6.7 %collective-permute-start.3 = (f32[3,2,32,16]{2,3,1,0:T(8,128)S(1)}, f32[3,2,32,16]{2,3,1,0:T(8,128)S(1)}, u32[]{:S(2)}, u32[]{:S(2)}) collective-permute-start(f32[3,2,32,16]{2,3,1,0:T(8,128)S(1)} %add.84), channel_id=1, source_target_pairs={{0,8},{1,9},{2,10},{3,11},{4,12},{5,13},{6,14},{7,15},{8,0},{9,1},... | collective-permute-start | bytes 36872 | tf_op jit(solution)/shard_map/ppermute | solution.py:23
  24.2 2.1 %collective-permute-done.3 = f32[3,2,32,16]{2,3,1,0:T(8,128)S(1)} collective-permute-done((f32[3,2,32,16]{2,3,1,0:T(8,128)S(1)}, f32[3,2,32,16]{2,3,1,0:T(8,128)S(1)}, u32[]{:S(2)}, u32[]{:S(2)}) %collective-permute-start.3) | collective-permute-done | bytes 12320 | tf_op jit(solution)/shard_map/ppermute | solution.py:23
  26.5 1.0 %fusion = f32[3,2,2,4,16,16]{4,5,2,1,0,3:T(8,128)S(1)} fusion(f32[3,2,2,16,16,1]{4,3,2,1,0,5:T(8,128)S(1)} %bitcast.79, f32[4,16,8]{1,2,0:T(8,128)S(1)} %get-tuple-element.30, f32[4,16,8]{1,2,0:T(8,128)S(1)} %get-tuple-element.29), kind=kOutput, calls=%fused_computation.2 | convolution fusion | flops 2372608 | bytes 65536 | tf_op jit(solution)/shard_map/kzyrm,xqm->kzyxrq/dot_general | solution.py:240
  27.5 0.2 copy.48
  27.7 0.2 mul.155
  28.3 0.9 %fusion.3 = f32[2,8,256,27]{2,3,1,0:T(8,128)S(1)} fusion(f32[27,27,1,1]{1,0,3,2:T(8,128)S(1)} %copy-done.6, f32[27,2,8,256]{3,0,2,1:T(8,128)S(1)} %fusion.5, f32[27,2,8,256]{3,2,1,0:T(8,128)S(1)} %bitcast.77, f32[27]{0:T(128)S(1)} %copy-done.10), kind=kOutput, calls=%fused_computation.10 | convolution fusion | flops 36163584 | bytes 1330128 | tf_op jit(solution)/shard_map/ij,jzpl->izpl/dot_general | solution.py:80
  29.5 0.7 %copy.56 = f32[28,2,8,256]{0,3,2,1:T(8,128)S(1)} copy(f32[28,2,8,256]{3,0,2,1:T(8,128)S(1)} %pad_maximum_fusion) | data formatting | bytes 917504 | tf_op jit(solution)/shard_map/concatenate | solution.py:246
  30.3 1.1 %collective-permute-start.4 = (f32[224,16]{1,0:T(8,128)S(1)}, f32[224,16]{1,0:T(8,128)S(1)}, u32[]{:S(2)}, u32[]{:S(2)}) collective-permute-start(f32[224,16]{1,0:T(8,128)S(1)} %bitcast.85), channel_id=1, source_target_pairs={{0,16},{16,32},{32,48},{48,64},{64,80},{80,96},{96,112},{112,128},... | collective-permute-start | bytes 43016 | tf_op jit(solution)/shard_map/ppermute | solution.py:253
  31.5 1.1 %collective-permute-start.5 = (f32[224,16]{1,0:T(8,128)S(1)}, f32[224,16]{1,0:T(8,128)S(1)}, u32[]{:S(2)}, u32[]{:S(2)}) collective-permute-start(f32[224,16]{1,0:T(8,128)S(1)} %bitcast.86), channel_id=1, source_target_pairs={{16,0},{32,16},{48,32},{64,48},{80,64},{96,80},{112,96},{128,112},... | collective-permute-start | bytes 43016 | tf_op jit(solution)/shard_map/ppermute | solution.py:254
  32.6 2.6 %collective-permute-done.4.below_ref = f32[224,16]{1,0:T(8,128)S(1)} collective-permute-done((f32[224,16]{1,0:T(8,128)S(1)}, f32[224,16]{1,0:T(8,128)S(1)}, u32[]{:S(2)}, u32[]{:S(2)}) %collective-permute-start.4) | collective-permute-done | bytes 14368 | tf_op jit(solution)/shard_map/ppermute | solution.py:253
  35.4 4.3 %collective-permute-done.5.above_ref = f32[224,16]{1,0:T(8,128)S(1)} collective-permute-done((f32[224,16]{1,0:T(8,128)S(1)}, f32[224,16]{1,0:T(8,128)S(1)}, u32[]{:S(2)}, u32[]{:S(2)}) %collective-permute-start.5) | collective-permute-done | bytes 14368 | tf_op jit(solution)/shard_map/ppermute | solution.py:254
  40.4 0.5 collective-permute-start.6
  40.9 1.5 %collective-permute-done.7.right_ref = f32[224,16]{1,0:T(8,128)S(1)} collective-permute-done((f32[224,16]{1,0:T(8,128)S(1)}, f32[224,16]{1,0:T(8,128)S(1)}, u32[]{:S(2)}, u32[]{:S(2)}) %collective-permute-start.7) | collective-permute-done | bytes 14368 | tf_op jit(solution)/shard_map/ppermute | solution.py:278
  42.4 4.2 %collective-permute-done.6.left_ref = f32[224,16]{1,0:T(8,128)S(1)} collective-permute-done((f32[224,16]{1,0:T(8,128)S(1)}, f32[224,16]{1,0:T(8,128)S(1)}, u32[]{:S(2)}, u32[]{:S(2)}) %collective-permute-start.6) | collective-permute-done | bytes 14368 | tf_op jit(solution)/shard_map/ppermute | solution.py:277
  46.6 0.6 %copy-done.4 = f32[224,16]{1,0:T(8,128)} copy-done((f32[224,16]{1,0:T(8,128)}, f32[224,16]{1,0:T(8,128)S(1)}, u32[]{:S(2)}) %copy-start.4) | copy-done | bytes 14360
  47.3 3.2 %shard_map.73 = f32[6,27,512]{2,1,0:T(8,128)} custom-call(f32[8]{0:T(128)} %copy-done.8, s32[6]{0:T(128)} %bitcast.93, f32[2,8,27,256]{3,2,1,0:T(8,128)} %bitcast.75, f32[224,16]{1,0:T(8,128)} %copy-done.1, f32[224,16]{1,0:T(8,128)} %copy-done.2, f32[224,16]{1,0:T(8,128)} %copy-done.4, f32[224,16]{1,0:T(8,128)} %copy-done.3), custom_call_target="tpu_custom_call" | custom-call | tf_op jit(solution)/shard_map/pallas_call | solution.py:191
  50.5 2.1 %copy.62 = f32[1,1,6,27,512]{4,1,3,2,0:T(1,128)} copy(f32[1,1,6,27,512]{4,3,2,1,0:T(8,128)} %bitcast.78) | data formatting | bytes 663552 | tf_op jit(solution)/shard_map/broadcast_in_dim | solution.py:280
  (71 shorter events, 2.6 us)
Async XLA Ops:
  0.0 4.1 %copy-start.7 = (f32[27,27,1,1]{1,0,3,2:T(8,128)S(1)}, f32[27,27,1,1]{1,0,3,2:T(8,128)}, u32[]{:S(2)}) copy-start(f32[27,27,1,1]{1,0,3,2:T(8,128)} %constant.68) | copy-start | bytes 8752
  0.8 3.9 %copy-start.8 = (f32[8]{0:T(128)}, f32[8]{0:T(128)S(1)}, u32[]{:S(2)}) copy-start(f32[8]{0:T(128)S(1)} %get-tuple-element.32.fluid_ref) | copy-start | bytes 100
  4.1 1.7 %copy-start.9 = (s32[8]{0:T(128)S(1)}, s32[8]{0:T(128)}, u32[]{:S(2)}) copy-start(s32[8]{0:T(128)} %param.9) | copy-start | bytes 100
  4.7 21.6 %copy-start.5 = (f32[3,2,32,16]{2,3,1,0:T(8,128)S(1)}, f32[3,2,32,16]{2,3,1,0:T(8,128)}, u32[]{:S(2)}) copy-start(f32[3,2,32,16]{2,3,1,0:T(8,128)} %param.10) | copy-start | bytes 36868
  6.3 1.3 %collective-permute-start = (f32[3,2,32,16]{2,3,1,0:T(8,128)S(1)}, f32[3,2,32,16]{2,3,1,0:T(8,128)S(1)}, u32[]{:S(2)}, u32[]{:S(2)}) collective-permute-start(f32[3,2,32,16]{2,3,1,0:T(8,128)S(1)} %convolution_bitcast_fusion), channel_id=1, source_target_pairs={{0,1},{1,0},{2,3},{3,2},{4,5},{5,4},{6,7},{7,6},{8,9},{9,8},{10,11... | collective-permute-start | bytes 36872 | tf_op jit(solution)/shard_map/ppermute | solution.py:23
  7.6 4.2 %collective-permute-start.1 = (f32[3,2,32,16]{2,3,1,0:T(8,128)S(1)}, f32[3,2,32,16]{2,3,1,0:T(8,128)S(1)}, u32[]{:S(2)}, u32[]{:S(2)}) collective-permute-start(f32[3,2,32,16]{2,3,1,0:T(8,128)S(1)} %add.82), channel_id=1, source_target_pairs={{0,2},{1,3},{2,0},{3,1},{4,6},{5,7},{6,4},{7,5},{8,10},{9,11},{10,... | collective-permute-start | bytes 36872 | tf_op jit(solution)/shard_map/ppermute | solution.py:23
  11.8 5.6 %collective-permute-start.2 = (f32[3,2,32,16]{2,3,1,0:T(8,128)S(1)}, f32[3,2,32,16]{2,3,1,0:T(8,128)S(1)}, u32[]{:S(2)}, u32[]{:S(2)}) collective-permute-start(f32[3,2,32,16]{2,3,1,0:T(8,128)S(1)} %add.83), channel_id=1, source_target_pairs={{0,4},{1,5},{2,6},{3,7},{4,0},{5,1},{6,2},{7,3},{8,12},{9,13},{10,... | collective-permute-start | bytes 36872 | tf_op jit(solution)/shard_map/ppermute | solution.py:23
  17.4 8.9 %collective-permute-start.3 = (f32[3,2,32,16]{2,3,1,0:T(8,128)S(1)}, f32[3,2,32,16]{2,3,1,0:T(8,128)S(1)}, u32[]{:S(2)}, u32[]{:S(2)}) collective-permute-start(f32[3,2,32,16]{2,3,1,0:T(8,128)S(1)} %add.84), channel_id=1, source_target_pairs={{0,8},{1,9},{2,10},{3,11},{4,12},{5,13},{6,14},{7,15},{8,0},{9,1},... | collective-permute-start | bytes 36872 | tf_op jit(solution)/shard_map/ppermute | solution.py:23
  24.2 4.1 %copy-start.6 = (f32[27,27,1,1]{1,0,3,2:T(8,128)S(1)}, f32[27,27,1,1]{1,0,3,2:T(8,128)}, u32[]{:S(2)}) copy-start(f32[27,27,1,1]{1,0,3,2:T(8,128)} %constant.69) | copy-start | bytes 8752
  24.2 4.1 %copy-start.10 = (f32[27]{0:T(128)S(1)}, f32[27]{0:T(128)}, u32[]{:S(2)}) copy-start(f32[27]{0:T(128)} %param.11) | copy-start | bytes 328
  29.3 0.9 %copy-start = (f32[2,8,256,27]{2,3,1,0:T(8,128)}, f32[2,8,256,27]{2,3,1,0:T(8,128)S(1)}, u32[]{:S(2)}) copy-start(f32[2,8,256,27]{2,3,1,0:T(8,128)S(1)} %fusion.3) | copy-start | bytes 1327108
  30.3 4.9 %collective-permute-start.4 = (f32[224,16]{1,0:T(8,128)S(1)}, f32[224,16]{1,0:T(8,128)S(1)}, u32[]{:S(2)}, u32[]{:S(2)}) collective-permute-start(f32[224,16]{1,0:T(8,128)S(1)} %bitcast.85), channel_id=1, source_target_pairs={{0,16},{16,32},{32,48},{48,64},{64,80},{80,96},{96,112},{112,128},... | collective-permute-start | bytes 43016 | tf_op jit(solution)/shard_map/ppermute | solution.py:253
  31.5 8.2 %collective-permute-start.5 = (f32[224,16]{1,0:T(8,128)S(1)}, f32[224,16]{1,0:T(8,128)S(1)}, u32[]{:S(2)}, u32[]{:S(2)}) collective-permute-start(f32[224,16]{1,0:T(8,128)S(1)} %bitcast.86), channel_id=1, source_target_pairs={{16,0},{32,16},{48,32},{64,48},{80,64},{96,80},{112,96},{128,112},... | collective-permute-start | bytes 43016 | tf_op jit(solution)/shard_map/ppermute | solution.py:254
  35.1 11.5 %copy-start.1 = (f32[224,16]{1,0:T(8,128)}, f32[224,16]{1,0:T(8,128)S(1)}, u32[]{:S(2)}) copy-start(f32[224,16]{1,0:T(8,128)S(1)} %collective-permute-done.4.below_ref) | copy-start | bytes 43012
  39.7 6.9 %copy-start.2 = (f32[224,16]{1,0:T(8,128)}, f32[224,16]{1,0:T(8,128)S(1)}, u32[]{:S(2)}) copy-start(f32[224,16]{1,0:T(8,128)S(1)} %collective-permute-done.5.above_ref) | copy-start | bytes 43012
  40.1 2.4 %collective-permute-start.7 = (f32[224,16]{1,0:T(8,128)S(1)}, f32[224,16]{1,0:T(8,128)S(1)}, u32[]{:S(2)}, u32[]{:S(2)}) collective-permute-start(f32[224,16]{1,0:T(8,128)S(1)} %bitcast.84), channel_id=1, source_target_pairs={{1,0},{2,1},{3,2},{4,3},{5,4},{6,5},{7,6},{8,7},{9,8},{10,9},{11,1... | collective-permute-start | bytes 43016 | tf_op jit(solution)/shard_map/ppermute | solution.py:278
  40.4 6.2 %collective-permute-start.6 = (f32[224,16]{1,0:T(8,128)S(1)}, f32[224,16]{1,0:T(8,128)S(1)}, u32[]{:S(2)}, u32[]{:S(2)}) collective-permute-start(f32[224,16]{1,0:T(8,128)S(1)} %bitcast.87), channel_id=1, source_target_pairs={{0,1},{1,2},{2,3},{3,4},{4,5},{5,6},{6,7},{7,8},{8,9},{9,10},{10,1... | collective-permute-start | bytes 43016 | tf_op jit(solution)/shard_map/ppermute | solution.py:277
  42.4 4.2 %copy-start.3 = (f32[224,16]{1,0:T(8,128)}, f32[224,16]{1,0:T(8,128)S(1)}, u32[]{:S(2)}) copy-start(f32[224,16]{1,0:T(8,128)S(1)} %collective-permute-done.7.right_ref) | copy-start | bytes 43012
  46.6 0.7 %copy-start.4 = (f32[224,16]{1,0:T(8,128)}, f32[224,16]{1,0:T(8,128)S(1)}, u32[]{:S(2)}) copy-start(f32[224,16]{1,0:T(8,128)S(1)} %collective-permute-done.6.left_ref) | copy-start | bytes 43012

commit v10 on v9

--- a/solution.py
+++ b/solution.py
@@ -176,10 +176,13 @@
             else:
                 source = gathered(heading + 2, 1, cx, cy)
             result_ref[:, heading, window] = jnp.where(blocked, bounced, source)
-    for seat_number in range(out_ref.shape[0]):
+    chunks = levels * cells // 128
+    for seat_number in range(keys_ref.shape[0]):
         key = keys_ref[seat_number]
-        picked = result_ref[jnp.maximum(key, 0)]
-        out_ref[seat_number] = jnp.where(key >= 0, picked, 0.0)
+        for chunk in range(chunks):
+            picked = result_ref[jnp.maximum(key, 0), :, chunk * 128:(chunk + 1) * 128]
+            rows = pl.ds(seat_number * channels * chunks + chunk, channels, stride=chunks)
+            out_ref[rows, :] = jnp.where(key >= 0, picked, 0.0)
 
 
 def stream(fluid, keys, post, below, above, from_left, from_right):
@@ -190,7 +193,7 @@
     smem = pl.BlockSpec(memory_space=pltpu.SMEM)
     return pl.pallas_call(
         stream_kernel,
-        out_shape=jax.ShapeDtypeStruct((seats, channels, levels * cells), jnp.float32),
+        out_shape=jax.ShapeDtypeStruct((seats * channels * levels * cells // 128, 128), jnp.float32),
         in_specs=[smem, smem] + [vmem] * 5,
         out_specs=vmem,
         scratch_shapes=[
@@ -277,7 +280,7 @@
     from_left = lax.ppermute(flat(to_right), "line", ahead)
     from_right = lax.ppermute(flat(to_left), "line", behind)
     new_state = stream(fluid, living_brick_keys, post, below_flat, above_flat, from_left, from_right)
-    return new_state[None, None]
+    return new_state.reshape((1, 1, seats, channels, levels * cells))
 
 
 def solution(mesh):

time: 52.9 us -> 50.8 us (0.960)
  local copies, waits for them, and re-layouts: 7.1 us -> 5.03 us
    broadcast_in_dim x1 -> x0, local copies, waits for them, and re-layouts: 2.06 us -> none  [on_device(): return new_state[None, None]]
where the time goes in v10:
time: 50.8 us; the launch traced here: 50.4 us
  waiting for transfers between devices  20.4 us (40%)
  starting transfers between devices  14.9 us (29%)
  local copies, waits for them, and re-layouts  5.03 us (10%)
  other arithmetic  3.78 us (7%)
  Pallas kernels  3.18 us (6%)
  matrix products  2.79 us (5%)
    ppermute x4, starting transfers between devices, butterfly_sum(): lax.ppermute(value, axis, [(i, i ^ stride) for i in range(count)])  12.2 us
    ppermute x4, waiting for transfers between devices, butterfly_sum(): lax.ppermute(value, axis, [(i, i ^ stride) for i in range(count)])  7.8 us
    ppermute x1, waiting for transfers between devices, on_device(): above_flat = lax.ppermute(flat(bottom_row), 'curve', behind)  4.3 us
    ppermute x1, waiting for transfers between devices, on_device(): from_left = lax.ppermute(flat(to_right), 'line', ahead)  4.18 us
    pallas_call x1, Pallas kernels, stream(): pl.pallas_call(stream_kernel, out_shape=jax.ShapeDtypeStruct((seats * cha...  3.18 us
    ppermute x1, waiting for transfers between devices, on_device(): below_flat = lax.ppermute(flat(top_row), 'curve', ahead)  2.55 us
    unnamed x1, other arithmetic  1.77 us
    ppermute x1, waiting for transfers between devices, on_device(): from_right = lax.ppermute(flat(to_left), 'line', behind)  1.52 us
  transfers between devices with their start and end apart: 8, of which 8 were waited for; matrix products, arithmetic and copies ran while one was open for 1% of the time, Pallas kernels for 0%

profile of v10, /device:TPU:30, one launch (start us, length us, event | category | flops | bytes accessed | tf_op | source)
XLA Modules:
  0.0 50.4 jit_solution(6005980014354703825)
XLA Ops:
  0.0 0.8 %select_reduce_fusion = s32[8]{0:T(128)S(1)} fusion(s32[6]{0:T(128)S(1)} %iota_add_fusion, s32[6]{0:T(128)} %bitcast.91), kind=kLoop, calls=%fused_computation.56 | loop fusion | flops 136 | bytes 80 | tf_op jit(solution)/shard_map/reduce_max | solution.py:225
  0.8 1.8 %reduce = f32[6,27,512]{2,1,0:T(8,128)S(1)} reduce(f32[1,1,6,27,512]{4,1,3,2,0:T(1,128)} %param.7, f32[]{:T(128)} %constant.70), dimensions={0,1}, to_apply=%param.7.reduce_sub_computation | reduce | bytes 663556 | tf_op args[0]
  2.6 0.2 reshape_squeeze.3
  2.8 1.0 %gather_fusion = f32[8,27,2,256]{3,2,1,0:T(2,128)S(1)} fusion(f32[6,27,2,256]{3,2,1,0:T(2,128)S(1)} %reshape_squeeze.3, s32[1024]{0:T(1024)S(1)} %pad_clamp_fusion), kind=kCustom, calls=%fused_computation | custom fusion | bytes 884768 | tf_op jit(solution)/shard_map/jit(_take)/gather | solution.py:229
  3.9 0.3 multiply_bitcast_fusion
  4.1 0.6 %fusion.5 = f32[27,2,8,256]{3,0,2,1:T(8,128)S(1)} fusion(f32[27,27,1,1]{1,0,3,2:T(8,128)S(1)} %copy-done.7, f32[27,2,8,256]{3,1,0,2:T(2,128)S(1)} %multiply_bitcast_fusion), kind=kOutput, calls=%fused_computation.11 | convolution fusion | flops 35831808 | bytes 887652 | tf_op jit(solution)/shard_map/ij,jzpl->izpl/dot_general | solution.py:231
  4.7 0.2 fusion.22
  5.4 0.2 copy.45
  5.6 0.2 dot_general.23
  5.9 0.2 fusion.18
  6.0 0.3 convolution_bitcast_fusion
  6.4 1.2 %collective-permute-done = f32[3,2,32,16]{2,3,1,0:T(8,128)S(1)} collective-permute-done((f32[3,2,32,16]{2,3,1,0:T(8,128)S(1)}, f32[3,2,32,16]{2,3,1,0:T(8,128)S(1)}, u32[]{:S(2)}, u32[]{:S(2)}) %collective-permute-start) | collective-permute-done | bytes 12320 | tf_op jit(solution)/shard_map/ppermute | solution.py:23
  7.6 2.0 %collective-permute-start.1 = (f32[3,2,32,16]{2,3,1,0:T(8,128)S(1)}, f32[3,2,32,16]{2,3,1,0:T(8,128)S(1)}, u32[]{:S(2)}, u32[]{:S(2)}) collective-permute-start(f32[3,2,32,16]{2,3,1,0:T(8,128)S(1)} %add.82), channel_id=1, source_target_pairs={{0,2},{1,3},{2,0},{3,1},{4,6},{5,7},{6,4},{7,5},{8,10},{9,11},{10,... | collective-permute-start | bytes 36872 | tf_op jit(solution)/shard_map/ppermute | solution.py:23
  9.6 2.2 %collective-permute-done.1 = f32[3,2,32,16]{2,3,1,0:T(8,128)S(1)} collective-permute-done((f32[3,2,32,16]{2,3,1,0:T(8,128)S(1)}, f32[3,2,32,16]{2,3,1,0:T(8,128)S(1)}, u32[]{:S(2)}, u32[]{:S(2)}) %collective-permute-start.1) | collective-permute-done | bytes 12320 | tf_op jit(solution)/shard_map/ppermute | solution.py:23
  11.8 3.4 %collective-permute-start.2 = (f32[3,2,32,16]{2,3,1,0:T(8,128)S(1)}, f32[3,2,32,16]{2,3,1,0:T(8,128)S(1)}, u32[]{:S(2)}, u32[]{:S(2)}) collective-permute-start(f32[3,2,32,16]{2,3,1,0:T(8,128)S(1)} %add.83), channel_id=1, source_target_pairs={{0,4},{1,5},{2,6},{3,7},{4,0},{5,1},{6,2},{7,3},{8,12},{9,13},{10,... | collective-permute-start | bytes 36872 | tf_op jit(solution)/shard_map/ppermute | solution.py:23
  15.2 2.3 %collective-permute-done.2 = f32[3,2,32,16]{2,3,1,0:T(8,128)S(1)} collective-permute-done((f32[3,2,32,16]{2,3,1,0:T(8,128)S(1)}, f32[3,2,32,16]{2,3,1,0:T(8,128)S(1)}, u32[]{:S(2)}, u32[]{:S(2)}) %collective-permute-start.2) | collective-permute-done | bytes 12320 | tf_op jit(solution)/shard_map/ppermute | solution.py:23
  17.4 6.7 %collective-permute-start.3 = (f32[3,2,32,16]{2,3,1,0:T(8,128)S(1)}, f32[3,2,32,16]{2,3,1,0:T(8,128)S(1)}, u32[]{:S(2)}, u32[]{:S(2)}) collective-permute-start(f32[3,2,32,16]{2,3,1,0:T(8,128)S(1)} %add.84), channel_id=1, source_target_pairs={{0,8},{1,9},{2,10},{3,11},{4,12},{5,13},{6,14},{7,15},{8,0},{9,1},... | collective-permute-start | bytes 36872 | tf_op jit(solution)/shard_map/ppermute | solution.py:23
  24.2 2.1 %collective-permute-done.3 = f32[3,2,32,16]{2,3,1,0:T(8,128)S(1)} collective-permute-done((f32[3,2,32,16]{2,3,1,0:T(8,128)S(1)}, f32[3,2,32,16]{2,3,1,0:T(8,128)S(1)}, u32[]{:S(2)}, u32[]{:S(2)}) %collective-permute-start.3) | collective-permute-done | bytes 12320 | tf_op jit(solution)/shard_map/ppermute | solution.py:23
  26.5 1.0 %fusion = f32[3,2,2,4,16,16]{4,5,2,1,0,3:T(8,128)S(1)} fusion(f32[3,2,2,16,16,1]{4,3,2,1,0,5:T(8,128)S(1)} %bitcast.78, f32[4,16,8]{1,2,0:T(8,128)S(1)} %get-tuple-element.30, f32[4,16,8]{1,2,0:T(8,128)S(1)} %get-tuple-element.29), kind=kOutput, calls=%fused_computation.2 | convolution fusion | flops 2372608 | bytes 65536 | tf_op jit(solution)/shard_map/kzyrm,xqm->kzyxrq/dot_general | solution.py:243
  27.5 0.2 copy.48
  27.7 0.2 mul.155
  28.3 0.9 %fusion.3 = f32[2,8,256,27]{2,3,1,0:T(8,128)S(1)} fusion(f32[27,27,1,1]{1,0,3,2:T(8,128)S(1)} %copy-done.6, f32[27,2,8,256]{3,0,2,1:T(8,128)S(1)} %fusion.5, f32[27,2,8,256]{3,2,1,0:T(8,128)S(1)} %bitcast.77, f32[27]{0:T(128)S(1)} %copy-done.10), kind=kOutput, calls=%fused_computation.10 | convolution fusion | flops 36163584 | bytes 1330128 | tf_op jit(solution)/shard_map/ij,jzpl->izpl/dot_general | solution.py:80
  29.5 0.7 %copy.56 = f32[28,2,8,256]{0,3,2,1:T(8,128)S(1)} copy(f32[28,2,8,256]{3,0,2,1:T(8,128)S(1)} %pad_maximum_fusion) | data formatting | bytes 917504 | tf_op jit(solution)/shard_map/concatenate | solution.py:249
  30.3 1.1 %collective-permute-start.4 = (f32[224,16]{1,0:T(8,128)S(1)}, f32[224,16]{1,0:T(8,128)S(1)}, u32[]{:S(2)}, u32[]{:S(2)}) collective-permute-start(f32[224,16]{1,0:T(8,128)S(1)} %bitcast.84), channel_id=1, source_target_pairs={{0,16},{16,32},{32,48},{48,64},{64,80},{80,96},{96,112},{112,128},... | collective-permute-start | bytes 43016 | tf_op jit(solution)/shard_map/ppermute | solution.py:256
  31.5 1.1 %collective-permute-start.5 = (f32[224,16]{1,0:T(8,128)S(1)}, f32[224,16]{1,0:T(8,128)S(1)}, u32[]{:S(2)}, u32[]{:S(2)}) collective-permute-start(f32[224,16]{1,0:T(8,128)S(1)} %bitcast.85), channel_id=1, source_target_pairs={{16,0},{32,16},{48,32},{64,48},{80,64},{96,80},{112,96},{128,112},... | collective-permute-start | bytes 43016 | tf_op jit(solution)/shard_map/ppermute | solution.py:257
  32.6 2.6 %collective-permute-done.4.below_ref = f32[224,16]{1,0:T(8,128)S(1)} collective-permute-done((f32[224,16]{1,0:T(8,128)S(1)}, f32[224,16]{1,0:T(8,128)S(1)}, u32[]{:S(2)}, u32[]{:S(2)}) %collective-permute-start.4) | collective-permute-done | bytes 14368 | tf_op jit(solution)/shard_map/ppermute | solution.py:256
  35.4 4.3 %collective-permute-done.5.above_ref = f32[224,16]{1,0:T(8,128)S(1)} collective-permute-done((f32[224,16]{1,0:T(8,128)S(1)}, f32[224,16]{1,0:T(8,128)S(1)}, u32[]{:S(2)}, u32[]{:S(2)}) %collective-permute-start.5) | collective-permute-done | bytes 14368 | tf_op jit(solution)/shard_map/ppermute | solution.py:257
  40.4 0.5 collective-permute-start.6
  40.9 1.5 %collective-permute-done.7.right_ref = f32[224,16]{1,0:T(8,128)S(1)} collective-permute-done((f32[224,16]{1,0:T(8,128)S(1)}, f32[224,16]{1,0:T(8,128)S(1)}, u32[]{:S(2)}, u32[]{:S(2)}) %collective-permute-start.7) | collective-permute-done | bytes 14368 | tf_op jit(solution)/shard_map/ppermute | solution.py:281
  42.4 4.2 %collective-permute-done.6.left_ref = f32[224,16]{1,0:T(8,128)S(1)} collective-permute-done((f32[224,16]{1,0:T(8,128)S(1)}, f32[224,16]{1,0:T(8,128)S(1)}, u32[]{:S(2)}, u32[]{:S(2)}) %collective-permute-start.6) | collective-permute-done | bytes 14368 | tf_op jit(solution)/shard_map/ppermute | solution.py:280
  46.6 0.6 %copy-done.4 = f32[224,16]{1,0:T(8,128)} copy-done((f32[224,16]{1,0:T(8,128)}, f32[224,16]{1,0:T(8,128)S(1)}, u32[]{:S(2)}) %copy-start.4) | copy-done | bytes 14360
  47.3 3.2 %shard_map.73 = f32[648,128]{1,0:T(8,128)} custom-call(f32[8]{0:T(128)} %copy-done.8, s32[6]{0:T(128)} %bitcast.92, f32[2,8,27,256]{3,2,1,0:T(8,128)} %bitcast.75, f32[224,16]{1,0:T(8,128)} %copy-done.1, f32[224,16]{1,0:T(8,128)} %copy-done.2, f32[224,16]{1,0:T(8,128)} %copy-done.4, f32[224,16]{1,0:T(8,128)} %copy-done.3), custom_call_target="tpu_custom_call" | custom-call | tf_op jit(solution)/shard_map/pallas_call | solution.py:194
  (70 shorter events, 2.4 us)
Async XLA Ops:
  0.0 4.1 %copy-start.7 = (f32[27,27,1,1]{1,0,3,2:T(8,128)S(1)}, f32[27,27,1,1]{1,0,3,2:T(8,128)}, u32[]{:S(2)}) copy-start(f32[27,27,1,1]{1,0,3,2:T(8,128)} %constant.68) | copy-start | bytes 8752
  0.8 3.9 %copy-start.8 = (f32[8]{0:T(128)}, f32[8]{0:T(128)S(1)}, u32[]{:S(2)}) copy-start(f32[8]{0:T(128)S(1)} %get-tuple-element.32.fluid_ref) | copy-start | bytes 100
  4.1 1.7 %copy-start.9 = (s32[8]{0:T(128)S(1)}, s32[8]{0:T(128)}, u32[]{:S(2)}) copy-start(s32[8]{0:T(128)} %param.9) | copy-start | bytes 100
  4.7 21.6 %copy-start.5 = (f32[3,2,32,16]{2,3,1,0:T(8,128)S(1)}, f32[3,2,32,16]{2,3,1,0:T(8,128)}, u32[]{:S(2)}) copy-start(f32[3,2,32,16]{2,3,1,0:T(8,128)} %param.10) | copy-start | bytes 36868
  6.3 1.3 %collective-permute-start = (f32[3,2,32,16]{2,3,1,0:T(8,128)S(1)}, f32[3,2,32,16]{2,3,1,0:T(8,128)S(1)}, u32[]{:S(2)}, u32[]{:S(2)}) collective-permute-start(f32[3,2,32,16]{2,3,1,0:T(8,128)S(1)} %convolution_bitcast_fusion), channel_id=1, source_target_pairs={{0,1},{1,0},{2,3},{3,2},{4,5},{5,4},{6,7},{7,6},{8,9},{9,8},{10,11... | collective-permute-start | bytes 36872 | tf_op jit(solution)/shard_map/ppermute | solution.py:23
  7.6 4.2 %collective-permute-start.1 = (f32[3,2,32,16]{2,3,1,0:T(8,128)S(1)}, f32[3,2,32,16]{2,3,1,0:T(8,128)S(1)}, u32[]{:S(2)}, u32[]{:S(2)}) collective-permute-start(f32[3,2,32,16]{2,3,1,0:T(8,128)S(1)} %add.82), channel_id=1, source_target_pairs={{0,2},{1,3},{2,0},{3,1},{4,6},{5,7},{6,4},{7,5},{8,10},{9,11},{10,... | collective-permute-start | bytes 36872 | tf_op jit(solution)/shard_map/ppermute | solution.py:23
  11.8 5.6 %collective-permute-start.2 = (f32[3,2,32,16]{2,3,1,0:T(8,128)S(1)}, f32[3,2,32,16]{2,3,1,0:T(8,128)S(1)}, u32[]{:S(2)}, u32[]{:S(2)}) collective-permute-start(f32[3,2,32,16]{2,3,1,0:T(8,128)S(1)} %add.83), channel_id=1, source_target_pairs={{0,4},{1,5},{2,6},{3,7},{4,0},{5,1},{6,2},{7,3},{8,12},{9,13},{10,... | collective-permute-start | bytes 36872 | tf_op jit(solution)/shard_map/ppermute | solution.py:23
  17.4 8.9 %collective-permute-start.3 = (f32[3,2,32,16]{2,3,1,0:T(8,128)S(1)}, f32[3,2,32,16]{2,3,1,0:T(8,128)S(1)}, u32[]{:S(2)}, u32[]{:S(2)}) collective-permute-start(f32[3,2,32,16]{2,3,1,0:T(8,128)S(1)} %add.84), channel_id=1, source_target_pairs={{0,8},{1,9},{2,10},{3,11},{4,12},{5,13},{6,14},{7,15},{8,0},{9,1},... | collective-permute-start | bytes 36872 | tf_op jit(solution)/shard_map/ppermute | solution.py:23
  24.2 4.1 %copy-start.6 = (f32[27,27,1,1]{1,0,3,2:T(8,128)S(1)}, f32[27,27,1,1]{1,0,3,2:T(8,128)}, u32[]{:S(2)}) copy-start(f32[27,27,1,1]{1,0,3,2:T(8,128)} %constant.69) | copy-start | bytes 8752
  24.2 4.1 %copy-start.10 = (f32[27]{0:T(128)S(1)}, f32[27]{0:T(128)}, u32[]{:S(2)}) copy-start(f32[27]{0:T(128)} %param.11) | copy-start | bytes 328
  29.3 0.9 %copy-start = (f32[2,8,256,27]{2,3,1,0:T(8,128)}, f32[2,8,256,27]{2,3,1,0:T(8,128)S(1)}, u32[]{:S(2)}) copy-start(f32[2,8,256,27]{2,3,1,0:T(8,128)S(1)} %fusion.3) | copy-start | bytes 1327108
  30.3 4.9 %collective-permute-start.4 = (f32[224,16]{1,0:T(8,128)S(1)}, f32[224,16]{1,0:T(8,128)S(1)}, u32[]{:S(2)}, u32[]{:S(2)}) collective-permute-start(f32[224,16]{1,0:T(8,128)S(1)} %bitcast.84), channel_id=1, source_target_pairs={{0,16},{16,32},{32,48},{48,64},{64,80},{80,96},{96,112},{112,128},... | collective-permute-start | bytes 43016 | tf_op jit(solution)/shard_map/ppermute | solution.py:256
  31.5 8.2 %collective-permute-start.5 = (f32[224,16]{1,0:T(8,128)S(1)}, f32[224,16]{1,0:T(8,128)S(1)}, u32[]{:S(2)}, u32[]{:S(2)}) collective-permute-start(f32[224,16]{1,0:T(8,128)S(1)} %bitcast.85), channel_id=1, source_target_pairs={{16,0},{32,16},{48,32},{64,48},{80,64},{96,80},{112,96},{128,112},... | collective-permute-start | bytes 43016 | tf_op jit(solution)/shard_map/ppermute | solution.py:257
  35.1 11.5 %copy-start.1 = (f32[224,16]{1,0:T(8,128)}, f32[224,16]{1,0:T(8,128)S(1)}, u32[]{:S(2)}) copy-start(f32[224,16]{1,0:T(8,128)S(1)} %collective-permute-done.4.below_ref) | copy-start | bytes 43012
  39.7 6.9 %copy-start.2 = (f32[224,16]{1,0:T(8,128)}, f32[224,16]{1,0:T(8,128)S(1)}, u32[]{:S(2)}) copy-start(f32[224,16]{1,0:T(8,128)S(1)} %collective-permute-done.5.above_ref) | copy-start | bytes 43012
  40.1 2.4 %collective-permute-start.7 = (f32[224,16]{1,0:T(8,128)S(1)}, f32[224,16]{1,0:T(8,128)S(1)}, u32[]{:S(2)}, u32[]{:S(2)}) collective-permute-start(f32[224,16]{1,0:T(8,128)S(1)} %bitcast.83), channel_id=1, source_target_pairs={{1,0},{2,1},{3,2},{4,3},{5,4},{6,5},{7,6},{8,7},{9,8},{10,9},{11,1... | collective-permute-start | bytes 43016 | tf_op jit(solution)/shard_map/ppermute | solution.py:281
  40.4 6.2 %collective-permute-start.6 = (f32[224,16]{1,0:T(8,128)S(1)}, f32[224,16]{1,0:T(8,128)S(1)}, u32[]{:S(2)}, u32[]{:S(2)}) collective-permute-start(f32[224,16]{1,0:T(8,128)S(1)} %bitcast.86), channel_id=1, source_target_pairs={{0,1},{1,2},{2,3},{3,4},{4,5},{5,6},{6,7},{7,8},{8,9},{9,10},{10,1... | collective-permute-start | bytes 43016 | tf_op jit(solution)/shard_map/ppermute | solution.py:280
  42.4 4.2 %copy-start.3 = (f32[224,16]{1,0:T(8,128)}, f32[224,16]{1,0:T(8,128)S(1)}, u32[]{:S(2)}) copy-start(f32[224,16]{1,0:T(8,128)S(1)} %collective-permute-done.7.right_ref) | copy-start | bytes 43012
  46.6 0.7 %copy-start.4 = (f32[224,16]{1,0:T(8,128)}, f32[224,16]{1,0:T(8,128)S(1)}, u32[]{:S(2)}) copy-start(f32[224,16]{1,0:T(8,128)S(1)} %collective-permute-done.6.left_ref) | copy-start | bytes 43012

commit v11 on v10

--- a/solution.py
+++ b/solution.py
@@ -78,6 +78,41 @@
     equilibrium = equilibrium.reshape(moments.shape)
     relaxed = moments - relaxation_frequencies[:, None, None, None] * (moments - equilibrium)
     return jnp.einsum("ij,jzpl->izpl", backward, relaxed, precision=HIGHEST)
+
+
+def moments_kernel(slot_ref, fluid_ref, forward_ref, state_ref, out_ref, scratch_ref):
+    levels, blocks, channels, cells = out_ref.shape
+    seats = scratch_ref.shape[0]
+    chunks = levels * cells // 128
+    forward = forward_ref[...]
+    for seat_number in range(seats):
+        pieces = [
+            state_ref[pl.ds(seat_number * channels * chunks + chunk, channels, stride=chunks), :]
+            for chunk in range(chunks)
+        ]
+        scratch_ref[seat_number] = jnp.dot(
+            forward, jnp.concatenate(pieces, axis=1), precision=HIGHEST,
+            preferred_element_type=jnp.float32,
+        )
+    for block in range(blocks):
+        slot = slot_ref[block]
+        keep = fluid_ref[block]
+        for level in range(levels):
+            out_ref[level, block] = scratch_ref[slot, :, level * cells:(level + 1) * cells] * keep
+
+
+def cell_moments(slot_of, fluid, forward, rows, seats, levels):
+    channels = forward.shape[0]
+    cells = rows.size // (seats * channels * levels)
+    vmem = pl.BlockSpec(memory_space=pltpu.VMEM)
+    smem = pl.BlockSpec(memory_space=pltpu.SMEM)
+    return pl.pallas_call(
+        moments_kernel,
+        out_shape=jax.ShapeDtypeStruct((levels, TX * TY, channels, cells), jnp.float32),
+        in_specs=[smem, smem, vmem, vmem],
+        out_specs=vmem,
+        scratch_shapes=[pltpu.VMEM((seats, channels, levels * cells), jnp.float32)],
+    )(slot_of, fluid, forward, rows)
 
 
 def stream_kernel(
@@ -226,9 +261,8 @@
     present = code > 0
     slot_of = jnp.maximum(code - 1, 0)
     fluid = present.astype(jnp.float32)
-    picked = jnp.take(slot_state.reshape(seats, channels, levels, cells), slot_of, axis=0)
-    pops = picked.transpose(1, 2, 0, 3) * fluid[None, None, :, None]
-    moments = jnp.einsum("ij,jzpl->izpl", forward, pops, precision=HIGHEST)
+    rows = slot_state.reshape(-1, 128)
+    moments = cell_moments(slot_of, fluid, forward, rows, seats, levels).transpose(2, 0, 1, 3)
     safe_density = jnp.where(present[None, :, None], moments[0], 1.0)
     wind = jnp.stack([moments[9], moments[3], moments[1]], axis=0) / safe_density[None]
     line_length = lax.axis_size("line") * cols_tile

time: 50.8 us -> 51.4 us (1.012)
  Pallas kernels: 3.18 us -> 5.46 us
  local copies, waits for them, and re-layouts: 5.03 us -> 3.79 us
  matrix products: 2.79 us -> 2.23 us
    pallas_call x0 -> x1, Pallas kernels: none -> 2.29 us  [cell_moments(): pl.pallas_call(moments_kernel, out_shape=jax.ShapeDtypeStruct((levels, TX...]
    unnamed x1 -> x0, other arithmetic: 1.77 us -> none
    select_n x1, other arithmetic: 0.2 us -> 1.4 us  [on_device(): safe_density = jnp.where(present[None, :, None], moments[0], 1.0)]
    gather x1 -> x0, local copies, waits for them, and re-layouts: 1.02 us -> none  [on_device(): jnp.take(slot_state.reshape(seats, channels, levels, cells), slot_of, axi...]
    dot_general x1 -> x0, matrix products: 0.56 us -> none  [on_device(): moments = jnp.einsum('ij,jzpl->izpl', forward, pops, precision=HIGHEST)]
    gt x1, other arithmetic: 0.01 us -> 0.54 us  [on_device(): present = code > 0]
    unnamed x27 -> x25, local copies, waits for them, and re-layouts: 1.07 us -> 1.06 us
where the time goes in v11:
time: 51.4 us; the launch traced here: 51.1 us
  waiting for transfers between devices  20.4 us (40%)
  starting transfers between devices  14.9 us (29%)
  Pallas kernels  5.46 us (11%)
  other arithmetic  4 us (8%)
  local copies, waits for them, and re-layouts  3.79 us (7%)
  matrix products  2.23 us (4%)
    ppermute x4, starting transfers between devices, butterfly_sum(): lax.ppermute(value, axis, [(i, i ^ stride) for i in range(count)])  12.2 us
    ppermute x4, waiting for transfers between devices, butterfly_sum(): lax.ppermute(value, axis, [(i, i ^ stride) for i in range(count)])  7.78 us
    ppermute x1, waiting for transfers between devices, on_device(): above_flat = lax.ppermute(flat(bottom_row), 'curve', behind)  4.31 us
    ppermute x1, waiting for transfers between devices, on_device(): from_left = lax.ppermute(flat(to_right), 'line', ahead)  4.18 us
    pallas_call x1, Pallas kernels, stream(): pl.pallas_call(stream_kernel, out_shape=jax.ShapeDtypeStruct((seats * cha...  3.17 us
    ppermute x1, waiting for transfers between devices, on_device(): below_flat = lax.ppermute(flat(top_row), 'curve', ahead)  2.55 us
    pallas_call x1, Pallas kernels, cell_moments(): pl.pallas_call(moments_kernel, out_shape=jax.ShapeDtypeStruct((levels, TX...  2.29 us
    ppermute x1, waiting for transfers between devices, on_device(): from_right = lax.ppermute(flat(to_left), 'line', behind)  1.52 us
  transfers between devices with their start and end apart: 8, of which 8 were waited for; matrix products, arithmetic and copies ran while one was open for 1% of the time, Pallas kernels for 0%

profile of v11, /device:TPU:30, one launch (start us, length us, event | category | flops | bytes accessed | tf_op | source)
XLA Modules:
  0.0 51.1 jit_solution(10145866840712471030)
XLA Ops:
  0.0 0.8 %select_reduce_fusion = s32[8]{0:T(128)S(1)} fusion(s32[6]{0:T(128)S(1)} %iota_add_fusion, s32[6]{0:T(128)} %bitcast.93), kind=kLoop, calls=%fused_computation.51 | loop fusion | flops 136 | bytes 80 | tf_op jit(solution)/shard_map/reduce_max | solution.py:260
  0.8 0.5 %broadcast_compare_fusion = (pred[8]{0:T(512)(128)(4,1)S(1)}, f32[8]{0:T(128)}) fusion(s32[8]{0:T(128)S(1)} %select_reduce_fusion), kind=kLoop, calls=%fused_computation.57 | loop fusion | flops 16 | bytes 72 | tf_op jit(solution)/shard_map/gt | solution.py:261
  1.3 0.5 %add_maximum_fusion.slot_ref = s32[8]{0:T(128)} fusion(s32[8]{0:T(128)S(1)} %select_reduce_fusion), kind=kLoop, calls=%fused_computation.54 | loop fusion | flops 16 | bytes 64 | tf_op jit(solution)/shard_map/max | solution.py:262
  1.8 2.3 %shard_map.73 = f32[2,8,27,256]{3,2,1,0:T(8,128)} custom-call(s32[8]{0:T(128)} %add_maximum_fusion.slot_ref, f32[8]{0:T(128)} %get-tuple-element.32.fluid_ref, f32[27,27]{1,0:T(8,128)} %constant.48.clone.forward_ref, f32[648,128]{1,0:T(8,128)} %bitcast.80), custom_call_target="tpu_custom_call" | custom-call | tf_op jit(solution)/shard_map/pallas_call | solution.py:109
  4.1 1.4 %fusion.21 = (f32[2,8,256]{2,1,0:T(8,128)S(1)}, f32[1,2,8,256]{3,0,2,1:T(1,128)S(1)}, f32[1,2,8,256]{3,0,2,1:T(1,128)S(1)}, f32[1,1,2,8,256]{4,0,3,2,1:T(1,128)S...) fusion(f32[27,2,8,256]{3,0,2,1:T(8,128)} %bitcast.76, ...), kind=kLoop, calls=%fused_computation.62 | loop fusion | flops 4096 | bytes 213000 | tf_op jit(solution)/shard_map/jit(_where)/select_n | solution.py:266
  6.0 0.2 copy.43
  6.2 0.2 dot_general.16
  6.5 0.2 fusion.16
  6.6 0.3 convolution_bitcast_fusion
  7.0 1.2 %collective-permute-done = f32[3,2,32,16]{2,3,1,0:T(8,128)S(1)} collective-permute-done((f32[3,2,32,16]{2,3,1,0:T(8,128)S(1)}, f32[3,2,32,16]{2,3,1,0:T(8,128)S(1)}, u32[]{:S(2)}, u32[]{:S(2)}) %collective-permute-start) | collective-permute-done | bytes 12320 | tf_op jit(solution)/shard_map/ppermute | solution.py:23
  8.2 2.0 %collective-permute-start.1 = (f32[3,2,32,16]{2,3,1,0:T(8,128)S(1)}, f32[3,2,32,16]{2,3,1,0:T(8,128)S(1)}, u32[]{:S(2)}, u32[]{:S(2)}) collective-permute-start(f32[3,2,32,16]{2,3,1,0:T(8,128)S(1)} %add.70), channel_id=1, source_target_pairs={{0,2},{1,3},{2,0},{3,1},{4,6},{5,7},{6,4},{7,5},{8,10},{9,11},{10,... | collective-permute-start | bytes 36872 | tf_op jit(solution)/shard_map/ppermute | solution.py:23
  10.2 2.2 %collective-permute-done.1 = f32[3,2,32,16]{2,3,1,0:T(8,128)S(1)} collective-permute-done((f32[3,2,32,16]{2,3,1,0:T(8,128)S(1)}, f32[3,2,32,16]{2,3,1,0:T(8,128)S(1)}, u32[]{:S(2)}, u32[]{:S(2)}) %collective-permute-start.1) | collective-permute-done | bytes 12320 | tf_op jit(solution)/shard_map/ppermute | solution.py:23
  12.4 3.4 %collective-permute-start.2 = (f32[3,2,32,16]{2,3,1,0:T(8,128)S(1)}, f32[3,2,32,16]{2,3,1,0:T(8,128)S(1)}, u32[]{:S(2)}, u32[]{:S(2)}) collective-permute-start(f32[3,2,32,16]{2,3,1,0:T(8,128)S(1)} %add.71), channel_id=1, source_target_pairs={{0,4},{1,5},{2,6},{3,7},{4,0},{5,1},{6,2},{7,3},{8,12},{9,13},{10,... | collective-permute-start | bytes 36872 | tf_op jit(solution)/shard_map/ppermute | solution.py:23
  15.8 2.3 %collective-permute-done.2 = f32[3,2,32,16]{2,3,1,0:T(8,128)S(1)} collective-permute-done((f32[3,2,32,16]{2,3,1,0:T(8,128)S(1)}, f32[3,2,32,16]{2,3,1,0:T(8,128)S(1)}, u32[]{:S(2)}, u32[]{:S(2)}) %collective-permute-start.2) | collective-permute-done | bytes 12320 | tf_op jit(solution)/shard_map/ppermute | solution.py:23
  18.0 6.7 %collective-permute-start.3 = (f32[3,2,32,16]{2,3,1,0:T(8,128)S(1)}, f32[3,2,32,16]{2,3,1,0:T(8,128)S(1)}, u32[]{:S(2)}, u32[]{:S(2)}) collective-permute-start(f32[3,2,32,16]{2,3,1,0:T(8,128)S(1)} %add.72), channel_id=1, source_target_pairs={{0,8},{1,9},{2,10},{3,11},{4,12},{5,13},{6,14},{7,15},{8,0},{9,1},... | collective-permute-start | bytes 36872 | tf_op jit(solution)/shard_map/ppermute | solution.py:23
  24.8 2.1 %collective-permute-done.3 = f32[3,2,32,16]{2,3,1,0:T(8,128)S(1)} collective-permute-done((f32[3,2,32,16]{2,3,1,0:T(8,128)S(1)}, f32[3,2,32,16]{2,3,1,0:T(8,128)S(1)}, u32[]{:S(2)}, u32[]{:S(2)}) %collective-permute-start.3) | collective-permute-done | bytes 12320 | tf_op jit(solution)/shard_map/ppermute | solution.py:23
  27.1 1.0 %fusion = f32[3,2,2,4,16,16]{4,5,2,1,0,3:T(8,128)S(1)} fusion(f32[3,2,2,16,16,1]{4,3,2,1,0,5:T(8,128)S(1)} %bitcast.79, f32[4,16,8]{1,2,0:T(8,128)S(1)} %get-tuple-element.30, f32[4,16,8]{1,2,0:T(8,128)S(1)} %get-tuple-element.29), kind=kOutput, calls=%fused_computation.1 | convolution fusion | flops 2372608 | bytes 65536 | tf_op jit(solution)/shard_map/kzyrm,xqm->kzyxrq/dot_general | solution.py:277
  28.1 0.2 copy.46
  28.3 0.2 mul.141
  28.6 0.1 pad_maximum_fusion.1
  28.9 0.9 %fusion.3 = f32[2,8,256,27]{2,3,1,0:T(8,128)S(1)} fusion(f32[27,27,1,1]{1,0,3,2:T(8,128)S(1)} %copy-done.7, f32[27,2,8,256]{3,2,1,0:T(8,128)S(1)} %bitcast.78, f32[27]{0:T(128)S(1)} %copy-done.9, f32[2,8,27,256]{3,2,1,0:T(8,128)S(1)} %copy-done.1), kind=kOutput, calls=%fused_computation.9 | convolution fusion | flops 36163584 | bytes 1330128 | tf_op jit(solution)/shard_map/ij,jzpl->izpl/dot_general | solution.py:80
  30.1 0.7 %copy.54 = f32[28,2,8,256]{0,3,2,1:T(8,128)S(1)} copy(f32[28,2,8,256]{3,0,2,1:T(8,128)S(1)} %pad_maximum_fusion) | data formatting | bytes 917504 | tf_op jit(solution)/shard_map/concatenate | solution.py:283
  30.9 1.1 %collective-permute-start.4 = (f32[224,16]{1,0:T(8,128)S(1)}, f32[224,16]{1,0:T(8,128)S(1)}, u32[]{:S(2)}, u32[]{:S(2)}) collective-permute-start(f32[224,16]{1,0:T(8,128)S(1)} %bitcast.86), channel_id=1, source_target_pairs={{0,16},{16,32},{32,48},{48,64},{64,80},{80,96},{96,112},{112,128},... | collective-permute-start | bytes 43016 | tf_op jit(solution)/shard_map/ppermute | solution.py:290
  32.1 1.1 %collective-permute-start.5 = (f32[224,16]{1,0:T(8,128)S(1)}, f32[224,16]{1,0:T(8,128)S(1)}, u32[]{:S(2)}, u32[]{:S(2)}) collective-permute-start(f32[224,16]{1,0:T(8,128)S(1)} %bitcast.87), channel_id=1, source_target_pairs={{16,0},{32,16},{48,32},{64,48},{80,64},{96,80},{112,96},{128,112},... | collective-permute-start | bytes 43016 | tf_op jit(solution)/shard_map/ppermute | solution.py:291
  33.2 2.6 %collective-permute-done.4.below_ref = f32[224,16]{1,0:T(8,128)S(1)} collective-permute-done((f32[224,16]{1,0:T(8,128)S(1)}, f32[224,16]{1,0:T(8,128)S(1)}, u32[]{:S(2)}, u32[]{:S(2)}) %collective-permute-start.4) | collective-permute-done | bytes 14368 | tf_op jit(solution)/shard_map/ppermute | solution.py:290
  36.0 4.3 %collective-permute-done.5.above_ref = f32[224,16]{1,0:T(8,128)S(1)} collective-permute-done((f32[224,16]{1,0:T(8,128)S(1)}, f32[224,16]{1,0:T(8,128)S(1)}, u32[]{:S(2)}, u32[]{:S(2)}) %collective-permute-start.5) | collective-permute-done | bytes 14368 | tf_op jit(solution)/shard_map/ppermute | solution.py:291
  40.5 0.1 copy.59
  41.0 0.5 collective-permute-start.6
  41.5 1.5 %collective-permute-done.7.right_ref = f32[224,16]{1,0:T(8,128)S(1)} collective-permute-done((f32[224,16]{1,0:T(8,128)S(1)}, f32[224,16]{1,0:T(8,128)S(1)}, u32[]{:S(2)}, u32[]{:S(2)}) %collective-permute-start.7) | collective-permute-done | bytes 14368 | tf_op jit(solution)/shard_map/ppermute | solution.py:315
  43.0 4.2 %collective-permute-done.6.left_ref = f32[224,16]{1,0:T(8,128)S(1)} collective-permute-done((f32[224,16]{1,0:T(8,128)S(1)}, f32[224,16]{1,0:T(8,128)S(1)}, u32[]{:S(2)}, u32[]{:S(2)}) %collective-permute-start.6) | collective-permute-done | bytes 14368 | tf_op jit(solution)/shard_map/ppermute | solution.py:314
  47.2 0.6 %copy-done.5 = f32[224,16]{1,0:T(8,128)} copy-done((f32[224,16]{1,0:T(8,128)}, f32[224,16]{1,0:T(8,128)S(1)}, u32[]{:S(2)}) %copy-start.5) | copy-done | bytes 14360
  47.9 3.2 %shard_map.74 = f32[648,128]{1,0:T(8,128)} custom-call(f32[8]{0:T(128)} %get-tuple-element.32.fluid_ref, s32[6]{0:T(128)} %bitcast.94, f32[2,8,27,256]{3,2,1,0:T(8,128)} %bitcast.75, f32[224,16]{1,0:T(8,128)} %copy-done.2, f32[224,16]{1,0:T(8,128)} %copy-done.3, f32[224,16]{1,0:T(8,128)} %copy-done.5, f32[224,16]{1,0:T(8,128)} %copy-done.4), custom_call_target="tpu_custom_call" | custom-call | tf_op jit(solution)/shard_map/pallas_call | solution.py:229
  (63 shorter events, 2.1 us)
Async XLA Ops:
  0.0 6.5 %copy-start.8 = (s32[8]{0:T(128)S(1)}, s32[8]{0:T(128)}, u32[]{:S(2)}) copy-start(s32[8]{0:T(128)} %param.9) | copy-start | bytes 100
  4.1 22.8 %copy-start.6 = (f32[3,2,32,16]{2,3,1,0:T(8,128)S(1)}, f32[3,2,32,16]{2,3,1,0:T(8,128)}, u32[]{:S(2)}) copy-start(f32[3,2,32,16]{2,3,1,0:T(8,128)} %param.10) | copy-start | bytes 36868
  6.9 1.3 %collective-permute-start = (f32[3,2,32,16]{2,3,1,0:T(8,128)S(1)}, f32[3,2,32,16]{2,3,1,0:T(8,128)S(1)}, u32[]{:S(2)}, u32[]{:S(2)}) collective-permute-start(f32[3,2,32,16]{2,3,1,0:T(8,128)S(1)} %convolution_bitcast_fusion), channel_id=1, source_target_pairs={{0,1},{1,0},{2,3},{3,2},{4,5},{5,4},{6,7},{7,6},{8,9},{9,8},{10,11... | collective-permute-start | bytes 36872 | tf_op jit(solution)/shard_map/ppermute | solution.py:23
  8.2 4.2 %collective-permute-start.1 = (f32[3,2,32,16]{2,3,1,0:T(8,128)S(1)}, f32[3,2,32,16]{2,3,1,0:T(8,128)S(1)}, u32[]{:S(2)}, u32[]{:S(2)}) collective-permute-start(f32[3,2,32,16]{2,3,1,0:T(8,128)S(1)} %add.70), channel_id=1, source_target_pairs={{0,2},{1,3},{2,0},{3,1},{4,6},{5,7},{6,4},{7,5},{8,10},{9,11},{10,... | collective-permute-start | bytes 36872 | tf_op jit(solution)/shard_map/ppermute | solution.py:23
  12.4 5.6 %collective-permute-start.2 = (f32[3,2,32,16]{2,3,1,0:T(8,128)S(1)}, f32[3,2,32,16]{2,3,1,0:T(8,128)S(1)}, u32[]{:S(2)}, u32[]{:S(2)}) collective-permute-start(f32[3,2,32,16]{2,3,1,0:T(8,128)S(1)} %add.71), channel_id=1, source_target_pairs={{0,4},{1,5},{2,6},{3,7},{4,0},{5,1},{6,2},{7,3},{8,12},{9,13},{10,... | collective-permute-start | bytes 36872 | tf_op jit(solution)/shard_map/ppermute | solution.py:23
  18.0 8.9 %collective-permute-start.3 = (f32[3,2,32,16]{2,3,1,0:T(8,128)S(1)}, f32[3,2,32,16]{2,3,1,0:T(8,128)S(1)}, u32[]{:S(2)}, u32[]{:S(2)}) collective-permute-start(f32[3,2,32,16]{2,3,1,0:T(8,128)S(1)} %add.72), channel_id=1, source_target_pairs={{0,8},{1,9},{2,10},{3,11},{4,12},{5,13},{6,14},{7,15},{8,0},{9,1},... | collective-permute-start | bytes 36872 | tf_op jit(solution)/shard_map/ppermute | solution.py:23
  24.8 4.1 %copy-start.1 = (f32[2,8,27,256]{3,2,1,0:T(8,128)S(1)}, f32[2,8,27,256]{3,2,1,0:T(8,128)}, u32[]{:S(2)}) copy-start(f32[2,8,27,256]{3,2,1,0:T(8,128)} %shard_map.73) | copy-start | bytes 1327108
  24.8 4.1 %copy-start.7 = (f32[27,27,1,1]{1,0,3,2:T(8,128)S(1)}, f32[27,27,1,1]{1,0,3,2:T(8,128)}, u32[]{:S(2)}) copy-start(f32[27,27,1,1]{1,0,3,2:T(8,128)} %constant.52) | copy-start | bytes 8752
  24.8 4.1 %copy-start.9 = (f32[27]{0:T(128)S(1)}, f32[27]{0:T(128)}, u32[]{:S(2)}) copy-start(f32[27]{0:T(128)} %param.11) | copy-start | bytes 328
  29.9 0.9 %copy-start = (f32[2,8,256,27]{2,3,1,0:T(8,128)}, f32[2,8,256,27]{2,3,1,0:T(8,128)S(1)}, u32[]{:S(2)}) copy-start(f32[2,8,256,27]{2,3,1,0:T(8,128)S(1)} %fusion.3) | copy-start | bytes 1327108
  30.9 4.9 %collective-permute-start.4 = (f32[224,16]{1,0:T(8,128)S(1)}, f32[224,16]{1,0:T(8,128)S(1)}, u32[]{:S(2)}, u32[]{:S(2)}) collective-permute-start(f32[224,16]{1,0:T(8,128)S(1)} %bitcast.86), channel_id=1, source_target_pairs={{0,16},{16,32},{32,48},{48,64},{64,80},{80,96},{96,112},{112,128},... | collective-permute-start | bytes 43016 | tf_op jit(solution)/shard_map/ppermute | solution.py:290
  32.1 8.2 %collective-permute-start.5 = (f32[224,16]{1,0:T(8,128)S(1)}, f32[224,16]{1,0:T(8,128)S(1)}, u32[]{:S(2)}, u32[]{:S(2)}) collective-permute-start(f32[224,16]{1,0:T(8,128)S(1)} %bitcast.87), channel_id=1, source_target_pairs={{16,0},{32,16},{48,32},{64,48},{80,64},{96,80},{112,96},{128,112},... | collective-permute-start | bytes 43016 | tf_op jit(solution)/shard_map/ppermute | solution.py:291
  35.8 11.5 %copy-start.2 = (f32[224,16]{1,0:T(8,128)}, f32[224,16]{1,0:T(8,128)S(1)}, u32[]{:S(2)}) copy-start(f32[224,16]{1,0:T(8,128)S(1)} %collective-permute-done.4.below_ref) | copy-start | bytes 43012
  40.3 6.9 %copy-start.3 = (f32[224,16]{1,0:T(8,128)}, f32[224,16]{1,0:T(8,128)S(1)}, u32[]{:S(2)}) copy-start(f32[224,16]{1,0:T(8,128)S(1)} %collective-permute-done.5.above_ref) | copy-start | bytes 43012
  40.7 2.4 %collective-permute-start.7 = (f32[224,16]{1,0:T(8,128)S(1)}, f32[224,16]{1,0:T(8,128)S(1)}, u32[]{:S(2)}, u32[]{:S(2)}) collective-permute-start(f32[224,16]{1,0:T(8,128)S(1)} %bitcast.85), channel_id=1, source_target_pairs={{1,0},{2,1},{3,2},{4,3},{5,4},{6,5},{7,6},{8,7},{9,8},{10,9},{11,1... | collective-permute-start | bytes 43016 | tf_op jit(solution)/shard_map/ppermute | solution.py:315
  41.0 6.2 %collective-permute-start.6 = (f32[224,16]{1,0:T(8,128)S(1)}, f32[224,16]{1,0:T(8,128)S(1)}, u32[]{:S(2)}, u32[]{:S(2)}) collective-permute-start(f32[224,16]{1,0:T(8,128)S(1)} %bitcast.88), channel_id=1, source_target_pairs={{0,1},{1,2},{2,3},{3,4},{4,5},{5,6},{6,7},{7,8},{8,9},{9,10},{10,1... | collective-permute-start | bytes 43016 | tf_op jit(solution)/shard_map/ppermute | solution.py:314
  43.0 4.2 %copy-start.4 = (f32[224,16]{1,0:T(8,128)}, f32[224,16]{1,0:T(8,128)S(1)}, u32[]{:S(2)}) copy-start(f32[224,16]{1,0:T(8,128)S(1)} %collective-permute-done.7.right_ref) | copy-start | bytes 43012
  47.2 0.7 %copy-start.5 = (f32[224,16]{1,0:T(8,128)}, f32[224,16]{1,0:T(8,128)S(1)}, u32[]{:S(2)}) copy-start(f32[224,16]{1,0:T(8,128)S(1)} %collective-permute-done.6.left_ref) | copy-start | bytes 43012

commit v12 on v11

--- a/solution.py
+++ b/solution.py
@@ -80,7 +80,7 @@
     return jnp.einsum("ij,jzpl->izpl", backward, relaxed, precision=HIGHEST)
 
 
-def moments_kernel(slot_ref, fluid_ref, forward_ref, state_ref, out_ref, scratch_ref):
+def moments_kernel(keys_ref, forward_ref, state_ref, out_ref, wind_ref, solid_ref, scratch_ref):
     levels, blocks, channels, cells = out_ref.shape
     seats = scratch_ref.shape[0]
     chunks = levels * cells // 128
@@ -95,28 +95,43 @@
             preferred_element_type=jnp.float32,
         )
     for block in range(blocks):
-        slot = slot_ref[block]
-        keep = fluid_ref[block]
+        slot = 0
+        found = False
+        for seat_number in range(seats):
+            hit = keys_ref[seat_number] == block
+            slot = jnp.where(hit, seat_number, slot)
+            found = jnp.logical_or(found, hit)
+        keep = jnp.where(found, 1.0, 0.0)
         for level in range(levels):
-            out_ref[level, block] = scratch_ref[slot, :, level * cells:(level + 1) * cells] * keep
-
-
-def cell_moments(slot_of, fluid, forward, rows, seats, levels):
+            values = scratch_ref[slot, :, level * cells:(level + 1) * cells] * keep
+            out_ref[level, block] = values
+            density = jnp.where(found, values[0:1], 1.0)
+            for component, row in enumerate((9, 3, 1)):
+                wind_ref[component, level, block:block + 1, :] = values[row:row + 1] / density
+            solid_ref[level, block:block + 1, :] = jnp.broadcast_to(1.0 - keep, (1, cells))
+
+
+def cell_moments(keys, forward, rows, seats, levels):
     channels = forward.shape[0]
+    blocks = TX * TY
     cells = rows.size // (seats * channels * levels)
     vmem = pl.BlockSpec(memory_space=pltpu.VMEM)
     smem = pl.BlockSpec(memory_space=pltpu.SMEM)
     return pl.pallas_call(
         moments_kernel,
-        out_shape=jax.ShapeDtypeStruct((levels, TX * TY, channels, cells), jnp.float32),
-        in_specs=[smem, smem, vmem, vmem],
-        out_specs=vmem,
+        out_shape=(
+            jax.ShapeDtypeStruct((levels, blocks, channels, cells), jnp.float32),
+            jax.ShapeDtypeStruct((3, levels, blocks, cells), jnp.float32),
+            jax.ShapeDtypeStruct((levels, blocks, cells), jnp.float32),
+        ),
+        in_specs=[smem, vmem, vmem],
+        out_specs=(vmem, vmem, vmem),
         scratch_shapes=[pltpu.VMEM((seats, channels, levels * cells), jnp.float32)],
-    )(slot_of, fluid, forward, rows)
+    )(keys, forward, rows)
 
 
 def stream_kernel(
-    fluid_ref, keys_ref, post_ref, below_ref, above_ref, left_ref, right_ref, out_ref, spread_ref, result_ref
+    keys_ref, solid_ref, post_ref, below_ref, above_ref, left_ref, right_ref, out_ref, spread_ref, result_ref
 ):
     levels, blocks, channels, cells = post_ref.shape
     _, _, speeds = lattice_tables()
@@ -138,9 +153,7 @@
     r = lane // BE
     py = seat // TX
 
-    solid_plane = jnp.zeros((blocks, cells), jnp.float32)
-    for block in range(blocks):
-        solid_plane = jnp.where(seat == block, 1.0 - fluid_ref[block], solid_plane)
+    solid_plane = solid_ref[...]
 
     def own(channel, level):
         if channel == channels:
@@ -220,7 +233,7 @@
             out_ref[rows, :] = jnp.where(key >= 0, picked, 0.0)
 
 
-def stream(fluid, keys, post, below, above, from_left, from_right):
+def stream(keys, solid_plane, post, below, above, from_left, from_right):
     channels, levels, blocks, cells = post.shape
     seats = keys.shape[0]
     halo_rows = below.shape[0]
@@ -229,13 +242,13 @@
     return pl.pallas_call(
         stream_kernel,
         out_shape=jax.ShapeDtypeStruct((seats * channels * levels * cells // 128, 128), jnp.float32),
-        in_specs=[smem, smem] + [vmem] * 5,
+        in_specs=[smem] + [vmem] * 6,
         out_specs=vmem,
         scratch_shapes=[
             pltpu.VMEM((4, halo_rows + 16, cells), jnp.float32),
             pltpu.VMEM((blocks, channels, levels * cells), jnp.float32),
         ],
-    )(fluid, keys, post.transpose(1, 2, 0, 3), below, above, from_left, from_right)
+    )(keys, solid_plane, post.transpose(1, 2, 0, 3), below, above, from_left, from_right)
 
 
 def on_device(
@@ -255,16 +268,9 @@
     blocks = TX * TY
     rows_tile = TY * BE
     cols_tile = TX * BE
-    positions = jnp.arange(blocks, dtype=jnp.int32)
-    matches = living_brick_keys[None, :] == positions[:, None]
-    code = jnp.max(jnp.where(matches, jnp.arange(1, seats + 1, dtype=jnp.int32)[None, :], 0), axis=1)
-    present = code > 0
-    slot_of = jnp.maximum(code - 1, 0)
-    fluid = present.astype(jnp.float32)
     rows = slot_state.reshape(-1, 128)
-    moments = cell_moments(slot_of, fluid, forward, rows, seats, levels).transpose(2, 0, 1, 3)
-    safe_density = jnp.where(present[None, :, None], moments[0], 1.0)
-    wind = jnp.stack([moments[9], moments[3], moments[1]], axis=0) / safe_density[None]
+    moments, wind, solid_plane = cell_moments(living_brick_keys, forward, rows, seats, levels)
+    moments = moments.transpose(2, 0, 1, 3)
     line_length = lax.axis_size("line") * cols_tile
     own_columns = lax.axis_index("line") * cols_tile + jnp.arange(cols_tile, dtype=jnp.int32)
     mode_basis = mode_basis_at(retained_wavenumbers, own_columns, line_length).reshape(TX, BE, -1)
@@ -279,7 +285,7 @@
         precision=HIGHEST,
     ).reshape(3, levels, blocks, cells)
     post = collide_blocks(moments, wind, nudge, backward, relaxation_frequencies)
-    solid = jnp.broadcast_to((1.0 - fluid)[None, None, :, None], (1, levels, blocks, cells))
+    solid = solid_plane[None]
     extended = jnp.concatenate([post, solid], axis=0)
     width = channels + 1
     ahead, behind = ring_pairs("curve")
@@ -313,7 +319,7 @@
     )
     from_left = lax.ppermute(flat(to_right), "line", ahead)
     from_right = lax.ppermute(flat(to_left), "line", behind)
-    new_state = stream(fluid, living_brick_keys, post, below_flat, above_flat, from_left, from_right)
+    new_state = stream(living_brick_keys, solid_plane[0], post, below_flat, above_flat, from_left, from_right)
     return new_state.reshape((1, 1, seats, channels, levels * cells))
 
 

time: 51.4 us -> 55.3 us (1.076)
  local copies, waits for them, and re-layouts: 3.79 us -> 13.9 us
  waiting for transfers between devices: 20.4 us -> 16 us
  other arithmetic: 4 us -> 1.94 us
    concatenate x1 -> x3, local copies, waits for them, and re-layouts: 0.65 us -> 3.53 us  [on_device(): extended = jnp.concatenate([post, solid], axis=0)]
    ppermute x4, waiting for transfers between devices: 7.78 us -> 5.65 us  [butterfly_sum(): lax.ppermute(value, axis, [(i, i ^ stride) for i in range(count)])]
    unnamed x25 -> x30, local copies, waits for them, and re-layouts: 1.06 us -> 2.88 us
    ppermute x1, waiting for transfers between devices: 2.55 us -> 0.91 us  [on_device(): below_flat = lax.ppermute(flat(top_row), 'curve', ahead)]
    slice x0 -> x2, local copies, waits for them, and re-layouts: none -> 1.58 us  [the longest x1 0.91 us: collide_blocks(): density = moments[0]]
    select_n x1 -> x0, other arithmetic: 1.4 us -> none  [on_device(): safe_density = jnp.where(present[None, :, None], moments[0], 1.0)]
    dot_general x0 -> x1, local copies, waits for them, and re-layouts: none -> 1.03 us  [collide_blocks(): return jnp.einsum('ij,jzpl->izpl', backward, relaxed, precision=HIGHEST)]
    reshape x0 -> x1, local copies, waits for them, and re-layouts: none -> 1.02 us  [on_device(): wind.reshape(3, levels, TY, TX, BE, BE)]
  transfers between devices with their start and end apart: 8 -> 8, of which waited for: 8 -> 7; matrix products, arithmetic and copies ran while one was open for 1% -> 11% of each run, Pallas kernels for 0% -> 0%
where the time goes in v12:
time: 55.3 us; the launch traced here: 54.8 us
  waiting for transfers between devices  16 us (29%)
  starting transfers between devices  14.9 us (27%)
  local copies, waits for them, and re-layouts  13.9 us (25%)
  Pallas kernels  5.56 us (10%)
  matrix products  2.22 us (4%)
  other arithmetic  1.94 us (4%)
    ppermute x4, starting transfers between devices, butterfly_sum(): lax.ppermute(value, axis, [(i, i ^ stride) for i in range(count)])  12.2 us
    ppermute x4, waiting for transfers between devices, butterfly_sum(): lax.ppermute(value, axis, [(i, i ^ stride) for i in range(count)])  5.65 us
    ppermute x1, waiting for transfers between devices, on_device(): above_flat = lax.ppermute(flat(bottom_row), 'curve', behind)  4.43 us
    ppermute x1, waiting for transfers between devices, on_device(): from_left = lax.ppermute(flat(to_right), 'line', ahead)  4.06 us
    concatenate x3, local copies, waits for them, and re-layouts, on_device(): extended = jnp.concatenate([post, solid], axis=0)  3.53 us
    pallas_call x1, Pallas kernels, stream(): pl.pallas_call(stream_kernel, out_shape=jax.ShapeDtypeStruct((seats * cha...  3.14 us
    unnamed x30, local copies, waits for them, and re-layouts  2.88 us
    pallas_call x1, Pallas kernels, cell_moments(): pl.pallas_call(moments_kernel, out_shape=(jax.ShapeDtypeStruct((levels, b...  2.42 us
  transfers between devices with their start and end apart: 8, of which 7 were waited for; matrix products, arithmetic and copies ran while one was open for 11% of the time, Pallas kernels for 0%

profile of v12, /device:TPU:30, one launch (start us, length us, event | category | flops | bytes accessed | tf_op | source)
XLA Modules:
  0.0 54.8 jit_solution(7948398865575931761)
XLA Ops:
  0.0 2.4 %shard_map.73 = (f32[2,8,27,256]{3,2,1,0:T(8,128)}, f32[3,2,8,256]{3,2,1,0:T(8,128)}, f32[2,8,256]{2,1,0:T(8,128)}) custom-call(s32[6]{0:T(128)} %bitcast.97, f32[27,27]{1,0:T(8,128)} %constant.37.clone.forward_ref, f32[648,128]{1,0:T(8,128)} %bitcast.82), custom_call_target="tpu_custom_call" | custom-call | tf_op jit(solution)/shard_map/pallas_call | solution.py:120
  2.4 1.0 %reshape.94 = f32[3,2,2,4,16,16]{5,4,3,2,1,0:T(8,128)S(1)} reshape(f32[3,2,8,256]{3,2,1,0:T(8,128)} %get-tuple-element.10) | data formatting | bytes 98304 | tf_op jit(solution)/shard_map/reshape | solution.py:278
  3.9 0.8 %fusion.13 = (f32[4,16,8]{1,2,0:T(8,128)S(1)}, f32[4,16,8]{1,2,0:T(8,128)S(1)}) fusion(s32[8]{0:T(128)} %param.9, s32[4,16]{1,0:T(4,128)S(1)} %add_add_fusion), kind=kLoop, calls=%fused_computation.35 | loop fusion | flops 7168 | bytes 4384 | tf_op jit(solution)/shard_map/cos | solution.py:65
  4.7 0.3 convolution_bitcast_fusion
  5.1 1.2 %collective-permute-done = f32[3,2,32,16]{2,3,1,0:T(8,128)S(1)} collective-permute-done((f32[3,2,32,16]{2,3,1,0:T(8,128)S(1)}, f32[3,2,32,16]{2,3,1,0:T(8,128)S(1)}, u32[]{:S(2)}, u32[]{:S(2)}) %collective-permute-start) | collective-permute-done | bytes 12320 | tf_op jit(solution)/shard_map/ppermute | solution.py:23
  6.3 2.0 %collective-permute-start.1 = (f32[3,2,32,16]{2,3,1,0:T(8,128)S(1)}, f32[3,2,32,16]{2,3,1,0:T(8,128)S(1)}, u32[]{:S(2)}, u32[]{:S(2)}) collective-permute-start(f32[3,2,32,16]{2,3,1,0:T(8,128)S(1)} %add.43), channel_id=1, source_target_pairs={{0,2},{1,3},{2,0},{3,1},{4,6},{5,7},{6,4},{7,5},{8,10},{9,11},{10,... | collective-permute-start | bytes 36872 | tf_op jit(solution)/shard_map/ppermute | solution.py:23
  8.3 2.2 %collective-permute-done.1 = f32[3,2,32,16]{2,3,1,0:T(8,128)S(1)} collective-permute-done((f32[3,2,32,16]{2,3,1,0:T(8,128)S(1)}, f32[3,2,32,16]{2,3,1,0:T(8,128)S(1)}, u32[]{:S(2)}, u32[]{:S(2)}) %collective-permute-start.1) | collective-permute-done | bytes 12320 | tf_op jit(solution)/shard_map/ppermute | solution.py:23
  10.5 3.4 %collective-permute-start.2 = (f32[3,2,32,16]{2,3,1,0:T(8,128)S(1)}, f32[3,2,32,16]{2,3,1,0:T(8,128)S(1)}, u32[]{:S(2)}, u32[]{:S(2)}) collective-permute-start(f32[3,2,32,16]{2,3,1,0:T(8,128)S(1)} %add.44), channel_id=1, source_target_pairs={{0,4},{1,5},{2,6},{3,7},{4,0},{5,1},{6,2},{7,3},{8,12},{9,13},{10,... | collective-permute-start | bytes 36872 | tf_op jit(solution)/shard_map/ppermute | solution.py:23
  13.9 2.3 %collective-permute-done.2 = f32[3,2,32,16]{2,3,1,0:T(8,128)S(1)} collective-permute-done((f32[3,2,32,16]{2,3,1,0:T(8,128)S(1)}, f32[3,2,32,16]{2,3,1,0:T(8,128)S(1)}, u32[]{:S(2)}, u32[]{:S(2)}) %collective-permute-start.2) | collective-permute-done | bytes 12320 | tf_op jit(solution)/shard_map/ppermute | solution.py:23
  16.1 6.8 %collective-permute-start.3 = (f32[3,2,32,16]{2,3,1,0:T(8,128)S(1)}, f32[3,2,32,16]{2,3,1,0:T(8,128)S(1)}, u32[]{:S(2)}, u32[]{:S(2)}) collective-permute-start(f32[3,2,32,16]{2,3,1,0:T(8,128)S(1)} %add.45), channel_id=1, source_target_pairs={{0,8},{1,9},{2,10},{3,11},{4,12},{5,13},{6,14},{7,15},{8,0},{9,1},... | collective-permute-start | bytes 36872 | tf_op jit(solution)/shard_map/ppermute | solution.py:23
  22.9 0.9 %slice.52 = f32[1,2,8,256]{3,0,2,1:T(1,128)S(1)} slice(f32[27,2,8,256]{3,0,2,1:T(8,128)} %bitcast.80), slice={[0:1], [0:2], [0:8], [0:256]} | slice | bytes 32768 | tf_op jit(solution)/shard_map/slice | solution.py:69
  23.8 1.5 %concatenate.23 = f32[1,2,2,4,16,16]{5,4,3,2,1,0:T(8,128)} reshape(f32[2,8,256]{2,1,0:T(8,128)} %get-tuple-element.8) | data formatting | bytes 32768 | tf_op jit(solution)/shard_map/concatenate | solution.py:289
  25.3 0.7 %copy.52 = f32[1,2,8,256]{3,0,2,1:T(1,128)S(1)} copy(f32[1,2,8,256]{3,2,1,0:T(8,128)} %bitcast.91) | data formatting | bytes 32768 | tf_op jit(solution)/shard_map/broadcast_in_dim | solution.py:288
  26.1 0.8 %multiply_subtract_fusion = f32[3,2,32,16]{2,3,1,0:T(8,128)S(1)} fusion(f32[3,2,32,16]{2,3,1,0:T(8,128)} %param.10, f32[3,2,32,16]{2,3,1,0:T(8,128)S(1)} %add.45, f32[3,2,32,16]{2,3,1,0:T(8,128)S(1)} %collective-permute-done.3), kind=kLoop, calls=%fused_computation.20 | loop fusion | flops 9216 | bytes 49152 | tf_op jit(solution)/shard_map/sub | solution.py:282
  27.0 1.0 %fusion = f32[3,2,2,4,16,16]{4,5,2,1,0,3:T(8,128)S(1)} fusion(f32[3,2,2,16,16,1]{4,3,2,1,0,5:T(8,128)S(1)} %bitcast.81, f32[4,16,8]{1,2,0:T(8,128)S(1)} %get-tuple-element.24, f32[4,16,8]{1,2,0:T(8,128)S(1)} %get-tuple-element.23), kind=kOutput, calls=%fused_computation.1 | convolution fusion | flops 2372608 | bytes 65536 | tf_op jit(solution)/shard_map/kzyrm,xqm->kzyxrq/dot_general | solution.py:283
  28.6 0.9 %fusion.3 = f32[2,8,256,27]{2,3,1,0:T(8,128)S(1)} fusion(f32[27,27,1,1]{1,0,3,2:T(8,128)S(1)} %copy-done.10, f32[27,2,8,256]{3,2,1,0:T(8,128)S(1)} %bitcast.78, f32[27]{0:T(128)S(1)} %copy-done.11, f32[2,8,27,256]{3,2,1,0:T(8,128)S(1)} %copy-done.2), kind=kOutput, calls=%fused_computation.6 | convolution fusion | flops 36163584 | bytes 1330128 | tf_op jit(solution)/shard_map/ij,jzpl->izpl/dot_general | solution.py:80
  29.5 0.8 %copy-done = f32[2,8,256,27]{2,3,1,0:T(8,128)} copy-done((f32[2,8,256,27]{2,3,1,0:T(8,128)}, f32[2,8,256,27]{2,3,1,0:T(8,128)S(1)}, u32[]{:S(2)}) %copy-start) | copy-done | bytes 442392
  30.4 1.0 %copy.56 = f32[27,2,8,256]{3,2,1,0:T(8,128)} copy(f32[27,2,8,256]{3,0,2,1:T(8,128)S(1)} %bitcast.75) | data formatting | bytes 884736 | tf_op jit(solution)/shard_map/ij,jzpl->izpl/dot_general | solution.py:80
  31.4 2.0 %concatenate.22 = f32[27,2,2,4,16,16]{5,4,3,2,1,0:T(8,128)S(1)} reshape(f32[27,2,8,256]{3,2,1,0:T(8,128)} %copy.56) | data formatting | bytes 884736 | tf_op jit(solution)/shard_map/concatenate | solution.py:289
  33.7 0.8 %copy-done.1 = f32[2,8,256,27]{2,3,1,0:T(8,128)S(1)} copy-done((f32[2,8,256,27]{2,3,1,0:T(8,128)S(1)}, f32[2,8,256,27]{2,3,1,0:T(8,128)}, u32[]{:S(2)}) %copy-start.1) | copy-done | bytes 442392
  34.9 0.3 fusion.17
  35.3 0.7 %copy.61 = f32[28,2,2,1,16,1]{0,4,5,3,2,1:T(8,128)S(1)} copy(f32[28,2,2,1,16,1]{5,4,3,2,1,0:T(8,128)S(1)} %get-tuple-element.11) | data formatting | bytes 14336 | tf_op jit(solution)/shard_map/slice | solution.py:303
  36.0 2.0 %collective-permute-start.5 = (f32[224,16]{1,0:T(8,128)S(1)}, f32[224,16]{1,0:T(8,128)S(1)}, u32[]{:S(2)}, u32[]{:S(2)}) collective-permute-start(f32[224,16]{1,0:T(8,128)S(1)} %bitcast.89), channel_id=1, source_target_pairs={{16,0},{32,16},{48,32},{64,48},{80,64},{96,80},{112,96},{128,112},... | collective-permute-start | bytes 43016 | tf_op jit(solution)/shard_map/ppermute | solution.py:297
  38.0 0.7 %copy.57 = f32[28,2,2,1,16,1]{0,4,5,3,2,1:T(8,128)S(1)} copy(f32[28,2,2,1,16,1]{5,4,3,2,1,0:T(8,128)S(1)} %get-tuple-element.12) | data formatting | bytes 14336 | tf_op jit(solution)/shard_map/slice | solution.py:302
  38.6 0.9 %collective-permute-done.4.below_ref = f32[224,16]{1,0:T(8,128)S(1)} collective-permute-done((f32[224,16]{1,0:T(8,128)S(1)}, f32[224,16]{1,0:T(8,128)S(1)}, u32[]{:S(2)}, u32[]{:S(2)}) %collective-permute-start.4) | collective-permute-done | bytes 14368 | tf_op jit(solution)/shard_map/ppermute | solution.py:296
  39.8 4.4 %collective-permute-done.5.above_ref = f32[224,16]{1,0:T(8,128)S(1)} collective-permute-done((f32[224,16]{1,0:T(8,128)S(1)}, f32[224,16]{1,0:T(8,128)S(1)}, u32[]{:S(2)}, u32[]{:S(2)}) %collective-permute-start.5) | collective-permute-done | bytes 14368 | tf_op jit(solution)/shard_map/ppermute | solution.py:297
  44.9 0.5 collective-permute-start.6
  45.4 0.6 %slice_bitcast_fusion.3.solid_ref = f32[8,256]{1,0:T(8,128)} fusion(f32[2,8,256]{2,1,0:T(8,128)S(1)} %copy-done.9), kind=kLoop, calls=%fused_computation.36 | loop fusion | bytes 16384 | tf_op jit(solution)/shard_map/squeeze | solution.py:322
  46.0 0.9 %collective-permute-done.7.right_ref = f32[224,16]{1,0:T(8,128)S(1)} collective-permute-done((f32[224,16]{1,0:T(8,128)S(1)}, f32[224,16]{1,0:T(8,128)S(1)}, u32[]{:S(2)}, u32[]{:S(2)}) %collective-permute-start.7) | collective-permute-done | bytes 14368 | tf_op jit(solution)/shard_map/ppermute | solution.py:321
  47.0 4.1 %collective-permute-done.6.left_ref = f32[224,16]{1,0:T(8,128)S(1)} collective-permute-done((f32[224,16]{1,0:T(8,128)S(1)}, f32[224,16]{1,0:T(8,128)S(1)}, u32[]{:S(2)}, u32[]{:S(2)}) %collective-permute-start.6) | collective-permute-done | bytes 14368 | tf_op jit(solution)/shard_map/ppermute | solution.py:320
  51.0 0.6 %copy-done.8 = f32[224,16]{1,0:T(8,128)} copy-done((f32[224,16]{1,0:T(8,128)}, f32[224,16]{1,0:T(8,128)S(1)}, u32[]{:S(2)}) %copy-start.8) | copy-done | bytes 14360
  51.7 3.1 %shard_map.74 = f32[648,128]{1,0:T(8,128)} custom-call(s32[6]{0:T(128)} %bitcast.98, f32[8,256]{1,0:T(8,128)} %slice_bitcast_fusion.3.solid_ref, f32[2,8,27,256]{3,2,1,0:T(8,128)} %bitcast.76, f32[224,16]{1,0:T(8,128)} %copy-done.4, f32[224,16]{1,0:T(8,128)} %copy-done.5, f32[224,16]{1,0:T(8,128)} %copy-done.8, f32[224,16]{1,0:T(8,128)} %copy-done.7), custom_call_target="tpu_custom_call" | custom-call | tf_op jit(solution)/shard_map/pallas_call | solution.py:242
  (61 shorter events, 2.9 us)
Async XLA Ops:
  0.0 28.6 %copy-start.10 = (f32[27,27,1,1]{1,0,3,2:T(8,128)S(1)}, f32[27,27,1,1]{1,0,3,2:T(8,128)}, u32[]{:S(2)}) copy-start(f32[27,27,1,1]{1,0,3,2:T(8,128)} %constant.41) | copy-start | bytes 8752
  0.0 28.6 %copy-start.11 = (f32[27]{0:T(128)S(1)}, f32[27]{0:T(128)}, u32[]{:S(2)}) copy-start(f32[27]{0:T(128)} %param.11) | copy-start | bytes 328
  2.4 26.0 %copy-start.6 = (f32[3,2,8,256]{3,2,1,0:T(8,128)S(1)}, f32[3,2,8,256]{3,2,1,0:T(8,128)}, u32[]{:S(2)}) copy-start(f32[3,2,8,256]{3,2,1,0:T(8,128)} %get-tuple-element.10) | copy-start | bytes 147460
  2.4 26.2 %copy-start.2 = (f32[2,8,27,256]{3,2,1,0:T(8,128)S(1)}, f32[2,8,27,256]{3,2,1,0:T(8,128)}, u32[]{:S(2)}) copy-start(f32[2,8,27,256]{3,2,1,0:T(8,128)} %get-tuple-element.9) | copy-start | bytes 1327108
  5.0 1.3 %collective-permute-start = (f32[3,2,32,16]{2,3,1,0:T(8,128)S(1)}, f32[3,2,32,16]{2,3,1,0:T(8,128)S(1)}, u32[]{:S(2)}, u32[]{:S(2)}) collective-permute-start(f32[3,2,32,16]{2,3,1,0:T(8,128)S(1)} %convolution_bitcast_fusion), channel_id=1, source_target_pairs={{0,1},{1,0},{2,3},{3,2},{4,5},{5,4},{6,7},{7,6},{8,9},{9,8},{10,11... | collective-permute-start | bytes 36872 | tf_op jit(solution)/shard_map/ppermute | solution.py:23
  6.3 4.2 %collective-permute-start.1 = (f32[3,2,32,16]{2,3,1,0:T(8,128)S(1)}, f32[3,2,32,16]{2,3,1,0:T(8,128)S(1)}, u32[]{:S(2)}, u32[]{:S(2)}) collective-permute-start(f32[3,2,32,16]{2,3,1,0:T(8,128)S(1)} %add.43), channel_id=1, source_target_pairs={{0,2},{1,3},{2,0},{3,1},{4,6},{5,7},{6,4},{7,5},{8,10},{9,11},{10,... | collective-permute-start | bytes 36872 | tf_op jit(solution)/shard_map/ppermute | solution.py:23
  10.5 5.6 %collective-permute-start.2 = (f32[3,2,32,16]{2,3,1,0:T(8,128)S(1)}, f32[3,2,32,16]{2,3,1,0:T(8,128)S(1)}, u32[]{:S(2)}, u32[]{:S(2)}) collective-permute-start(f32[3,2,32,16]{2,3,1,0:T(8,128)S(1)} %add.44), channel_id=1, source_target_pairs={{0,4},{1,5},{2,6},{3,7},{4,0},{5,1},{6,2},{7,3},{8,12},{9,13},{10,... | collective-permute-start | bytes 36872 | tf_op jit(solution)/shard_map/ppermute | solution.py:23
  16.1 9.9 %collective-permute-start.3 = (f32[3,2,32,16]{2,3,1,0:T(8,128)S(1)}, f32[3,2,32,16]{2,3,1,0:T(8,128)S(1)}, u32[]{:S(2)}, u32[]{:S(2)}) collective-permute-start(f32[3,2,32,16]{2,3,1,0:T(8,128)S(1)} %add.45), channel_id=1, source_target_pairs={{0,8},{1,9},{2,10},{3,11},{4,12},{5,13},{6,14},{7,15},{8,0},{9,1},... | collective-permute-start | bytes 36872 | tf_op jit(solution)/shard_map/ppermute | solution.py:23
  29.5 0.8 %copy-start = (f32[2,8,256,27]{2,3,1,0:T(8,128)}, f32[2,8,256,27]{2,3,1,0:T(8,128)S(1)}, u32[]{:S(2)}) copy-start(f32[2,8,256,27]{2,3,1,0:T(8,128)S(1)} %fusion.3) | copy-start | bytes 1327108
  33.4 1.0 %copy-start.1 = (f32[2,8,256,27]{2,3,1,0:T(8,128)S(1)}, f32[2,8,256,27]{2,3,1,0:T(8,128)}, u32[]{:S(2)}) copy-start(f32[2,8,256,27]{2,3,1,0:T(8,128)} %copy-done) | copy-start | bytes 1327108
  33.5 1.4 %copy-start.3 = (f32[1,2,2,4,16,16]{5,4,3,2,1,0:T(8,128)S(1)}, f32[1,2,2,4,16,16]{5,4,3,2,1,0:T(8,128)}, u32[]{:S(2)}) copy-start(f32[1,2,2,4,16,16]{5,4,3,2,1,0:T(8,128)} %concatenate.23) | copy-start | bytes 49156
  34.6 10.9 %copy-start.9 = (f32[2,8,256]{2,1,0:T(8,128)S(1)}, f32[2,8,256]{2,1,0:T(8,128)}, u32[]{:S(2)}) copy-start(f32[2,8,256]{2,1,0:T(8,128)} %get-tuple-element.8) | copy-start | bytes 49156
  34.7 4.9 %collective-permute-start.4 = (f32[224,16]{1,0:T(8,128)S(1)}, f32[224,16]{1,0:T(8,128)S(1)}, u32[]{:S(2)}, u32[]{:S(2)}) collective-permute-start(f32[224,16]{1,0:T(8,128)S(1)} %bitcast.88), channel_id=1, source_target_pairs={{0,16},{16,32},{32,48},{48,64},{64,80},{80,96},{96,112},{112,128},... | collective-permute-start | bytes 43016 | tf_op jit(solution)/shard_map/ppermute | solution.py:296
  36.0 8.2 %collective-permute-start.5 = (f32[224,16]{1,0:T(8,128)S(1)}, f32[224,16]{1,0:T(8,128)S(1)}, u32[]{:S(2)}, u32[]{:S(2)}) collective-permute-start(f32[224,16]{1,0:T(8,128)S(1)} %bitcast.89), channel_id=1, source_target_pairs={{16,0},{32,16},{48,32},{64,48},{80,64},{96,80},{112,96},{128,112},... | collective-permute-start | bytes 43016 | tf_op jit(solution)/shard_map/ppermute | solution.py:297
  39.6 11.5 %copy-start.4 = (f32[224,16]{1,0:T(8,128)}, f32[224,16]{1,0:T(8,128)S(1)}, u32[]{:S(2)}) copy-start(f32[224,16]{1,0:T(8,128)S(1)} %collective-permute-done.4.below_ref) | copy-start | bytes 43012
  44.2 6.8 %copy-start.5 = (f32[224,16]{1,0:T(8,128)}, f32[224,16]{1,0:T(8,128)S(1)}, u32[]{:S(2)}) copy-start(f32[224,16]{1,0:T(8,128)S(1)} %collective-permute-done.5.above_ref) | copy-start | bytes 43012
  44.6 2.4 %collective-permute-start.7 = (f32[224,16]{1,0:T(8,128)S(1)}, f32[224,16]{1,0:T(8,128)S(1)}, u32[]{:S(2)}, u32[]{:S(2)}) collective-permute-start(f32[224,16]{1,0:T(8,128)S(1)} %bitcast.87), channel_id=1, source_target_pairs={{1,0},{2,1},{3,2},{4,3},{5,4},{6,5},{7,6},{8,7},{9,8},{10,9},{11,1... | collective-permute-start | bytes 43016 | tf_op jit(solution)/shard_map/ppermute | solution.py:321
  44.9 6.1 %collective-permute-start.6 = (f32[224,16]{1,0:T(8,128)S(1)}, f32[224,16]{1,0:T(8,128)S(1)}, u32[]{:S(2)}, u32[]{:S(2)}) collective-permute-start(f32[224,16]{1,0:T(8,128)S(1)} %bitcast.90), channel_id=1, source_target_pairs={{0,1},{1,2},{2,3},{3,4},{4,5},{5,6},{6,7},{7,8},{8,9},{9,10},{10,1... | collective-permute-start | bytes 43016 | tf_op jit(solution)/shard_map/ppermute | solution.py:320
  47.0 4.1 %copy-start.7 = (f32[224,16]{1,0:T(8,128)}, f32[224,16]{1,0:T(8,128)S(1)}, u32[]{:S(2)}) copy-start(f32[224,16]{1,0:T(8,128)S(1)} %collective-permute-done.7.right_ref) | copy-start | bytes 43012
  51.0 0.7 %copy-start.8 = (f32[224,16]{1,0:T(8,128)}, f32[224,16]{1,0:T(8,128)S(1)}, u32[]{:S(2)}) copy-start(f32[224,16]{1,0:T(8,128)S(1)} %collective-permute-done.6.left_ref) | copy-start | bytes 43012

commit v13 on v12

--- a/solution.py
+++ b/solution.py
@@ -80,7 +80,7 @@
     return jnp.einsum("ij,jzpl->izpl", backward, relaxed, precision=HIGHEST)
 
 
-def moments_kernel(keys_ref, forward_ref, state_ref, out_ref, wind_ref, solid_ref, scratch_ref):
+def moments_kernel(keys_ref, forward_ref, state_ref, out_ref, wind_ref, scratch_ref):
     levels, blocks, channels, cells = out_ref.shape
     seats = scratch_ref.shape[0]
     chunks = levels * cells // 128
@@ -108,7 +108,6 @@
             density = jnp.where(found, values[0:1], 1.0)
             for component, row in enumerate((9, 3, 1)):
                 wind_ref[component, level, block:block + 1, :] = values[row:row + 1] / density
-            solid_ref[level, block:block + 1, :] = jnp.broadcast_to(1.0 - keep, (1, cells))
 
 
 def cell_moments(keys, forward, rows, seats, levels):
@@ -122,16 +121,15 @@
         out_shape=(
             jax.ShapeDtypeStruct((levels, blocks, channels, cells), jnp.float32),
             jax.ShapeDtypeStruct((3, levels, blocks, cells), jnp.float32),
-            jax.ShapeDtypeStruct((levels, blocks, cells), jnp.float32),
         ),
         in_specs=[smem, vmem, vmem],
-        out_specs=(vmem, vmem, vmem),
+        out_specs=(vmem, vmem),
         scratch_shapes=[pltpu.VMEM((seats, channels, levels * cells), jnp.float32)],
     )(keys, forward, rows)
 
 
 def stream_kernel(
-    keys_ref, solid_ref, post_ref, below_ref, above_ref, left_ref, right_ref, out_ref, spread_ref, result_ref
+    keys_ref, post_ref, below_ref, above_ref, left_ref, right_ref, out_ref, spread_ref, result_ref
 ):
     levels, blocks, channels, cells = post_ref.shape
     _, _, speeds = lattice_tables()
@@ -153,7 +151,12 @@
     r = lane // BE
     py = seat // TX
 
-    solid_plane = solid_ref[...]
+    solid_plane = jnp.zeros((blocks, cells), jnp.float32)
+    for block in range(blocks):
+        found = False
+        for seat_number in range(keys_ref.shape[0]):
+            found = jnp.logical_or(found, keys_ref[seat_number] == block)
+        solid_plane = jnp.where(seat == block, jnp.where(found, 0.0, 1.0), solid_plane)
 
     def own(channel, level):
         if channel == channels:
@@ -233,7 +236,7 @@
             out_ref[rows, :] = jnp.where(key >= 0, picked, 0.0)
 
 
-def stream(keys, solid_plane, post, below, above, from_left, from_right):
+def stream(keys, post, below, above, from_left, from_right):
     channels, levels, blocks, cells = post.shape
     seats = keys.shape[0]
     halo_rows = below.shape[0]
@@ -242,13 +245,13 @@
     return pl.pallas_call(
         stream_kernel,
         out_shape=jax.ShapeDtypeStruct((seats * channels * levels * cells // 128, 128), jnp.float32),
-        in_specs=[smem] + [vmem] * 6,
+        in_specs=[smem] + [vmem] * 5,
         out_specs=vmem,
         scratch_shapes=[
             pltpu.VMEM((4, halo_rows + 16, cells), jnp.float32),
             pltpu.VMEM((blocks, channels, levels * cells), jnp.float32),
         ],
-    )(keys, solid_plane, post.transpose(1, 2, 0, 3), below, above, from_left, from_right)
+    )(keys, post.transpose(1, 2, 0, 3), below, above, from_left, from_right)
 
 
 def on_device(
@@ -269,7 +272,7 @@
     rows_tile = TY * BE
     cols_tile = TX * BE
     rows = slot_state.reshape(-1, 128)
-    moments, wind, solid_plane = cell_moments(living_brick_keys, forward, rows, seats, levels)
+    moments, wind = cell_moments(living_brick_keys, forward, rows, seats, levels)
     moments = moments.transpose(2, 0, 1, 3)
     line_length = lax.axis_size("line") * cols_tile
     own_columns = lax.axis_index("line") * cols_tile + jnp.arange(cols_tile, dtype=jnp.int32)
@@ -285,7 +288,9 @@
         precision=HIGHEST,
     ).reshape(3, levels, blocks, cells)
     post = collide_blocks(moments, wind, nudge, backward, relaxation_frequencies)
-    solid = solid_plane[None]
+    present = jnp.any(living_brick_keys[None, :] == jnp.arange(blocks, dtype=jnp.int32)[:, None], axis=1)
+    fluid = present.astype(jnp.float32)
+    solid = jnp.broadcast_to((1.0 - fluid)[None, None, :, None], (1, levels, blocks, cells))
     extended = jnp.concatenate([post, solid], axis=0)
     width = channels + 1
     ahead, behind = ring_pairs("curve")
@@ -319,7 +324,7 @@
     )
     from_left = lax.ppermute(flat(to_right), "line", ahead)
     from_right = lax.ppermute(flat(to_left), "line", behind)
-    new_state = stream(living_brick_keys, solid_plane[0], post, below_flat, above_flat, from_left, from_right)
+    new_state = stream(living_brick_keys, post, below_flat, above_flat, from_left, from_right)
     return new_state.reshape((1, 1, seats, channels, levels * cells))
 
 

time: 55.3 us -> 48.6 us (0.88)
  local copies, waits for them, and re-layouts: 13.9 us -> 4.4 us
  waiting for transfers between devices: 16 us -> 20.2 us
  other arithmetic: 1.94 us -> 0.66 us
    concatenate x3 -> x1, local copies, waits for them, and re-layouts: 3.53 us -> 0.65 us  [on_device(): extended = jnp.concatenate([post, solid], axis=0)]
    ppermute x4, waiting for transfers between devices: 5.65 us -> 7.65 us  [butterfly_sum(): lax.ppermute(value, axis, [(i, i ^ stride) for i in range(count)])]
    unnamed x30 -> x29, local copies, waits for them, and re-layouts: 2.88 us -> 1.06 us
    ppermute x1, waiting for transfers between devices: 0.91 us -> 2.55 us  [on_device(): below_flat = lax.ppermute(flat(top_row), 'curve', ahead)]
    dot_general x1 -> x0, local copies, waits for them, and re-layouts: 1.03 us -> none  [collide_blocks(): return jnp.einsum('ij,jzpl->izpl', backward, relaxed, precision=HIGHEST)]
    slice x2 -> x1, local copies, waits for them, and re-layouts: 1.01 us -> 0.05 us  [on_device(): left_cols = by_rows[:, :, :, 0, :, 0]]
    slice x1, local copies, waits for them, and re-layouts: 0.91 us -> 0.01 us  [collide_blocks(): density = moments[0]]
    ppermute x1, starting transfers between devices: 0.21 us -> 1.07 us  [on_device(): below_flat = lax.ppermute(flat(top_row), 'curve', ahead)]
  transfers between devices with their start and end apart: 8 -> 8, of which waited for: 7 -> 8; matrix products, arithmetic and copies ran while one was open for 11% -> 2% of each run, Pallas kernels for 0% -> 0%
where the time goes in v13:
time: 48.6 us; the launch traced here: 48.3 us
  waiting for transfers between devices  20.2 us (42%)
  starting transfers between devices  14.9 us (31%)
  Pallas kernels  5.57 us (11%)
  local copies, waits for them, and re-layouts  4.4 us (9%)
  matrix products  2.23 us (5%)
  other arithmetic  0.66 us (1%)
    ppermute x4, starting transfers between devices, butterfly_sum(): lax.ppermute(value, axis, [(i, i ^ stride) for i in range(count)])  12.2 us
    ppermute x4, waiting for transfers between devices, butterfly_sum(): lax.ppermute(value, axis, [(i, i ^ stride) for i in range(count)])  7.65 us
    ppermute x1, waiting for transfers between devices, on_device(): above_flat = lax.ppermute(flat(bottom_row), 'curve', behind)  4.31 us
    ppermute x1, waiting for transfers between devices, on_device(): from_left = lax.ppermute(flat(to_right), 'line', ahead)  4.18 us
    pallas_call x1, Pallas kernels, stream(): pl.pallas_call(stream_kernel, out_shape=jax.ShapeDtypeStruct((seats * cha...  3.18 us
    ppermute x1, waiting for transfers between devices, on_device(): below_flat = lax.ppermute(flat(top_row), 'curve', ahead)  2.55 us
    pallas_call x1, Pallas kernels, cell_moments(): pl.pallas_call(moments_kernel, out_shape=(jax.ShapeDtypeStruct((levels, b...  2.39 us
    ppermute x1, waiting for transfers between devices, on_device(): from_right = lax.ppermute(flat(to_left), 'line', behind)  1.52 us
  transfers between devices with their start and end apart: 8, of which 8 were waited for; matrix products, arithmetic and copies ran while one was open for 2% of the time, Pallas kernels for 0%

profile of v13, /device:TPU:30, one launch (start us, length us, event | category | flops | bytes accessed | tf_op | source)
XLA Modules:
  0.0 48.3 jit_solution(1754147809015390848)
XLA Ops:
  0.0 2.4 %shard_map.73 = (f32[2,8,27,256]{3,2,1,0:T(8,128)}, f32[3,2,8,256]{3,2,1,0:T(8,128)}) custom-call(s32[6]{0:T(128)} %bitcast.93, f32[27,27]{1,0:T(8,128)} %constant.40.clone.forward_ref, f32[648,128]{1,0:T(8,128)} %bitcast.79), custom_call_target="tpu_custom_call" | custom-call | tf_op jit(solution)/shard_map/pallas_call | solution.py:119
  2.4 1.0 %reshape.100 = f32[3,2,2,4,16,16]{5,4,3,2,1,0:T(8,128)S(1)} reshape(f32[3,2,8,256]{3,2,1,0:T(8,128)} %get-tuple-element.8) | data formatting | bytes 98304 | tf_op jit(solution)/shard_map/reshape | solution.py:281
  3.4 0.2 copy.43
  3.6 0.2 dot_general.16
  3.9 0.2 fusion.15
  4.1 0.3 convolution_bitcast_fusion
  4.4 1.2 %collective-permute-done = f32[3,2,32,16]{2,3,1,0:T(8,128)S(1)} collective-permute-done((f32[3,2,32,16]{2,3,1,0:T(8,128)S(1)}, f32[3,2,32,16]{2,3,1,0:T(8,128)S(1)}, u32[]{:S(2)}, u32[]{:S(2)}) %collective-permute-start) | collective-permute-done | bytes 12320 | tf_op jit(solution)/shard_map/ppermute | solution.py:23
  5.7 2.0 %collective-permute-start.1 = (f32[3,2,32,16]{2,3,1,0:T(8,128)S(1)}, f32[3,2,32,16]{2,3,1,0:T(8,128)S(1)}, u32[]{:S(2)}, u32[]{:S(2)}) collective-permute-start(f32[3,2,32,16]{2,3,1,0:T(8,128)S(1)} %add.43), channel_id=1, source_target_pairs={{0,2},{1,3},{2,0},{3,1},{4,6},{5,7},{6,4},{7,5},{8,10},{9,11},{10,... | collective-permute-start | bytes 36872 | tf_op jit(solution)/shard_map/ppermute | solution.py:23
  7.7 2.2 %collective-permute-done.1 = f32[3,2,32,16]{2,3,1,0:T(8,128)S(1)} collective-permute-done((f32[3,2,32,16]{2,3,1,0:T(8,128)S(1)}, f32[3,2,32,16]{2,3,1,0:T(8,128)S(1)}, u32[]{:S(2)}, u32[]{:S(2)}) %collective-permute-start.1) | collective-permute-done | bytes 12320 | tf_op jit(solution)/shard_map/ppermute | solution.py:23
  9.9 3.4 %collective-permute-start.2 = (f32[3,2,32,16]{2,3,1,0:T(8,128)S(1)}, f32[3,2,32,16]{2,3,1,0:T(8,128)S(1)}, u32[]{:S(2)}, u32[]{:S(2)}) collective-permute-start(f32[3,2,32,16]{2,3,1,0:T(8,128)S(1)} %add.44), channel_id=1, source_target_pairs={{0,4},{1,5},{2,6},{3,7},{4,0},{5,1},{6,2},{7,3},{8,12},{9,13},{10,... | collective-permute-start | bytes 36872 | tf_op jit(solution)/shard_map/ppermute | solution.py:23
  13.2 0.1 fusion.16
  13.4 2.1 %collective-permute-done.2 = f32[3,2,32,16]{2,3,1,0:T(8,128)S(1)} collective-permute-done((f32[3,2,32,16]{2,3,1,0:T(8,128)S(1)}, f32[3,2,32,16]{2,3,1,0:T(8,128)S(1)}, u32[]{:S(2)}, u32[]{:S(2)}) %collective-permute-start.2) | collective-permute-done | bytes 12320 | tf_op jit(solution)/shard_map/ppermute | solution.py:23
  15.5 6.8 %collective-permute-start.3 = (f32[3,2,32,16]{2,3,1,0:T(8,128)S(1)}, f32[3,2,32,16]{2,3,1,0:T(8,128)S(1)}, u32[]{:S(2)}, u32[]{:S(2)}) collective-permute-start(f32[3,2,32,16]{2,3,1,0:T(8,128)S(1)} %add.45), channel_id=1, source_target_pairs={{0,8},{1,9},{2,10},{3,11},{4,12},{5,13},{6,14},{7,15},{8,0},{9,1},... | collective-permute-start | bytes 36872 | tf_op jit(solution)/shard_map/ppermute | solution.py:23
  22.3 2.1 %collective-permute-done.3 = f32[3,2,32,16]{2,3,1,0:T(8,128)S(1)} collective-permute-done((f32[3,2,32,16]{2,3,1,0:T(8,128)S(1)}, f32[3,2,32,16]{2,3,1,0:T(8,128)S(1)}, u32[]{:S(2)}, u32[]{:S(2)}) %collective-permute-start.3) | collective-permute-done | bytes 12320 | tf_op jit(solution)/shard_map/ppermute | solution.py:23
  24.5 1.0 %fusion = f32[3,2,2,4,16,16]{4,5,2,1,0,3:T(8,128)S(1)} fusion(f32[3,2,2,16,16,1]{4,3,2,1,0,5:T(8,128)S(1)} %bitcast.78, f32[4,16,8]{1,2,0:T(8,128)S(1)} %get-tuple-element.22, f32[4,16,8]{1,2,0:T(8,128)S(1)} %get-tuple-element.21), kind=kOutput, calls=%fused_computation.1 | convolution fusion | flops 2372608 | bytes 65536 | tf_op jit(solution)/shard_map/kzyrm,xqm->kzyxrq/dot_general | solution.py:286
  25.6 0.2 copy.46
  25.8 0.2 mul.123
  26.2 0.9 %fusion.3 = f32[2,8,256,27]{2,3,1,0:T(8,128)S(1)} fusion(f32[27,27,1,1]{1,0,3,2:T(8,128)S(1)} %copy-done.8, f32[27,2,8,256]{3,2,1,0:T(8,128)S(1)} %bitcast.75, f32[27]{0:T(128)S(1)} %copy-done.11, f32[2,8,27,256]{3,2,1,0:T(8,128)S(1)} %copy-done.1), kind=kOutput, calls=%fused_computation.9 | convolution fusion | flops 36163584 | bytes 1330128 | tf_op jit(solution)/shard_map/ij,jzpl->izpl/dot_general | solution.py:80
  27.4 0.7 %copy.51 = f32[28,2,8,256]{0,3,2,1:T(8,128)S(1)} copy(f32[28,2,8,256]{3,0,2,1:T(8,128)S(1)} %pad_maximum_fusion) | data formatting | bytes 917504 | tf_op jit(solution)/shard_map/concatenate | solution.py:294
  28.1 1.1 %collective-permute-start.4 = (f32[224,16]{1,0:T(8,128)S(1)}, f32[224,16]{1,0:T(8,128)S(1)}, u32[]{:S(2)}, u32[]{:S(2)}) collective-permute-start(f32[224,16]{1,0:T(8,128)S(1)} %bitcast.85), channel_id=1, source_target_pairs={{0,16},{16,32},{32,48},{48,64},{64,80},{80,96},{96,112},{112,128},... | collective-permute-start | bytes 43016 | tf_op jit(solution)/shard_map/ppermute | solution.py:301
  29.3 1.1 %collective-permute-start.5 = (f32[224,16]{1,0:T(8,128)S(1)}, f32[224,16]{1,0:T(8,128)S(1)}, u32[]{:S(2)}, u32[]{:S(2)}) collective-permute-start(f32[224,16]{1,0:T(8,128)S(1)} %bitcast.86), channel_id=1, source_target_pairs={{16,0},{32,16},{48,32},{64,48},{80,64},{96,80},{112,96},{128,112},... | collective-permute-start | bytes 43016 | tf_op jit(solution)/shard_map/ppermute | solution.py:302
  30.4 2.6 %collective-permute-done.4.below_ref = f32[224,16]{1,0:T(8,128)S(1)} collective-permute-done((f32[224,16]{1,0:T(8,128)S(1)}, f32[224,16]{1,0:T(8,128)S(1)}, u32[]{:S(2)}, u32[]{:S(2)}) %collective-permute-start.4) | collective-permute-done | bytes 14368 | tf_op jit(solution)/shard_map/ppermute | solution.py:301
  33.0 0.1 fusion.21
  33.2 4.3 %collective-permute-done.5.above_ref = f32[224,16]{1,0:T(8,128)S(1)} collective-permute-done((f32[224,16]{1,0:T(8,128)S(1)}, f32[224,16]{1,0:T(8,128)S(1)}, u32[]{:S(2)}, u32[]{:S(2)}) %collective-permute-start.5) | collective-permute-done | bytes 14368 | tf_op jit(solution)/shard_map/ppermute | solution.py:302
  37.5 0.1 fusion.22
  37.8 0.1 copy.56
  38.1 0.1 copy.53
  38.3 0.5 %collective-permute-start.6 = (f32[224,16]{1,0:T(8,128)S(1)}, f32[224,16]{1,0:T(8,128)S(1)}, u32[]{:S(2)}, u32[]{:S(2)}) collective-permute-start(f32[224,16]{1,0:T(8,128)S(1)} %bitcast.87), channel_id=1, source_target_pairs={{0,1},{1,2},{2,3},{3,4},{4,5},{5,6},{6,7},{7,8},{8,9},{9,10},{10,1... | collective-permute-start | bytes 43016 | tf_op jit(solution)/shard_map/ppermute | solution.py:325
  38.8 1.5 %collective-permute-done.7.right_ref = f32[224,16]{1,0:T(8,128)S(1)} collective-permute-done((f32[224,16]{1,0:T(8,128)S(1)}, f32[224,16]{1,0:T(8,128)S(1)}, u32[]{:S(2)}, u32[]{:S(2)}) %collective-permute-start.7) | collective-permute-done | bytes 14368 | tf_op jit(solution)/shard_map/ppermute | solution.py:326
  40.3 4.2 %collective-permute-done.6.left_ref = f32[224,16]{1,0:T(8,128)S(1)} collective-permute-done((f32[224,16]{1,0:T(8,128)S(1)}, f32[224,16]{1,0:T(8,128)S(1)}, u32[]{:S(2)}, u32[]{:S(2)}) %collective-permute-start.6) | collective-permute-done | bytes 14368 | tf_op jit(solution)/shard_map/ppermute | solution.py:325
  44.5 0.6 %copy-done.6 = f32[224,16]{1,0:T(8,128)} copy-done((f32[224,16]{1,0:T(8,128)}, f32[224,16]{1,0:T(8,128)S(1)}, u32[]{:S(2)}) %copy-start.6) | copy-done | bytes 14360
  45.1 3.2 %shard_map.74 = f32[648,128]{1,0:T(8,128)} custom-call(s32[6]{0:T(128)} %bitcast.94, f32[2,8,27,256]{3,2,1,0:T(8,128)} %bitcast.73, f32[224,16]{1,0:T(8,128)} %copy-done.2, f32[224,16]{1,0:T(8,128)} %copy-done.3, f32[224,16]{1,0:T(8,128)} %copy-done.6, f32[224,16]{1,0:T(8,128)} %copy-done.5), custom_call_target="tpu_custom_call" | custom-call | tf_op jit(solution)/shard_map/pallas_call | solution.py:245
  (57 shorter events, 1.3 us)
Async XLA Ops:
  0.0 13.2 %copy-start.9 = (s32[1,1,6]{2,1,0:T(1,128)S(1)}, s32[1,1,6]{2,1,0:T(1,128)}, u32[]{:S(2)}) copy-start(s32[1,1,6]{2,1,0:T(1,128)} %param.8) | copy-start | bytes 76
  0.0 3.9 %copy-start.10 = (s32[8]{0:T(128)S(1)}, s32[8]{0:T(128)}, u32[]{:S(2)}) copy-start(s32[8]{0:T(128)} %param.9) | copy-start | bytes 100
  0.0 24.4 %copy-start.7 = (f32[3,2,32,16]{2,3,1,0:T(8,128)S(1)}, f32[3,2,32,16]{2,3,1,0:T(8,128)}, u32[]{:S(2)}) copy-start(f32[3,2,32,16]{2,3,1,0:T(8,128)} %param.10) | copy-start | bytes 36868
  2.4 19.9 %copy-start.1 = (f32[2,8,27,256]{3,2,1,0:T(8,128)S(1)}, f32[2,8,27,256]{3,2,1,0:T(8,128)}, u32[]{:S(2)}) copy-start(f32[2,8,27,256]{3,2,1,0:T(8,128)} %get-tuple-element.7) | copy-start | bytes 1327108
  3.4 22.5 %copy-start.4 = (f32[3,2,8,256]{3,2,1,0:T(8,128)S(1)}, f32[3,2,8,256]{3,2,1,0:T(8,128)}, u32[]{:S(2)}) copy-start(f32[3,2,8,256]{3,2,1,0:T(8,128)} %get-tuple-element.8) | copy-start | bytes 147460
  4.3 1.3 %collective-permute-start = (f32[3,2,32,16]{2,3,1,0:T(8,128)S(1)}, f32[3,2,32,16]{2,3,1,0:T(8,128)S(1)}, u32[]{:S(2)}, u32[]{:S(2)}) collective-permute-start(f32[3,2,32,16]{2,3,1,0:T(8,128)S(1)} %convolution_bitcast_fusion), channel_id=1, source_target_pairs={{0,1},{1,0},{2,3},{3,2},{4,5},{5,4},{6,7},{7,6},{8,9},{9,8},{10,11... | collective-permute-start | bytes 36872 | tf_op jit(solution)/shard_map/ppermute | solution.py:23
  5.7 20.5 %copy-start.8 = (f32[27,27,1,1]{1,0,3,2:T(8,128)S(1)}, f32[27,27,1,1]{1,0,3,2:T(8,128)}, u32[]{:S(2)}) copy-start(f32[27,27,1,1]{1,0,3,2:T(8,128)} %constant.44) | copy-start | bytes 8752
  5.7 20.5 %copy-start.11 = (f32[27]{0:T(128)S(1)}, f32[27]{0:T(128)}, u32[]{:S(2)}) copy-start(f32[27]{0:T(128)} %param.11) | copy-start | bytes 328
  5.7 4.2 %collective-permute-start.1 = (f32[3,2,32,16]{2,3,1,0:T(8,128)S(1)}, f32[3,2,32,16]{2,3,1,0:T(8,128)S(1)}, u32[]{:S(2)}, u32[]{:S(2)}) collective-permute-start(f32[3,2,32,16]{2,3,1,0:T(8,128)S(1)} %add.43), channel_id=1, source_target_pairs={{0,2},{1,3},{2,0},{3,1},{4,6},{5,7},{6,4},{7,5},{8,10},{9,11},{10,... | collective-permute-start | bytes 36872 | tf_op jit(solution)/shard_map/ppermute | solution.py:23
  9.9 5.6 %collective-permute-start.2 = (f32[3,2,32,16]{2,3,1,0:T(8,128)S(1)}, f32[3,2,32,16]{2,3,1,0:T(8,128)S(1)}, u32[]{:S(2)}, u32[]{:S(2)}) collective-permute-start(f32[3,2,32,16]{2,3,1,0:T(8,128)S(1)} %add.44), channel_id=1, source_target_pairs={{0,4},{1,5},{2,6},{3,7},{4,0},{5,1},{6,2},{7,3},{8,12},{9,13},{10,... | collective-permute-start | bytes 36872 | tf_op jit(solution)/shard_map/ppermute | solution.py:23
  15.5 8.9 %collective-permute-start.3 = (f32[3,2,32,16]{2,3,1,0:T(8,128)S(1)}, f32[3,2,32,16]{2,3,1,0:T(8,128)S(1)}, u32[]{:S(2)}, u32[]{:S(2)}) collective-permute-start(f32[3,2,32,16]{2,3,1,0:T(8,128)S(1)} %add.45), channel_id=1, source_target_pairs={{0,8},{1,9},{2,10},{3,11},{4,12},{5,13},{6,14},{7,15},{8,0},{9,1},... | collective-permute-start | bytes 36872 | tf_op jit(solution)/shard_map/ppermute | solution.py:23
  27.1 0.9 %copy-start = (f32[2,8,256,27]{2,3,1,0:T(8,128)}, f32[2,8,256,27]{2,3,1,0:T(8,128)S(1)}, u32[]{:S(2)}) copy-start(f32[2,8,256,27]{2,3,1,0:T(8,128)S(1)} %fusion.3) | copy-start | bytes 1327108
  28.1 4.9 %collective-permute-start.4 = (f32[224,16]{1,0:T(8,128)S(1)}, f32[224,16]{1,0:T(8,128)S(1)}, u32[]{:S(2)}, u32[]{:S(2)}) collective-permute-start(f32[224,16]{1,0:T(8,128)S(1)} %bitcast.85), channel_id=1, source_target_pairs={{0,16},{16,32},{32,48},{48,64},{64,80},{80,96},{96,112},{112,128},... | collective-permute-start | bytes 43016 | tf_op jit(solution)/shard_map/ppermute | solution.py:301
  29.3 8.2 %collective-permute-start.5 = (f32[224,16]{1,0:T(8,128)S(1)}, f32[224,16]{1,0:T(8,128)S(1)}, u32[]{:S(2)}, u32[]{:S(2)}) collective-permute-start(f32[224,16]{1,0:T(8,128)S(1)} %bitcast.86), channel_id=1, source_target_pairs={{16,0},{32,16},{48,32},{64,48},{80,64},{96,80},{112,96},{128,112},... | collective-permute-start | bytes 43016 | tf_op jit(solution)/shard_map/ppermute | solution.py:302
  33.0 11.5 %copy-start.2 = (f32[224,16]{1,0:T(8,128)}, f32[224,16]{1,0:T(8,128)S(1)}, u32[]{:S(2)}) copy-start(f32[224,16]{1,0:T(8,128)S(1)} %collective-permute-done.4.below_ref) | copy-start | bytes 43012
  37.5 6.9 %copy-start.3 = (f32[224,16]{1,0:T(8,128)}, f32[224,16]{1,0:T(8,128)S(1)}, u32[]{:S(2)}) copy-start(f32[224,16]{1,0:T(8,128)S(1)} %collective-permute-done.5.above_ref) | copy-start | bytes 43012
  37.9 2.4 %collective-permute-start.7 = (f32[224,16]{1,0:T(8,128)S(1)}, f32[224,16]{1,0:T(8,128)S(1)}, u32[]{:S(2)}, u32[]{:S(2)}) collective-permute-start(f32[224,16]{1,0:T(8,128)S(1)} %bitcast.84), channel_id=1, source_target_pairs={{1,0},{2,1},{3,2},{4,3},{5,4},{6,5},{7,6},{8,7},{9,8},{10,9},{11,1... | collective-permute-start | bytes 43016 | tf_op jit(solution)/shard_map/ppermute | solution.py:326
  38.3 6.2 %collective-permute-start.6 = (f32[224,16]{1,0:T(8,128)S(1)}, f32[224,16]{1,0:T(8,128)S(1)}, u32[]{:S(2)}, u32[]{:S(2)}) collective-permute-start(f32[224,16]{1,0:T(8,128)S(1)} %bitcast.87), channel_id=1, source_target_pairs={{0,1},{1,2},{2,3},{3,4},{4,5},{5,6},{6,7},{7,8},{8,9},{9,10},{10,1... | collective-permute-start | bytes 43016 | tf_op jit(solution)/shard_map/ppermute | solution.py:325
  40.3 4.2 %copy-start.5 = (f32[224,16]{1,0:T(8,128)}, f32[224,16]{1,0:T(8,128)S(1)}, u32[]{:S(2)}) copy-start(f32[224,16]{1,0:T(8,128)S(1)} %collective-permute-done.7.right_ref) | copy-start | bytes 43012
  44.5 0.6 %copy-start.6 = (f32[224,16]{1,0:T(8,128)}, f32[224,16]{1,0:T(8,128)S(1)}, u32[]{:S(2)}) copy-start(f32[224,16]{1,0:T(8,128)S(1)} %collective-permute-done.6.left_ref) | copy-start | bytes 43012

commit v14 on v13

--- a/solution.py
+++ b/solution.py
@@ -18,10 +18,10 @@
 
 def butterfly_sum(value, axis):
     count = lax.axis_size(axis)
-    stride = 1
-    while stride < count:
+    stride = count // 2
+    while stride >= 1:
         value = value + lax.ppermute(value, axis, [(i, i ^ stride) for i in range(count)])
-        stride *= 2
+        stride //= 2
     return value
 
 

time: 48.6 us -> 50.3 us (1.035)
  waiting for transfers between devices: 20.2 us -> 21.2 us
  starting transfers between devices: 14.9 us -> 15.8 us
    ppermute x1, starting transfers between devices: 0.01 us -> 2.47 us  [on_device(): from_right = lax.ppermute(flat(to_left), 'line', behind)]
    ppermute x4, starting transfers between devices: 12.2 us -> 11.2 us  [butterfly_sum(): lax.ppermute(value, axis, [(i, i ^ stride) for i in range(count)])]
    ppermute x4, waiting for transfers between devices: 7.65 us -> 8.56 us  [butterfly_sum(): lax.ppermute(value, axis, [(i, i ^ stride) for i in range(count)])]
    ppermute x1, waiting for transfers between devices: 4.18 us -> 3.4 us  [on_device(): from_left = lax.ppermute(flat(to_right), 'line', ahead)]
where the time goes in v14:
time: 50.3 us; the launch traced here: 50.2 us
  waiting for transfers between devices  21.2 us (42%)
  starting transfers between devices  15.8 us (31%)
  Pallas kernels  5.57 us (11%)
  local copies, waits for them, and re-layouts  4.4 us (9%)
  matrix products  2.23 us (4%)
  other arithmetic  0.66 us (1%)
    ppermute x4, starting transfers between devices, butterfly_sum(): lax.ppermute(value, axis, [(i, i ^ stride) for i in range(count)])  11.2 us
    ppermute x4, waiting for transfers between devices, butterfly_sum(): lax.ppermute(value, axis, [(i, i ^ stride) for i in range(count)])  8.56 us
    ppermute x1, waiting for transfers between devices, on_device(): above_flat = lax.ppermute(flat(bottom_row), 'curve', behind)  4.24 us
    ppermute x1, waiting for transfers between devices, on_device(): from_left = lax.ppermute(flat(to_right), 'line', ahead)  3.4 us
    pallas_call x1, Pallas kernels, stream(): pl.pallas_call(stream_kernel, out_shape=jax.ShapeDtypeStruct((seats * cha...  3.18 us
    ppermute x1, waiting for transfers between devices, on_device(): below_flat = lax.ppermute(flat(top_row), 'curve', ahead)  2.97 us
    ppermute x1, starting transfers between devices, on_device(): from_right = lax.ppermute(flat(to_left), 'line', behind)  2.47 us
    pallas_call x1, Pallas kernels, cell_moments(): pl.pallas_call(moments_kernel, out_shape=(jax.ShapeDtypeStruct((levels, b...  2.39 us
  transfers between devices with their start and end apart: 8, of which 8 were waited for; matrix products, arithmetic and copies ran while one was open for 2% of the time, Pallas kernels for 0%

profile of v14, /device:TPU:30, one launch (start us, length us, event | category | flops | bytes accessed | tf_op | source)
XLA Modules:
  0.0 50.2 jit_solution(6844293395606715129)
XLA Ops:
  0.0 2.4 %shard_map.73 = (f32[2,8,27,256]{3,2,1,0:T(8,128)}, f32[3,2,8,256]{3,2,1,0:T(8,128)}) custom-call(s32[6]{0:T(128)} %bitcast.93, f32[27,27]{1,0:T(8,128)} %constant.40.clone.forward_ref, f32[648,128]{1,0:T(8,128)} %bitcast.79), custom_call_target="tpu_custom_call" | custom-call | tf_op jit(solution)/shard_map/pallas_call | solution.py:119
  2.4 1.0 %reshape.100 = f32[3,2,2,4,16,16]{5,4,3,2,1,0:T(8,128)S(1)} reshape(f32[3,2,8,256]{3,2,1,0:T(8,128)} %get-tuple-element.8) | data formatting | bytes 98304 | tf_op jit(solution)/shard_map/reshape | solution.py:281
  3.4 0.2 copy.43
  3.6 0.2 dot_general.16
  3.9 0.2 fusion.15
  4.1 0.3 convolution_bitcast_fusion
  4.3 7.3 %collective-permute-start = (f32[3,2,32,16]{2,3,1,0:T(8,128)S(1)}, f32[3,2,32,16]{2,3,1,0:T(8,128)S(1)}, u32[]{:S(2)}, u32[]{:S(2)}) collective-permute-start(f32[3,2,32,16]{2,3,1,0:T(8,128)S(1)} %convolution_bitcast_fusion), channel_id=1, source_target_pairs={{0,8},{1,9},{2,10},{3,11},{4,12},{5,13},{6,14},{7,15},{8,0},{9,1},... | collective-permute-start | bytes 36872 | tf_op jit(solution)/shard_map/ppermute | solution.py:23
  11.6 2.1 %collective-permute-done = f32[3,2,32,16]{2,3,1,0:T(8,128)S(1)} collective-permute-done((f32[3,2,32,16]{2,3,1,0:T(8,128)S(1)}, f32[3,2,32,16]{2,3,1,0:T(8,128)S(1)}, u32[]{:S(2)}, u32[]{:S(2)}) %collective-permute-start) | collective-permute-done | bytes 12320 | tf_op jit(solution)/shard_map/ppermute | solution.py:23
  13.7 2.6 %collective-permute-start.1 = (f32[3,2,32,16]{2,3,1,0:T(8,128)S(1)}, f32[3,2,32,16]{2,3,1,0:T(8,128)S(1)}, u32[]{:S(2)}, u32[]{:S(2)}) collective-permute-start(f32[3,2,32,16]{2,3,1,0:T(8,128)S(1)} %add.43), channel_id=1, source_target_pairs={{0,4},{1,5},{2,6},{3,7},{4,0},{5,1},{6,2},{7,3},{8,12},{9,13},{10,... | collective-permute-start | bytes 36872 | tf_op jit(solution)/shard_map/ppermute | solution.py:23
  16.4 2.4 %collective-permute-done.1 = f32[3,2,32,16]{2,3,1,0:T(8,128)S(1)} collective-permute-done((f32[3,2,32,16]{2,3,1,0:T(8,128)S(1)}, f32[3,2,32,16]{2,3,1,0:T(8,128)S(1)}, u32[]{:S(2)}, u32[]{:S(2)}) %collective-permute-start.1) | collective-permute-done | bytes 12320 | tf_op jit(solution)/shard_map/ppermute | solution.py:23
  18.8 1.2 %collective-permute-start.2 = (f32[3,2,32,16]{2,3,1,0:T(8,128)S(1)}, f32[3,2,32,16]{2,3,1,0:T(8,128)S(1)}, u32[]{:S(2)}, u32[]{:S(2)}) collective-permute-start(f32[3,2,32,16]{2,3,1,0:T(8,128)S(1)} %add.44), channel_id=1, source_target_pairs={{0,2},{1,3},{2,0},{3,1},{4,6},{5,7},{6,4},{7,5},{8,10},{9,11},{10,... | collective-permute-start | bytes 36872 | tf_op jit(solution)/shard_map/ppermute | solution.py:23
  20.0 0.1 fusion.16
  20.1 2.9 %collective-permute-done.2 = f32[3,2,32,16]{2,3,1,0:T(8,128)S(1)} collective-permute-done((f32[3,2,32,16]{2,3,1,0:T(8,128)S(1)}, f32[3,2,32,16]{2,3,1,0:T(8,128)S(1)}, u32[]{:S(2)}, u32[]{:S(2)}) %collective-permute-start.2) | collective-permute-done | bytes 12320 | tf_op jit(solution)/shard_map/ppermute | solution.py:23
  23.2 1.2 %collective-permute-done.3 = f32[3,2,32,16]{2,3,1,0:T(8,128)S(1)} collective-permute-done((f32[3,2,32,16]{2,3,1,0:T(8,128)S(1)}, f32[3,2,32,16]{2,3,1,0:T(8,128)S(1)}, u32[]{:S(2)}, u32[]{:S(2)}) %collective-permute-start.3) | collective-permute-done | bytes 12320 | tf_op jit(solution)/shard_map/ppermute | solution.py:23
  24.4 1.0 %fusion = f32[3,2,2,4,16,16]{4,5,2,1,0,3:T(8,128)S(1)} fusion(f32[3,2,2,16,16,1]{4,3,2,1,0,5:T(8,128)S(1)} %bitcast.78, f32[4,16,8]{1,2,0:T(8,128)S(1)} %get-tuple-element.22, f32[4,16,8]{1,2,0:T(8,128)S(1)} %get-tuple-element.21), kind=kOutput, calls=%fused_computation.1 | convolution fusion | flops 2372608 | bytes 65536 | tf_op jit(solution)/shard_map/kzyrm,xqm->kzyxrq/dot_general | solution.py:286
  25.5 0.2 copy.46
  25.7 0.2 mul.123
  26.1 0.9 %fusion.3 = f32[2,8,256,27]{2,3,1,0:T(8,128)S(1)} fusion(f32[27,27,1,1]{1,0,3,2:T(8,128)S(1)} %copy-done.8, f32[27,2,8,256]{3,2,1,0:T(8,128)S(1)} %bitcast.75, f32[27]{0:T(128)S(1)} %copy-done.11, f32[2,8,27,256]{3,2,1,0:T(8,128)S(1)} %copy-done.1), kind=kOutput, calls=%fused_computation.9 | convolution fusion | flops 36163584 | bytes 1330128 | tf_op jit(solution)/shard_map/ij,jzpl->izpl/dot_general | solution.py:80
  27.3 0.7 %copy.51 = f32[28,2,8,256]{0,3,2,1:T(8,128)S(1)} copy(f32[28,2,8,256]{3,0,2,1:T(8,128)S(1)} %pad_maximum_fusion) | data formatting | bytes 917504 | tf_op jit(solution)/shard_map/concatenate | solution.py:294
  28.0 1.3 %collective-permute-start.4 = (f32[224,16]{1,0:T(8,128)S(1)}, f32[224,16]{1,0:T(8,128)S(1)}, u32[]{:S(2)}, u32[]{:S(2)}) collective-permute-start(f32[224,16]{1,0:T(8,128)S(1)} %bitcast.85), channel_id=1, source_target_pairs={{0,16},{16,32},{32,48},{48,64},{64,80},{80,96},{96,112},{112,128},... | collective-permute-start | bytes 43016 | tf_op jit(solution)/shard_map/ppermute | solution.py:301
  29.4 0.9 %collective-permute-start.5 = (f32[224,16]{1,0:T(8,128)S(1)}, f32[224,16]{1,0:T(8,128)S(1)}, u32[]{:S(2)}, u32[]{:S(2)}) collective-permute-start(f32[224,16]{1,0:T(8,128)S(1)} %bitcast.86), channel_id=1, source_target_pairs={{16,0},{32,16},{48,32},{64,48},{80,64},{96,80},{112,96},{128,112},... | collective-permute-start | bytes 43016 | tf_op jit(solution)/shard_map/ppermute | solution.py:302
  30.3 3.0 %collective-permute-done.4.below_ref = f32[224,16]{1,0:T(8,128)S(1)} collective-permute-done((f32[224,16]{1,0:T(8,128)S(1)}, f32[224,16]{1,0:T(8,128)S(1)}, u32[]{:S(2)}, u32[]{:S(2)}) %collective-permute-start.4) | collective-permute-done | bytes 14368 | tf_op jit(solution)/shard_map/ppermute | solution.py:301
  33.3 0.1 fusion.21
  33.5 4.2 %collective-permute-done.5.above_ref = f32[224,16]{1,0:T(8,128)S(1)} collective-permute-done((f32[224,16]{1,0:T(8,128)S(1)}, f32[224,16]{1,0:T(8,128)S(1)}, u32[]{:S(2)}, u32[]{:S(2)}) %collective-permute-start.5) | collective-permute-done | bytes 14368 | tf_op jit(solution)/shard_map/ppermute | solution.py:302
  37.8 0.1 fusion.22
  38.0 0.1 copy.56
  38.1 2.5 %collective-permute-start.7 = (f32[224,16]{1,0:T(8,128)S(1)}, f32[224,16]{1,0:T(8,128)S(1)}, u32[]{:S(2)}, u32[]{:S(2)}) collective-permute-start(f32[224,16]{1,0:T(8,128)S(1)} %bitcast.84), channel_id=1, source_target_pairs={{1,0},{2,1},{3,2},{4,3},{5,4},{6,5},{7,6},{8,7},{9,8},{10,9},{11,1... | collective-permute-start | bytes 43016 | tf_op jit(solution)/shard_map/ppermute | solution.py:326
  40.8 0.1 copy.53
  41.0 2.0 %collective-permute-done.7.right_ref = f32[224,16]{1,0:T(8,128)S(1)} collective-permute-done((f32[224,16]{1,0:T(8,128)S(1)}, f32[224,16]{1,0:T(8,128)S(1)}, u32[]{:S(2)}, u32[]{:S(2)}) %collective-permute-start.7) | collective-permute-done | bytes 14368 | tf_op jit(solution)/shard_map/ppermute | solution.py:326
  43.0 3.4 %collective-permute-done.6.left_ref = f32[224,16]{1,0:T(8,128)S(1)} collective-permute-done((f32[224,16]{1,0:T(8,128)S(1)}, f32[224,16]{1,0:T(8,128)S(1)}, u32[]{:S(2)}, u32[]{:S(2)}) %collective-permute-start.6) | collective-permute-done | bytes 14368 | tf_op jit(solution)/shard_map/ppermute | solution.py:325
  46.4 0.6 %copy-done.6 = f32[224,16]{1,0:T(8,128)} copy-done((f32[224,16]{1,0:T(8,128)}, f32[224,16]{1,0:T(8,128)S(1)}, u32[]{:S(2)}) %copy-start.6) | copy-done | bytes 14360
  47.0 3.2 %shard_map.74 = f32[648,128]{1,0:T(8,128)} custom-call(s32[6]{0:T(128)} %bitcast.94, f32[2,8,27,256]{3,2,1,0:T(8,128)} %bitcast.73, f32[224,16]{1,0:T(8,128)} %copy-done.2, f32[224,16]{1,0:T(8,128)} %copy-done.3, f32[224,16]{1,0:T(8,128)} %copy-done.6, f32[224,16]{1,0:T(8,128)} %copy-done.5), custom_call_target="tpu_custom_call" | custom-call | tf_op jit(solution)/shard_map/pallas_call | solution.py:245
  (57 shorter events, 1.3 us)
Async XLA Ops:
  0.0 20.0 %copy-start.9 = (s32[1,1,6]{2,1,0:T(1,128)S(1)}, s32[1,1,6]{2,1,0:T(1,128)}, u32[]{:S(2)}) copy-start(s32[1,1,6]{2,1,0:T(1,128)} %param.8) | copy-start | bytes 76
  0.0 3.9 %copy-start.10 = (s32[8]{0:T(128)S(1)}, s32[8]{0:T(128)}, u32[]{:S(2)}) copy-start(s32[8]{0:T(128)} %param.9) | copy-start | bytes 100
  0.0 24.3 %copy-start.7 = (f32[3,2,32,16]{2,3,1,0:T(8,128)S(1)}, f32[3,2,32,16]{2,3,1,0:T(8,128)}, u32[]{:S(2)}) copy-start(f32[3,2,32,16]{2,3,1,0:T(8,128)} %param.10) | copy-start | bytes 36868
  2.4 20.7 %copy-start.1 = (f32[2,8,27,256]{3,2,1,0:T(8,128)S(1)}, f32[2,8,27,256]{3,2,1,0:T(8,128)}, u32[]{:S(2)}) copy-start(f32[2,8,27,256]{3,2,1,0:T(8,128)} %get-tuple-element.7) | copy-start | bytes 1327108
  3.4 22.4 %copy-start.4 = (f32[3,2,8,256]{3,2,1,0:T(8,128)S(1)}, f32[3,2,8,256]{3,2,1,0:T(8,128)}, u32[]{:S(2)}) copy-start(f32[3,2,8,256]{3,2,1,0:T(8,128)} %get-tuple-element.8) | copy-start | bytes 147460
  4.3 9.4 %collective-permute-start = (f32[3,2,32,16]{2,3,1,0:T(8,128)S(1)}, f32[3,2,32,16]{2,3,1,0:T(8,128)S(1)}, u32[]{:S(2)}, u32[]{:S(2)}) collective-permute-start(f32[3,2,32,16]{2,3,1,0:T(8,128)S(1)} %convolution_bitcast_fusion), channel_id=1, source_target_pairs={{0,8},{1,9},{2,10},{3,11},{4,12},{5,13},{6,14},{7,15},{8,0},{9,1},... | collective-permute-start | bytes 36872 | tf_op jit(solution)/shard_map/ppermute | solution.py:23
  13.7 12.4 %copy-start.8 = (f32[27,27,1,1]{1,0,3,2:T(8,128)S(1)}, f32[27,27,1,1]{1,0,3,2:T(8,128)}, u32[]{:S(2)}) copy-start(f32[27,27,1,1]{1,0,3,2:T(8,128)} %constant.44) | copy-start | bytes 8752
  13.7 12.4 %copy-start.11 = (f32[27]{0:T(128)S(1)}, f32[27]{0:T(128)}, u32[]{:S(2)}) copy-start(f32[27]{0:T(128)} %param.11) | copy-start | bytes 328
  13.7 5.1 %collective-permute-start.1 = (f32[3,2,32,16]{2,3,1,0:T(8,128)S(1)}, f32[3,2,32,16]{2,3,1,0:T(8,128)S(1)}, u32[]{:S(2)}, u32[]{:S(2)}) collective-permute-start(f32[3,2,32,16]{2,3,1,0:T(8,128)S(1)} %add.43), channel_id=1, source_target_pairs={{0,4},{1,5},{2,6},{3,7},{4,0},{5,1},{6,2},{7,3},{8,12},{9,13},{10,... | collective-permute-start | bytes 36872 | tf_op jit(solution)/shard_map/ppermute | solution.py:23
  18.8 4.2 %collective-permute-start.2 = (f32[3,2,32,16]{2,3,1,0:T(8,128)S(1)}, f32[3,2,32,16]{2,3,1,0:T(8,128)S(1)}, u32[]{:S(2)}, u32[]{:S(2)}) collective-permute-start(f32[3,2,32,16]{2,3,1,0:T(8,128)S(1)} %add.44), channel_id=1, source_target_pairs={{0,2},{1,3},{2,0},{3,1},{4,6},{5,7},{6,4},{7,5},{8,10},{9,11},{10,... | collective-permute-start | bytes 36872 | tf_op jit(solution)/shard_map/ppermute | solution.py:23
  23.0 1.3 %collective-permute-start.3 = (f32[3,2,32,16]{2,3,1,0:T(8,128)S(1)}, f32[3,2,32,16]{2,3,1,0:T(8,128)S(1)}, u32[]{:S(2)}, u32[]{:S(2)}) collective-permute-start(f32[3,2,32,16]{2,3,1,0:T(8,128)S(1)} %add.45), channel_id=1, source_target_pairs={{0,1},{1,0},{2,3},{3,2},{4,5},{5,4},{6,7},{7,6},{8,9},{9,8},{10,11... | collective-permute-start | bytes 36872 | tf_op jit(solution)/shard_map/ppermute | solution.py:23
  27.0 0.9 %copy-start = (f32[2,8,256,27]{2,3,1,0:T(8,128)}, f32[2,8,256,27]{2,3,1,0:T(8,128)S(1)}, u32[]{:S(2)}) copy-start(f32[2,8,256,27]{2,3,1,0:T(8,128)S(1)} %fusion.3) | copy-start | bytes 1327108
  28.0 5.3 %collective-permute-start.4 = (f32[224,16]{1,0:T(8,128)S(1)}, f32[224,16]{1,0:T(8,128)S(1)}, u32[]{:S(2)}, u32[]{:S(2)}) collective-permute-start(f32[224,16]{1,0:T(8,128)S(1)} %bitcast.85), channel_id=1, source_target_pairs={{0,16},{16,32},{32,48},{48,64},{64,80},{80,96},{96,112},{112,128},... | collective-permute-start | bytes 43016 | tf_op jit(solution)/shard_map/ppermute | solution.py:301
  29.4 8.3 %collective-permute-start.5 = (f32[224,16]{1,0:T(8,128)S(1)}, f32[224,16]{1,0:T(8,128)S(1)}, u32[]{:S(2)}, u32[]{:S(2)}) collective-permute-start(f32[224,16]{1,0:T(8,128)S(1)} %bitcast.86), channel_id=1, source_target_pairs={{16,0},{32,16},{48,32},{64,48},{80,64},{96,80},{112,96},{128,112},... | collective-permute-start | bytes 43016 | tf_op jit(solution)/shard_map/ppermute | solution.py:302
  33.3 13.1 %copy-start.2 = (f32[224,16]{1,0:T(8,128)}, f32[224,16]{1,0:T(8,128)S(1)}, u32[]{:S(2)}) copy-start(f32[224,16]{1,0:T(8,128)S(1)} %collective-permute-done.4.below_ref) | copy-start | bytes 43012
  37.8 8.6 %copy-start.3 = (f32[224,16]{1,0:T(8,128)}, f32[224,16]{1,0:T(8,128)S(1)}, u32[]{:S(2)}) copy-start(f32[224,16]{1,0:T(8,128)S(1)} %collective-permute-done.5.above_ref) | copy-start | bytes 43012
  38.1 4.8 %collective-permute-start.7 = (f32[224,16]{1,0:T(8,128)S(1)}, f32[224,16]{1,0:T(8,128)S(1)}, u32[]{:S(2)}, u32[]{:S(2)}) collective-permute-start(f32[224,16]{1,0:T(8,128)S(1)} %bitcast.84), channel_id=1, source_target_pairs={{1,0},{2,1},{3,2},{4,3},{5,4},{6,5},{7,6},{8,7},{9,8},{10,9},{11,1... | collective-permute-start | bytes 43016 | tf_op jit(solution)/shard_map/ppermute | solution.py:326
  40.9 5.4 %collective-permute-start.6 = (f32[224,16]{1,0:T(8,128)S(1)}, f32[224,16]{1,0:T(8,128)S(1)}, u32[]{:S(2)}, u32[]{:S(2)}) collective-permute-start(f32[224,16]{1,0:T(8,128)S(1)} %bitcast.87), channel_id=1, source_target_pairs={{0,1},{1,2},{2,3},{3,4},{4,5},{5,6},{6,7},{7,8},{8,9},{9,10},{10,1... | collective-permute-start | bytes 43016 | tf_op jit(solution)/shard_map/ppermute | solution.py:325
  43.0 3.4 %copy-start.5 = (f32[224,16]{1,0:T(8,128)}, f32[224,16]{1,0:T(8,128)S(1)}, u32[]{:S(2)}) copy-start(f32[224,16]{1,0:T(8,128)S(1)} %collective-permute-done.7.right_ref) | copy-start | bytes 43012
  46.4 0.6 %copy-start.6 = (f32[224,16]{1,0:T(8,128)}, f32[224,16]{1,0:T(8,128)S(1)}, u32[]{:S(2)}) copy-start(f32[224,16]{1,0:T(8,128)S(1)} %collective-permute-done.6.left_ref) | copy-start | bytes 43012

commit v15 on v13

--- a/solution.py
+++ b/solution.py
@@ -293,37 +293,34 @@
     solid = jnp.broadcast_to((1.0 - fluid)[None, None, :, None], (1, levels, blocks, cells))
     extended = jnp.concatenate([post, solid], axis=0)
     width = channels + 1
-    ahead, behind = ring_pairs("curve")
     flat = lambda halo: halo.reshape(-1, BE)
-    halo_shape = (width, levels, TX, BE)
-    top_row = extended[:, :, blocks - TX:, cells - BE:]
-    bottom_row = extended[:, :, :TX, :BE]
-    below_flat = lax.ppermute(flat(top_row), "curve", ahead)
-    above_flat = lax.ppermute(flat(bottom_row), "curve", behind)
-    below = below_flat.reshape(halo_shape)
-    above = above_flat.reshape(halo_shape)
     ahead, behind = ring_pairs("line")
     by_rows = extended.reshape(width, levels, TY, TX, BE, BE)
-    right_cols = by_rows[:, :, :, TX - 1, :, BE - 1]
-    left_cols = by_rows[:, :, :, 0, :, 0]
-    to_right = jnp.concatenate(
+    column_shape = (width, levels, TY, BE)
+    left_cols = lax.ppermute(flat(by_rows[:, :, :, TX - 1, :, BE - 1]), "line", ahead).reshape(column_shape)
+    right_cols = lax.ppermute(flat(by_rows[:, :, :, 0, :, 0]), "line", behind).reshape(column_shape)
+    corner = lambda cols, py, r: jnp.broadcast_to(cols[:, :, py:py + 1, r:r + 1], (width, levels, 1, BE))
+    top_row = jnp.concatenate(
         [
-            jnp.broadcast_to(below[:, :, TX - 1:, BE - 1:], (width, levels, 1, BE)),
-            right_cols,
-            jnp.broadcast_to(above[:, :, TX - 1:, BE - 1:], (width, levels, 1, BE)),
+            corner(left_cols, TY - 1, BE - 1),
+            extended[:, :, blocks - TX:, cells - BE:],
+            corner(right_cols, TY - 1, BE - 1),
         ],
         axis=2,
     )
-    to_left = jnp.concatenate(
-        [
-            jnp.broadcast_to(below[:, :, :1, :1], (width, levels, 1, BE)),
-            left_cols,
-            jnp.broadcast_to(above[:, :, :1, :1], (width, levels, 1, BE)),
-        ],
-        axis=2,
-    )
-    from_left = lax.ppermute(flat(to_right), "line", ahead)
-    from_right = lax.ppermute(flat(to_left), "line", behind)
+    bottom_row = jnp.concatenate(
+        [corner(left_cols, 0, 0), extended[:, :, :TX, :BE], corner(right_cols, 0, 0)], axis=2
+    )
+    ahead, behind = ring_pairs("curve")
+    row_shape = (width, levels, TX + 2, BE)
+    below = lax.ppermute(flat(top_row), "curve", ahead).reshape(row_shape)
+    above = lax.ppermute(flat(bottom_row), "curve", behind).reshape(row_shape)
+    below_flat = flat(below[:, :, 1:TX + 1])
+    above_flat = flat(above[:, :, 1:TX + 1])
+    from_left = flat(jnp.concatenate([below[:, :, :1], left_cols, above[:, :, :1]], axis=2))
+    from_right = flat(
+        jnp.concatenate([below[:, :, TX + 1:], right_cols, above[:, :, TX + 1:]], axis=2)
+    )
     new_state = stream(living_brick_keys, post, below_flat, above_flat, from_left, from_right)
     return new_state.reshape((1, 1, seats, channels, levels * cells))
 

time: 48.6 us -> 50.3 us (1.035); the launches traced: 48.3 us -> 49.5 us
  waiting for transfers between devices: 20.2 us -> 16.2 us
  starting transfers between devices: 14.9 us -> 17.4 us
  other arithmetic: 0.66 us -> 2.19 us
  local copies, waits for them, and re-layouts: 4.4 us -> 5.6 us
    ppermute x4, waiting for transfers between devices: 12.6 us -> 8.55 us  [the longest x1 3.92 us: on_device(): below = lax.ppermute(flat(top_row), 'curve', ahead).reshape(row_shape)]
    ppermute x4, starting transfers between devices: 2.7 us -> 5.15 us  [the longest x1 2.95 us: on_device(): lax.ppermute(flat(by_rows[:, :, :, 0, :, 0]), 'line', behind)]
    slice x5 -> x13, local copies, waits for them, and re-layouts: 0.43 us -> 2.34 us  [the longest x1 0.69 us: on_device(): below_flat = flat(below[:, :, 1:TX + 1])]
    concatenate x2 -> x3, other arithmetic: 0.02 us -> 1.54 us  [the longest x1 0.75 us: on_device(): jnp.concatenate([below[:, :, TX + 1:], right_cols, above[:, :, TX + 1:]],...]
    unnamed x29 -> x17, local copies, waits for them, and re-layouts: 1.06 us -> 0.04 us
  transfers between devices with their start and end apart: 8 -> 8, of which waited for: 8 -> 7; matrix products, arithmetic and copies ran while one was open for 2% -> 3% of each run, Pallas kernels for 0% -> 0%
where the time goes in v15:
time: 50.3 us; the launch traced here: 49.5 us
  starting transfers between devices  17.4 us (35%)
  waiting for transfers between devices  16.2 us (32%)
  local copies, waits for them, and re-layouts  5.6 us (11%)
  Pallas kernels  5.57 us (11%)
  matrix products  2.23 us (4%)
  other arithmetic  2.19 us (4%)
    ppermute x4, starting transfers between devices, butterfly_sum(): lax.ppermute(value, axis, [(i, i ^ stride) for i in range(count)])  12.2 us
    ppermute x4, waiting for transfers between devices, butterfly_sum(): lax.ppermute(value, axis, [(i, i ^ stride) for i in range(count)])  7.65 us
    ppermute x1, waiting for transfers between devices, on_device(): below = lax.ppermute(flat(top_row), 'curve', ahead).reshape(row_shape)  3.92 us
    pallas_call x1, Pallas kernels, stream(): pl.pallas_call(stream_kernel, out_shape=jax.ShapeDtypeStruct((seats * cha...  3.18 us
    ppermute x1, waiting for transfers between devices, on_device(): above = lax.ppermute(flat(bottom_row), 'curve', behind).reshape(row_shape)  3 us
    ppermute x1, starting transfers between devices, on_device(): lax.ppermute(flat(by_rows[:, :, :, 0, :, 0]), 'line', behind)  2.95 us
    pallas_call x1, Pallas kernels, cell_moments(): pl.pallas_call(moments_kernel, out_shape=(jax.ShapeDtypeStruct((levels, b...  2.39 us
    ppermute x1, waiting for transfers between devices, on_device(): lax.ppermute(flat(by_rows[:, :, :, TX - 1, :, BE - 1]), 'line', ahead)  1.62 us
  transfers between devices with their start and end apart: 8, of which 7 were waited for; matrix products, arithmetic and copies ran while one was open for 3% of the time, Pallas kernels for 0%

profile of v15, /device:TPU:30, one launch (start us, length us, event | category | flops | bytes accessed | tf_op | source)
XLA Modules:
  0.0 49.5 jit_solution(9651546616734305703)
XLA Ops:
  0.0 2.4 %shard_map.73 = (f32[2,8,27,256]{3,2,1,0:T(8,128)}, f32[3,2,8,256]{3,2,1,0:T(8,128)}) custom-call(s32[6]{0:T(128)} %bitcast.95, f32[27,27]{1,0:T(8,128)} %constant.40.clone.forward_ref, f32[648,128]{1,0:T(8,128)} %bitcast.83), custom_call_target="tpu_custom_call" | custom-call | tf_op jit(solution)/shard_map/pallas_call | solution.py:119
  2.4 1.0 %reshape.112 = f32[3,2,2,4,16,16]{5,4,3,2,1,0:T(8,128)S(1)} reshape(f32[3,2,8,256]{3,2,1,0:T(8,128)} %get-tuple-element.8) | data formatting | bytes 98304 | tf_op jit(solution)/shard_map/reshape | solution.py:281
  3.4 0.2 copy.35
  3.6 0.2 dot_general.16
  3.9 0.2 fusion.15
  4.1 0.3 convolution_bitcast_fusion
  4.4 1.2 %collective-permute-done = f32[3,2,32,16]{2,3,1,0:T(8,128)S(1)} collective-permute-done((f32[3,2,32,16]{2,3,1,0:T(8,128)S(1)}, f32[3,2,32,16]{2,3,1,0:T(8,128)S(1)}, u32[]{:S(2)}, u32[]{:S(2)}) %collective-permute-start) | collective-permute-done | bytes 12320 | tf_op jit(solution)/shard_map/ppermute | solution.py:23
  5.7 2.0 %collective-permute-start.1 = (f32[3,2,32,16]{2,3,1,0:T(8,128)S(1)}, f32[3,2,32,16]{2,3,1,0:T(8,128)S(1)}, u32[]{:S(2)}, u32[]{:S(2)}) collective-permute-start(f32[3,2,32,16]{2,3,1,0:T(8,128)S(1)} %add.43), channel_id=1, source_target_pairs={{0,2},{1,3},{2,0},{3,1},{4,6},{5,7},{6,4},{7,5},{8,10},{9,11},{10,... | collective-permute-start | bytes 36872 | tf_op jit(solution)/shard_map/ppermute | solution.py:23
  7.7 2.2 %collective-permute-done.1 = f32[3,2,32,16]{2,3,1,0:T(8,128)S(1)} collective-permute-done((f32[3,2,32,16]{2,3,1,0:T(8,128)S(1)}, f32[3,2,32,16]{2,3,1,0:T(8,128)S(1)}, u32[]{:S(2)}, u32[]{:S(2)}) %collective-permute-start.1) | collective-permute-done | bytes 12320 | tf_op jit(solution)/shard_map/ppermute | solution.py:23
  9.9 3.4 %collective-permute-start.2 = (f32[3,2,32,16]{2,3,1,0:T(8,128)S(1)}, f32[3,2,32,16]{2,3,1,0:T(8,128)S(1)}, u32[]{:S(2)}, u32[]{:S(2)}) collective-permute-start(f32[3,2,32,16]{2,3,1,0:T(8,128)S(1)} %add.44), channel_id=1, source_target_pairs={{0,4},{1,5},{2,6},{3,7},{4,0},{5,1},{6,2},{7,3},{8,12},{9,13},{10,... | collective-permute-start | bytes 36872 | tf_op jit(solution)/shard_map/ppermute | solution.py:23
  13.2 0.1 fusion.16
  13.4 2.1 %collective-permute-done.2 = f32[3,2,32,16]{2,3,1,0:T(8,128)S(1)} collective-permute-done((f32[3,2,32,16]{2,3,1,0:T(8,128)S(1)}, f32[3,2,32,16]{2,3,1,0:T(8,128)S(1)}, u32[]{:S(2)}, u32[]{:S(2)}) %collective-permute-start.2) | collective-permute-done | bytes 12320 | tf_op jit(solution)/shard_map/ppermute | solution.py:23
  15.5 6.8 %collective-permute-start.3 = (f32[3,2,32,16]{2,3,1,0:T(8,128)S(1)}, f32[3,2,32,16]{2,3,1,0:T(8,128)S(1)}, u32[]{:S(2)}, u32[]{:S(2)}) collective-permute-start(f32[3,2,32,16]{2,3,1,0:T(8,128)S(1)} %add.45), channel_id=1, source_target_pairs={{0,8},{1,9},{2,10},{3,11},{4,12},{5,13},{6,14},{7,15},{8,0},{9,1},... | collective-permute-start | bytes 36872 | tf_op jit(solution)/shard_map/ppermute | solution.py:23
  22.3 2.1 %collective-permute-done.3 = f32[3,2,32,16]{2,3,1,0:T(8,128)S(1)} collective-permute-done((f32[3,2,32,16]{2,3,1,0:T(8,128)S(1)}, f32[3,2,32,16]{2,3,1,0:T(8,128)S(1)}, u32[]{:S(2)}, u32[]{:S(2)}) %collective-permute-start.3) | collective-permute-done | bytes 12320 | tf_op jit(solution)/shard_map/ppermute | solution.py:23
  24.5 1.0 %fusion = f32[3,2,2,4,16,16]{4,5,2,1,0,3:T(8,128)S(1)} fusion(f32[3,2,2,16,16,1]{4,3,2,1,0,5:T(8,128)S(1)} %bitcast.82, f32[4,16,8]{1,2,0:T(8,128)S(1)} %get-tuple-element.26, f32[4,16,8]{1,2,0:T(8,128)S(1)} %get-tuple-element.25), kind=kOutput, calls=%fused_computation.1 | convolution fusion | flops 2372608 | bytes 65536 | tf_op jit(solution)/shard_map/kzyrm,xqm->kzyxrq/dot_general | solution.py:286
  25.6 0.2 copy.38
  25.8 0.2 mul.123
  26.2 0.9 %fusion.3 = f32[2,8,256,27]{2,3,1,0:T(8,128)S(1)} fusion(f32[27,27,1,1]{1,0,3,2:T(8,128)S(1)} %copy-done.4, f32[27,2,8,256]{3,2,1,0:T(8,128)S(1)} %bitcast.75, f32[27]{0:T(128)S(1)} %copy-done.7, f32[2,8,27,256]{3,2,1,0:T(8,128)S(1)} %copy-done.1), kind=kOutput, calls=%fused_computation.9 | convolution fusion | flops 36163584 | bytes 1330128 | tf_op jit(solution)/shard_map/ij,jzpl->izpl/dot_general | solution.py:80
  27.3 0.6 %copy.40 = f32[28,2,8,256]{0,3,2,1:T(8,128)S(1)} copy(f32[28,2,8,256]{3,0,2,1:T(8,128)S(1)} %pad_maximum_fusion) | data formatting | bytes 917504 | tf_op jit(solution)/shard_map/concatenate | solution.py:294
  28.3 3.0 %collective-permute-start.5 = (f32[112,16]{1,0:T(8,128)S(1)}, f32[112,16]{1,0:T(8,128)S(1)}, u32[]{:S(2)}, u32[]{:S(2)}) collective-permute-start(f32[112,16]{1,0:T(8,128)S(1)} %bitcast.90), channel_id=1, source_target_pairs={{1,0},{2,1},{3,2},{4,3},{5,4},{6,5},{7,6},{8,7},{9,8},{10,9},{11,1... | collective-permute-start | bytes 21512 | tf_op jit(solution)/shard_map/ppermute | solution.py:301
  31.3 1.6 %collective-permute-done.4 = f32[112,16]{1,0:T(8,128)S(1)} collective-permute-done((f32[112,16]{1,0:T(8,128)S(1)}, f32[112,16]{1,0:T(8,128)S(1)}, u32[]{:S(2)}, u32[]{:S(2)}) %collective-permute-start.4) | collective-permute-done | bytes 7200 | tf_op jit(solution)/shard_map/ppermute | solution.py:300
  32.9 0.1 fusion.23
  33.1 0.1 fusion.24
  34.0 1.1 %collective-permute-start.6 = (f32[336,16]{1,0:T(8,128)S(1)}, f32[336,16]{1,0:T(8,128)S(1)}, u32[]{:S(2)}, u32[]{:S(2)}) collective-permute-start(f32[336,16]{1,0:T(8,128)S(1)} %reshape.117), channel_id=1, source_target_pairs={{0,16},{16,32},{32,48},{48,64},{64,80},{80,96},{96,112},{112,128},... | collective-permute-start | bytes 64520 | tf_op jit(solution)/shard_map/ppermute | solution.py:316
  35.3 1.1 %collective-permute-start.7 = (f32[336,16]{1,0:T(8,128)S(1)}, f32[336,16]{1,0:T(8,128)S(1)}, u32[]{:S(2)}, u32[]{:S(2)}) collective-permute-start(f32[336,16]{1,0:T(8,128)S(1)} %reshape.120), channel_id=1, source_target_pairs={{16,0},{32,16},{48,32},{64,48},{80,64},{96,80},{112,96},{128,112},... | collective-permute-start | bytes 64520 | tf_op jit(solution)/shard_map/ppermute | solution.py:317
  36.4 3.9 %collective-permute-done.6 = f32[336,16]{1,0:T(8,128)S(1)} collective-permute-done((f32[336,16]{1,0:T(8,128)S(1)}, f32[336,16]{1,0:T(8,128)S(1)}, u32[]{:S(2)}, u32[]{:S(2)}) %collective-permute-start.6) | collective-permute-done | bytes 21536 | tf_op jit(solution)/shard_map/ppermute | solution.py:316
  40.4 0.7 %slice.82 = f32[28,2,4,16]{3,2,1,0:T(4,128)} slice(f32[28,2,6,16]{3,2,1,0:T(8,128)S(1)} %reshape.118), slice={[0:28], [0:2], [1:5], [0:16]} | slice | bytes 28672 | tf_op jit(solution)/shard_map/slice | solution.py:318
  41.1 3.0 %collective-permute-done.7 = f32[336,16]{1,0:T(8,128)S(1)} collective-permute-done((f32[336,16]{1,0:T(8,128)S(1)}, f32[336,16]{1,0:T(8,128)S(1)}, u32[]{:S(2)}, u32[]{:S(2)}) %collective-permute-start.7) | collective-permute-done | bytes 21536 | tf_op jit(solution)/shard_map/ppermute | solution.py:317
  44.1 0.7 %slice.87 = f32[28,2,4,16]{3,2,1,0:T(4,128)} slice(f32[28,2,6,16]{3,2,1,0:T(8,128)S(1)} %reshape.121), slice={[0:28], [0:2], [1:5], [0:16]} | slice | bytes 28672 | tf_op jit(solution)/shard_map/slice | solution.py:319
  44.8 0.7 %pad_maximum_fusion.5 = f32[28,2,4,16]{3,2,1,0:T(4,128)} fusion(f32[28,2,1,16]{3,2,1,0:T(1,128)S(1)} %get-tuple-element.15, f32[28,2,2,16]{3,2,1,0:T(2,128)S(1)} %bitcast.87, f32[28,2,1,16]{3,2,1,0:T(1,128)S(1)} %get-tuple-element.13), kind=kLoop, calls=%fused_computation.20 | loop fusion | flops 7168 | bytes 28672 | tf_op jit(solution)/shard_map/concatenate | solution.py:322
  45.6 0.7 %pad_maximum_fusion.4 = f32[28,2,4,16]{3,2,1,0:T(4,128)} fusion(f32[28,2,1,16]{3,2,1,0:T(1,128)S(1)} %get-tuple-element.16, f32[28,2,2,16]{3,2,1,0:T(2,128)S(1)} %bitcast.85, f32[28,2,1,16]{3,2,1,0:T(1,128)S(1)} %get-tuple-element.14), kind=kLoop, calls=%fused_computation.19 | loop fusion | flops 7168 | bytes 28672 | tf_op jit(solution)/shard_map/concatenate | solution.py:320
  46.3 3.2 %shard_map.74 = f32[648,128]{1,0:T(8,128)} custom-call(s32[6]{0:T(128)} %bitcast.96, f32[2,8,27,256]{3,2,1,0:T(8,128)} %bitcast.73, f32[224,16]{1,0:T(8,128)} %bitcast.78, f32[224,16]{1,0:T(8,128)} %bitcast.79, f32[224,16]{1,0:T(8,128)} %bitcast.81, f32[224,16]{1,0:T(8,128)} %bitcast.80), custom_call_target="tpu_custom_call" | custom-call | tf_op jit(solution)/shard_map/pallas_call | solution.py:245
  (58 shorter events, 2.1 us)
Async XLA Ops:
  0.0 13.2 %copy-start.5 = (s32[1,1,6]{2,1,0:T(1,128)S(1)}, s32[1,1,6]{2,1,0:T(1,128)}, u32[]{:S(2)}) copy-start(s32[1,1,6]{2,1,0:T(1,128)} %param.8) | copy-start | bytes 76
  0.0 3.9 %copy-start.6 = (s32[8]{0:T(128)S(1)}, s32[8]{0:T(128)}, u32[]{:S(2)}) copy-start(s32[8]{0:T(128)} %param.9) | copy-start | bytes 100
  0.0 24.4 %copy-start.3 = (f32[3,2,32,16]{2,3,1,0:T(8,128)S(1)}, f32[3,2,32,16]{2,3,1,0:T(8,128)}, u32[]{:S(2)}) copy-start(f32[3,2,32,16]{2,3,1,0:T(8,128)} %param.10) | copy-start | bytes 36868
  2.4 19.9 %copy-start.1 = (f32[2,8,27,256]{3,2,1,0:T(8,128)S(1)}, f32[2,8,27,256]{3,2,1,0:T(8,128)}, u32[]{:S(2)}) copy-start(f32[2,8,27,256]{3,2,1,0:T(8,128)} %get-tuple-element.7) | copy-start | bytes 1327108
  3.4 22.5 %copy-start.2 = (f32[3,2,8,256]{3,2,1,0:T(8,128)S(1)}, f32[3,2,8,256]{3,2,1,0:T(8,128)}, u32[]{:S(2)}) copy-start(f32[3,2,8,256]{3,2,1,0:T(8,128)} %get-tuple-element.8) | copy-start | bytes 147460
  4.3 1.3 %collective-permute-start = (f32[3,2,32,16]{2,3,1,0:T(8,128)S(1)}, f32[3,2,32,16]{2,3,1,0:T(8,128)S(1)}, u32[]{:S(2)}, u32[]{:S(2)}) collective-permute-start(f32[3,2,32,16]{2,3,1,0:T(8,128)S(1)} %convolution_bitcast_fusion), channel_id=1, source_target_pairs={{0,1},{1,0},{2,3},{3,2},{4,5},{5,4},{6,7},{7,6},{8,9},{9,8},{10,11... | collective-permute-start | bytes 36872 | tf_op jit(solution)/shard_map/ppermute | solution.py:23
  5.7 20.5 %copy-start.4 = (f32[27,27,1,1]{1,0,3,2:T(8,128)S(1)}, f32[27,27,1,1]{1,0,3,2:T(8,128)}, u32[]{:S(2)}) copy-start(f32[27,27,1,1]{1,0,3,2:T(8,128)} %constant.44) | copy-start | bytes 8752
  5.7 20.5 %copy-start.7 = (f32[27]{0:T(128)S(1)}, f32[27]{0:T(128)}, u32[]{:S(2)}) copy-start(f32[27]{0:T(128)} %param.11) | copy-start | bytes 328
  5.7 4.2 %collective-permute-start.1 = (f32[3,2,32,16]{2,3,1,0:T(8,128)S(1)}, f32[3,2,32,16]{2,3,1,0:T(8,128)S(1)}, u32[]{:S(2)}, u32[]{:S(2)}) collective-permute-start(f32[3,2,32,16]{2,3,1,0:T(8,128)S(1)} %add.43), channel_id=1, source_target_pairs={{0,2},{1,3},{2,0},{3,1},{4,6},{5,7},{6,4},{7,5},{8,10},{9,11},{10,... | collective-permute-start | bytes 36872 | tf_op jit(solution)/shard_map/ppermute | solution.py:23
  9.9 5.6 %collective-permute-start.2 = (f32[3,2,32,16]{2,3,1,0:T(8,128)S(1)}, f32[3,2,32,16]{2,3,1,0:T(8,128)S(1)}, u32[]{:S(2)}, u32[]{:S(2)}) collective-permute-start(f32[3,2,32,16]{2,3,1,0:T(8,128)S(1)} %add.44), channel_id=1, source_target_pairs={{0,4},{1,5},{2,6},{3,7},{4,0},{5,1},{6,2},{7,3},{8,12},{9,13},{10,... | collective-permute-start | bytes 36872 | tf_op jit(solution)/shard_map/ppermute | solution.py:23
  15.5 8.9 %collective-permute-start.3 = (f32[3,2,32,16]{2,3,1,0:T(8,128)S(1)}, f32[3,2,32,16]{2,3,1,0:T(8,128)S(1)}, u32[]{:S(2)}, u32[]{:S(2)}) collective-permute-start(f32[3,2,32,16]{2,3,1,0:T(8,128)S(1)} %add.45), channel_id=1, source_target_pairs={{0,8},{1,9},{2,10},{3,11},{4,12},{5,13},{6,14},{7,15},{8,0},{9,1},... | collective-permute-start | bytes 36872 | tf_op jit(solution)/shard_map/ppermute | solution.py:23
  27.1 1.1 %copy-start = (f32[2,8,256,27]{2,3,1,0:T(8,128)}, f32[2,8,256,27]{2,3,1,0:T(8,128)S(1)}, u32[]{:S(2)}) copy-start(f32[2,8,256,27]{2,3,1,0:T(8,128)S(1)} %fusion.3) | copy-start | bytes 1327108
  28.1 4.8 %collective-permute-start.4 = (f32[112,16]{1,0:T(8,128)S(1)}, f32[112,16]{1,0:T(8,128)S(1)}, u32[]{:S(2)}, u32[]{:S(2)}) collective-permute-start(f32[112,16]{1,0:T(8,128)S(1)} %bitcast.89), channel_id=1, source_target_pairs={{0,1},{1,2},{2,3},{3,4},{4,5},{5,6},{6,7},{7,8},{8,9},{9,10},{10,1... | collective-permute-start | bytes 21512 | tf_op jit(solution)/shard_map/ppermute | solution.py:300
  28.3 4.8 %collective-permute-start.5 = (f32[112,16]{1,0:T(8,128)S(1)}, f32[112,16]{1,0:T(8,128)S(1)}, u32[]{:S(2)}, u32[]{:S(2)}) collective-permute-start(f32[112,16]{1,0:T(8,128)S(1)} %bitcast.90), channel_id=1, source_target_pairs={{1,0},{2,1},{3,2},{4,3},{5,4},{6,5},{7,6},{8,7},{9,8},{10,9},{11,1... | collective-permute-start | bytes 21512 | tf_op jit(solution)/shard_map/ppermute | solution.py:301
  34.0 6.2 %collective-permute-start.6 = (f32[336,16]{1,0:T(8,128)S(1)}, f32[336,16]{1,0:T(8,128)S(1)}, u32[]{:S(2)}, u32[]{:S(2)}) collective-permute-start(f32[336,16]{1,0:T(8,128)S(1)} %reshape.117), channel_id=1, source_target_pairs={{0,16},{16,32},{32,48},{48,64},{64,80},{80,96},{96,112},{112,128},... | collective-permute-start | bytes 64520 | tf_op jit(solution)/shard_map/ppermute | solution.py:316
  35.3 8.8 %collective-permute-start.7 = (f32[336,16]{1,0:T(8,128)S(1)}, f32[336,16]{1,0:T(8,128)S(1)}, u32[]{:S(2)}, u32[]{:S(2)}) collective-permute-start(f32[336,16]{1,0:T(8,128)S(1)} %reshape.120), channel_id=1, source_target_pairs={{16,0},{32,16},{48,32},{64,48},{80,64},{96,80},{112,96},{128,112},... | collective-permute-start | bytes 64520 | tf_op jit(solution)/shard_map/ppermute | solution.py:317

commit v16 on v15

--- a/solution.py
+++ b/solution.py
@@ -129,7 +129,7 @@
 
 
 def stream_kernel(
-    keys_ref, post_ref, below_ref, above_ref, left_ref, right_ref, out_ref, spread_ref, result_ref
+    keys_ref, post_ref, below_ref, above_ref, left_ref, right_ref, out_ref, spread_ref, column_ref, result_ref
 ):
     levels, blocks, channels, cells = post_ref.shape
     _, _, speeds = lattice_tables()
@@ -138,12 +138,15 @@
     grid_lane = lax.broadcasted_iota(jnp.int32, (BE, cells), 1)
     tile_copy = (grid_lane % BE == grid_row).astype(jnp.float32)
     group_copy = (grid_lane // BE == grid_row).astype(jnp.float32)
-    halo_rows = below_ref.shape[0]
-    for slot, (source, copier) in enumerate(
-        ((below_ref, tile_copy), (above_ref, tile_copy), (left_ref, group_copy), (right_ref, group_copy))
-    ):
-        spread_ref[slot, front:front + halo_rows, :] = jnp.dot(
-            source[...], copier, precision=HIGHEST, preferred_element_type=jnp.float32
+    row_count = below_ref.shape[0]
+    column_count = left_ref.shape[0]
+    for slot, source in enumerate((below_ref, above_ref)):
+        spread_ref[slot, front:front + row_count, :] = jnp.dot(
+            source[...], tile_copy, precision=HIGHEST, preferred_element_type=jnp.float32
+        )
+    for slot, source in enumerate((left_ref, right_ref)):
+        column_ref[slot, front:front + column_count, :] = jnp.dot(
+            source[...], group_copy, precision=HIGHEST, preferred_element_type=jnp.float32
         )
     lane = lax.broadcasted_iota(jnp.int32, (blocks, cells), 1)
     seat = lax.broadcasted_iota(jnp.int32, (blocks, cells), 0)
@@ -171,28 +174,36 @@
 
     def gathered(channel, level, cx, cy):
         shift = cy * BE + cx
-        first = front + (channel * levels + level) * (TY + 2)
+        entry = channel * levels + level
+        first = front + entry * (TX + 2)
+        first_column = front + entry * TY
         base = own(channel, level)
         if cy != 0:
             stepped = pltpu.roll(base, TX, 0)
             if cy == 1:
-                halo = spread_ref[0, first:first + blocks, :]
+                halo = spread_ref[0, first + 1:first + 1 + blocks, :]
                 yplane = jnp.where(py == 0, halo, stepped)
             else:
-                halo = spread_ref[1, first - TX:first - TX + blocks, :]
+                halo = spread_ref[1, first + 1 - TX:first + 1 - TX + blocks, :]
                 yplane = jnp.where(py == TY - 1, halo, stepped)
+
+        def side_row(k, dx):
+            corner_at = first if dx == 1 else first + TX + 1
+            if k == 0:
+                return spread_ref[0, corner_at:corner_at + 1, :]
+            if k == TY + 1:
+                return spread_ref[1, corner_at:corner_at + 1, :]
+            at = first_column + k - 1
+            return column_ref[0 if dx == 1 else 1, at:at + 1, :]
 
         def sideways(plane, dy, dx):
             plane = pltpu.roll(plane, dx % blocks, 0)
             edge = 0 if dx == 1 else TX - 1
-            side = 2 if dx == 1 else 3
-            at = first + 1 - dy
             return jnp.where(
                 seat == edge,
-                spread_ref[side, at:at + 1, :],
-                jnp.where(seat == edge + TX, spread_ref[side, at + 1:at + 2, :], plane),
+                side_row(1 - dy, dx),
+                jnp.where(seat == edge + TX, side_row(2 - dy, dx), plane),
             )
-
         value = moved(base, shift)
         if cy != 0:
             ycross = r == (0 if cy == 1 else BE - 1)
@@ -239,7 +250,8 @@
 def stream(keys, post, below, above, from_left, from_right):
     channels, levels, blocks, cells = post.shape
     seats = keys.shape[0]
-    halo_rows = below.shape[0]
+    row_count = below.shape[0]
+    column_count = from_left.shape[0]
     vmem = pl.BlockSpec(memory_space=pltpu.VMEM)
     smem = pl.BlockSpec(memory_space=pltpu.SMEM)
     return pl.pallas_call(
@@ -248,7 +260,8 @@
         in_specs=[smem] + [vmem] * 5,
         out_specs=vmem,
         scratch_shapes=[
-            pltpu.VMEM((4, halo_rows + 16, cells), jnp.float32),
+            pltpu.VMEM((2, row_count + 16, cells), jnp.float32),
+            pltpu.VMEM((2, column_count + 16, cells), jnp.float32),
             pltpu.VMEM((blocks, channels, levels * cells), jnp.float32),
         ],
     )(keys, post.transpose(1, 2, 0, 3), below, above, from_left, from_right)
@@ -315,12 +328,10 @@
     row_shape = (width, levels, TX + 2, BE)
     below = lax.ppermute(flat(top_row), "curve", ahead).reshape(row_shape)
     above = lax.ppermute(flat(bottom_row), "curve", behind).reshape(row_shape)
-    below_flat = flat(below[:, :, 1:TX + 1])
-    above_flat = flat(above[:, :, 1:TX + 1])
-    from_left = flat(jnp.concatenate([below[:, :, :1], left_cols, above[:, :, :1]], axis=2))
-    from_right = flat(
-        jnp.concatenate([below[:, :, TX + 1:], right_cols, above[:, :, TX + 1:]], axis=2)
-    )
+    below_flat = flat(below)
+    above_flat = flat(above)
+    from_left = flat(left_cols)
+    from_right = flat(right_cols)
     new_state = stream(living_brick_keys, post, below_flat, above_flat, from_left, from_right)
     return new_state.reshape((1, 1, seats, channels, levels * cells))
 

time: 50.3 us -> 48 us (0.954); the launches traced: 49.5 us -> 47.9 us
  other arithmetic: 2.19 us -> 0.7 us
  local copies, waits for them, and re-layouts: 5.6 us -> 4.77 us
  waiting for transfers between devices: 16.2 us -> 17 us
    concatenate x2 -> x0, other arithmetic: 1.49 us -> none  [the longest x1 0.75 us: on_device(): jnp.concatenate([below[:, :, TX + 1:], right_cols, above[:, :, TX + 1:]],...]
    slice x4 -> x0, local copies, waits for them, and re-layouts: 1.46 us -> none  [the longest x1 0.69 us: on_device(): below_flat = flat(below[:, :, 1:TX + 1])]
    unnamed x17 -> x29, local copies, waits for them, and re-layouts: 0.04 us -> 1.09 us
    ppermute x1, waiting for transfers between devices: 3 us -> 3.78 us  [on_device(): above = lax.ppermute(flat(bottom_row), 'curve', behind).reshape(row_shape)]
  transfers between devices with their start and end apart: 8 -> 8, of which waited for: 7 -> 7; matrix products, arithmetic and copies ran while one was open for 3% -> 1% of each run, Pallas kernels for 0% -> 0%
where the time goes in v16:
time: 48 us; the launch traced here: 47.9 us
  starting transfers between devices  17.4 us (36%)
  waiting for transfers between devices  17 us (35%)
  Pallas kernels  5.57 us (12%)
  local copies, waits for them, and re-layouts  4.77 us (10%)
  matrix products  2.22 us (5%)
  other arithmetic  0.7 us (1%)
    ppermute x4, starting transfers between devices, butterfly_sum(): lax.ppermute(value, axis, [(i, i ^ stride) for i in range(count)])  12.2 us
    ppermute x4, waiting for transfers between devices, butterfly_sum(): lax.ppermute(value, axis, [(i, i ^ stride) for i in range(count)])  7.65 us
    ppermute x1, waiting for transfers between devices, on_device(): below = lax.ppermute(flat(top_row), 'curve', ahead).reshape(row_shape)  3.92 us
    ppermute x1, waiting for transfers between devices, on_device(): above = lax.ppermute(flat(bottom_row), 'curve', behind).reshape(row_shape)  3.78 us
    pallas_call x1, Pallas kernels, stream(): pl.pallas_call(stream_kernel, out_shape=jax.ShapeDtypeStruct((seats * cha...  3.18 us
    ppermute x1, starting transfers between devices, on_device(): lax.ppermute(flat(by_rows[:, :, :, 0, :, 0]), 'line', behind)  2.95 us
    pallas_call x1, Pallas kernels, cell_moments(): pl.pallas_call(moments_kernel, out_shape=(jax.ShapeDtypeStruct((levels, b...  2.38 us
    ppermute x1, waiting for transfers between devices, on_device(): lax.ppermute(flat(by_rows[:, :, :, TX - 1, :, BE - 1]), 'line', ahead)  1.62 us
  transfers between devices with their start and end apart: 8, of which 7 were waited for; matrix products, arithmetic and copies ran while one was open for 1% of the time, Pallas kernels for 0%

profile of v16, /device:TPU:30, one launch (start us, length us, event | category | flops | bytes accessed | tf_op | source)
XLA Modules:
  0.0 47.9 jit_solution(7382427343140617324)
XLA Ops:
  0.0 2.4 %shard_map.73 = (f32[2,8,27,256]{3,2,1,0:T(8,128)}, f32[3,2,8,256]{3,2,1,0:T(8,128)}) custom-call(s32[6]{0:T(128)} %bitcast.85, f32[27,27]{1,0:T(8,128)} %constant.40.clone.forward_ref, f32[648,128]{1,0:T(8,128)} %bitcast.75), custom_call_target="tpu_custom_call" | custom-call | tf_op jit(solution)/shard_map/pallas_call | solution.py:119
  2.4 1.0 %reshape.94 = f32[3,2,2,4,16,16]{5,4,3,2,1,0:T(8,128)S(1)} reshape(f32[3,2,8,256]{3,2,1,0:T(8,128)} %get-tuple-element.8) | data formatting | bytes 98304 | tf_op jit(solution)/shard_map/reshape | solution.py:294
  3.4 0.2 copy.39
  3.6 0.2 dot_general.16
  3.9 0.2 fusion.15
  4.1 0.3 convolution_bitcast_fusion
  4.4 1.2 %collective-permute-done = f32[3,2,32,16]{2,3,1,0:T(8,128)S(1)} collective-permute-done((f32[3,2,32,16]{2,3,1,0:T(8,128)S(1)}, f32[3,2,32,16]{2,3,1,0:T(8,128)S(1)}, u32[]{:S(2)}, u32[]{:S(2)}) %collective-permute-start) | collective-permute-done | bytes 12320 | tf_op jit(solution)/shard_map/ppermute | solution.py:23
  5.7 2.0 %collective-permute-start.1 = (f32[3,2,32,16]{2,3,1,0:T(8,128)S(1)}, f32[3,2,32,16]{2,3,1,0:T(8,128)S(1)}, u32[]{:S(2)}, u32[]{:S(2)}) collective-permute-start(f32[3,2,32,16]{2,3,1,0:T(8,128)S(1)} %add.43), channel_id=1, source_target_pairs={{0,2},{1,3},{2,0},{3,1},{4,6},{5,7},{6,4},{7,5},{8,10},{9,11},{10,... | collective-permute-start | bytes 36872 | tf_op jit(solution)/shard_map/ppermute | solution.py:23
  7.7 2.2 %collective-permute-done.1 = f32[3,2,32,16]{2,3,1,0:T(8,128)S(1)} collective-permute-done((f32[3,2,32,16]{2,3,1,0:T(8,128)S(1)}, f32[3,2,32,16]{2,3,1,0:T(8,128)S(1)}, u32[]{:S(2)}, u32[]{:S(2)}) %collective-permute-start.1) | collective-permute-done | bytes 12320 | tf_op jit(solution)/shard_map/ppermute | solution.py:23
  9.9 3.4 %collective-permute-start.2 = (f32[3,2,32,16]{2,3,1,0:T(8,128)S(1)}, f32[3,2,32,16]{2,3,1,0:T(8,128)S(1)}, u32[]{:S(2)}, u32[]{:S(2)}) collective-permute-start(f32[3,2,32,16]{2,3,1,0:T(8,128)S(1)} %add.44), channel_id=1, source_target_pairs={{0,4},{1,5},{2,6},{3,7},{4,0},{5,1},{6,2},{7,3},{8,12},{9,13},{10,... | collective-permute-start | bytes 36872 | tf_op jit(solution)/shard_map/ppermute | solution.py:23
  13.2 0.1 fusion.16
  13.4 2.1 %collective-permute-done.2 = f32[3,2,32,16]{2,3,1,0:T(8,128)S(1)} collective-permute-done((f32[3,2,32,16]{2,3,1,0:T(8,128)S(1)}, f32[3,2,32,16]{2,3,1,0:T(8,128)S(1)}, u32[]{:S(2)}, u32[]{:S(2)}) %collective-permute-start.2) | collective-permute-done | bytes 12320 | tf_op jit(solution)/shard_map/ppermute | solution.py:23
  15.5 6.8 %collective-permute-start.3 = (f32[3,2,32,16]{2,3,1,0:T(8,128)S(1)}, f32[3,2,32,16]{2,3,1,0:T(8,128)S(1)}, u32[]{:S(2)}, u32[]{:S(2)}) collective-permute-start(f32[3,2,32,16]{2,3,1,0:T(8,128)S(1)} %add.45), channel_id=1, source_target_pairs={{0,8},{1,9},{2,10},{3,11},{4,12},{5,13},{6,14},{7,15},{8,0},{9,1},... | collective-permute-start | bytes 36872 | tf_op jit(solution)/shard_map/ppermute | solution.py:23
  22.3 2.1 %collective-permute-done.3 = f32[3,2,32,16]{2,3,1,0:T(8,128)S(1)} collective-permute-done((f32[3,2,32,16]{2,3,1,0:T(8,128)S(1)}, f32[3,2,32,16]{2,3,1,0:T(8,128)S(1)}, u32[]{:S(2)}, u32[]{:S(2)}) %collective-permute-start.3) | collective-permute-done | bytes 12320 | tf_op jit(solution)/shard_map/ppermute | solution.py:23
  24.5 1.0 %fusion = f32[3,2,2,4,16,16]{4,5,2,1,0,3:T(8,128)S(1)} fusion(f32[3,2,2,16,16,1]{4,3,2,1,0,5:T(8,128)S(1)} %bitcast.74, f32[4,16,8]{1,2,0:T(8,128)S(1)} %get-tuple-element.22, f32[4,16,8]{1,2,0:T(8,128)S(1)} %get-tuple-element.21), kind=kOutput, calls=%fused_computation.1 | convolution fusion | flops 2372608 | bytes 65536 | tf_op jit(solution)/shard_map/kzyrm,xqm->kzyxrq/dot_general | solution.py:299
  25.6 0.2 copy.42
  25.8 0.2 mul.123
  26.2 0.9 %fusion.3 = f32[2,8,256,27]{2,3,1,0:T(8,128)S(1)} fusion(f32[27,27,1,1]{1,0,3,2:T(8,128)S(1)} %copy-done.8, f32[27,2,8,256]{3,2,1,0:T(8,128)S(1)} %bitcast.71, f32[27]{0:T(128)S(1)} %copy-done.11, f32[2,8,27,256]{3,2,1,0:T(8,128)S(1)} %copy-done.1), kind=kOutput, calls=%fused_computation.9 | convolution fusion | flops 36163584 | bytes 1330128 | tf_op jit(solution)/shard_map/ij,jzpl->izpl/dot_general | solution.py:80
  27.2 0.6 %copy.44 = f32[28,2,8,256]{0,3,2,1:T(8,128)S(1)} copy(f32[28,2,8,256]{3,0,2,1:T(8,128)S(1)} %pad_maximum_fusion) | data formatting | bytes 917504 | tf_op jit(solution)/shard_map/concatenate | solution.py:307
  28.0 0.1 copy.45
  28.2 0.1 copy.47
  28.3 3.0 %collective-permute-start.5 = (f32[112,16]{1,0:T(8,128)S(1)}, f32[112,16]{1,0:T(8,128)S(1)}, u32[]{:S(2)}, u32[]{:S(2)}) collective-permute-start(f32[112,16]{1,0:T(8,128)S(1)} %bitcast.80), channel_id=1, source_target_pairs={{1,0},{2,1},{3,2},{4,3},{5,4},{6,5},{7,6},{8,7},{9,8},{10,9},{11,1... | collective-permute-start | bytes 21512 | tf_op jit(solution)/shard_map/ppermute | solution.py:314
  31.3 1.6 %collective-permute-done.4.left_ref = f32[112,16]{1,0:T(8,128)S(1)} collective-permute-done((f32[112,16]{1,0:T(8,128)S(1)}, f32[112,16]{1,0:T(8,128)S(1)}, u32[]{:S(2)}, u32[]{:S(2)}) %collective-permute-start.4) | collective-permute-done | bytes 7200 | tf_op jit(solution)/shard_map/ppermute | solution.py:313
  32.9 0.1 fusion.21
  33.1 0.1 fusion.22
  33.9 0.1 copy.49
  34.0 1.1 %collective-permute-start.6 = (f32[336,16]{1,0:T(8,128)S(1)}, f32[336,16]{1,0:T(8,128)S(1)}, u32[]{:S(2)}, u32[]{:S(2)}) collective-permute-start(f32[336,16]{1,0:T(8,128)S(1)} %reshape.99), channel_id=1, source_target_pairs={{0,16},{16,32},{32,48},{48,64},{64,80},{80,96},{96,112},{112,128},... | collective-permute-start | bytes 64520 | tf_op jit(solution)/shard_map/ppermute | solution.py:329
  35.2 1.1 %collective-permute-start.7 = (f32[336,16]{1,0:T(8,128)S(1)}, f32[336,16]{1,0:T(8,128)S(1)}, u32[]{:S(2)}, u32[]{:S(2)}) collective-permute-start(f32[336,16]{1,0:T(8,128)S(1)} %reshape.100), channel_id=1, source_target_pairs={{16,0},{32,16},{48,32},{64,48},{80,64},{96,80},{112,96},{128,112},... | collective-permute-start | bytes 64520 | tf_op jit(solution)/shard_map/ppermute | solution.py:330
  36.3 3.9 %collective-permute-done.6.below_ref = f32[336,16]{1,0:T(8,128)S(1)} collective-permute-done((f32[336,16]{1,0:T(8,128)S(1)}, f32[336,16]{1,0:T(8,128)S(1)}, u32[]{:S(2)}, u32[]{:S(2)}) %collective-permute-start.6) | collective-permute-done | bytes 21536 | tf_op jit(solution)/shard_map/ppermute | solution.py:329
  40.3 3.8 %collective-permute-done.7.above_ref = f32[336,16]{1,0:T(8,128)S(1)} collective-permute-done((f32[336,16]{1,0:T(8,128)S(1)}, f32[336,16]{1,0:T(8,128)S(1)}, u32[]{:S(2)}, u32[]{:S(2)}) %collective-permute-start.7) | collective-permute-done | bytes 21536 | tf_op jit(solution)/shard_map/ppermute | solution.py:330
  44.1 0.7 %copy-done.6 = f32[336,16]{1,0:T(8,128)} copy-done((f32[336,16]{1,0:T(8,128)}, f32[336,16]{1,0:T(8,128)S(1)}, u32[]{:S(2)}) %copy-start.6) | copy-done | bytes 21528
  44.7 3.2 %shard_map.74 = f32[648,128]{1,0:T(8,128)} custom-call(s32[6]{0:T(128)} %bitcast.86, f32[2,8,27,256]{3,2,1,0:T(8,128)} %bitcast.69, f32[336,16]{1,0:T(8,128)} %copy-done.5, f32[336,16]{1,0:T(8,128)} %copy-done.6, f32[112,16]{1,0:T(8,128)} %copy-done.2, f32[112,16]{1,0:T(8,128)} %copy-done.3), custom_call_target="tpu_custom_call" | custom-call | tf_op jit(solution)/shard_map/pallas_call | solution.py:257
  (58 shorter events, 1.6 us)
Async XLA Ops:
  0.0 13.2 %copy-start.9 = (s32[1,1,6]{2,1,0:T(1,128)S(1)}, s32[1,1,6]{2,1,0:T(1,128)}, u32[]{:S(2)}) copy-start(s32[1,1,6]{2,1,0:T(1,128)} %param.8) | copy-start | bytes 76
  0.0 3.9 %copy-start.10 = (s32[8]{0:T(128)S(1)}, s32[8]{0:T(128)}, u32[]{:S(2)}) copy-start(s32[8]{0:T(128)} %param.9) | copy-start | bytes 100
  0.0 24.4 %copy-start.7 = (f32[3,2,32,16]{2,3,1,0:T(8,128)S(1)}, f32[3,2,32,16]{2,3,1,0:T(8,128)}, u32[]{:S(2)}) copy-start(f32[3,2,32,16]{2,3,1,0:T(8,128)} %param.10) | copy-start | bytes 36868
  2.4 19.9 %copy-start.1 = (f32[2,8,27,256]{3,2,1,0:T(8,128)S(1)}, f32[2,8,27,256]{3,2,1,0:T(8,128)}, u32[]{:S(2)}) copy-start(f32[2,8,27,256]{3,2,1,0:T(8,128)} %get-tuple-element.7) | copy-start | bytes 1327108
  3.4 22.5 %copy-start.4 = (f32[3,2,8,256]{3,2,1,0:T(8,128)S(1)}, f32[3,2,8,256]{3,2,1,0:T(8,128)}, u32[]{:S(2)}) copy-start(f32[3,2,8,256]{3,2,1,0:T(8,128)} %get-tuple-element.8) | copy-start | bytes 147460
  4.3 1.3 %collective-permute-start = (f32[3,2,32,16]{2,3,1,0:T(8,128)S(1)}, f32[3,2,32,16]{2,3,1,0:T(8,128)S(1)}, u32[]{:S(2)}, u32[]{:S(2)}) collective-permute-start(f32[3,2,32,16]{2,3,1,0:T(8,128)S(1)} %convolution_bitcast_fusion), channel_id=1, source_target_pairs={{0,1},{1,0},{2,3},{3,2},{4,5},{5,4},{6,7},{7,6},{8,9},{9,8},{10,11... | collective-permute-start | bytes 36872 | tf_op jit(solution)/shard_map/ppermute | solution.py:23
  5.7 20.5 %copy-start.8 = (f32[27,27,1,1]{1,0,3,2:T(8,128)S(1)}, f32[27,27,1,1]{1,0,3,2:T(8,128)}, u32[]{:S(2)}) copy-start(f32[27,27,1,1]{1,0,3,2:T(8,128)} %constant.44) | copy-start | bytes 8752
  5.7 20.5 %copy-start.11 = (f32[27]{0:T(128)S(1)}, f32[27]{0:T(128)}, u32[]{:S(2)}) copy-start(f32[27]{0:T(128)} %param.11) | copy-start | bytes 328
  5.7 4.2 %collective-permute-start.1 = (f32[3,2,32,16]{2,3,1,0:T(8,128)S(1)}, f32[3,2,32,16]{2,3,1,0:T(8,128)S(1)}, u32[]{:S(2)}, u32[]{:S(2)}) collective-permute-start(f32[3,2,32,16]{2,3,1,0:T(8,128)S(1)} %add.43), channel_id=1, source_target_pairs={{0,2},{1,3},{2,0},{3,1},{4,6},{5,7},{6,4},{7,5},{8,10},{9,11},{10,... | collective-permute-start | bytes 36872 | tf_op jit(solution)/shard_map/ppermute | solution.py:23
  9.9 5.6 %collective-permute-start.2 = (f32[3,2,32,16]{2,3,1,0:T(8,128)S(1)}, f32[3,2,32,16]{2,3,1,0:T(8,128)S(1)}, u32[]{:S(2)}, u32[]{:S(2)}) collective-permute-start(f32[3,2,32,16]{2,3,1,0:T(8,128)S(1)} %add.44), channel_id=1, source_target_pairs={{0,4},{1,5},{2,6},{3,7},{4,0},{5,1},{6,2},{7,3},{8,12},{9,13},{10,... | collective-permute-start | bytes 36872 | tf_op jit(solution)/shard_map/ppermute | solution.py:23
  15.5 8.9 %collective-permute-start.3 = (f32[3,2,32,16]{2,3,1,0:T(8,128)S(1)}, f32[3,2,32,16]{2,3,1,0:T(8,128)S(1)}, u32[]{:S(2)}, u32[]{:S(2)}) collective-permute-start(f32[3,2,32,16]{2,3,1,0:T(8,128)S(1)} %add.45), channel_id=1, source_target_pairs={{0,8},{1,9},{2,10},{3,11},{4,12},{5,13},{6,14},{7,15},{8,0},{9,1},... | collective-permute-start | bytes 36872 | tf_op jit(solution)/shard_map/ppermute | solution.py:23
  27.1 1.1 %copy-start = (f32[2,8,256,27]{2,3,1,0:T(8,128)}, f32[2,8,256,27]{2,3,1,0:T(8,128)S(1)}, u32[]{:S(2)}) copy-start(f32[2,8,256,27]{2,3,1,0:T(8,128)S(1)} %fusion.3) | copy-start | bytes 1327108
  28.1 4.8 %collective-permute-start.4 = (f32[112,16]{1,0:T(8,128)S(1)}, f32[112,16]{1,0:T(8,128)S(1)}, u32[]{:S(2)}, u32[]{:S(2)}) collective-permute-start(f32[112,16]{1,0:T(8,128)S(1)} %bitcast.79), channel_id=1, source_target_pairs={{0,1},{1,2},{2,3},{3,4},{4,5},{5,6},{6,7},{7,8},{8,9},{9,10},{10,1... | collective-permute-start | bytes 21512 | tf_op jit(solution)/shard_map/ppermute | solution.py:313
  28.3 4.8 %collective-permute-start.5 = (f32[112,16]{1,0:T(8,128)S(1)}, f32[112,16]{1,0:T(8,128)S(1)}, u32[]{:S(2)}, u32[]{:S(2)}) collective-permute-start(f32[112,16]{1,0:T(8,128)S(1)} %bitcast.80), channel_id=1, source_target_pairs={{1,0},{2,1},{3,2},{4,3},{5,4},{6,5},{7,6},{8,7},{9,8},{10,9},{11,1... | collective-permute-start | bytes 21512 | tf_op jit(solution)/shard_map/ppermute | solution.py:314
  32.9 11.2 %copy-start.2 = (f32[112,16]{1,0:T(8,128)}, f32[112,16]{1,0:T(8,128)S(1)}, u32[]{:S(2)}) copy-start(f32[112,16]{1,0:T(8,128)S(1)} %collective-permute-done.4.left_ref) | copy-start | bytes 21508
  33.1 10.9 %copy-start.3 = (f32[112,16]{1,0:T(8,128)}, f32[112,16]{1,0:T(8,128)S(1)}, u32[]{:S(2)}) copy-start(f32[112,16]{1,0:T(8,128)S(1)} %collective-permute-done.5.right_ref) | copy-start | bytes 21508
  34.0 6.2 %collective-permute-start.6 = (f32[336,16]{1,0:T(8,128)S(1)}, f32[336,16]{1,0:T(8,128)S(1)}, u32[]{:S(2)}, u32[]{:S(2)}) collective-permute-start(f32[336,16]{1,0:T(8,128)S(1)} %reshape.99), channel_id=1, source_target_pairs={{0,16},{16,32},{32,48},{48,64},{64,80},{80,96},{96,112},{112,128},... | collective-permute-start | bytes 64520 | tf_op jit(solution)/shard_map/ppermute | solution.py:329
  35.2 8.8 %collective-permute-start.7 = (f32[336,16]{1,0:T(8,128)S(1)}, f32[336,16]{1,0:T(8,128)S(1)}, u32[]{:S(2)}, u32[]{:S(2)}) collective-permute-start(f32[336,16]{1,0:T(8,128)S(1)} %reshape.100), channel_id=1, source_target_pairs={{16,0},{32,16},{48,32},{64,48},{80,64},{96,80},{112,96},{128,112},... | collective-permute-start | bytes 64520 | tf_op jit(solution)/shard_map/ppermute | solution.py:330
  40.3 3.8 %copy-start.5 = (f32[336,16]{1,0:T(8,128)}, f32[336,16]{1,0:T(8,128)S(1)}, u32[]{:S(2)}) copy-start(f32[336,16]{1,0:T(8,128)S(1)} %collective-permute-done.6.below_ref) | copy-start | bytes 64516
  44.1 0.7 %copy-start.6 = (f32[336,16]{1,0:T(8,128)}, f32[336,16]{1,0:T(8,128)S(1)}, u32[]{:S(2)}) copy-start(f32[336,16]{1,0:T(8,128)S(1)} %collective-permute-done.7.above_ref) | copy-start | bytes 64516

commit v17 on v16

--- a/solution.py
+++ b/solution.py
@@ -304,25 +304,28 @@
     present = jnp.any(living_brick_keys[None, :] == jnp.arange(blocks, dtype=jnp.int32)[:, None], axis=1)
     fluid = present.astype(jnp.float32)
     solid = jnp.broadcast_to((1.0 - fluid)[None, None, :, None], (1, levels, blocks, cells))
-    extended = jnp.concatenate([post, solid], axis=0)
+    pick = lambda cut: jnp.concatenate([cut(post), cut(solid)], axis=0)
     width = channels + 1
     flat = lambda halo: halo.reshape(-1, BE)
     ahead, behind = ring_pairs("line")
-    by_rows = extended.reshape(width, levels, TY, TX, BE, BE)
     column_shape = (width, levels, TY, BE)
-    left_cols = lax.ppermute(flat(by_rows[:, :, :, TX - 1, :, BE - 1]), "line", ahead).reshape(column_shape)
-    right_cols = lax.ppermute(flat(by_rows[:, :, :, 0, :, 0]), "line", behind).reshape(column_shape)
+    by_rows = lambda part: part.reshape(part.shape[:2] + (TY, TX, BE, BE))
+    right_edge = pick(lambda part: by_rows(part)[:, :, :, TX - 1, :, BE - 1])
+    left_edge = pick(lambda part: by_rows(part)[:, :, :, 0, :, 0])
+    left_cols = lax.ppermute(flat(right_edge), "line", ahead).reshape(column_shape)
+    right_cols = lax.ppermute(flat(left_edge), "line", behind).reshape(column_shape)
     corner = lambda cols, py, r: jnp.broadcast_to(cols[:, :, py:py + 1, r:r + 1], (width, levels, 1, BE))
     top_row = jnp.concatenate(
         [
             corner(left_cols, TY - 1, BE - 1),
-            extended[:, :, blocks - TX:, cells - BE:],
+            pick(lambda part: part[:, :, blocks - TX:, cells - BE:]),
             corner(right_cols, TY - 1, BE - 1),
         ],
         axis=2,
     )
     bottom_row = jnp.concatenate(
-        [corner(left_cols, 0, 0), extended[:, :, :TX, :BE], corner(right_cols, 0, 0)], axis=2
+        [corner(left_cols, 0, 0), pick(lambda part: part[:, :, :TX, :BE]), corner(right_cols, 0, 0)],
+        axis=2,
     )
     ahead, behind = ring_pairs("curve")
     row_shape = (width, levels, TX + 2, BE)

time: 48 us -> 58.9 us (1.23)
  local copies, waits for them, and re-layouts: 4.77 us -> 14.5 us
  other arithmetic: 0.7 us -> 3.85 us
  waiting for transfers between devices: 17 us -> 14.8 us
    slice x3 -> x6, local copies, waits for them, and re-layouts: 0.26 us -> 6.02 us  [the longest x3 3.45 us: on_device(): right_edge = pick(lambda part: by_rows(part)[:, :, :, TX - 1, :, BE - 1])]
    ppermute x4, waiting for transfers between devices: 7.65 us -> 5.47 us  [butterfly_sum(): lax.ppermute(value, axis, [(i, i ^ stride) for i in range(count)])]
    reshape x0 -> x1, local copies, waits for them, and re-layouts: none -> 2.05 us  [on_device(): by_rows = lambda part: part.reshape(part.shape[:2] + (TY, TX, BE, BE))]
    concatenate x3, other arithmetic: 0.23 us -> 1.27 us  [the longest x1 1.11 us: on_device(): jnp.concatenate([corner(left_cols, TY - 1, BE - 1), pick(lambda part: par...]
    dot_general x0 -> x1, local copies, waits for them, and re-layouts: none -> 1.02 us  [collide_blocks(): return jnp.einsum('ij,jzpl->izpl', backward, relaxed, precision=HIGHEST)]
    slice x1, local copies, waits for them, and re-layouts: 0.01 us -> 0.91 us  [collide_blocks(): density = moments[0]]
    sub x1, other arithmetic: 0.01 us -> 0.81 us  [on_device(): misfit = regional_amplitudes - 2.0 / line_length * coefficients]
    reduce_or x1, other arithmetic: 0.12 us -> 0.77 us  [on_device(): jnp.any(living_brick_keys[None, :] == jnp.arange(blocks, dtype=jnp.int32)...]
  transfers between devices with their start and end apart: 8 -> 8, of which waited for: 7 -> 7; matrix products, arithmetic and copies ran while one was open for 1% -> 8% of each run, Pallas kernels for 0% -> 0%
where the time goes in v17:
time: 58.9 us; the launch traced here: 58.5 us
  starting transfers between devices  17.4 us (30%)
  waiting for transfers between devices  14.8 us (25%)
  local copies, waits for them, and re-layouts  14.5 us (25%)
  Pallas kernels  5.57 us (9%)
  other arithmetic  3.85 us (7%)
  matrix products  2.22 us (4%)
    ppermute x4, starting transfers between devices, butterfly_sum(): lax.ppermute(value, axis, [(i, i ^ stride) for i in range(count)])  12.2 us
    ppermute x4, waiting for transfers between devices, butterfly_sum(): lax.ppermute(value, axis, [(i, i ^ stride) for i in range(count)])  5.47 us
    ppermute x1, waiting for transfers between devices, on_device(): below = lax.ppermute(flat(top_row), 'curve', ahead).reshape(row_shape)  3.94 us
    ppermute x1, waiting for transfers between devices, on_device(): above = lax.ppermute(flat(bottom_row), 'curve', behind).reshape(row_shape)  3.75 us
    slice x3, local copies, waits for them, and re-layouts, on_device(): right_edge = pick(lambda part: by_rows(part)[:, :, :, TX - 1, :, BE - 1])  3.45 us
    pallas_call x1, Pallas kernels, stream(): pl.pallas_call(stream_kernel, out_shape=jax.ShapeDtypeStruct((seats * cha...  3.18 us
    ppermute x1, starting transfers between devices, on_device(): lax.ppermute(flat(left_edge), 'line', behind).reshape(column_shape)  2.95 us
    pallas_call x1, Pallas kernels, cell_moments(): pl.pallas_call(moments_kernel, out_shape=(jax.ShapeDtypeStruct((levels, b...  2.39 us
  transfers between devices with their start and end apart: 8, of which 7 were waited for; matrix products, arithmetic and copies ran while one was open for 8% of the time, Pallas kernels for 0%

profile of v17, /device:TPU:30, one launch (start us, length us, event | category | flops | bytes accessed | tf_op | source)
XLA Modules:
  0.0 58.5 jit_solution(6747457921948279104)
XLA Ops:
  0.0 2.4 %shard_map.73 = (f32[2,8,27,256]{3,2,1,0:T(8,128)}, f32[3,2,8,256]{3,2,1,0:T(8,128)}) custom-call(s32[6]{0:T(128)} %bitcast.95, f32[27,27]{1,0:T(8,128)} %constant.40.clone.forward_ref, f32[648,128]{1,0:T(8,128)} %bitcast.83), custom_call_target="tpu_custom_call" | custom-call | tf_op jit(solution)/shard_map/pallas_call | solution.py:119
  2.4 1.0 %reshape.122 = f32[3,2,2,4,16,16]{5,4,3,2,1,0:T(8,128)S(1)} reshape(f32[3,2,8,256]{3,2,1,0:T(8,128)} %get-tuple-element.8) | data formatting | bytes 98304 | tf_op jit(solution)/shard_map/reshape | solution.py:294
  3.6 0.2 dot_general.16
  3.9 0.8 %fusion.13 = (f32[4,16,8]{1,2,0:T(8,128)S(1)}, f32[4,16,8]{1,2,0:T(8,128)S(1)}) fusion(s32[8]{0:T(128)} %param.9, s32[4,16]{1,0:T(4,128)S(1)} %add_add_fusion), kind=kLoop, calls=%fused_computation.35 | loop fusion | flops 7168 | bytes 4384 | tf_op jit(solution)/shard_map/cos | solution.py:65
  4.7 0.3 convolution_bitcast_fusion
  5.1 0.8 %fusion.14 = pred[8]{0:T(512)(128)(4,1)S(1)} fusion(s32[6]{0:T(128)} %bitcast.96), kind=kLoop, calls=%fused_computation.37 | loop fusion | flops 88 | bytes 32 | tf_op jit(solution)/shard_map/reduce_or | solution.py:304
  5.8 0.4 collective-permute-done
  6.3 2.0 %collective-permute-start.1 = (f32[3,2,32,16]{2,3,1,0:T(8,128)S(1)}, f32[3,2,32,16]{2,3,1,0:T(8,128)S(1)}, u32[]{:S(2)}, u32[]{:S(2)}) collective-permute-start(f32[3,2,32,16]{2,3,1,0:T(8,128)S(1)} %add.43), channel_id=1, source_target_pairs={{0,2},{1,3},{2,0},{3,1},{4,6},{5,7},{6,4},{7,5},{8,10},{9,11},{10,... | collective-permute-start | bytes 36872 | tf_op jit(solution)/shard_map/ppermute | solution.py:23
  8.3 2.2 %collective-permute-done.1 = f32[3,2,32,16]{2,3,1,0:T(8,128)S(1)} collective-permute-done((f32[3,2,32,16]{2,3,1,0:T(8,128)S(1)}, f32[3,2,32,16]{2,3,1,0:T(8,128)S(1)}, u32[]{:S(2)}, u32[]{:S(2)}) %collective-permute-start.1) | collective-permute-done | bytes 12320 | tf_op jit(solution)/shard_map/ppermute | solution.py:23
  10.5 3.4 %collective-permute-start.2 = (f32[3,2,32,16]{2,3,1,0:T(8,128)S(1)}, f32[3,2,32,16]{2,3,1,0:T(8,128)S(1)}, u32[]{:S(2)}, u32[]{:S(2)}) collective-permute-start(f32[3,2,32,16]{2,3,1,0:T(8,128)S(1)} %add.44), channel_id=1, source_target_pairs={{0,4},{1,5},{2,6},{3,7},{4,0},{5,1},{6,2},{7,3},{8,12},{9,13},{10,... | collective-permute-start | bytes 36872 | tf_op jit(solution)/shard_map/ppermute | solution.py:23
  14.0 2.1 %collective-permute-done.2 = f32[3,2,32,16]{2,3,1,0:T(8,128)S(1)} collective-permute-done((f32[3,2,32,16]{2,3,1,0:T(8,128)S(1)}, f32[3,2,32,16]{2,3,1,0:T(8,128)S(1)}, u32[]{:S(2)}, u32[]{:S(2)}) %collective-permute-start.2) | collective-permute-done | bytes 12320 | tf_op jit(solution)/shard_map/ppermute | solution.py:23
  16.1 6.8 %collective-permute-start.3 = (f32[3,2,32,16]{2,3,1,0:T(8,128)S(1)}, f32[3,2,32,16]{2,3,1,0:T(8,128)S(1)}, u32[]{:S(2)}, u32[]{:S(2)}) collective-permute-start(f32[3,2,32,16]{2,3,1,0:T(8,128)S(1)} %add.45), channel_id=1, source_target_pairs={{0,8},{1,9},{2,10},{3,11},{4,12},{5,13},{6,14},{7,15},{8,0},{9,1},... | collective-permute-start | bytes 36872 | tf_op jit(solution)/shard_map/ppermute | solution.py:23
  23.1 0.9 %slice.82 = f32[1,2,8,256]{3,0,2,1:T(1,128)S(1)} slice(f32[27,2,8,256]{3,0,2,1:T(8,128)} %bitcast.81), slice={[0:1], [0:2], [0:8], [0:256]} | slice | bytes 32768 | tf_op jit(solution)/shard_map/slice | solution.py:69
  24.3 0.8 %collective-permute-done.3 = f32[3,2,32,16]{2,3,1,0:T(8,128)S(1)} collective-permute-done((f32[3,2,32,16]{2,3,1,0:T(8,128)S(1)}, f32[3,2,32,16]{2,3,1,0:T(8,128)S(1)}, u32[]{:S(2)}, u32[]{:S(2)}) %collective-permute-start.3) | collective-permute-done | bytes 12320 | tf_op jit(solution)/shard_map/ppermute | solution.py:23
  25.0 0.8 %multiply_subtract_fusion = f32[3,2,32,16]{2,3,1,0:T(8,128)S(1)} fusion(f32[3,2,32,16]{2,3,1,0:T(8,128)} %param.10, f32[3,2,32,16]{2,3,1,0:T(8,128)S(1)} %add.45, f32[3,2,32,16]{2,3,1,0:T(8,128)S(1)} %collective-permute-done.3), kind=kLoop, calls=%fused_computation.18 | loop fusion | flops 9216 | bytes 49152 | tf_op jit(solution)/shard_map/sub | solution.py:298
  25.9 1.0 %fusion = f32[3,2,2,4,16,16]{4,5,2,1,0,3:T(8,128)S(1)} fusion(f32[3,2,2,16,16,1]{4,3,2,1,0,5:T(8,128)S(1)} %bitcast.82, f32[4,16,8]{1,2,0:T(8,128)S(1)} %get-tuple-element.24, f32[4,16,8]{1,2,0:T(8,128)S(1)} %get-tuple-element.23), kind=kOutput, calls=%fused_computation.1 | convolution fusion | flops 2372608 | bytes 65536 | tf_op jit(solution)/shard_map/kzyrm,xqm->kzyxrq/dot_general | solution.py:299
  27.6 0.9 %fusion.3 = f32[2,8,256,27]{2,3,1,0:T(8,128)S(1)} fusion(f32[27,27,1,1]{1,0,3,2:T(8,128)S(1)} %copy-done.7, f32[27,2,8,256]{3,2,1,0:T(8,128)S(1)} %bitcast.79, f32[27]{0:T(128)S(1)} %copy-done.8, f32[2,8,27,256]{3,2,1,0:T(8,128)S(1)} %copy-done.1), kind=kOutput, calls=%fused_computation.6 | convolution fusion | flops 36163584 | bytes 1330128 | tf_op jit(solution)/shard_map/ij,jzpl->izpl/dot_general | solution.py:80
  28.5 1.0 %copy.59 = f32[27,2,8,256]{3,2,1,0:T(8,128)} copy(f32[27,2,8,256]{3,0,2,1:T(8,128)S(1)} %bitcast.76) | data formatting | bytes 884736 | tf_op jit(solution)/shard_map/ij,jzpl->izpl/dot_general | solution.py:80
  29.6 0.7 %fusion.20 = (f32[27,2,4,16]{3,0,2,1:T(8,128)}, f32[27,2,4,16]{3,0,2,1:T(8,128)}) fusion(f32[27,2,8,256]{3,0,2,1:T(8,128)S(1)} %bitcast.77), kind=kLoop, calls=%fused_computation.49 | loop fusion | bytes 55296 | tf_op jit(solution)/shard_map/slice | solution.py:327
  30.3 2.0 %reshape.124 = f32[27,2,2,4,16,16]{5,4,3,2,1,0:T(8,128)S(1)} reshape(f32[27,2,8,256]{3,2,1,0:T(8,128)} %copy.59) | data formatting | bytes 884736 | tf_op jit(solution)/shard_map/reshape | solution.py:312
  32.4 1.5 %fusion.19 = (f32[27,2,2,1,16,1]{5,4,3,2,1,0:T(8,128)}, f32[27,2,2,1,16,1]{5,4,3,2,1,0:T(8,128)}) fusion(f32[27,2,2,4,16,16]{5,4,3,2,1,0:T(8,128)S(1)} %reshape.124), kind=kLoop, calls=%fused_computation.48 | loop fusion | bytes 27648 | tf_op jit(solution)/shard_map/slice | solution.py:313
  33.9 1.7 %copy.60 = f32[27,2,2,1,16,1]{0,4,5,3,2,1:T(8,128)S(1)} copy(f32[27,2,2,1,16,1]{5,4,3,2,1,0:T(8,128)} %get-tuple-element.11) | data formatting | bytes 13824 | tf_op jit(solution)/shard_map/slice | solution.py:313
  35.9 1.7 %copy.63 = f32[27,2,2,1,16,1]{0,4,5,3,2,1:T(8,128)S(1)} copy(f32[27,2,2,1,16,1]{5,4,3,2,1,0:T(8,128)} %get-tuple-element.12) | data formatting | bytes 13824 | tf_op jit(solution)/shard_map/slice | solution.py:314
  37.9 3.0 %collective-permute-start.5 = (f32[112,16]{1,0:T(8,128)S(1)}, f32[112,16]{1,0:T(8,128)S(1)}, u32[]{:S(2)}, u32[]{:S(2)}) collective-permute-start(f32[112,16]{1,0:T(8,128)S(1)} %bitcast.90), channel_id=1, source_target_pairs={{1,0},{2,1},{3,2},{4,3},{5,4},{6,5},{7,6},{8,7},{9,8},{10,9},{11,1... | collective-permute-start | bytes 21512 | tf_op jit(solution)/shard_map/ppermute | solution.py:316
  41.1 1.6 %collective-permute-done.5.right_ref = f32[112,16]{1,0:T(8,128)S(1)} collective-permute-done((f32[112,16]{1,0:T(8,128)S(1)}, f32[112,16]{1,0:T(8,128)S(1)}, u32[]{:S(2)}, u32[]{:S(2)}) %collective-permute-start.5) | collective-permute-done | bytes 7200 | tf_op jit(solution)/shard_map/ppermute | solution.py:316
  43.4 1.1 %pad_maximum_fusion = (f32[28,2,6,16]{3,0,2,1:T(8,128)S(1)}, f32[28,2,6,16]{3,0,2,1:T(8,128)S(1)}) fusion(f32[28,2,1,16]{3,0,2,1:T(8,128)S(1)} %broadcast_in_dim.44, f32[27,2,4,16]{3,0,2,1:T(8,128)} %get-tuple-element.14, f32[28,2,1,16]{3,0,2,1:T(8,128)S(1)} %broadcast_in_dim.41, f32[28,6]{0,1:T(8,128)S(1)} %pad.6.clone, ...), kind=kLoop, calls=%fused_computation.9 | loop fusion | flops 32256 | bytes 86336 | tf_op jit(solution)/shard_map/concatenate | solution.py:318
  44.7 1.1 %collective-permute-start.6 = (f32[336,16]{1,0:T(8,128)S(1)}, f32[336,16]{1,0:T(8,128)S(1)}, u32[]{:S(2)}, u32[]{:S(2)}) collective-permute-start(f32[336,16]{1,0:T(8,128)S(1)} %reshape.129), channel_id=1, source_target_pairs={{0,16},{16,32},{32,48},{48,64},{64,80},{80,96},{96,112},{112,128},... | collective-permute-start | bytes 64520 | tf_op jit(solution)/shard_map/ppermute | solution.py:332
  45.9 1.1 %collective-permute-start.7 = (f32[336,16]{1,0:T(8,128)S(1)}, f32[336,16]{1,0:T(8,128)S(1)}, u32[]{:S(2)}, u32[]{:S(2)}) collective-permute-start(f32[336,16]{1,0:T(8,128)S(1)} %reshape.130), channel_id=1, source_target_pairs={{16,0},{32,16},{48,32},{64,48},{80,64},{96,80},{112,96},{128,112},... | collective-permute-start | bytes 64520 | tf_op jit(solution)/shard_map/ppermute | solution.py:333
  47.0 3.9 %collective-permute-done.6.below_ref = f32[336,16]{1,0:T(8,128)S(1)} collective-permute-done((f32[336,16]{1,0:T(8,128)S(1)}, f32[336,16]{1,0:T(8,128)S(1)}, u32[]{:S(2)}, u32[]{:S(2)}) %collective-permute-start.6) | collective-permute-done | bytes 21536 | tf_op jit(solution)/shard_map/ppermute | solution.py:332
  50.9 3.8 %collective-permute-done.7.above_ref = f32[336,16]{1,0:T(8,128)S(1)} collective-permute-done((f32[336,16]{1,0:T(8,128)S(1)}, f32[336,16]{1,0:T(8,128)S(1)}, u32[]{:S(2)}, u32[]{:S(2)}) %collective-permute-start.7) | collective-permute-done | bytes 21536 | tf_op jit(solution)/shard_map/ppermute | solution.py:333
  54.7 0.7 %copy-done.6 = f32[336,16]{1,0:T(8,128)} copy-done((f32[336,16]{1,0:T(8,128)}, f32[336,16]{1,0:T(8,128)S(1)}, u32[]{:S(2)}) %copy-start.6) | copy-done | bytes 21528
  55.4 3.2 %shard_map.74 = f32[648,128]{1,0:T(8,128)} custom-call(s32[6]{0:T(128)} %bitcast.97, f32[2,8,27,256]{3,2,1,0:T(8,128)} %bitcast.78, f32[336,16]{1,0:T(8,128)} %copy-done.5, f32[336,16]{1,0:T(8,128)} %copy-done.6, f32[112,16]{1,0:T(8,128)} %copy-done.2, f32[112,16]{1,0:T(8,128)} %copy-done.3), custom_call_target="tpu_custom_call" | custom-call | tf_op jit(solution)/shard_map/pallas_call | solution.py:257
  (64 shorter events, 3.3 us)
Async XLA Ops:
  0.0 27.6 %copy-start.7 = (f32[27,27,1,1]{1,0,3,2:T(8,128)S(1)}, f32[27,27,1,1]{1,0,3,2:T(8,128)}, u32[]{:S(2)}) copy-start(f32[27,27,1,1]{1,0,3,2:T(8,128)} %constant.44) | copy-start | bytes 8752
  0.0 27.6 %copy-start.8 = (f32[27]{0:T(128)S(1)}, f32[27]{0:T(128)}, u32[]{:S(2)}) copy-start(f32[27]{0:T(128)} %param.11) | copy-start | bytes 328
  2.4 25.0 %copy-start.4 = (f32[3,2,8,256]{3,2,1,0:T(8,128)S(1)}, f32[3,2,8,256]{3,2,1,0:T(8,128)}, u32[]{:S(2)}) copy-start(f32[3,2,8,256]{3,2,1,0:T(8,128)} %get-tuple-element.8) | copy-start | bytes 147460
  2.4 25.2 %copy-start.1 = (f32[2,8,27,256]{3,2,1,0:T(8,128)S(1)}, f32[2,8,27,256]{3,2,1,0:T(8,128)}, u32[]{:S(2)}) copy-start(f32[2,8,27,256]{3,2,1,0:T(8,128)} %get-tuple-element.7) | copy-start | bytes 1327108
  5.0 1.3 %collective-permute-start = (f32[3,2,32,16]{2,3,1,0:T(8,128)S(1)}, f32[3,2,32,16]{2,3,1,0:T(8,128)S(1)}, u32[]{:S(2)}, u32[]{:S(2)}) collective-permute-start(f32[3,2,32,16]{2,3,1,0:T(8,128)S(1)} %convolution_bitcast_fusion), channel_id=1, source_target_pairs={{0,1},{1,0},{2,3},{3,2},{4,5},{5,4},{6,7},{7,6},{8,9},{9,8},{10,11... | collective-permute-start | bytes 36872 | tf_op jit(solution)/shard_map/ppermute | solution.py:23
  6.3 4.2 %collective-permute-start.1 = (f32[3,2,32,16]{2,3,1,0:T(8,128)S(1)}, f32[3,2,32,16]{2,3,1,0:T(8,128)S(1)}, u32[]{:S(2)}, u32[]{:S(2)}) collective-permute-start(f32[3,2,32,16]{2,3,1,0:T(8,128)S(1)} %add.43), channel_id=1, source_target_pairs={{0,2},{1,3},{2,0},{3,1},{4,6},{5,7},{6,4},{7,5},{8,10},{9,11},{10,... | collective-permute-start | bytes 36872 | tf_op jit(solution)/shard_map/ppermute | solution.py:23
  10.5 5.6 %collective-permute-start.2 = (f32[3,2,32,16]{2,3,1,0:T(8,128)S(1)}, f32[3,2,32,16]{2,3,1,0:T(8,128)S(1)}, u32[]{:S(2)}, u32[]{:S(2)}) collective-permute-start(f32[3,2,32,16]{2,3,1,0:T(8,128)S(1)} %add.44), channel_id=1, source_target_pairs={{0,4},{1,5},{2,6},{3,7},{4,0},{5,1},{6,2},{7,3},{8,12},{9,13},{10,... | collective-permute-start | bytes 36872 | tf_op jit(solution)/shard_map/ppermute | solution.py:23
  16.1 8.9 %collective-permute-start.3 = (f32[3,2,32,16]{2,3,1,0:T(8,128)S(1)}, f32[3,2,32,16]{2,3,1,0:T(8,128)S(1)}, u32[]{:S(2)}, u32[]{:S(2)}) collective-permute-start(f32[3,2,32,16]{2,3,1,0:T(8,128)S(1)} %add.45), channel_id=1, source_target_pairs={{0,8},{1,9},{2,10},{3,11},{4,12},{5,13},{6,14},{7,15},{8,0},{9,1},... | collective-permute-start | bytes 36872 | tf_op jit(solution)/shard_map/ppermute | solution.py:23
  28.5 1.0 %copy-start = (f32[2,8,256,27]{2,3,1,0:T(8,128)}, f32[2,8,256,27]{2,3,1,0:T(8,128)S(1)}, u32[]{:S(2)}) copy-start(f32[2,8,256,27]{2,3,1,0:T(8,128)S(1)} %fusion.3) | copy-start | bytes 1327108
  35.9 5.0 %collective-permute-start.4 = (f32[112,16]{1,0:T(8,128)S(1)}, f32[112,16]{1,0:T(8,128)S(1)}, u32[]{:S(2)}, u32[]{:S(2)}) collective-permute-start(f32[112,16]{1,0:T(8,128)S(1)} %bitcast.89), channel_id=1, source_target_pairs={{0,1},{1,2},{2,3},{3,4},{4,5},{5,6},{6,7},{7,8},{8,9},{9,10},{10,1... | collective-permute-start | bytes 21512 | tf_op jit(solution)/shard_map/ppermute | solution.py:315
  37.9 4.8 %collective-permute-start.5 = (f32[112,16]{1,0:T(8,128)S(1)}, f32[112,16]{1,0:T(8,128)S(1)}, u32[]{:S(2)}, u32[]{:S(2)}) collective-permute-start(f32[112,16]{1,0:T(8,128)S(1)} %bitcast.90), channel_id=1, source_target_pairs={{1,0},{2,1},{3,2},{4,3},{5,4},{6,5},{7,6},{8,7},{9,8},{10,9},{11,1... | collective-permute-start | bytes 21512 | tf_op jit(solution)/shard_map/ppermute | solution.py:316
  40.9 13.8 %copy-start.2 = (f32[112,16]{1,0:T(8,128)}, f32[112,16]{1,0:T(8,128)S(1)}, u32[]{:S(2)}) copy-start(f32[112,16]{1,0:T(8,128)S(1)} %collective-permute-done.4.left_ref) | copy-start | bytes 21508
  42.7 12.0 %copy-start.3 = (f32[112,16]{1,0:T(8,128)}, f32[112,16]{1,0:T(8,128)S(1)}, u32[]{:S(2)}) copy-start(f32[112,16]{1,0:T(8,128)S(1)} %collective-permute-done.5.right_ref) | copy-start | bytes 21508
  44.7 6.3 %collective-permute-start.6 = (f32[336,16]{1,0:T(8,128)S(1)}, f32[336,16]{1,0:T(8,128)S(1)}, u32[]{:S(2)}, u32[]{:S(2)}) collective-permute-start(f32[336,16]{1,0:T(8,128)S(1)} %reshape.129), channel_id=1, source_target_pairs={{0,16},{16,32},{32,48},{48,64},{64,80},{80,96},{96,112},{112,128},... | collective-permute-start | bytes 64520 | tf_op jit(solution)/shard_map/ppermute | solution.py:332
  45.9 8.8 %collective-permute-start.7 = (f32[336,16]{1,0:T(8,128)S(1)}, f32[336,16]{1,0:T(8,128)S(1)}, u32[]{:S(2)}, u32[]{:S(2)}) collective-permute-start(f32[336,16]{1,0:T(8,128)S(1)} %reshape.130), channel_id=1, source_target_pairs={{16,0},{32,16},{48,32},{64,48},{80,64},{96,80},{112,96},{128,112},... | collective-permute-start | bytes 64520 | tf_op jit(solution)/shard_map/ppermute | solution.py:333
  50.9 3.8 %copy-start.5 = (f32[336,16]{1,0:T(8,128)}, f32[336,16]{1,0:T(8,128)S(1)}, u32[]{:S(2)}) copy-start(f32[336,16]{1,0:T(8,128)S(1)} %collective-permute-done.6.below_ref) | copy-start | bytes 64516
  54.7 0.7 %copy-start.6 = (f32[336,16]{1,0:T(8,128)}, f32[336,16]{1,0:T(8,128)S(1)}, u32[]{:S(2)}) copy-start(f32[336,16]{1,0:T(8,128)S(1)} %collective-permute-done.7.above_ref) | copy-start | bytes 64516

commit v18 on v16

--- a/solution.py
+++ b/solution.py
@@ -128,8 +128,23 @@
     )(keys, forward, rows)
 
 
+def level_steps_kernel(keys_ref, post_ref, left_ref, right_ref, result_ref, column_ref):
+    stream_body(0, keys_ref, post_ref, None, None, left_ref, right_ref, None, None, None, column_ref, result_ref)
+
+
 def stream_kernel(
-    keys_ref, post_ref, below_ref, above_ref, left_ref, right_ref, out_ref, spread_ref, column_ref, result_ref
+    keys_ref, post_ref, below_ref, above_ref, left_ref, right_ref, partial_ref, out_ref, spread_ref,
+    column_ref, result_ref,
+):
+    stream_body(
+        1, keys_ref, post_ref, below_ref, above_ref, left_ref, right_ref, partial_ref, out_ref, spread_ref,
+        column_ref, result_ref,
+    )
+
+
+def stream_body(
+    part, keys_ref, post_ref, below_ref, above_ref, left_ref, right_ref, partial_ref, out_ref, spread_ref,
+    column_ref, result_ref,
 ):
     levels, blocks, channels, cells = post_ref.shape
     _, _, speeds = lattice_tables()
@@ -138,12 +153,14 @@
     grid_lane = lax.broadcasted_iota(jnp.int32, (BE, cells), 1)
     tile_copy = (grid_lane % BE == grid_row).astype(jnp.float32)
     group_copy = (grid_lane // BE == grid_row).astype(jnp.float32)
-    row_count = below_ref.shape[0]
     column_count = left_ref.shape[0]
-    for slot, source in enumerate((below_ref, above_ref)):
-        spread_ref[slot, front:front + row_count, :] = jnp.dot(
-            source[...], tile_copy, precision=HIGHEST, preferred_element_type=jnp.float32
-        )
+    if part == 1:
+        row_count = below_ref.shape[0]
+        for slot, source in enumerate((below_ref, above_ref)):
+            spread_ref[slot, front:front + row_count, :] = jnp.dot(
+                source[...], tile_copy, precision=HIGHEST, preferred_element_type=jnp.float32
+            )
+        result_ref[...] = partial_ref[...]
     for slot, source in enumerate((left_ref, right_ref)):
         column_ref[slot, front:front + column_count, :] = jnp.dot(
             source[...], group_copy, precision=HIGHEST, preferred_element_type=jnp.float32
@@ -217,11 +234,12 @@
         return value
 
     blocked_of = {}
-    for cx in (-1, 0, 1):
-        for cy in (-1, 0, 1):
-            blocked_of[(cx, cy)] = gathered(channels, 0, cx, cy) > 0.5
     for heading in range(27):
         cx, cy, cz = (int(v) for v in speeds[heading])
+        if (cy == 0) != (part == 0):
+            continue
+        if (cx, cy) not in blocked_of:
+            blocked_of[(cx, cy)] = gathered(channels, 0, cx, cy) > 0.5
         blocked = blocked_of[(cx, cy)]
         for level in range(levels):
             bounced = post_ref[level, :, 26 - heading, :]
@@ -238,6 +256,8 @@
             else:
                 source = gathered(heading + 2, 1, cx, cy)
             result_ref[:, heading, window] = jnp.where(blocked, bounced, source)
+    if part == 0:
+        return
     chunks = levels * cells // 128
     for seat_number in range(keys_ref.shape[0]):
         key = keys_ref[seat_number]
@@ -254,17 +274,25 @@
     column_count = from_left.shape[0]
     vmem = pl.BlockSpec(memory_space=pltpu.VMEM)
     smem = pl.BlockSpec(memory_space=pltpu.SMEM)
+    by_level = post.transpose(1, 2, 0, 3)
+    partial = pl.pallas_call(
+        level_steps_kernel,
+        out_shape=jax.ShapeDtypeStruct((blocks, channels, levels * cells), jnp.float32),
+        in_specs=[smem] + [vmem] * 3,
+        out_specs=vmem,
+        scratch_shapes=[pltpu.VMEM((2, column_count + 16, cells), jnp.float32)],
+    )(keys, by_level, from_left, from_right)
     return pl.pallas_call(
         stream_kernel,
         out_shape=jax.ShapeDtypeStruct((seats * channels * levels * cells // 128, 128), jnp.float32),
-        in_specs=[smem] + [vmem] * 5,
+        in_specs=[smem] + [vmem] * 6,
         out_specs=vmem,
         scratch_shapes=[
             pltpu.VMEM((2, row_count + 16, cells), jnp.float32),
             pltpu.VMEM((2, column_count + 16, cells), jnp.float32),
             pltpu.VMEM((blocks, channels, levels * cells), jnp.float32),
         ],
-    )(keys, post.transpose(1, 2, 0, 3), below, above, from_left, from_right)
+    )(keys, by_level, below, above, from_left, from_right, partial)
 
 
 def on_device(

time: 48 us -> 48.7 us (1.015); the launches traced: 47.9 us -> 48 us
  Pallas kernels: 5.57 us -> 8.01 us
  waiting for transfers between devices: 17 us -> 14.6 us
    ppermute x1, waiting for transfers between devices: 3.92 us -> 1.59 us  [on_device(): below = lax.ppermute(flat(top_row), 'curve', ahead).reshape(row_shape)]
    pallas_call x0 -> x1, Pallas kernels: none -> 2.32 us  [stream(): pl.pallas_call(level_steps_kernel, out_shape=jax.ShapeDtypeStruct((blocks...]
  transfers between devices with their start and end apart: 8 -> 8, of which waited for: 7 -> 7; matrix products, arithmetic and copies ran while one was open for 1% -> 1% of each run, Pallas kernels for 0% -> 5%
where the time goes in v18:
time: 48.7 us; the launch traced here: 48 us
  starting transfers between devices  17.4 us (36%)
  waiting for transfers between devices  14.6 us (30%)
  Pallas kernels  8.01 us (16%)
  local copies, waits for them, and re-layouts  4.78 us (10%)
  matrix products  2.22 us (5%)
  other arithmetic  0.7 us (1%)
    ppermute x4, starting transfers between devices, butterfly_sum(): lax.ppermute(value, axis, [(i, i ^ stride) for i in range(count)])  12.2 us
    ppermute x4, waiting for transfers between devices, butterfly_sum(): lax.ppermute(value, axis, [(i, i ^ stride) for i in range(count)])  7.65 us
    ppermute x1, waiting for transfers between devices, on_device(): above = lax.ppermute(flat(bottom_row), 'curve', behind).reshape(row_shape)  3.78 us
    pallas_call x1, Pallas kernels, stream(): pl.pallas_call(stream_kernel, out_shape=jax.ShapeDtypeStruct((seats * cha...  3.3 us
    ppermute x1, starting transfers between devices, on_device(): lax.ppermute(flat(by_rows[:, :, :, 0, :, 0]), 'line', behind)  2.95 us
    pallas_call x1, Pallas kernels, cell_moments(): pl.pallas_call(moments_kernel, out_shape=(jax.ShapeDtypeStruct((levels, b...  2.38 us
    pallas_call x1, Pallas kernels, stream(): pl.pallas_call(level_steps_kernel, out_shape=jax.ShapeDtypeStruct((blocks...  2.32 us
    ppermute x1, waiting for transfers between devices, on_device(): lax.ppermute(flat(by_rows[:, :, :, TX - 1, :, BE - 1]), 'line', ahead)  1.62 us
  transfers between devices with their start and end apart: 8, of which 7 were waited for; matrix products, arithmetic and copies ran while one was open for 1% of the time, Pallas kernels for 5%

profile of v18, /device:TPU:30, one launch (start us, length us, event | category | flops | bytes accessed | tf_op | source)
XLA Modules:
  0.0 48.0 jit_solution(13140544692675764225)
XLA Ops:
  0.0 2.4 %shard_map.73 = (f32[2,8,27,256]{3,2,1,0:T(8,128)}, f32[3,2,8,256]{3,2,1,0:T(8,128)}) custom-call(s32[6]{0:T(128)} %bitcast.82, f32[27,27]{1,0:T(8,128)} %constant.40.clone.forward_ref, f32[648,128]{1,0:T(8,128)} %bitcast.78), custom_call_target="tpu_custom_call" | custom-call | tf_op jit(solution)/shard_map/pallas_call | solution.py:119
  2.4 1.0 %reshape.94 = f32[3,2,2,4,16,16]{5,4,3,2,1,0:T(8,128)S(1)} reshape(f32[3,2,8,256]{3,2,1,0:T(8,128)} %get-tuple-element.8) | data formatting | bytes 98304 | tf_op jit(solution)/shard_map/reshape | solution.py:322
  3.4 0.2 copy.39
  3.6 0.2 dot_general.16
  3.9 0.2 fusion.15
  4.1 0.3 convolution_bitcast_fusion
  4.4 1.2 %collective-permute-done = f32[3,2,32,16]{2,3,1,0:T(8,128)S(1)} collective-permute-done((f32[3,2,32,16]{2,3,1,0:T(8,128)S(1)}, f32[3,2,32,16]{2,3,1,0:T(8,128)S(1)}, u32[]{:S(2)}, u32[]{:S(2)}) %collective-permute-start) | collective-permute-done | bytes 12320 | tf_op jit(solution)/shard_map/ppermute | solution.py:23
  5.7 2.0 %collective-permute-start.1 = (f32[3,2,32,16]{2,3,1,0:T(8,128)S(1)}, f32[3,2,32,16]{2,3,1,0:T(8,128)S(1)}, u32[]{:S(2)}, u32[]{:S(2)}) collective-permute-start(f32[3,2,32,16]{2,3,1,0:T(8,128)S(1)} %add.43), channel_id=1, source_target_pairs={{0,2},{1,3},{2,0},{3,1},{4,6},{5,7},{6,4},{7,5},{8,10},{9,11},{10,... | collective-permute-start | bytes 36872 | tf_op jit(solution)/shard_map/ppermute | solution.py:23
  7.7 2.2 %collective-permute-done.1 = f32[3,2,32,16]{2,3,1,0:T(8,128)S(1)} collective-permute-done((f32[3,2,32,16]{2,3,1,0:T(8,128)S(1)}, f32[3,2,32,16]{2,3,1,0:T(8,128)S(1)}, u32[]{:S(2)}, u32[]{:S(2)}) %collective-permute-start.1) | collective-permute-done | bytes 12320 | tf_op jit(solution)/shard_map/ppermute | solution.py:23
  9.9 3.4 %collective-permute-start.2 = (f32[3,2,32,16]{2,3,1,0:T(8,128)S(1)}, f32[3,2,32,16]{2,3,1,0:T(8,128)S(1)}, u32[]{:S(2)}, u32[]{:S(2)}) collective-permute-start(f32[3,2,32,16]{2,3,1,0:T(8,128)S(1)} %add.44), channel_id=1, source_target_pairs={{0,4},{1,5},{2,6},{3,7},{4,0},{5,1},{6,2},{7,3},{8,12},{9,13},{10,... | collective-permute-start | bytes 36872 | tf_op jit(solution)/shard_map/ppermute | solution.py:23
  13.2 0.1 fusion.16
  13.4 2.1 %collective-permute-done.2 = f32[3,2,32,16]{2,3,1,0:T(8,128)S(1)} collective-permute-done((f32[3,2,32,16]{2,3,1,0:T(8,128)S(1)}, f32[3,2,32,16]{2,3,1,0:T(8,128)S(1)}, u32[]{:S(2)}, u32[]{:S(2)}) %collective-permute-start.2) | collective-permute-done | bytes 12320 | tf_op jit(solution)/shard_map/ppermute | solution.py:23
  15.5 6.8 %collective-permute-start.3 = (f32[3,2,32,16]{2,3,1,0:T(8,128)S(1)}, f32[3,2,32,16]{2,3,1,0:T(8,128)S(1)}, u32[]{:S(2)}, u32[]{:S(2)}) collective-permute-start(f32[3,2,32,16]{2,3,1,0:T(8,128)S(1)} %add.45), channel_id=1, source_target_pairs={{0,8},{1,9},{2,10},{3,11},{4,12},{5,13},{6,14},{7,15},{8,0},{9,1},... | collective-permute-start | bytes 36872 | tf_op jit(solution)/shard_map/ppermute | solution.py:23
  22.3 2.1 %collective-permute-done.3 = f32[3,2,32,16]{2,3,1,0:T(8,128)S(1)} collective-permute-done((f32[3,2,32,16]{2,3,1,0:T(8,128)S(1)}, f32[3,2,32,16]{2,3,1,0:T(8,128)S(1)}, u32[]{:S(2)}, u32[]{:S(2)}) %collective-permute-start.3) | collective-permute-done | bytes 12320 | tf_op jit(solution)/shard_map/ppermute | solution.py:23
  24.5 1.0 %fusion = f32[3,2,2,4,16,16]{4,5,2,1,0,3:T(8,128)S(1)} fusion(f32[3,2,2,16,16,1]{4,3,2,1,0,5:T(8,128)S(1)} %bitcast.77, f32[4,16,8]{1,2,0:T(8,128)S(1)} %get-tuple-element.22, f32[4,16,8]{1,2,0:T(8,128)S(1)} %get-tuple-element.21), kind=kOutput, calls=%fused_computation.1 | convolution fusion | flops 2372608 | bytes 65536 | tf_op jit(solution)/shard_map/kzyrm,xqm->kzyxrq/dot_general | solution.py:327
  25.6 0.2 copy.42
  25.8 0.2 mul.123
  26.2 0.9 %fusion.3 = f32[2,8,256,27]{2,3,1,0:T(8,128)S(1)} fusion(f32[27,27,1,1]{1,0,3,2:T(8,128)S(1)} %copy-done.8, f32[27,2,8,256]{3,2,1,0:T(8,128)S(1)} %bitcast.72, f32[27]{0:T(128)S(1)} %copy-done.11, f32[2,8,27,256]{3,2,1,0:T(8,128)S(1)} %copy-done.1), kind=kOutput, calls=%fused_computation.9 | convolution fusion | flops 36163584 | bytes 1330128 | tf_op jit(solution)/shard_map/ij,jzpl->izpl/dot_general | solution.py:80
  27.2 0.6 %copy.44 = f32[28,2,8,256]{0,3,2,1:T(8,128)S(1)} copy(f32[28,2,8,256]{3,0,2,1:T(8,128)S(1)} %pad_maximum_fusion) | data formatting | bytes 917504 | tf_op jit(solution)/shard_map/concatenate | solution.py:335
  28.0 0.1 copy.45
  28.3 3.0 %collective-permute-start.5 = (f32[112,16]{1,0:T(8,128)S(1)}, f32[112,16]{1,0:T(8,128)S(1)}, u32[]{:S(2)}, u32[]{:S(2)}) collective-permute-start(f32[112,16]{1,0:T(8,128)S(1)} %bitcast.81), channel_id=1, source_target_pairs={{1,0},{2,1},{3,2},{4,3},{5,4},{6,5},{7,6},{8,7},{9,8},{10,9},{11,1... | collective-permute-start | bytes 21512 | tf_op jit(solution)/shard_map/ppermute | solution.py:342
  31.3 1.6 %collective-permute-done.4.left_ref = f32[112,16]{1,0:T(8,128)S(1)} collective-permute-done((f32[112,16]{1,0:T(8,128)S(1)}, f32[112,16]{1,0:T(8,128)S(1)}, u32[]{:S(2)}, u32[]{:S(2)}) %collective-permute-start.4) | collective-permute-done | bytes 7200 | tf_op jit(solution)/shard_map/ppermute | solution.py:341
  32.9 0.1 fusion.21
  33.1 0.1 fusion.22
  33.9 0.1 copy.49
  34.0 1.1 %collective-permute-start.6 = (f32[336,16]{1,0:T(8,128)S(1)}, f32[336,16]{1,0:T(8,128)S(1)}, u32[]{:S(2)}, u32[]{:S(2)}) collective-permute-start(f32[336,16]{1,0:T(8,128)S(1)} %reshape.99), channel_id=1, source_target_pairs={{0,16},{16,32},{32,48},{48,64},{64,80},{80,96},{96,112},{112,128},... | collective-permute-start | bytes 64520 | tf_op jit(solution)/shard_map/ppermute | solution.py:357
  35.2 1.1 %collective-permute-start.7 = (f32[336,16]{1,0:T(8,128)S(1)}, f32[336,16]{1,0:T(8,128)S(1)}, u32[]{:S(2)}, u32[]{:S(2)}) collective-permute-start(f32[336,16]{1,0:T(8,128)S(1)} %reshape.100), channel_id=1, source_target_pairs={{16,0},{32,16},{48,32},{64,48},{80,64},{96,80},{112,96},{128,112},... | collective-permute-start | bytes 64520 | tf_op jit(solution)/shard_map/ppermute | solution.py:358
  36.4 2.3 %shard_map.74.partial_ref = f32[8,27,512]{2,1,0:T(8,128)} custom-call(s32[6]{0:T(128)} %bitcast.83, f32[2,8,27,256]{3,2,1,0:T(8,128)} %bitcast.69, f32[112,16]{1,0:T(8,128)} %copy-done.2, f32[112,16]{1,0:T(8,128)} %copy-done.3), custom_call_target="tpu_custom_call" | custom-call | tf_op jit(solution)/shard_map/pallas_call | solution.py:278
  38.7 1.6 %collective-permute-done.6.below_ref = f32[336,16]{1,0:T(8,128)S(1)} collective-permute-done((f32[336,16]{1,0:T(8,128)S(1)}, f32[336,16]{1,0:T(8,128)S(1)}, u32[]{:S(2)}, u32[]{:S(2)}) %collective-permute-start.6) | collective-permute-done | bytes 21536 | tf_op jit(solution)/shard_map/ppermute | solution.py:357
  40.3 3.8 %collective-permute-done.7.above_ref = f32[336,16]{1,0:T(8,128)S(1)} collective-permute-done((f32[336,16]{1,0:T(8,128)S(1)}, f32[336,16]{1,0:T(8,128)S(1)}, u32[]{:S(2)}, u32[]{:S(2)}) %collective-permute-start.7) | collective-permute-done | bytes 21536 | tf_op jit(solution)/shard_map/ppermute | solution.py:358
  44.1 0.7 %copy-done.6 = f32[336,16]{1,0:T(8,128)} copy-done((f32[336,16]{1,0:T(8,128)}, f32[336,16]{1,0:T(8,128)S(1)}, u32[]{:S(2)}) %copy-start.6) | copy-done | bytes 21528
  44.7 3.3 %shard_map.75 = f32[648,128]{1,0:T(8,128)} custom-call(s32[6]{0:T(128)} %bitcast.84, f32[2,8,27,256]{3,2,1,0:T(8,128)} %bitcast.70, f32[336,16]{1,0:T(8,128)} %copy-done.5, f32[336,16]{1,0:T(8,128)} %copy-done.6, f32[112,16]{1,0:T(8,128)} %copy-done.2, f32[112,16]{1,0:T(8,128)} %copy-done.3, f32[8,27,512]{2,1,0:T(8,128)} %shard_map.74.partial_ref), custom_call_target="tpu_custom_call" | custom-call | tf_op jit(solution)/shard_map/pallas_call | solution.py:285
  (59 shorter events, 1.7 us)
Async XLA Ops:
  0.0 13.2 %copy-start.9 = (s32[1,1,6]{2,1,0:T(1,128)S(1)}, s32[1,1,6]{2,1,0:T(1,128)}, u32[]{:S(2)}) copy-start(s32[1,1,6]{2,1,0:T(1,128)} %param.8) | copy-start | bytes 76
  0.0 3.9 %copy-start.10 = (s32[8]{0:T(128)S(1)}, s32[8]{0:T(128)}, u32[]{:S(2)}) copy-start(s32[8]{0:T(128)} %param.9) | copy-start | bytes 100
  0.0 24.4 %copy-start.7 = (f32[3,2,32,16]{2,3,1,0:T(8,128)S(1)}, f32[3,2,32,16]{2,3,1,0:T(8,128)}, u32[]{:S(2)}) copy-start(f32[3,2,32,16]{2,3,1,0:T(8,128)} %param.10) | copy-start | bytes 36868
  2.4 19.9 %copy-start.1 = (f32[2,8,27,256]{3,2,1,0:T(8,128)S(1)}, f32[2,8,27,256]{3,2,1,0:T(8,128)}, u32[]{:S(2)}) copy-start(f32[2,8,27,256]{3,2,1,0:T(8,128)} %get-tuple-element.7) | copy-start | bytes 1327108
  3.4 22.5 %copy-start.4 = (f32[3,2,8,256]{3,2,1,0:T(8,128)S(1)}, f32[3,2,8,256]{3,2,1,0:T(8,128)}, u32[]{:S(2)}) copy-start(f32[3,2,8,256]{3,2,1,0:T(8,128)} %get-tuple-element.8) | copy-start | bytes 147460
  4.3 1.3 %collective-permute-start = (f32[3,2,32,16]{2,3,1,0:T(8,128)S(1)}, f32[3,2,32,16]{2,3,1,0:T(8,128)S(1)}, u32[]{:S(2)}, u32[]{:S(2)}) collective-permute-start(f32[3,2,32,16]{2,3,1,0:T(8,128)S(1)} %convolution_bitcast_fusion), channel_id=1, source_target_pairs={{0,1},{1,0},{2,3},{3,2},{4,5},{5,4},{6,7},{7,6},{8,9},{9,8},{10,11... | collective-permute-start | bytes 36872 | tf_op jit(solution)/shard_map/ppermute | solution.py:23
  5.7 20.5 %copy-start.8 = (f32[27,27,1,1]{1,0,3,2:T(8,128)S(1)}, f32[27,27,1,1]{1,0,3,2:T(8,128)}, u32[]{:S(2)}) copy-start(f32[27,27,1,1]{1,0,3,2:T(8,128)} %constant.44) | copy-start | bytes 8752
  5.7 20.5 %copy-start.11 = (f32[27]{0:T(128)S(1)}, f32[27]{0:T(128)}, u32[]{:S(2)}) copy-start(f32[27]{0:T(128)} %param.11) | copy-start | bytes 328
  5.7 4.2 %collective-permute-start.1 = (f32[3,2,32,16]{2,3,1,0:T(8,128)S(1)}, f32[3,2,32,16]{2,3,1,0:T(8,128)S(1)}, u32[]{:S(2)}, u32[]{:S(2)}) collective-permute-start(f32[3,2,32,16]{2,3,1,0:T(8,128)S(1)} %add.43), channel_id=1, source_target_pairs={{0,2},{1,3},{2,0},{3,1},{4,6},{5,7},{6,4},{7,5},{8,10},{9,11},{10,... | collective-permute-start | bytes 36872 | tf_op jit(solution)/shard_map/ppermute | solution.py:23
  9.9 5.6 %collective-permute-start.2 = (f32[3,2,32,16]{2,3,1,0:T(8,128)S(1)}, f32[3,2,32,16]{2,3,1,0:T(8,128)S(1)}, u32[]{:S(2)}, u32[]{:S(2)}) collective-permute-start(f32[3,2,32,16]{2,3,1,0:T(8,128)S(1)} %add.44), channel_id=1, source_target_pairs={{0,4},{1,5},{2,6},{3,7},{4,0},{5,1},{6,2},{7,3},{8,12},{9,13},{10,... | collective-permute-start | bytes 36872 | tf_op jit(solution)/shard_map/ppermute | solution.py:23
  15.5 8.9 %collective-permute-start.3 = (f32[3,2,32,16]{2,3,1,0:T(8,128)S(1)}, f32[3,2,32,16]{2,3,1,0:T(8,128)S(1)}, u32[]{:S(2)}, u32[]{:S(2)}) collective-permute-start(f32[3,2,32,16]{2,3,1,0:T(8,128)S(1)} %add.45), channel_id=1, source_target_pairs={{0,8},{1,9},{2,10},{3,11},{4,12},{5,13},{6,14},{7,15},{8,0},{9,1},... | collective-permute-start | bytes 36872 | tf_op jit(solution)/shard_map/ppermute | solution.py:23
  27.1 1.1 %copy-start = (f32[2,8,256,27]{2,3,1,0:T(8,128)}, f32[2,8,256,27]{2,3,1,0:T(8,128)S(1)}, u32[]{:S(2)}) copy-start(f32[2,8,256,27]{2,3,1,0:T(8,128)S(1)} %fusion.3) | copy-start | bytes 1327108
  28.1 4.8 %collective-permute-start.4 = (f32[112,16]{1,0:T(8,128)S(1)}, f32[112,16]{1,0:T(8,128)S(1)}, u32[]{:S(2)}, u32[]{:S(2)}) collective-permute-start(f32[112,16]{1,0:T(8,128)S(1)} %bitcast.80), channel_id=1, source_target_pairs={{0,1},{1,2},{2,3},{3,4},{4,5},{5,6},{6,7},{7,8},{8,9},{9,10},{10,1... | collective-permute-start | bytes 21512 | tf_op jit(solution)/shard_map/ppermute | solution.py:341
  28.3 4.8 %collective-permute-start.5 = (f32[112,16]{1,0:T(8,128)S(1)}, f32[112,16]{1,0:T(8,128)S(1)}, u32[]{:S(2)}, u32[]{:S(2)}) collective-permute-start(f32[112,16]{1,0:T(8,128)S(1)} %bitcast.81), channel_id=1, source_target_pairs={{1,0},{2,1},{3,2},{4,3},{5,4},{6,5},{7,6},{8,7},{9,8},{10,9},{11,1... | collective-permute-start | bytes 21512 | tf_op jit(solution)/shard_map/ppermute | solution.py:342
  32.9 3.5 %copy-start.2 = (f32[112,16]{1,0:T(8,128)}, f32[112,16]{1,0:T(8,128)S(1)}, u32[]{:S(2)}) copy-start(f32[112,16]{1,0:T(8,128)S(1)} %collective-permute-done.4.left_ref) | copy-start | bytes 21508
  33.1 3.2 %copy-start.3 = (f32[112,16]{1,0:T(8,128)}, f32[112,16]{1,0:T(8,128)S(1)}, u32[]{:S(2)}) copy-start(f32[112,16]{1,0:T(8,128)S(1)} %collective-permute-done.5.right_ref) | copy-start | bytes 21508
  34.0 6.2 %collective-permute-start.6 = (f32[336,16]{1,0:T(8,128)S(1)}, f32[336,16]{1,0:T(8,128)S(1)}, u32[]{:S(2)}, u32[]{:S(2)}) collective-permute-start(f32[336,16]{1,0:T(8,128)S(1)} %reshape.99), channel_id=1, source_target_pairs={{0,16},{16,32},{32,48},{48,64},{64,80},{80,96},{96,112},{112,128},... | collective-permute-start | bytes 64520 | tf_op jit(solution)/shard_map/ppermute | solution.py:357
  35.2 8.8 %collective-permute-start.7 = (f32[336,16]{1,0:T(8,128)S(1)}, f32[336,16]{1,0:T(8,128)S(1)}, u32[]{:S(2)}, u32[]{:S(2)}) collective-permute-start(f32[336,16]{1,0:T(8,128)S(1)} %reshape.100), channel_id=1, source_target_pairs={{16,0},{32,16},{48,32},{64,48},{80,64},{96,80},{112,96},{128,112},... | collective-permute-start | bytes 64520 | tf_op jit(solution)/shard_map/ppermute | solution.py:358
  40.3 3.8 %copy-start.5 = (f32[336,16]{1,0:T(8,128)}, f32[336,16]{1,0:T(8,128)S(1)}, u32[]{:S(2)}) copy-start(f32[336,16]{1,0:T(8,128)S(1)} %collective-permute-done.6.below_ref) | copy-start | bytes 64516
  44.1 0.7 %copy-start.6 = (f32[336,16]{1,0:T(8,128)}, f32[336,16]{1,0:T(8,128)S(1)}, u32[]{:S(2)}) copy-start(f32[336,16]{1,0:T(8,128)S(1)} %collective-permute-done.7.above_ref) | copy-start | bytes 64516

commit v19 on v16

--- a/solution.py
+++ b/solution.py
@@ -292,13 +292,13 @@
     mode_basis = mode_basis_at(retained_wavenumbers, own_columns, line_length).reshape(TX, BE, -1)
     partial = jnp.einsum(
         "kzyxrq,xqm->kzyrm", wind.reshape(3, levels, TY, TX, BE, BE), mode_basis,
-        precision=HIGHEST,
+        precision=lax.Precision.HIGH,
     ).reshape(3, levels, rows_tile, -1)
     coefficients = butterfly_sum(partial, "line")
     misfit = regional_amplitudes - 2.0 / line_length * coefficients
     nudge = NUDGE_GAIN * jnp.einsum(
         "kzyrm,xqm->kzyxrq", misfit.reshape(3, levels, TY, BE, -1), mode_basis,
-        precision=HIGHEST,
+        precision=lax.Precision.HIGH,
     ).reshape(3, levels, blocks, cells)
     post = collide_blocks(moments, wind, nudge, backward, relaxation_frequencies)
     present = jnp.any(living_brick_keys[None, :] == jnp.arange(blocks, dtype=jnp.int32)[:, None], axis=1)

time: 48 us -> 47.6 us (level)
  no operation moved by 1% of the time
where the time goes in v19:
time: 47.6 us; the launch traced here: 47.4 us
  starting transfers between devices  17.4 us (37%)
  waiting for transfers between devices  17 us (36%)
  Pallas kernels  5.57 us (12%)
  local copies, waits for them, and re-layouts  4.77 us (10%)
  matrix products  1.75 us (4%)
  other arithmetic  0.7 us (1%)
    ppermute x4, starting transfers between devices, butterfly_sum(): lax.ppermute(value, axis, [(i, i ^ stride) for i in range(count)])  12.2 us
    ppermute x4, waiting for transfers between devices, butterfly_sum(): lax.ppermute(value, axis, [(i, i ^ stride) for i in range(count)])  7.65 us
    ppermute x1, waiting for transfers between devices, on_device(): below = lax.ppermute(flat(top_row), 'curve', ahead).reshape(row_shape)  3.92 us
    ppermute x1, waiting for transfers between devices, on_device(): above = lax.ppermute(flat(bottom_row), 'curve', behind).reshape(row_shape)  3.78 us
    pallas_call x1, Pallas kernels, stream(): pl.pallas_call(stream_kernel, out_shape=jax.ShapeDtypeStruct((seats * cha...  3.18 us
    ppermute x1, starting transfers between devices, on_device(): lax.ppermute(flat(by_rows[:, :, :, 0, :, 0]), 'line', behind)  2.95 us
    pallas_call x1, Pallas kernels, cell_moments(): pl.pallas_call(moments_kernel, out_shape=(jax.ShapeDtypeStruct((levels, b...  2.38 us
    ppermute x1, waiting for transfers between devices, on_device(): lax.ppermute(flat(by_rows[:, :, :, TX - 1, :, BE - 1]), 'line', ahead)  1.62 us
  transfers between devices with their start and end apart: 8, of which 7 were waited for; matrix products, arithmetic and copies ran while one was open for 1% of the time, Pallas kernels for 0%

profile of v19, /device:TPU:30, one launch (start us, length us, event | category | flops | bytes accessed | tf_op | source)
XLA Modules:
  0.0 47.4 jit_solution(7425025012861393764)
XLA Ops:
  0.0 2.4 %shard_map.73 = (f32[2,8,27,256]{3,2,1,0:T(8,128)}, f32[3,2,8,256]{3,2,1,0:T(8,128)}) custom-call(s32[6]{0:T(128)} %bitcast.85, f32[27,27]{1,0:T(8,128)} %constant.40.clone.forward_ref, f32[648,128]{1,0:T(8,128)} %bitcast.75), custom_call_target="tpu_custom_call" | custom-call | tf_op jit(solution)/shard_map/pallas_call | solution.py:119
  2.4 1.0 %reshape.94 = f32[3,2,2,4,16,16]{5,4,3,2,1,0:T(8,128)S(1)} reshape(f32[3,2,8,256]{3,2,1,0:T(8,128)} %get-tuple-element.8) | data formatting | bytes 98304 | tf_op jit(solution)/shard_map/reshape | solution.py:294
  3.4 0.2 copy.39
  3.6 0.2 dot_general.16
  3.9 0.2 fusion.15
  4.1 0.2 convolution_bitcast_fusion
  4.4 1.2 %collective-permute-done = f32[3,2,32,16]{2,3,1,0:T(8,128)S(1)} collective-permute-done((f32[3,2,32,16]{2,3,1,0:T(8,128)S(1)}, f32[3,2,32,16]{2,3,1,0:T(8,128)S(1)}, u32[]{:S(2)}, u32[]{:S(2)}) %collective-permute-start) | collective-permute-done | bytes 12320 | tf_op jit(solution)/shard_map/ppermute | solution.py:23
  5.6 2.0 %collective-permute-start.1 = (f32[3,2,32,16]{2,3,1,0:T(8,128)S(1)}, f32[3,2,32,16]{2,3,1,0:T(8,128)S(1)}, u32[]{:S(2)}, u32[]{:S(2)}) collective-permute-start(f32[3,2,32,16]{2,3,1,0:T(8,128)S(1)} %add.43), channel_id=1, source_target_pairs={{0,2},{1,3},{2,0},{3,1},{4,6},{5,7},{6,4},{7,5},{8,10},{9,11},{10,... | collective-permute-start | bytes 36872 | tf_op jit(solution)/shard_map/ppermute | solution.py:23
  7.6 2.2 %collective-permute-done.1 = f32[3,2,32,16]{2,3,1,0:T(8,128)S(1)} collective-permute-done((f32[3,2,32,16]{2,3,1,0:T(8,128)S(1)}, f32[3,2,32,16]{2,3,1,0:T(8,128)S(1)}, u32[]{:S(2)}, u32[]{:S(2)}) %collective-permute-start.1) | collective-permute-done | bytes 12320 | tf_op jit(solution)/shard_map/ppermute | solution.py:23
  9.8 3.4 %collective-permute-start.2 = (f32[3,2,32,16]{2,3,1,0:T(8,128)S(1)}, f32[3,2,32,16]{2,3,1,0:T(8,128)S(1)}, u32[]{:S(2)}, u32[]{:S(2)}) collective-permute-start(f32[3,2,32,16]{2,3,1,0:T(8,128)S(1)} %add.44), channel_id=1, source_target_pairs={{0,4},{1,5},{2,6},{3,7},{4,0},{5,1},{6,2},{7,3},{8,12},{9,13},{10,... | collective-permute-start | bytes 36872 | tf_op jit(solution)/shard_map/ppermute | solution.py:23
  13.2 0.1 fusion.16
  13.3 2.1 %collective-permute-done.2 = f32[3,2,32,16]{2,3,1,0:T(8,128)S(1)} collective-permute-done((f32[3,2,32,16]{2,3,1,0:T(8,128)S(1)}, f32[3,2,32,16]{2,3,1,0:T(8,128)S(1)}, u32[]{:S(2)}, u32[]{:S(2)}) %collective-permute-start.2) | collective-permute-done | bytes 12320 | tf_op jit(solution)/shard_map/ppermute | solution.py:23
  15.5 6.8 %collective-permute-start.3 = (f32[3,2,32,16]{2,3,1,0:T(8,128)S(1)}, f32[3,2,32,16]{2,3,1,0:T(8,128)S(1)}, u32[]{:S(2)}, u32[]{:S(2)}) collective-permute-start(f32[3,2,32,16]{2,3,1,0:T(8,128)S(1)} %add.45), channel_id=1, source_target_pairs={{0,8},{1,9},{2,10},{3,11},{4,12},{5,13},{6,14},{7,15},{8,0},{9,1},... | collective-permute-start | bytes 36872 | tf_op jit(solution)/shard_map/ppermute | solution.py:23
  22.3 2.1 %collective-permute-done.3 = f32[3,2,32,16]{2,3,1,0:T(8,128)S(1)} collective-permute-done((f32[3,2,32,16]{2,3,1,0:T(8,128)S(1)}, f32[3,2,32,16]{2,3,1,0:T(8,128)S(1)}, u32[]{:S(2)}, u32[]{:S(2)}) %collective-permute-start.3) | collective-permute-done | bytes 12320 | tf_op jit(solution)/shard_map/ppermute | solution.py:23
  24.5 0.6 %fusion = f32[3,2,2,4,16,16]{4,5,2,1,0,3:T(8,128)S(1)} fusion(f32[3,2,2,16,16,1]{4,3,2,1,0,5:T(8,128)S(1)} %bitcast.74, f32[4,16,8]{1,2,0:T(8,128)S(1)} %get-tuple-element.22, f32[4,16,8]{1,2,0:T(8,128)S(1)} %get-tuple-element.21), kind=kOutput, calls=%fused_computation.1 | convolution fusion | flops 1192960 | bytes 65536 | tf_op jit(solution)/shard_map/kzyrm,xqm->kzyxrq/dot_general | solution.py:299
  25.1 0.2 copy.42
  25.3 0.2 mul.123
  25.7 0.9 %fusion.3 = f32[2,8,256,27]{2,3,1,0:T(8,128)S(1)} fusion(f32[27,27,1,1]{1,0,3,2:T(8,128)S(1)} %copy-done.8, f32[27,2,8,256]{3,2,1,0:T(8,128)S(1)} %bitcast.71, f32[27]{0:T(128)S(1)} %copy-done.11, f32[2,8,27,256]{3,2,1,0:T(8,128)S(1)} %copy-done.1), kind=kOutput, calls=%fused_computation.9 | convolution fusion | flops 36163584 | bytes 1330128 | tf_op jit(solution)/shard_map/ij,jzpl->izpl/dot_general | solution.py:80
  26.8 0.6 %copy.44 = f32[28,2,8,256]{0,3,2,1:T(8,128)S(1)} copy(f32[28,2,8,256]{3,0,2,1:T(8,128)S(1)} %pad_maximum_fusion) | data formatting | bytes 917504 | tf_op jit(solution)/shard_map/concatenate | solution.py:307
  27.5 0.1 copy.45
  27.7 0.1 copy.47
  27.8 3.0 %collective-permute-start.5 = (f32[112,16]{1,0:T(8,128)S(1)}, f32[112,16]{1,0:T(8,128)S(1)}, u32[]{:S(2)}, u32[]{:S(2)}) collective-permute-start(f32[112,16]{1,0:T(8,128)S(1)} %bitcast.80), channel_id=1, source_target_pairs={{1,0},{2,1},{3,2},{4,3},{5,4},{6,5},{7,6},{8,7},{9,8},{10,9},{11,1... | collective-permute-start | bytes 21512 | tf_op jit(solution)/shard_map/ppermute | solution.py:314
  30.8 1.6 %collective-permute-done.4.left_ref = f32[112,16]{1,0:T(8,128)S(1)} collective-permute-done((f32[112,16]{1,0:T(8,128)S(1)}, f32[112,16]{1,0:T(8,128)S(1)}, u32[]{:S(2)}, u32[]{:S(2)}) %collective-permute-start.4) | collective-permute-done | bytes 7200 | tf_op jit(solution)/shard_map/ppermute | solution.py:313
  32.4 0.1 fusion.21
  32.6 0.1 fusion.22
  33.4 0.1 copy.49
  33.5 1.1 %collective-permute-start.6 = (f32[336,16]{1,0:T(8,128)S(1)}, f32[336,16]{1,0:T(8,128)S(1)}, u32[]{:S(2)}, u32[]{:S(2)}) collective-permute-start(f32[336,16]{1,0:T(8,128)S(1)} %reshape.99), channel_id=1, source_target_pairs={{0,16},{16,32},{32,48},{48,64},{64,80},{80,96},{96,112},{112,128},... | collective-permute-start | bytes 64520 | tf_op jit(solution)/shard_map/ppermute | solution.py:329
  34.8 1.1 %collective-permute-start.7 = (f32[336,16]{1,0:T(8,128)S(1)}, f32[336,16]{1,0:T(8,128)S(1)}, u32[]{:S(2)}, u32[]{:S(2)}) collective-permute-start(f32[336,16]{1,0:T(8,128)S(1)} %reshape.100), channel_id=1, source_target_pairs={{16,0},{32,16},{48,32},{64,48},{80,64},{96,80},{112,96},{128,112},... | collective-permute-start | bytes 64520 | tf_op jit(solution)/shard_map/ppermute | solution.py:330
  35.9 3.9 %collective-permute-done.6.below_ref = f32[336,16]{1,0:T(8,128)S(1)} collective-permute-done((f32[336,16]{1,0:T(8,128)S(1)}, f32[336,16]{1,0:T(8,128)S(1)}, u32[]{:S(2)}, u32[]{:S(2)}) %collective-permute-start.6) | collective-permute-done | bytes 21536 | tf_op jit(solution)/shard_map/ppermute | solution.py:329
  39.8 3.8 %collective-permute-done.7.above_ref = f32[336,16]{1,0:T(8,128)S(1)} collective-permute-done((f32[336,16]{1,0:T(8,128)S(1)}, f32[336,16]{1,0:T(8,128)S(1)}, u32[]{:S(2)}, u32[]{:S(2)}) %collective-permute-start.7) | collective-permute-done | bytes 21536 | tf_op jit(solution)/shard_map/ppermute | solution.py:330
  43.6 0.7 %copy-done.6 = f32[336,16]{1,0:T(8,128)} copy-done((f32[336,16]{1,0:T(8,128)}, f32[336,16]{1,0:T(8,128)S(1)}, u32[]{:S(2)}) %copy-start.6) | copy-done | bytes 21528
  44.2 3.2 %shard_map.74 = f32[648,128]{1,0:T(8,128)} custom-call(s32[6]{0:T(128)} %bitcast.86, f32[2,8,27,256]{3,2,1,0:T(8,128)} %bitcast.69, f32[336,16]{1,0:T(8,128)} %copy-done.5, f32[336,16]{1,0:T(8,128)} %copy-done.6, f32[112,16]{1,0:T(8,128)} %copy-done.2, f32[112,16]{1,0:T(8,128)} %copy-done.3), custom_call_target="tpu_custom_call" | custom-call | tf_op jit(solution)/shard_map/pallas_call | solution.py:257
  (58 shorter events, 1.6 us)
Async XLA Ops:
  0.0 13.2 %copy-start.9 = (s32[1,1,6]{2,1,0:T(1,128)S(1)}, s32[1,1,6]{2,1,0:T(1,128)}, u32[]{:S(2)}) copy-start(s32[1,1,6]{2,1,0:T(1,128)} %param.8) | copy-start | bytes 76
  0.0 3.9 %copy-start.10 = (s32[8]{0:T(128)S(1)}, s32[8]{0:T(128)}, u32[]{:S(2)}) copy-start(s32[8]{0:T(128)} %param.9) | copy-start | bytes 100
  0.0 24.4 %copy-start.7 = (f32[3,2,32,16]{2,3,1,0:T(8,128)S(1)}, f32[3,2,32,16]{2,3,1,0:T(8,128)}, u32[]{:S(2)}) copy-start(f32[3,2,32,16]{2,3,1,0:T(8,128)} %param.10) | copy-start | bytes 36868
  2.4 19.8 %copy-start.1 = (f32[2,8,27,256]{3,2,1,0:T(8,128)S(1)}, f32[2,8,27,256]{3,2,1,0:T(8,128)}, u32[]{:S(2)}) copy-start(f32[2,8,27,256]{3,2,1,0:T(8,128)} %get-tuple-element.7) | copy-start | bytes 1327108
  3.4 22.1 %copy-start.4 = (f32[3,2,8,256]{3,2,1,0:T(8,128)S(1)}, f32[3,2,8,256]{3,2,1,0:T(8,128)}, u32[]{:S(2)}) copy-start(f32[3,2,8,256]{3,2,1,0:T(8,128)} %get-tuple-element.8) | copy-start | bytes 147460
  4.3 1.3 %collective-permute-start = (f32[3,2,32,16]{2,3,1,0:T(8,128)S(1)}, f32[3,2,32,16]{2,3,1,0:T(8,128)S(1)}, u32[]{:S(2)}, u32[]{:S(2)}) collective-permute-start(f32[3,2,32,16]{2,3,1,0:T(8,128)S(1)} %convolution_bitcast_fusion), channel_id=1, source_target_pairs={{0,1},{1,0},{2,3},{3,2},{4,5},{5,4},{6,7},{7,6},{8,9},{9,8},{10,11... | collective-permute-start | bytes 36872 | tf_op jit(solution)/shard_map/ppermute | solution.py:23
  5.6 20.1 %copy-start.8 = (f32[27,27,1,1]{1,0,3,2:T(8,128)S(1)}, f32[27,27,1,1]{1,0,3,2:T(8,128)}, u32[]{:S(2)}) copy-start(f32[27,27,1,1]{1,0,3,2:T(8,128)} %constant.44) | copy-start | bytes 8752
  5.6 20.1 %copy-start.11 = (f32[27]{0:T(128)S(1)}, f32[27]{0:T(128)}, u32[]{:S(2)}) copy-start(f32[27]{0:T(128)} %param.11) | copy-start | bytes 328
  5.6 4.2 %collective-permute-start.1 = (f32[3,2,32,16]{2,3,1,0:T(8,128)S(1)}, f32[3,2,32,16]{2,3,1,0:T(8,128)S(1)}, u32[]{:S(2)}, u32[]{:S(2)}) collective-permute-start(f32[3,2,32,16]{2,3,1,0:T(8,128)S(1)} %add.43), channel_id=1, source_target_pairs={{0,2},{1,3},{2,0},{3,1},{4,6},{5,7},{6,4},{7,5},{8,10},{9,11},{10,... | collective-permute-start | bytes 36872 | tf_op jit(solution)/shard_map/ppermute | solution.py:23
  9.8 5.6 %collective-permute-start.2 = (f32[3,2,32,16]{2,3,1,0:T(8,128)S(1)}, f32[3,2,32,16]{2,3,1,0:T(8,128)S(1)}, u32[]{:S(2)}, u32[]{:S(2)}) collective-permute-start(f32[3,2,32,16]{2,3,1,0:T(8,128)S(1)} %add.44), channel_id=1, source_target_pairs={{0,4},{1,5},{2,6},{3,7},{4,0},{5,1},{6,2},{7,3},{8,12},{9,13},{10,... | collective-permute-start | bytes 36872 | tf_op jit(solution)/shard_map/ppermute | solution.py:23
  15.5 8.9 %collective-permute-start.3 = (f32[3,2,32,16]{2,3,1,0:T(8,128)S(1)}, f32[3,2,32,16]{2,3,1,0:T(8,128)S(1)}, u32[]{:S(2)}, u32[]{:S(2)}) collective-permute-start(f32[3,2,32,16]{2,3,1,0:T(8,128)S(1)} %add.45), channel_id=1, source_target_pairs={{0,8},{1,9},{2,10},{3,11},{4,12},{5,13},{6,14},{7,15},{8,0},{9,1},... | collective-permute-start | bytes 36872 | tf_op jit(solution)/shard_map/ppermute | solution.py:23
  26.6 1.1 %copy-start = (f32[2,8,256,27]{2,3,1,0:T(8,128)}, f32[2,8,256,27]{2,3,1,0:T(8,128)S(1)}, u32[]{:S(2)}) copy-start(f32[2,8,256,27]{2,3,1,0:T(8,128)S(1)} %fusion.3) | copy-start | bytes 1327108
  27.6 4.8 %collective-permute-start.4 = (f32[112,16]{1,0:T(8,128)S(1)}, f32[112,16]{1,0:T(8,128)S(1)}, u32[]{:S(2)}, u32[]{:S(2)}) collective-permute-start(f32[112,16]{1,0:T(8,128)S(1)} %bitcast.79), channel_id=1, source_target_pairs={{0,1},{1,2},{2,3},{3,4},{4,5},{5,6},{6,7},{7,8},{8,9},{9,10},{10,1... | collective-permute-start | bytes 21512 | tf_op jit(solution)/shard_map/ppermute | solution.py:313
  27.8 4.8 %collective-permute-start.5 = (f32[112,16]{1,0:T(8,128)S(1)}, f32[112,16]{1,0:T(8,128)S(1)}, u32[]{:S(2)}, u32[]{:S(2)}) collective-permute-start(f32[112,16]{1,0:T(8,128)S(1)} %bitcast.80), channel_id=1, source_target_pairs={{1,0},{2,1},{3,2},{4,3},{5,4},{6,5},{7,6},{8,7},{9,8},{10,9},{11,1... | collective-permute-start | bytes 21512 | tf_op jit(solution)/shard_map/ppermute | solution.py:314
  32.4 11.2 %copy-start.2 = (f32[112,16]{1,0:T(8,128)}, f32[112,16]{1,0:T(8,128)S(1)}, u32[]{:S(2)}) copy-start(f32[112,16]{1,0:T(8,128)S(1)} %collective-permute-done.4.left_ref) | copy-start | bytes 21508
  32.6 10.9 %copy-start.3 = (f32[112,16]{1,0:T(8,128)}, f32[112,16]{1,0:T(8,128)S(1)}, u32[]{:S(2)}) copy-start(f32[112,16]{1,0:T(8,128)S(1)} %collective-permute-done.5.right_ref) | copy-start | bytes 21508
  33.5 6.2 %collective-permute-start.6 = (f32[336,16]{1,0:T(8,128)S(1)}, f32[336,16]{1,0:T(8,128)S(1)}, u32[]{:S(2)}, u32[]{:S(2)}) collective-permute-start(f32[336,16]{1,0:T(8,128)S(1)} %reshape.99), channel_id=1, source_target_pairs={{0,16},{16,32},{32,48},{48,64},{64,80},{80,96},{96,112},{112,128},... | collective-permute-start | bytes 64520 | tf_op jit(solution)/shard_map/ppermute | solution.py:329
  34.8 8.8 %collective-permute-start.7 = (f32[336,16]{1,0:T(8,128)S(1)}, f32[336,16]{1,0:T(8,128)S(1)}, u32[]{:S(2)}, u32[]{:S(2)}) collective-permute-start(f32[336,16]{1,0:T(8,128)S(1)} %reshape.100), channel_id=1, source_target_pairs={{16,0},{32,16},{48,32},{64,48},{80,64},{96,80},{112,96},{128,112},... | collective-permute-start | bytes 64520 | tf_op jit(solution)/shard_map/ppermute | solution.py:330
  39.8 3.8 %copy-start.5 = (f32[336,16]{1,0:T(8,128)}, f32[336,16]{1,0:T(8,128)S(1)}, u32[]{:S(2)}) copy-start(f32[336,16]{1,0:T(8,128)S(1)} %collective-permute-done.6.below_ref) | copy-start | bytes 64516
  43.6 0.7 %copy-start.6 = (f32[336,16]{1,0:T(8,128)}, f32[336,16]{1,0:T(8,128)S(1)}, u32[]{:S(2)}) copy-start(f32[336,16]{1,0:T(8,128)S(1)} %collective-permute-done.7.above_ref) | copy-start | bytes 64516

commit v20 on v19

--- a/solution.py
+++ b/solution.py
@@ -142,11 +142,11 @@
     column_count = left_ref.shape[0]
     for slot, source in enumerate((below_ref, above_ref)):
         spread_ref[slot, front:front + row_count, :] = jnp.dot(
-            source[...], tile_copy, precision=HIGHEST, preferred_element_type=jnp.float32
+            source[...], tile_copy, precision=lax.Precision.HIGH, preferred_element_type=jnp.float32
         )
     for slot, source in enumerate((left_ref, right_ref)):
         column_ref[slot, front:front + column_count, :] = jnp.dot(
-            source[...], group_copy, precision=HIGHEST, preferred_element_type=jnp.float32
+            source[...], group_copy, precision=lax.Precision.HIGH, preferred_element_type=jnp.float32
         )
     lane = lax.broadcasted_iota(jnp.int32, (blocks, cells), 1)
     seat = lax.broadcasted_iota(jnp.int32, (blocks, cells), 0)

time: 47.6 us -> 47.2 us (level)
  no operation moved by 1% of the time
where the time goes in v20:
time: 47.2 us; the launch traced here: 47.1 us
  starting transfers between devices  17.4 us (37%)
  waiting for transfers between devices  17 us (36%)
  Pallas kernels  5.23 us (11%)
  local copies, waits for them, and re-layouts  4.77 us (10%)
  matrix products  1.75 us (4%)
  other arithmetic  0.7 us (1%)
    ppermute x4, starting transfers between devices, butterfly_sum(): lax.ppermute(value, axis, [(i, i ^ stride) for i in range(count)])  12.2 us
    ppermute x4, waiting for transfers between devices, butterfly_sum(): lax.ppermute(value, axis, [(i, i ^ stride) for i in range(count)])  7.65 us
    ppermute x1, waiting for transfers between devices, on_device(): below = lax.ppermute(flat(top_row), 'curve', ahead).reshape(row_shape)  3.92 us
    ppermute x1, waiting for transfers between devices, on_device(): above = lax.ppermute(flat(bottom_row), 'curve', behind).reshape(row_shape)  3.78 us
    ppermute x1, starting transfers between devices, on_device(): lax.ppermute(flat(by_rows[:, :, :, 0, :, 0]), 'line', behind)  2.95 us
    pallas_call x1, Pallas kernels, stream(): pl.pallas_call(stream_kernel, out_shape=jax.ShapeDtypeStruct((seats * cha...  2.85 us
    pallas_call x1, Pallas kernels, cell_moments(): pl.pallas_call(moments_kernel, out_shape=(jax.ShapeDtypeStruct((levels, b...  2.38 us
    ppermute x1, waiting for transfers between devices, on_device(): lax.ppermute(flat(by_rows[:, :, :, TX - 1, :, BE - 1]), 'line', ahead)  1.62 us
  transfers between devices with their start and end apart: 8, of which 7 were waited for; matrix products, arithmetic and copies ran while one was open for 1% of the time, Pallas kernels for 0%

profile of v20, /device:TPU:30, one launch (start us, length us, event | category | flops | bytes accessed | tf_op | source)
XLA Modules:
  0.0 47.1 jit_solution(10144316346297496993)
XLA Ops:
  0.0 2.4 %shard_map.73 = (f32[2,8,27,256]{3,2,1,0:T(8,128)}, f32[3,2,8,256]{3,2,1,0:T(8,128)}) custom-call(s32[6]{0:T(128)} %bitcast.85, f32[27,27]{1,0:T(8,128)} %constant.40.clone.forward_ref, f32[648,128]{1,0:T(8,128)} %bitcast.75), custom_call_target="tpu_custom_call" | custom-call | tf_op jit(solution)/shard_map/pallas_call | solution.py:119
  2.4 1.0 %reshape.94 = f32[3,2,2,4,16,16]{5,4,3,2,1,0:T(8,128)S(1)} reshape(f32[3,2,8,256]{3,2,1,0:T(8,128)} %get-tuple-element.8) | data formatting | bytes 98304 | tf_op jit(solution)/shard_map/reshape | solution.py:294
  3.4 0.2 copy.39
  3.6 0.2 dot_general.16
  3.9 0.2 fusion.15
  4.1 0.2 convolution_bitcast_fusion
  4.4 1.2 %collective-permute-done = f32[3,2,32,16]{2,3,1,0:T(8,128)S(1)} collective-permute-done((f32[3,2,32,16]{2,3,1,0:T(8,128)S(1)}, f32[3,2,32,16]{2,3,1,0:T(8,128)S(1)}, u32[]{:S(2)}, u32[]{:S(2)}) %collective-permute-start) | collective-permute-done | bytes 12320 | tf_op jit(solution)/shard_map/ppermute | solution.py:23
  5.6 2.0 %collective-permute-start.1 = (f32[3,2,32,16]{2,3,1,0:T(8,128)S(1)}, f32[3,2,32,16]{2,3,1,0:T(8,128)S(1)}, u32[]{:S(2)}, u32[]{:S(2)}) collective-permute-start(f32[3,2,32,16]{2,3,1,0:T(8,128)S(1)} %add.43), channel_id=1, source_target_pairs={{0,2},{1,3},{2,0},{3,1},{4,6},{5,7},{6,4},{7,5},{8,10},{9,11},{10,... | collective-permute-start | bytes 36872 | tf_op jit(solution)/shard_map/ppermute | solution.py:23
  7.6 2.2 %collective-permute-done.1 = f32[3,2,32,16]{2,3,1,0:T(8,128)S(1)} collective-permute-done((f32[3,2,32,16]{2,3,1,0:T(8,128)S(1)}, f32[3,2,32,16]{2,3,1,0:T(8,128)S(1)}, u32[]{:S(2)}, u32[]{:S(2)}) %collective-permute-start.1) | collective-permute-done | bytes 12320 | tf_op jit(solution)/shard_map/ppermute | solution.py:23
  9.8 3.4 %collective-permute-start.2 = (f32[3,2,32,16]{2,3,1,0:T(8,128)S(1)}, f32[3,2,32,16]{2,3,1,0:T(8,128)S(1)}, u32[]{:S(2)}, u32[]{:S(2)}) collective-permute-start(f32[3,2,32,16]{2,3,1,0:T(8,128)S(1)} %add.44), channel_id=1, source_target_pairs={{0,4},{1,5},{2,6},{3,7},{4,0},{5,1},{6,2},{7,3},{8,12},{9,13},{10,... | collective-permute-start | bytes 36872 | tf_op jit(solution)/shard_map/ppermute | solution.py:23
  13.2 0.1 fusion.16
  13.3 2.1 %collective-permute-done.2 = f32[3,2,32,16]{2,3,1,0:T(8,128)S(1)} collective-permute-done((f32[3,2,32,16]{2,3,1,0:T(8,128)S(1)}, f32[3,2,32,16]{2,3,1,0:T(8,128)S(1)}, u32[]{:S(2)}, u32[]{:S(2)}) %collective-permute-start.2) | collective-permute-done | bytes 12320 | tf_op jit(solution)/shard_map/ppermute | solution.py:23
  15.5 6.8 %collective-permute-start.3 = (f32[3,2,32,16]{2,3,1,0:T(8,128)S(1)}, f32[3,2,32,16]{2,3,1,0:T(8,128)S(1)}, u32[]{:S(2)}, u32[]{:S(2)}) collective-permute-start(f32[3,2,32,16]{2,3,1,0:T(8,128)S(1)} %add.45), channel_id=1, source_target_pairs={{0,8},{1,9},{2,10},{3,11},{4,12},{5,13},{6,14},{7,15},{8,0},{9,1},... | collective-permute-start | bytes 36872 | tf_op jit(solution)/shard_map/ppermute | solution.py:23
  22.3 2.1 %collective-permute-done.3 = f32[3,2,32,16]{2,3,1,0:T(8,128)S(1)} collective-permute-done((f32[3,2,32,16]{2,3,1,0:T(8,128)S(1)}, f32[3,2,32,16]{2,3,1,0:T(8,128)S(1)}, u32[]{:S(2)}, u32[]{:S(2)}) %collective-permute-start.3) | collective-permute-done | bytes 12320 | tf_op jit(solution)/shard_map/ppermute | solution.py:23
  24.5 0.6 %fusion = f32[3,2,2,4,16,16]{4,5,2,1,0,3:T(8,128)S(1)} fusion(f32[3,2,2,16,16,1]{4,3,2,1,0,5:T(8,128)S(1)} %bitcast.74, f32[4,16,8]{1,2,0:T(8,128)S(1)} %get-tuple-element.22, f32[4,16,8]{1,2,0:T(8,128)S(1)} %get-tuple-element.21), kind=kOutput, calls=%fused_computation.1 | convolution fusion | flops 1192960 | bytes 65536 | tf_op jit(solution)/shard_map/kzyrm,xqm->kzyxrq/dot_general | solution.py:299
  25.1 0.2 copy.42
  25.3 0.2 mul.123
  25.7 0.9 %fusion.3 = f32[2,8,256,27]{2,3,1,0:T(8,128)S(1)} fusion(f32[27,27,1,1]{1,0,3,2:T(8,128)S(1)} %copy-done.8, f32[27,2,8,256]{3,2,1,0:T(8,128)S(1)} %bitcast.71, f32[27]{0:T(128)S(1)} %copy-done.11, f32[2,8,27,256]{3,2,1,0:T(8,128)S(1)} %copy-done.1), kind=kOutput, calls=%fused_computation.9 | convolution fusion | flops 36163584 | bytes 1330128 | tf_op jit(solution)/shard_map/ij,jzpl->izpl/dot_general | solution.py:80
  26.8 0.6 %copy.44 = f32[28,2,8,256]{0,3,2,1:T(8,128)S(1)} copy(f32[28,2,8,256]{3,0,2,1:T(8,128)S(1)} %pad_maximum_fusion) | data formatting | bytes 917504 | tf_op jit(solution)/shard_map/concatenate | solution.py:307
  27.5 0.1 copy.45
  27.7 0.1 copy.47
  27.8 3.0 %collective-permute-start.5 = (f32[112,16]{1,0:T(8,128)S(1)}, f32[112,16]{1,0:T(8,128)S(1)}, u32[]{:S(2)}, u32[]{:S(2)}) collective-permute-start(f32[112,16]{1,0:T(8,128)S(1)} %bitcast.80), channel_id=1, source_target_pairs={{1,0},{2,1},{3,2},{4,3},{5,4},{6,5},{7,6},{8,7},{9,8},{10,9},{11,1... | collective-permute-start | bytes 21512 | tf_op jit(solution)/shard_map/ppermute | solution.py:314
  30.8 1.6 %collective-permute-done.4.left_ref = f32[112,16]{1,0:T(8,128)S(1)} collective-permute-done((f32[112,16]{1,0:T(8,128)S(1)}, f32[112,16]{1,0:T(8,128)S(1)}, u32[]{:S(2)}, u32[]{:S(2)}) %collective-permute-start.4) | collective-permute-done | bytes 7200 | tf_op jit(solution)/shard_map/ppermute | solution.py:313
  32.4 0.1 fusion.21
  32.6 0.1 fusion.22
  33.4 0.1 copy.49
  33.5 1.1 %collective-permute-start.6 = (f32[336,16]{1,0:T(8,128)S(1)}, f32[336,16]{1,0:T(8,128)S(1)}, u32[]{:S(2)}, u32[]{:S(2)}) collective-permute-start(f32[336,16]{1,0:T(8,128)S(1)} %reshape.99), channel_id=1, source_target_pairs={{0,16},{16,32},{32,48},{48,64},{64,80},{80,96},{96,112},{112,128},... | collective-permute-start | bytes 64520 | tf_op jit(solution)/shard_map/ppermute | solution.py:329
  34.8 1.1 %collective-permute-start.7 = (f32[336,16]{1,0:T(8,128)S(1)}, f32[336,16]{1,0:T(8,128)S(1)}, u32[]{:S(2)}, u32[]{:S(2)}) collective-permute-start(f32[336,16]{1,0:T(8,128)S(1)} %reshape.100), channel_id=1, source_target_pairs={{16,0},{32,16},{48,32},{64,48},{80,64},{96,80},{112,96},{128,112},... | collective-permute-start | bytes 64520 | tf_op jit(solution)/shard_map/ppermute | solution.py:330
  35.9 3.9 %collective-permute-done.6.below_ref = f32[336,16]{1,0:T(8,128)S(1)} collective-permute-done((f32[336,16]{1,0:T(8,128)S(1)}, f32[336,16]{1,0:T(8,128)S(1)}, u32[]{:S(2)}, u32[]{:S(2)}) %collective-permute-start.6) | collective-permute-done | bytes 21536 | tf_op jit(solution)/shard_map/ppermute | solution.py:329
  39.8 3.8 %collective-permute-done.7.above_ref = f32[336,16]{1,0:T(8,128)S(1)} collective-permute-done((f32[336,16]{1,0:T(8,128)S(1)}, f32[336,16]{1,0:T(8,128)S(1)}, u32[]{:S(2)}, u32[]{:S(2)}) %collective-permute-start.7) | collective-permute-done | bytes 21536 | tf_op jit(solution)/shard_map/ppermute | solution.py:330
  43.6 0.7 %copy-done.6 = f32[336,16]{1,0:T(8,128)} copy-done((f32[336,16]{1,0:T(8,128)}, f32[336,16]{1,0:T(8,128)S(1)}, u32[]{:S(2)}) %copy-start.6) | copy-done | bytes 21528
  44.2 2.8 %shard_map.74 = f32[648,128]{1,0:T(8,128)} custom-call(s32[6]{0:T(128)} %bitcast.86, f32[2,8,27,256]{3,2,1,0:T(8,128)} %bitcast.69, f32[336,16]{1,0:T(8,128)} %copy-done.5, f32[336,16]{1,0:T(8,128)} %copy-done.6, f32[112,16]{1,0:T(8,128)} %copy-done.2, f32[112,16]{1,0:T(8,128)} %copy-done.3), custom_call_target="tpu_custom_call" | custom-call | tf_op jit(solution)/shard_map/pallas_call | solution.py:257
  (58 shorter events, 1.6 us)
Async XLA Ops:
  0.0 13.2 %copy-start.9 = (s32[1,1,6]{2,1,0:T(1,128)S(1)}, s32[1,1,6]{2,1,0:T(1,128)}, u32[]{:S(2)}) copy-start(s32[1,1,6]{2,1,0:T(1,128)} %param.8) | copy-start | bytes 76
  0.0 3.9 %copy-start.10 = (s32[8]{0:T(128)S(1)}, s32[8]{0:T(128)}, u32[]{:S(2)}) copy-start(s32[8]{0:T(128)} %param.9) | copy-start | bytes 100
  0.0 24.4 %copy-start.7 = (f32[3,2,32,16]{2,3,1,0:T(8,128)S(1)}, f32[3,2,32,16]{2,3,1,0:T(8,128)}, u32[]{:S(2)}) copy-start(f32[3,2,32,16]{2,3,1,0:T(8,128)} %param.10) | copy-start | bytes 36868
  2.4 19.8 %copy-start.1 = (f32[2,8,27,256]{3,2,1,0:T(8,128)S(1)}, f32[2,8,27,256]{3,2,1,0:T(8,128)}, u32[]{:S(2)}) copy-start(f32[2,8,27,256]{3,2,1,0:T(8,128)} %get-tuple-element.7) | copy-start | bytes 1327108
  3.4 22.1 %copy-start.4 = (f32[3,2,8,256]{3,2,1,0:T(8,128)S(1)}, f32[3,2,8,256]{3,2,1,0:T(8,128)}, u32[]{:S(2)}) copy-start(f32[3,2,8,256]{3,2,1,0:T(8,128)} %get-tuple-element.8) | copy-start | bytes 147460
  4.3 1.3 %collective-permute-start = (f32[3,2,32,16]{2,3,1,0:T(8,128)S(1)}, f32[3,2,32,16]{2,3,1,0:T(8,128)S(1)}, u32[]{:S(2)}, u32[]{:S(2)}) collective-permute-start(f32[3,2,32,16]{2,3,1,0:T(8,128)S(1)} %convolution_bitcast_fusion), channel_id=1, source_target_pairs={{0,1},{1,0},{2,3},{3,2},{4,5},{5,4},{6,7},{7,6},{8,9},{9,8},{10,11... | collective-permute-start | bytes 36872 | tf_op jit(solution)/shard_map/ppermute | solution.py:23
  5.6 20.1 %copy-start.8 = (f32[27,27,1,1]{1,0,3,2:T(8,128)S(1)}, f32[27,27,1,1]{1,0,3,2:T(8,128)}, u32[]{:S(2)}) copy-start(f32[27,27,1,1]{1,0,3,2:T(8,128)} %constant.44) | copy-start | bytes 8752
  5.6 20.1 %copy-start.11 = (f32[27]{0:T(128)S(1)}, f32[27]{0:T(128)}, u32[]{:S(2)}) copy-start(f32[27]{0:T(128)} %param.11) | copy-start | bytes 328
  5.6 4.2 %collective-permute-start.1 = (f32[3,2,32,16]{2,3,1,0:T(8,128)S(1)}, f32[3,2,32,16]{2,3,1,0:T(8,128)S(1)}, u32[]{:S(2)}, u32[]{:S(2)}) collective-permute-start(f32[3,2,32,16]{2,3,1,0:T(8,128)S(1)} %add.43), channel_id=1, source_target_pairs={{0,2},{1,3},{2,0},{3,1},{4,6},{5,7},{6,4},{7,5},{8,10},{9,11},{10,... | collective-permute-start | bytes 36872 | tf_op jit(solution)/shard_map/ppermute | solution.py:23
  9.8 5.6 %collective-permute-start.2 = (f32[3,2,32,16]{2,3,1,0:T(8,128)S(1)}, f32[3,2,32,16]{2,3,1,0:T(8,128)S(1)}, u32[]{:S(2)}, u32[]{:S(2)}) collective-permute-start(f32[3,2,32,16]{2,3,1,0:T(8,128)S(1)} %add.44), channel_id=1, source_target_pairs={{0,4},{1,5},{2,6},{3,7},{4,0},{5,1},{6,2},{7,3},{8,12},{9,13},{10,... | collective-permute-start | bytes 36872 | tf_op jit(solution)/shard_map/ppermute | solution.py:23
  15.5 8.9 %collective-permute-start.3 = (f32[3,2,32,16]{2,3,1,0:T(8,128)S(1)}, f32[3,2,32,16]{2,3,1,0:T(8,128)S(1)}, u32[]{:S(2)}, u32[]{:S(2)}) collective-permute-start(f32[3,2,32,16]{2,3,1,0:T(8,128)S(1)} %add.45), channel_id=1, source_target_pairs={{0,8},{1,9},{2,10},{3,11},{4,12},{5,13},{6,14},{7,15},{8,0},{9,1},... | collective-permute-start | bytes 36872 | tf_op jit(solution)/shard_map/ppermute | solution.py:23
  26.6 1.1 %copy-start = (f32[2,8,256,27]{2,3,1,0:T(8,128)}, f32[2,8,256,27]{2,3,1,0:T(8,128)S(1)}, u32[]{:S(2)}) copy-start(f32[2,8,256,27]{2,3,1,0:T(8,128)S(1)} %fusion.3) | copy-start | bytes 1327108
  27.6 4.8 %collective-permute-start.4 = (f32[112,16]{1,0:T(8,128)S(1)}, f32[112,16]{1,0:T(8,128)S(1)}, u32[]{:S(2)}, u32[]{:S(2)}) collective-permute-start(f32[112,16]{1,0:T(8,128)S(1)} %bitcast.79), channel_id=1, source_target_pairs={{0,1},{1,2},{2,3},{3,4},{4,5},{5,6},{6,7},{7,8},{8,9},{9,10},{10,1... | collective-permute-start | bytes 21512 | tf_op jit(solution)/shard_map/ppermute | solution.py:313
  27.8 4.8 %collective-permute-start.5 = (f32[112,16]{1,0:T(8,128)S(1)}, f32[112,16]{1,0:T(8,128)S(1)}, u32[]{:S(2)}, u32[]{:S(2)}) collective-permute-start(f32[112,16]{1,0:T(8,128)S(1)} %bitcast.80), channel_id=1, source_target_pairs={{1,0},{2,1},{3,2},{4,3},{5,4},{6,5},{7,6},{8,7},{9,8},{10,9},{11,1... | collective-permute-start | bytes 21512 | tf_op jit(solution)/shard_map/ppermute | solution.py:314
  32.4 11.2 %copy-start.2 = (f32[112,16]{1,0:T(8,128)}, f32[112,16]{1,0:T(8,128)S(1)}, u32[]{:S(2)}) copy-start(f32[112,16]{1,0:T(8,128)S(1)} %collective-permute-done.4.left_ref) | copy-start | bytes 21508
  32.6 10.9 %copy-start.3 = (f32[112,16]{1,0:T(8,128)}, f32[112,16]{1,0:T(8,128)S(1)}, u32[]{:S(2)}) copy-start(f32[112,16]{1,0:T(8,128)S(1)} %collective-permute-done.5.right_ref) | copy-start | bytes 21508
  33.5 6.2 %collective-permute-start.6 = (f32[336,16]{1,0:T(8,128)S(1)}, f32[336,16]{1,0:T(8,128)S(1)}, u32[]{:S(2)}, u32[]{:S(2)}) collective-permute-start(f32[336,16]{1,0:T(8,128)S(1)} %reshape.99), channel_id=1, source_target_pairs={{0,16},{16,32},{32,48},{48,64},{64,80},{80,96},{96,112},{112,128},... | collective-permute-start | bytes 64520 | tf_op jit(solution)/shard_map/ppermute | solution.py:329
  34.8 8.8 %collective-permute-start.7 = (f32[336,16]{1,0:T(8,128)S(1)}, f32[336,16]{1,0:T(8,128)S(1)}, u32[]{:S(2)}, u32[]{:S(2)}) collective-permute-start(f32[336,16]{1,0:T(8,128)S(1)} %reshape.100), channel_id=1, source_target_pairs={{16,0},{32,16},{48,32},{64,48},{80,64},{96,80},{112,96},{128,112},... | collective-permute-start | bytes 64520 | tf_op jit(solution)/shard_map/ppermute | solution.py:330
  39.8 3.8 %copy-start.5 = (f32[336,16]{1,0:T(8,128)}, f32[336,16]{1,0:T(8,128)S(1)}, u32[]{:S(2)}) copy-start(f32[336,16]{1,0:T(8,128)S(1)} %collective-permute-done.6.below_ref) | copy-start | bytes 64516
  43.6 0.7 %copy-start.6 = (f32[336,16]{1,0:T(8,128)}, f32[336,16]{1,0:T(8,128)S(1)}, u32[]{:S(2)}) copy-start(f32[336,16]{1,0:T(8,128)S(1)} %collective-permute-done.7.above_ref) | copy-start | bytes 64516

commit v21 on v20

--- a/solution.py
+++ b/solution.py
@@ -77,7 +77,7 @@
     )
     equilibrium = equilibrium.reshape(moments.shape)
     relaxed = moments - relaxation_frequencies[:, None, None, None] * (moments - equilibrium)
-    return jnp.einsum("ij,jzpl->izpl", backward, relaxed, precision=HIGHEST)
+    return jnp.einsum("ij,jzpl->izpl", backward, relaxed, precision=lax.Precision.HIGH)
 
 
 def moments_kernel(keys_ref, forward_ref, state_ref, out_ref, wind_ref, scratch_ref):

time: 47.2 us -> 47 us (level)
  no operation moved by 1% of the time
where the time goes in v21:
time: 47 us; the launch traced here: 46.8 us
  starting transfers between devices  17.4 us (37%)
  waiting for transfers between devices  17 us (36%)
  Pallas kernels  5.23 us (11%)
  local copies, waits for them, and re-layouts  4.77 us (10%)
  matrix products  1.5 us (3%)
  other arithmetic  0.7 us (1%)
    ppermute x4, starting transfers between devices, butterfly_sum(): lax.ppermute(value, axis, [(i, i ^ stride) for i in range(count)])  12.2 us
    ppermute x4, waiting for transfers between devices, butterfly_sum(): lax.ppermute(value, axis, [(i, i ^ stride) for i in range(count)])  7.65 us
    ppermute x1, waiting for transfers between devices, on_device(): below = lax.ppermute(flat(top_row), 'curve', ahead).reshape(row_shape)  3.92 us
    ppermute x1, waiting for transfers between devices, on_device(): above = lax.ppermute(flat(bottom_row), 'curve', behind).reshape(row_shape)  3.78 us
    ppermute x1, starting transfers between devices, on_device(): lax.ppermute(flat(by_rows[:, :, :, 0, :, 0]), 'line', behind)  2.95 us
    pallas_call x1, Pallas kernels, stream(): pl.pallas_call(stream_kernel, out_shape=jax.ShapeDtypeStruct((seats * cha...  2.85 us
    pallas_call x1, Pallas kernels, cell_moments(): pl.pallas_call(moments_kernel, out_shape=(jax.ShapeDtypeStruct((levels, b...  2.38 us
    ppermute x1, waiting for transfers between devices, on_device(): lax.ppermute(flat(by_rows[:, :, :, TX - 1, :, BE - 1]), 'line', ahead)  1.62 us
  transfers between devices with their start and end apart: 8, of which 7 were waited for; matrix products, arithmetic and copies ran while one was open for 1% of the time, Pallas kernels for 0%

profile of v21, /device:TPU:30, one launch (start us, length us, event | category | flops | bytes accessed | tf_op | source)
XLA Modules:
  0.0 46.8 jit_solution(10586965071054066977)
XLA Ops:
  0.0 2.4 %shard_map.73 = (f32[2,8,27,256]{3,2,1,0:T(8,128)}, f32[3,2,8,256]{3,2,1,0:T(8,128)}) custom-call(s32[6]{0:T(128)} %bitcast.85, f32[27,27]{1,0:T(8,128)} %constant.40.clone.forward_ref, f32[648,128]{1,0:T(8,128)} %bitcast.75), custom_call_target="tpu_custom_call" | custom-call | tf_op jit(solution)/shard_map/pallas_call | solution.py:119
  2.4 1.0 %reshape.94 = f32[3,2,2,4,16,16]{5,4,3,2,1,0:T(8,128)S(1)} reshape(f32[3,2,8,256]{3,2,1,0:T(8,128)} %get-tuple-element.8) | data formatting | bytes 98304 | tf_op jit(solution)/shard_map/reshape | solution.py:294
  3.4 0.2 copy.39
  3.6 0.2 dot_general.16
  3.9 0.2 fusion.15
  4.1 0.2 convolution_bitcast_fusion
  4.4 1.2 %collective-permute-done = f32[3,2,32,16]{2,3,1,0:T(8,128)S(1)} collective-permute-done((f32[3,2,32,16]{2,3,1,0:T(8,128)S(1)}, f32[3,2,32,16]{2,3,1,0:T(8,128)S(1)}, u32[]{:S(2)}, u32[]{:S(2)}) %collective-permute-start) | collective-permute-done | bytes 12320 | tf_op jit(solution)/shard_map/ppermute | solution.py:23
  5.6 2.0 %collective-permute-start.1 = (f32[3,2,32,16]{2,3,1,0:T(8,128)S(1)}, f32[3,2,32,16]{2,3,1,0:T(8,128)S(1)}, u32[]{:S(2)}, u32[]{:S(2)}) collective-permute-start(f32[3,2,32,16]{2,3,1,0:T(8,128)S(1)} %add.43), channel_id=1, source_target_pairs={{0,2},{1,3},{2,0},{3,1},{4,6},{5,7},{6,4},{7,5},{8,10},{9,11},{10,... | collective-permute-start | bytes 36872 | tf_op jit(solution)/shard_map/ppermute | solution.py:23
  7.6 2.2 %collective-permute-done.1 = f32[3,2,32,16]{2,3,1,0:T(8,128)S(1)} collective-permute-done((f32[3,2,32,16]{2,3,1,0:T(8,128)S(1)}, f32[3,2,32,16]{2,3,1,0:T(8,128)S(1)}, u32[]{:S(2)}, u32[]{:S(2)}) %collective-permute-start.1) | collective-permute-done | bytes 12320 | tf_op jit(solution)/shard_map/ppermute | solution.py:23
  9.8 3.4 %collective-permute-start.2 = (f32[3,2,32,16]{2,3,1,0:T(8,128)S(1)}, f32[3,2,32,16]{2,3,1,0:T(8,128)S(1)}, u32[]{:S(2)}, u32[]{:S(2)}) collective-permute-start(f32[3,2,32,16]{2,3,1,0:T(8,128)S(1)} %add.44), channel_id=1, source_target_pairs={{0,4},{1,5},{2,6},{3,7},{4,0},{5,1},{6,2},{7,3},{8,12},{9,13},{10,... | collective-permute-start | bytes 36872 | tf_op jit(solution)/shard_map/ppermute | solution.py:23
  13.2 0.1 fusion.16
  13.3 2.1 %collective-permute-done.2 = f32[3,2,32,16]{2,3,1,0:T(8,128)S(1)} collective-permute-done((f32[3,2,32,16]{2,3,1,0:T(8,128)S(1)}, f32[3,2,32,16]{2,3,1,0:T(8,128)S(1)}, u32[]{:S(2)}, u32[]{:S(2)}) %collective-permute-start.2) | collective-permute-done | bytes 12320 | tf_op jit(solution)/shard_map/ppermute | solution.py:23
  15.5 6.8 %collective-permute-start.3 = (f32[3,2,32,16]{2,3,1,0:T(8,128)S(1)}, f32[3,2,32,16]{2,3,1,0:T(8,128)S(1)}, u32[]{:S(2)}, u32[]{:S(2)}) collective-permute-start(f32[3,2,32,16]{2,3,1,0:T(8,128)S(1)} %add.45), channel_id=1, source_target_pairs={{0,8},{1,9},{2,10},{3,11},{4,12},{5,13},{6,14},{7,15},{8,0},{9,1},... | collective-permute-start | bytes 36872 | tf_op jit(solution)/shard_map/ppermute | solution.py:23
  22.3 2.1 %collective-permute-done.3 = f32[3,2,32,16]{2,3,1,0:T(8,128)S(1)} collective-permute-done((f32[3,2,32,16]{2,3,1,0:T(8,128)S(1)}, f32[3,2,32,16]{2,3,1,0:T(8,128)S(1)}, u32[]{:S(2)}, u32[]{:S(2)}) %collective-permute-start.3) | collective-permute-done | bytes 12320 | tf_op jit(solution)/shard_map/ppermute | solution.py:23
  24.5 0.6 %fusion = f32[3,2,2,4,16,16]{4,5,2,1,0,3:T(8,128)S(1)} fusion(f32[3,2,2,16,16,1]{4,3,2,1,0,5:T(8,128)S(1)} %bitcast.74, f32[4,16,8]{1,2,0:T(8,128)S(1)} %get-tuple-element.22, f32[4,16,8]{1,2,0:T(8,128)S(1)} %get-tuple-element.21), kind=kOutput, calls=%fused_computation.1 | convolution fusion | flops 1192960 | bytes 65536 | tf_op jit(solution)/shard_map/kzyrm,xqm->kzyxrq/dot_general | solution.py:299
  25.1 0.2 copy.42
  25.3 0.2 mul.123
  25.7 0.7 %fusion.3 = f32[2,8,256,27]{2,3,1,0:T(8,128)S(1)} fusion(f32[27,27,1,1]{1,0,3,2:T(8,128)S(1)} %copy-done.8, f32[27,2,8,256]{3,2,1,0:T(8,128)S(1)} %bitcast.71, f32[27]{0:T(128)S(1)} %copy-done.11, f32[2,8,27,256]{3,2,1,0:T(8,128)S(1)} %copy-done.1), kind=kOutput, calls=%fused_computation.9 | convolution fusion | flops 18247680 | bytes 1330128 | tf_op jit(solution)/shard_map/ij,jzpl->izpl/dot_general | solution.py:80
  26.5 0.6 %copy.44 = f32[28,2,8,256]{0,3,2,1:T(8,128)S(1)} copy(f32[28,2,8,256]{3,0,2,1:T(8,128)S(1)} %pad_maximum_fusion) | data formatting | bytes 917504 | tf_op jit(solution)/shard_map/concatenate | solution.py:307
  27.2 0.1 copy.45
  27.5 0.1 copy.47
  27.6 3.0 %collective-permute-start.5 = (f32[112,16]{1,0:T(8,128)S(1)}, f32[112,16]{1,0:T(8,128)S(1)}, u32[]{:S(2)}, u32[]{:S(2)}) collective-permute-start(f32[112,16]{1,0:T(8,128)S(1)} %bitcast.80), channel_id=1, source_target_pairs={{1,0},{2,1},{3,2},{4,3},{5,4},{6,5},{7,6},{8,7},{9,8},{10,9},{11,1... | collective-permute-start | bytes 21512 | tf_op jit(solution)/shard_map/ppermute | solution.py:314
  30.5 1.6 %collective-permute-done.4.left_ref = f32[112,16]{1,0:T(8,128)S(1)} collective-permute-done((f32[112,16]{1,0:T(8,128)S(1)}, f32[112,16]{1,0:T(8,128)S(1)}, u32[]{:S(2)}, u32[]{:S(2)}) %collective-permute-start.4) | collective-permute-done | bytes 7200 | tf_op jit(solution)/shard_map/ppermute | solution.py:313
  32.2 0.1 fusion.21
  32.4 0.1 fusion.22
  33.2 0.1 copy.49
  33.3 1.1 %collective-permute-start.6 = (f32[336,16]{1,0:T(8,128)S(1)}, f32[336,16]{1,0:T(8,128)S(1)}, u32[]{:S(2)}, u32[]{:S(2)}) collective-permute-start(f32[336,16]{1,0:T(8,128)S(1)} %reshape.99), channel_id=1, source_target_pairs={{0,16},{16,32},{32,48},{48,64},{64,80},{80,96},{96,112},{112,128},... | collective-permute-start | bytes 64520 | tf_op jit(solution)/shard_map/ppermute | solution.py:329
  34.5 1.1 %collective-permute-start.7 = (f32[336,16]{1,0:T(8,128)S(1)}, f32[336,16]{1,0:T(8,128)S(1)}, u32[]{:S(2)}, u32[]{:S(2)}) collective-permute-start(f32[336,16]{1,0:T(8,128)S(1)} %reshape.100), channel_id=1, source_target_pairs={{16,0},{32,16},{48,32},{64,48},{80,64},{96,80},{112,96},{128,112},... | collective-permute-start | bytes 64520 | tf_op jit(solution)/shard_map/ppermute | solution.py:330
  35.6 3.9 %collective-permute-done.6.below_ref = f32[336,16]{1,0:T(8,128)S(1)} collective-permute-done((f32[336,16]{1,0:T(8,128)S(1)}, f32[336,16]{1,0:T(8,128)S(1)}, u32[]{:S(2)}, u32[]{:S(2)}) %collective-permute-start.6) | collective-permute-done | bytes 21536 | tf_op jit(solution)/shard_map/ppermute | solution.py:329
  39.5 3.8 %collective-permute-done.7.above_ref = f32[336,16]{1,0:T(8,128)S(1)} collective-permute-done((f32[336,16]{1,0:T(8,128)S(1)}, f32[336,16]{1,0:T(8,128)S(1)}, u32[]{:S(2)}, u32[]{:S(2)}) %collective-permute-start.7) | collective-permute-done | bytes 21536 | tf_op jit(solution)/shard_map/ppermute | solution.py:330
  43.3 0.7 %copy-done.6 = f32[336,16]{1,0:T(8,128)} copy-done((f32[336,16]{1,0:T(8,128)}, f32[336,16]{1,0:T(8,128)S(1)}, u32[]{:S(2)}) %copy-start.6) | copy-done | bytes 21528
  44.0 2.8 %shard_map.74 = f32[648,128]{1,0:T(8,128)} custom-call(s32[6]{0:T(128)} %bitcast.86, f32[2,8,27,256]{3,2,1,0:T(8,128)} %bitcast.69, f32[336,16]{1,0:T(8,128)} %copy-done.5, f32[336,16]{1,0:T(8,128)} %copy-done.6, f32[112,16]{1,0:T(8,128)} %copy-done.2, f32[112,16]{1,0:T(8,128)} %copy-done.3), custom_call_target="tpu_custom_call" | custom-call | tf_op jit(solution)/shard_map/pallas_call | solution.py:257
  (58 shorter events, 1.6 us)
Async XLA Ops:
  0.0 13.2 %copy-start.9 = (s32[1,1,6]{2,1,0:T(1,128)S(1)}, s32[1,1,6]{2,1,0:T(1,128)}, u32[]{:S(2)}) copy-start(s32[1,1,6]{2,1,0:T(1,128)} %param.8) | copy-start | bytes 76
  0.0 3.9 %copy-start.10 = (s32[8]{0:T(128)S(1)}, s32[8]{0:T(128)}, u32[]{:S(2)}) copy-start(s32[8]{0:T(128)} %param.9) | copy-start | bytes 100
  0.0 24.4 %copy-start.7 = (f32[3,2,32,16]{2,3,1,0:T(8,128)S(1)}, f32[3,2,32,16]{2,3,1,0:T(8,128)}, u32[]{:S(2)}) copy-start(f32[3,2,32,16]{2,3,1,0:T(8,128)} %param.10) | copy-start | bytes 36868
  2.4 19.8 %copy-start.1 = (f32[2,8,27,256]{3,2,1,0:T(8,128)S(1)}, f32[2,8,27,256]{3,2,1,0:T(8,128)}, u32[]{:S(2)}) copy-start(f32[2,8,27,256]{3,2,1,0:T(8,128)} %get-tuple-element.7) | copy-start | bytes 1327108
  3.4 22.1 %copy-start.4 = (f32[3,2,8,256]{3,2,1,0:T(8,128)S(1)}, f32[3,2,8,256]{3,2,1,0:T(8,128)}, u32[]{:S(2)}) copy-start(f32[3,2,8,256]{3,2,1,0:T(8,128)} %get-tuple-element.8) | copy-start | bytes 147460
  4.3 1.3 %collective-permute-start = (f32[3,2,32,16]{2,3,1,0:T(8,128)S(1)}, f32[3,2,32,16]{2,3,1,0:T(8,128)S(1)}, u32[]{:S(2)}, u32[]{:S(2)}) collective-permute-start(f32[3,2,32,16]{2,3,1,0:T(8,128)S(1)} %convolution_bitcast_fusion), channel_id=1, source_target_pairs={{0,1},{1,0},{2,3},{3,2},{4,5},{5,4},{6,7},{7,6},{8,9},{9,8},{10,11... | collective-permute-start | bytes 36872 | tf_op jit(solution)/shard_map/ppermute | solution.py:23
  5.6 20.1 %copy-start.8 = (f32[27,27,1,1]{1,0,3,2:T(8,128)S(1)}, f32[27,27,1,1]{1,0,3,2:T(8,128)}, u32[]{:S(2)}) copy-start(f32[27,27,1,1]{1,0,3,2:T(8,128)} %constant.44) | copy-start | bytes 8752
  5.6 20.1 %copy-start.11 = (f32[27]{0:T(128)S(1)}, f32[27]{0:T(128)}, u32[]{:S(2)}) copy-start(f32[27]{0:T(128)} %param.11) | copy-start | bytes 328
  5.6 4.2 %collective-permute-start.1 = (f32[3,2,32,16]{2,3,1,0:T(8,128)S(1)}, f32[3,2,32,16]{2,3,1,0:T(8,128)S(1)}, u32[]{:S(2)}, u32[]{:S(2)}) collective-permute-start(f32[3,2,32,16]{2,3,1,0:T(8,128)S(1)} %add.43), channel_id=1, source_target_pairs={{0,2},{1,3},{2,0},{3,1},{4,6},{5,7},{6,4},{7,5},{8,10},{9,11},{10,... | collective-permute-start | bytes 36872 | tf_op jit(solution)/shard_map/ppermute | solution.py:23
  9.8 5.6 %collective-permute-start.2 = (f32[3,2,32,16]{2,3,1,0:T(8,128)S(1)}, f32[3,2,32,16]{2,3,1,0:T(8,128)S(1)}, u32[]{:S(2)}, u32[]{:S(2)}) collective-permute-start(f32[3,2,32,16]{2,3,1,0:T(8,128)S(1)} %add.44), channel_id=1, source_target_pairs={{0,4},{1,5},{2,6},{3,7},{4,0},{5,1},{6,2},{7,3},{8,12},{9,13},{10,... | collective-permute-start | bytes 36872 | tf_op jit(solution)/shard_map/ppermute | solution.py:23
  15.5 8.9 %collective-permute-start.3 = (f32[3,2,32,16]{2,3,1,0:T(8,128)S(1)}, f32[3,2,32,16]{2,3,1,0:T(8,128)S(1)}, u32[]{:S(2)}, u32[]{:S(2)}) collective-permute-start(f32[3,2,32,16]{2,3,1,0:T(8,128)S(1)} %add.45), channel_id=1, source_target_pairs={{0,8},{1,9},{2,10},{3,11},{4,12},{5,13},{6,14},{7,15},{8,0},{9,1},... | collective-permute-start | bytes 36872 | tf_op jit(solution)/shard_map/ppermute | solution.py:23
  26.4 1.1 %copy-start = (f32[2,8,256,27]{2,3,1,0:T(8,128)}, f32[2,8,256,27]{2,3,1,0:T(8,128)S(1)}, u32[]{:S(2)}) copy-start(f32[2,8,256,27]{2,3,1,0:T(8,128)S(1)} %fusion.3) | copy-start | bytes 1327108
  27.3 4.8 %collective-permute-start.4 = (f32[112,16]{1,0:T(8,128)S(1)}, f32[112,16]{1,0:T(8,128)S(1)}, u32[]{:S(2)}, u32[]{:S(2)}) collective-permute-start(f32[112,16]{1,0:T(8,128)S(1)} %bitcast.79), channel_id=1, source_target_pairs={{0,1},{1,2},{2,3},{3,4},{4,5},{5,6},{6,7},{7,8},{8,9},{9,10},{10,1... | collective-permute-start | bytes 21512 | tf_op jit(solution)/shard_map/ppermute | solution.py:313
  27.6 4.8 %collective-permute-start.5 = (f32[112,16]{1,0:T(8,128)S(1)}, f32[112,16]{1,0:T(8,128)S(1)}, u32[]{:S(2)}, u32[]{:S(2)}) collective-permute-start(f32[112,16]{1,0:T(8,128)S(1)} %bitcast.80), channel_id=1, source_target_pairs={{1,0},{2,1},{3,2},{4,3},{5,4},{6,5},{7,6},{8,7},{9,8},{10,9},{11,1... | collective-permute-start | bytes 21512 | tf_op jit(solution)/shard_map/ppermute | solution.py:314
  32.2 11.2 %copy-start.2 = (f32[112,16]{1,0:T(8,128)}, f32[112,16]{1,0:T(8,128)S(1)}, u32[]{:S(2)}) copy-start(f32[112,16]{1,0:T(8,128)S(1)} %collective-permute-done.4.left_ref) | copy-start | bytes 21508
  32.4 10.9 %copy-start.3 = (f32[112,16]{1,0:T(8,128)}, f32[112,16]{1,0:T(8,128)S(1)}, u32[]{:S(2)}) copy-start(f32[112,16]{1,0:T(8,128)S(1)} %collective-permute-done.5.right_ref) | copy-start | bytes 21508
  33.3 6.2 %collective-permute-start.6 = (f32[336,16]{1,0:T(8,128)S(1)}, f32[336,16]{1,0:T(8,128)S(1)}, u32[]{:S(2)}, u32[]{:S(2)}) collective-permute-start(f32[336,16]{1,0:T(8,128)S(1)} %reshape.99), channel_id=1, source_target_pairs={{0,16},{16,32},{32,48},{48,64},{64,80},{80,96},{96,112},{112,128},... | collective-permute-start | bytes 64520 | tf_op jit(solution)/shard_map/ppermute | solution.py:329
  34.5 8.8 %collective-permute-start.7 = (f32[336,16]{1,0:T(8,128)S(1)}, f32[336,16]{1,0:T(8,128)S(1)}, u32[]{:S(2)}, u32[]{:S(2)}) collective-permute-start(f32[336,16]{1,0:T(8,128)S(1)} %reshape.100), channel_id=1, source_target_pairs={{16,0},{32,16},{48,32},{64,48},{80,64},{96,80},{112,96},{128,112},... | collective-permute-start | bytes 64520 | tf_op jit(solution)/shard_map/ppermute | solution.py:330
  39.5 3.8 %copy-start.5 = (f32[336,16]{1,0:T(8,128)}, f32[336,16]{1,0:T(8,128)S(1)}, u32[]{:S(2)}) copy-start(f32[336,16]{1,0:T(8,128)S(1)} %collective-permute-done.6.below_ref) | copy-start | bytes 64516
  43.3 0.7 %copy-start.6 = (f32[336,16]{1,0:T(8,128)}, f32[336,16]{1,0:T(8,128)S(1)}, u32[]{:S(2)}) copy-start(f32[336,16]{1,0:T(8,128)S(1)} %collective-permute-done.7.above_ref) | copy-start | bytes 64516

commit v22 on v21

--- a/solution.py
+++ b/solution.py
@@ -91,7 +91,7 @@
             for chunk in range(chunks)
         ]
         scratch_ref[seat_number] = jnp.dot(
-            forward, jnp.concatenate(pieces, axis=1), precision=HIGHEST,
+            forward, jnp.concatenate(pieces, axis=1), precision=lax.Precision.HIGH,
             preferred_element_type=jnp.float32,
         )
     for block in range(blocks):

time: 47 us -> 46.8 us (level)
  no operation moved by 1% of the time
where the time goes in v22:
time: 46.8 us; the launch traced here: 46.7 us
  starting transfers between devices  17.3 us (37%)
  waiting for transfers between devices  17 us (36%)
  Pallas kernels  5.08 us (11%)
  local copies, waits for them, and re-layouts  4.77 us (10%)
  matrix products  1.5 us (3%)
  other arithmetic  0.7 us (1%)
    ppermute x4, starting transfers between devices, butterfly_sum(): lax.ppermute(value, axis, [(i, i ^ stride) for i in range(count)])  12.2 us
    ppermute x4, waiting for transfers between devices, butterfly_sum(): lax.ppermute(value, axis, [(i, i ^ stride) for i in range(count)])  7.67 us
    ppermute x1, waiting for transfers between devices, on_device(): below = lax.ppermute(flat(top_row), 'curve', ahead).reshape(row_shape)  3.92 us
    ppermute x1, waiting for transfers between devices, on_device(): above = lax.ppermute(flat(bottom_row), 'curve', behind).reshape(row_shape)  3.77 us
    ppermute x1, starting transfers between devices, on_device(): lax.ppermute(flat(by_rows[:, :, :, 0, :, 0]), 'line', behind)  2.95 us
    pallas_call x1, Pallas kernels, stream(): pl.pallas_call(stream_kernel, out_shape=jax.ShapeDtypeStruct((seats * cha...  2.84 us
    pallas_call x1, Pallas kernels, cell_moments(): pl.pallas_call(moments_kernel, out_shape=(jax.ShapeDtypeStruct((levels, b...  2.23 us
    ppermute x1, waiting for transfers between devices, on_device(): lax.ppermute(flat(by_rows[:, :, :, TX - 1, :, BE - 1]), 'line', ahead)  1.62 us
  transfers between devices with their start and end apart: 8, of which 7 were waited for; matrix products, arithmetic and copies ran while one was open for 1% of the time, Pallas kernels for 0%

profile of v22, /device:TPU:30, one launch (start us, length us, event | category | flops | bytes accessed | tf_op | source)
XLA Modules:
  0.0 46.7 jit_solution(8785746751184370036)
XLA Ops:
  0.0 2.2 %shard_map.73 = (f32[2,8,27,256]{3,2,1,0:T(8,128)}, f32[3,2,8,256]{3,2,1,0:T(8,128)}) custom-call(s32[6]{0:T(128)} %bitcast.85, f32[27,27]{1,0:T(8,128)} %constant.40.clone.forward_ref, f32[648,128]{1,0:T(8,128)} %bitcast.75), custom_call_target="tpu_custom_call" | custom-call | tf_op jit(solution)/shard_map/pallas_call | solution.py:119
  2.2 1.0 %reshape.94 = f32[3,2,2,4,16,16]{5,4,3,2,1,0:T(8,128)S(1)} reshape(f32[3,2,8,256]{3,2,1,0:T(8,128)} %get-tuple-element.8) | data formatting | bytes 98304 | tf_op jit(solution)/shard_map/reshape | solution.py:294
  3.3 0.2 copy.39
  3.5 0.2 dot_general.16
  3.7 0.2 fusion.15
  3.9 0.2 convolution_bitcast_fusion
  4.2 1.2 %collective-permute-done = f32[3,2,32,16]{2,3,1,0:T(8,128)S(1)} collective-permute-done((f32[3,2,32,16]{2,3,1,0:T(8,128)S(1)}, f32[3,2,32,16]{2,3,1,0:T(8,128)S(1)}, u32[]{:S(2)}, u32[]{:S(2)}) %collective-permute-start) | collective-permute-done | bytes 12320 | tf_op jit(solution)/shard_map/ppermute | solution.py:23
  5.5 2.0 %collective-permute-start.1 = (f32[3,2,32,16]{2,3,1,0:T(8,128)S(1)}, f32[3,2,32,16]{2,3,1,0:T(8,128)S(1)}, u32[]{:S(2)}, u32[]{:S(2)}) collective-permute-start(f32[3,2,32,16]{2,3,1,0:T(8,128)S(1)} %add.43), channel_id=1, source_target_pairs={{0,2},{1,3},{2,0},{3,1},{4,6},{5,7},{6,4},{7,5},{8,10},{9,11},{10,... | collective-permute-start | bytes 36872 | tf_op jit(solution)/shard_map/ppermute | solution.py:23
  7.5 2.2 %collective-permute-done.1 = f32[3,2,32,16]{2,3,1,0:T(8,128)S(1)} collective-permute-done((f32[3,2,32,16]{2,3,1,0:T(8,128)S(1)}, f32[3,2,32,16]{2,3,1,0:T(8,128)S(1)}, u32[]{:S(2)}, u32[]{:S(2)}) %collective-permute-start.1) | collective-permute-done | bytes 12320 | tf_op jit(solution)/shard_map/ppermute | solution.py:23
  9.7 3.4 %collective-permute-start.2 = (f32[3,2,32,16]{2,3,1,0:T(8,128)S(1)}, f32[3,2,32,16]{2,3,1,0:T(8,128)S(1)}, u32[]{:S(2)}, u32[]{:S(2)}) collective-permute-start(f32[3,2,32,16]{2,3,1,0:T(8,128)S(1)} %add.44), channel_id=1, source_target_pairs={{0,4},{1,5},{2,6},{3,7},{4,0},{5,1},{6,2},{7,3},{8,12},{9,13},{10,... | collective-permute-start | bytes 36872 | tf_op jit(solution)/shard_map/ppermute | solution.py:23
  13.0 0.1 fusion.16
  13.2 2.1 %collective-permute-done.2 = f32[3,2,32,16]{2,3,1,0:T(8,128)S(1)} collective-permute-done((f32[3,2,32,16]{2,3,1,0:T(8,128)S(1)}, f32[3,2,32,16]{2,3,1,0:T(8,128)S(1)}, u32[]{:S(2)}, u32[]{:S(2)}) %collective-permute-start.2) | collective-permute-done | bytes 12320 | tf_op jit(solution)/shard_map/ppermute | solution.py:23
  15.3 6.7 %collective-permute-start.3 = (f32[3,2,32,16]{2,3,1,0:T(8,128)S(1)}, f32[3,2,32,16]{2,3,1,0:T(8,128)S(1)}, u32[]{:S(2)}, u32[]{:S(2)}) collective-permute-start(f32[3,2,32,16]{2,3,1,0:T(8,128)S(1)} %add.45), channel_id=1, source_target_pairs={{0,8},{1,9},{2,10},{3,11},{4,12},{5,13},{6,14},{7,15},{8,0},{9,1},... | collective-permute-start | bytes 36872 | tf_op jit(solution)/shard_map/ppermute | solution.py:23
  22.1 2.1 %collective-permute-done.3 = f32[3,2,32,16]{2,3,1,0:T(8,128)S(1)} collective-permute-done((f32[3,2,32,16]{2,3,1,0:T(8,128)S(1)}, f32[3,2,32,16]{2,3,1,0:T(8,128)S(1)}, u32[]{:S(2)}, u32[]{:S(2)}) %collective-permute-start.3) | collective-permute-done | bytes 12320 | tf_op jit(solution)/shard_map/ppermute | solution.py:23
  24.3 0.6 %fusion = f32[3,2,2,4,16,16]{4,5,2,1,0,3:T(8,128)S(1)} fusion(f32[3,2,2,16,16,1]{4,3,2,1,0,5:T(8,128)S(1)} %bitcast.74, f32[4,16,8]{1,2,0:T(8,128)S(1)} %get-tuple-element.22, f32[4,16,8]{1,2,0:T(8,128)S(1)} %get-tuple-element.21), kind=kOutput, calls=%fused_computation.1 | convolution fusion | flops 1192960 | bytes 65536 | tf_op jit(solution)/shard_map/kzyrm,xqm->kzyxrq/dot_general | solution.py:299
  24.9 0.2 copy.42
  25.1 0.2 mul.123
  25.5 0.7 %fusion.3 = f32[2,8,256,27]{2,3,1,0:T(8,128)S(1)} fusion(f32[27,27,1,1]{1,0,3,2:T(8,128)S(1)} %copy-done.8, f32[27,2,8,256]{3,2,1,0:T(8,128)S(1)} %bitcast.71, f32[27]{0:T(128)S(1)} %copy-done.11, f32[2,8,27,256]{3,2,1,0:T(8,128)S(1)} %copy-done.1), kind=kOutput, calls=%fused_computation.9 | convolution fusion | flops 18247680 | bytes 1330128 | tf_op jit(solution)/shard_map/ij,jzpl->izpl/dot_general | solution.py:80
  26.4 0.6 %copy.44 = f32[28,2,8,256]{0,3,2,1:T(8,128)S(1)} copy(f32[28,2,8,256]{3,0,2,1:T(8,128)S(1)} %pad_maximum_fusion) | data formatting | bytes 917504 | tf_op jit(solution)/shard_map/concatenate | solution.py:307
  27.1 0.1 copy.45
  27.3 0.1 copy.47
  27.4 3.0 %collective-permute-start.5 = (f32[112,16]{1,0:T(8,128)S(1)}, f32[112,16]{1,0:T(8,128)S(1)}, u32[]{:S(2)}, u32[]{:S(2)}) collective-permute-start(f32[112,16]{1,0:T(8,128)S(1)} %bitcast.80), channel_id=1, source_target_pairs={{1,0},{2,1},{3,2},{4,3},{5,4},{6,5},{7,6},{8,7},{9,8},{10,9},{11,1... | collective-permute-start | bytes 21512 | tf_op jit(solution)/shard_map/ppermute | solution.py:314
  30.4 1.6 %collective-permute-done.4.left_ref = f32[112,16]{1,0:T(8,128)S(1)} collective-permute-done((f32[112,16]{1,0:T(8,128)S(1)}, f32[112,16]{1,0:T(8,128)S(1)}, u32[]{:S(2)}, u32[]{:S(2)}) %collective-permute-start.4) | collective-permute-done | bytes 7200 | tf_op jit(solution)/shard_map/ppermute | solution.py:313
  32.0 0.1 fusion.21
  32.2 0.1 fusion.22
  33.0 0.1 copy.49
  33.2 1.1 %collective-permute-start.6 = (f32[336,16]{1,0:T(8,128)S(1)}, f32[336,16]{1,0:T(8,128)S(1)}, u32[]{:S(2)}, u32[]{:S(2)}) collective-permute-start(f32[336,16]{1,0:T(8,128)S(1)} %reshape.99), channel_id=1, source_target_pairs={{0,16},{16,32},{32,48},{48,64},{64,80},{80,96},{96,112},{112,128},... | collective-permute-start | bytes 64520 | tf_op jit(solution)/shard_map/ppermute | solution.py:329
  34.4 1.1 %collective-permute-start.7 = (f32[336,16]{1,0:T(8,128)S(1)}, f32[336,16]{1,0:T(8,128)S(1)}, u32[]{:S(2)}, u32[]{:S(2)}) collective-permute-start(f32[336,16]{1,0:T(8,128)S(1)} %reshape.100), channel_id=1, source_target_pairs={{16,0},{32,16},{48,32},{64,48},{80,64},{96,80},{112,96},{128,112},... | collective-permute-start | bytes 64520 | tf_op jit(solution)/shard_map/ppermute | solution.py:330
  35.5 3.9 %collective-permute-done.6.below_ref = f32[336,16]{1,0:T(8,128)S(1)} collective-permute-done((f32[336,16]{1,0:T(8,128)S(1)}, f32[336,16]{1,0:T(8,128)S(1)}, u32[]{:S(2)}, u32[]{:S(2)}) %collective-permute-start.6) | collective-permute-done | bytes 21536 | tf_op jit(solution)/shard_map/ppermute | solution.py:329
  39.4 3.8 %collective-permute-done.7.above_ref = f32[336,16]{1,0:T(8,128)S(1)} collective-permute-done((f32[336,16]{1,0:T(8,128)S(1)}, f32[336,16]{1,0:T(8,128)S(1)}, u32[]{:S(2)}, u32[]{:S(2)}) %collective-permute-start.7) | collective-permute-done | bytes 21536 | tf_op jit(solution)/shard_map/ppermute | solution.py:330
  43.2 0.7 %copy-done.6 = f32[336,16]{1,0:T(8,128)} copy-done((f32[336,16]{1,0:T(8,128)}, f32[336,16]{1,0:T(8,128)S(1)}, u32[]{:S(2)}) %copy-start.6) | copy-done | bytes 21528
  43.8 2.8 %shard_map.74 = f32[648,128]{1,0:T(8,128)} custom-call(s32[6]{0:T(128)} %bitcast.86, f32[2,8,27,256]{3,2,1,0:T(8,128)} %bitcast.69, f32[336,16]{1,0:T(8,128)} %copy-done.5, f32[336,16]{1,0:T(8,128)} %copy-done.6, f32[112,16]{1,0:T(8,128)} %copy-done.2, f32[112,16]{1,0:T(8,128)} %copy-done.3), custom_call_target="tpu_custom_call" | custom-call | tf_op jit(solution)/shard_map/pallas_call | solution.py:257
  (58 shorter events, 1.6 us)
Async XLA Ops:
  0.0 13.0 %copy-start.9 = (s32[1,1,6]{2,1,0:T(1,128)S(1)}, s32[1,1,6]{2,1,0:T(1,128)}, u32[]{:S(2)}) copy-start(s32[1,1,6]{2,1,0:T(1,128)} %param.8) | copy-start | bytes 76
  0.0 3.7 %copy-start.10 = (s32[8]{0:T(128)S(1)}, s32[8]{0:T(128)}, u32[]{:S(2)}) copy-start(s32[8]{0:T(128)} %param.9) | copy-start | bytes 100
  0.0 24.2 %copy-start.7 = (f32[3,2,32,16]{2,3,1,0:T(8,128)S(1)}, f32[3,2,32,16]{2,3,1,0:T(8,128)}, u32[]{:S(2)}) copy-start(f32[3,2,32,16]{2,3,1,0:T(8,128)} %param.10) | copy-start | bytes 36868
  2.2 19.8 %copy-start.1 = (f32[2,8,27,256]{3,2,1,0:T(8,128)S(1)}, f32[2,8,27,256]{3,2,1,0:T(8,128)}, u32[]{:S(2)}) copy-start(f32[2,8,27,256]{3,2,1,0:T(8,128)} %get-tuple-element.7) | copy-start | bytes 1327108
  3.3 22.1 %copy-start.4 = (f32[3,2,8,256]{3,2,1,0:T(8,128)S(1)}, f32[3,2,8,256]{3,2,1,0:T(8,128)}, u32[]{:S(2)}) copy-start(f32[3,2,8,256]{3,2,1,0:T(8,128)} %get-tuple-element.8) | copy-start | bytes 147460
  4.1 1.3 %collective-permute-start = (f32[3,2,32,16]{2,3,1,0:T(8,128)S(1)}, f32[3,2,32,16]{2,3,1,0:T(8,128)S(1)}, u32[]{:S(2)}, u32[]{:S(2)}) collective-permute-start(f32[3,2,32,16]{2,3,1,0:T(8,128)S(1)} %convolution_bitcast_fusion), channel_id=1, source_target_pairs={{0,1},{1,0},{2,3},{3,2},{4,5},{5,4},{6,7},{7,6},{8,9},{9,8},{10,11... | collective-permute-start | bytes 36872 | tf_op jit(solution)/shard_map/ppermute | solution.py:23
  5.5 20.1 %copy-start.8 = (f32[27,27,1,1]{1,0,3,2:T(8,128)S(1)}, f32[27,27,1,1]{1,0,3,2:T(8,128)}, u32[]{:S(2)}) copy-start(f32[27,27,1,1]{1,0,3,2:T(8,128)} %constant.44) | copy-start | bytes 8752
  5.5 20.1 %copy-start.11 = (f32[27]{0:T(128)S(1)}, f32[27]{0:T(128)}, u32[]{:S(2)}) copy-start(f32[27]{0:T(128)} %param.11) | copy-start | bytes 328
  5.5 4.2 %collective-permute-start.1 = (f32[3,2,32,16]{2,3,1,0:T(8,128)S(1)}, f32[3,2,32,16]{2,3,1,0:T(8,128)S(1)}, u32[]{:S(2)}, u32[]{:S(2)}) collective-permute-start(f32[3,2,32,16]{2,3,1,0:T(8,128)S(1)} %add.43), channel_id=1, source_target_pairs={{0,2},{1,3},{2,0},{3,1},{4,6},{5,7},{6,4},{7,5},{8,10},{9,11},{10,... | collective-permute-start | bytes 36872 | tf_op jit(solution)/shard_map/ppermute | solution.py:23
  9.7 5.6 %collective-permute-start.2 = (f32[3,2,32,16]{2,3,1,0:T(8,128)S(1)}, f32[3,2,32,16]{2,3,1,0:T(8,128)S(1)}, u32[]{:S(2)}, u32[]{:S(2)}) collective-permute-start(f32[3,2,32,16]{2,3,1,0:T(8,128)S(1)} %add.44), channel_id=1, source_target_pairs={{0,4},{1,5},{2,6},{3,7},{4,0},{5,1},{6,2},{7,3},{8,12},{9,13},{10,... | collective-permute-start | bytes 36872 | tf_op jit(solution)/shard_map/ppermute | solution.py:23
  15.3 8.9 %collective-permute-start.3 = (f32[3,2,32,16]{2,3,1,0:T(8,128)S(1)}, f32[3,2,32,16]{2,3,1,0:T(8,128)S(1)}, u32[]{:S(2)}, u32[]{:S(2)}) collective-permute-start(f32[3,2,32,16]{2,3,1,0:T(8,128)S(1)} %add.45), channel_id=1, source_target_pairs={{0,8},{1,9},{2,10},{3,11},{4,12},{5,13},{6,14},{7,15},{8,0},{9,1},... | collective-permute-start | bytes 36872 | tf_op jit(solution)/shard_map/ppermute | solution.py:23
  26.2 1.1 %copy-start = (f32[2,8,256,27]{2,3,1,0:T(8,128)}, f32[2,8,256,27]{2,3,1,0:T(8,128)S(1)}, u32[]{:S(2)}) copy-start(f32[2,8,256,27]{2,3,1,0:T(8,128)S(1)} %fusion.3) | copy-start | bytes 1327108
  27.2 4.8 %collective-permute-start.4 = (f32[112,16]{1,0:T(8,128)S(1)}, f32[112,16]{1,0:T(8,128)S(1)}, u32[]{:S(2)}, u32[]{:S(2)}) collective-permute-start(f32[112,16]{1,0:T(8,128)S(1)} %bitcast.79), channel_id=1, source_target_pairs={{0,1},{1,2},{2,3},{3,4},{4,5},{5,6},{6,7},{7,8},{8,9},{9,10},{10,1... | collective-permute-start | bytes 21512 | tf_op jit(solution)/shard_map/ppermute | solution.py:313
  27.4 4.8 %collective-permute-start.5 = (f32[112,16]{1,0:T(8,128)S(1)}, f32[112,16]{1,0:T(8,128)S(1)}, u32[]{:S(2)}, u32[]{:S(2)}) collective-permute-start(f32[112,16]{1,0:T(8,128)S(1)} %bitcast.80), channel_id=1, source_target_pairs={{1,0},{2,1},{3,2},{4,3},{5,4},{6,5},{7,6},{8,7},{9,8},{10,9},{11,1... | collective-permute-start | bytes 21512 | tf_op jit(solution)/shard_map/ppermute | solution.py:314
  32.0 11.2 %copy-start.2 = (f32[112,16]{1,0:T(8,128)}, f32[112,16]{1,0:T(8,128)S(1)}, u32[]{:S(2)}) copy-start(f32[112,16]{1,0:T(8,128)S(1)} %collective-permute-done.4.left_ref) | copy-start | bytes 21508
  32.2 10.9 %copy-start.3 = (f32[112,16]{1,0:T(8,128)}, f32[112,16]{1,0:T(8,128)S(1)}, u32[]{:S(2)}) copy-start(f32[112,16]{1,0:T(8,128)S(1)} %collective-permute-done.5.right_ref) | copy-start | bytes 21508
  33.2 6.2 %collective-permute-start.6 = (f32[336,16]{1,0:T(8,128)S(1)}, f32[336,16]{1,0:T(8,128)S(1)}, u32[]{:S(2)}, u32[]{:S(2)}) collective-permute-start(f32[336,16]{1,0:T(8,128)S(1)} %reshape.99), channel_id=1, source_target_pairs={{0,16},{16,32},{32,48},{48,64},{64,80},{80,96},{96,112},{112,128},... | collective-permute-start | bytes 64520 | tf_op jit(solution)/shard_map/ppermute | solution.py:329
  34.4 8.8 %collective-permute-start.7 = (f32[336,16]{1,0:T(8,128)S(1)}, f32[336,16]{1,0:T(8,128)S(1)}, u32[]{:S(2)}, u32[]{:S(2)}) collective-permute-start(f32[336,16]{1,0:T(8,128)S(1)} %reshape.100), channel_id=1, source_target_pairs={{16,0},{32,16},{48,32},{64,48},{80,64},{96,80},{112,96},{128,112},... | collective-permute-start | bytes 64520 | tf_op jit(solution)/shard_map/ppermute | solution.py:330
  39.4 3.8 %copy-start.5 = (f32[336,16]{1,0:T(8,128)}, f32[336,16]{1,0:T(8,128)S(1)}, u32[]{:S(2)}) copy-start(f32[336,16]{1,0:T(8,128)S(1)} %collective-permute-done.6.below_ref) | copy-start | bytes 64516
  43.2 0.7 %copy-start.6 = (f32[336,16]{1,0:T(8,128)}, f32[336,16]{1,0:T(8,128)S(1)}, u32[]{:S(2)}) copy-start(f32[336,16]{1,0:T(8,128)S(1)} %collective-permute-done.7.above_ref) | copy-start | bytes 64516
